TPU v7x, 32 devices: a whole 2x2x4 slice. The times are simulated.
32 devices in a mesh: groups: 2 (over y), space: 8 (over z, core), member: 2 (over x).
Axes of the slice: x: 2, y: 2, z: 4, core: 2. Of those that a mesh axis runs over, the one named last changes fastest.
Arguments:
- features: bfloat16 [4, 256, 128, 256], P(('groups', 'member'), None, 'space'), parts along dimension 0, may hold values from -6 to 6
- views: int32 [4], P('groups'), parts along dimension 0, may hold values from 8 to 29
- conv_first: bfloat16 [3, 3, 256, 256], replicated, may hold values from -0.125 to 0.125
- bias_first: float32 [256], replicated, may hold values from -3 to 3
- conv_second: bfloat16 [3, 3, 256, 256], replicated, may hold values from -0.125 to 0.125
- bias_second: float32 [256], replicated, may hold values from -3 to 3
- classify: bfloat16 [19, 256], replicated, may hold values from -0.375 to 0.375
- class_bias: float32 [19], replicated, may hold values from -3 to 3
Outputs:
- ensemble_logits: float32 [1024, 19, 1024], P(('groups', 'space', 'member')), parts along dimension 0
There are 2 independent parts, one for each index of `groups`. A program takes and returns all parts, laid end to end along the dimension named above; an argument that names none is the same for every part. Nothing has to cross between parts.
All inputs are finite; a program needn't handle non-finite values.
Results may differ from a plain program's by a relative error of at most 0.0035.
Values may be sent and summed in bfloat16 or wider, within the bound.
No kernel may reach another device: no remote copies, remote signals or barrier semaphores. Data moves between devices by JAX's collectives and lax.ppermute only.
A program may use at most 128 MiB of HBM per device.

v0:
```python
import jax
import jax.numpy as jnp
from jax import lax
from jax.sharding import PartitionSpec as P

UP = 4


def with_halo(block, sides, width):
    for axis, dim in sides:
        count = lax.axis_size(axis)
        forward = [(i, i + 1) for i in range(count - 1)]
        backward = [(target, source) for source, target in forward]
        low = lax.ppermute(
            lax.slice_in_dim(block, block.shape[dim] - width, None, axis=dim), axis, forward
        )
        high = lax.ppermute(lax.slice_in_dim(block, 0, width, axis=dim), axis, backward)
        block = jnp.concatenate([low, block, high], axis=dim)
    return block


def resize_matrix(positions, out_len, valid, in_len):
    numer = (2 * positions + 1) * valid - out_len
    denom = 2 * out_len
    lower = numer // denom
    frac = (numer - lower * denom).astype(jnp.float32) / denom
    below = numer < 0
    frac = jnp.where(below, jnp.float32(0.0), frac)
    lower = jnp.where(below, 0, lower)
    top_index = valid - 1
    over = lower >= top_index
    frac = jnp.where(over, jnp.float32(0.0), frac)
    lower = jnp.where(over, top_index, lower)
    columns = jnp.arange(in_len, dtype=jnp.int32)
    first = jnp.where(columns[None, :] == lower[:, None], 1.0 - frac[:, None], jnp.float32(0.0))
    second = jnp.where(columns[None, :] == lower[:, None] + 1, frac[:, None], jnp.float32(0.0))
    return (first + second).astype(jnp.bfloat16)


def convolve(field, weights):
    height, width = (field.shape[1], field.shape[2])
    padded = with_halo(field, (("space", 1),), 1)
    padded = jnp.pad(padded, ((0, 0), (0, 0), (1, 1)))
    total = jnp.zeros((weights.shape[2], height, width), jnp.float32)
    for row_tap in range(3):
        for col_tap in range(3):
            window = padded[:, row_tap : row_tap + height, col_tap : col_tap + width]
            total = total + jnp.einsum(
                "oc,cyx->oyx", weights[row_tap, col_tap], window, preferred_element_type=jnp.float32
            )
    return total


def window_start(numer, first_row, full_rows, out_rows, window_rows):
    valid = full_rows * numer // 14
    numer_pos = (2 * first_row + 1) * valid - out_rows
    lower = numer_pos // (2 * out_rows)
    lower = jnp.where(numer_pos < 0, 0, lower)
    lower = jnp.where(lower >= valid - 1, valid - 1, lower)
    return jnp.clip(lower, 0, full_rows - window_rows)


def column_table(numer, flip, cols, out_cols):
    valid_cols = cols * numer // 14
    col_pos = jnp.arange(out_cols, dtype=jnp.int32)
    col_pos = jnp.where(flip == 1, out_cols - 1 - col_pos, col_pos)
    return resize_matrix(col_pos, out_cols, valid_cols, cols)


def shards(features, views, conv_first, bias_first, conv_second, bias_second, classify, class_bias):
    feat = features[0]
    rows_dev, cols = (feat.shape[1], feat.shape[2])
    spaces = lax.axis_size("space")
    full_rows = rows_dev * spaces
    place = lax.axis_index("space")
    member_index = lax.axis_index("member")
    members = views.shape[0]
    picked = jnp.arange(members, dtype=jnp.int32) == member_index
    code = jnp.sum(jnp.where(picked, views, 0))
    numer = code // 2
    valid_rows = full_rows * numer // 14
    valid_cols = cols * numer // 14
    row_ids = place * rows_dev + jnp.arange(rows_dev, dtype=jnp.int32)
    row_ok = row_ids < valid_rows
    col_ok = jnp.arange(cols, dtype=jnp.int32) < valid_cols
    mask = (row_ok[:, None] & col_ok[None, :]).astype(jnp.float32)
    first = feat * mask.astype(jnp.bfloat16)
    hidden = (jax.nn.relu(convolve(first, conv_first) + bias_first[:, None, None]) * mask).astype(
        jnp.bfloat16
    )
    second = (
        jax.nn.relu(convolve(hidden, conv_second) + bias_second[:, None, None]) * mask
    ).astype(jnp.bfloat16)
    logits = (
        jnp.einsum("kc,cyx->kyx", classify, second, preferred_element_type=jnp.float32)
        + class_bias[:, None, None]
    ).astype(jnp.bfloat16)
    out_rows = UP * full_rows
    out_cols = UP * cols
    own_rows = out_rows // spaces
    part_rows = own_rows // members
    window_rows = (part_rows - 1) // UP + 3
    gathered = lax.all_gather(logits, "space", axis=1, tiled=True)
    pieces = []
    for target in range(members):
        first_row = place * own_rows + target * part_rows
        begin = window_start(numer, first_row, full_rows, out_rows, window_rows)
        pieces.append(lax.dynamic_slice_in_dim(gathered, begin, window_rows, 1))
    outgoing = jnp.stack(pieces, 0)
    incoming = lax.all_to_all(outgoing, "member", split_axis=0, concat_axis=0, tiled=True)
    own_first = place * own_rows + member_index * part_rows
    positions = own_first + jnp.arange(part_rows, dtype=jnp.int32)
    result = jnp.zeros((part_rows, logits.shape[0], out_cols), jnp.float32)
    for source in range(members):
        source_numer = views[source] // 2
        source_flip = views[source] % 2
        source_valid = full_rows * source_numer // 14
        begin = window_start(source_numer, own_first, full_rows, out_rows, window_rows)
        source_cols = column_table(source_numer, source_flip, cols, out_cols)
        row_table = resize_matrix(positions, out_rows, source_valid, full_rows)
        row_part = lax.dynamic_slice_in_dim(row_table, begin, window_rows, 1)
        widened = jnp.einsum(
            "cyx,jx->cyj", incoming[source], source_cols, preferred_element_type=jnp.float32
        ).astype(jnp.bfloat16)
        result = result + jnp.einsum(
            "iy,cyj->icj", row_part, widened, preferred_element_type=jnp.float32
        )
    return result


def solution(mesh):
    placed = (
        P(("groups", "member"), None, "space", None),
        P("groups"),
        P(),
        P(),
        P(),
        P(),
        P(),
        P(),
    )
    return jax.shard_map(
        shards,
        mesh=mesh,
        in_specs=placed,
        out_specs=P(("groups", "space", "member"), None, None),
        check_vma=False,
    )
```

profile of v0, /device:TPU:0, one launch (start us, length us, event | category | flops | bytes accessed | tf_op | source)
XLA Modules:
  0.0 144.4 jit_solution(15678336219757409563)
XLA Ops:
  6.5 1.3 fusion.170
  10.5 4.3 %copy.22 = bf16[1,256,16,256]{1,3,2,0:T(8,128)(2,1)} copy(bf16[1,256,16,256]{3,2,1,0:T(8,128)(2,1)} %param.8) | data formatting | bytes 4194304 | tf_op args[0]
  14.9 2.1 %bitcast_multiply_fusion = bf16[256,16,256]{0,2,1:T(8,128)(2,1)S(1)} fusion(bf16[1,256,16,256]{1,3,2,0:T(8,128)(2,1)} %copy.22, bf16[16,256]{1,0:T(8,128)(2,1)S(1)} %get-tuple-element.21), kind=kLoop, calls=%fused_computation.54 | loop fusion | flops 1048576 | bytes 4202496 | tf_op jit(solution)/shard_map/mul | solution.py:87
  17.0 2.5 %collective-permute-start = (bf16[256,1,256]{0,2,1:T(8,128)(2,1)S(1)}, bf16[256,1,256]{0,2,1:T(8,128)(2,1)S(1)}, u32[]{:S(2)}, u32[]{:S(2)}) collective-permute-start(bf16[256,1,256]{0,2,1:T(8,128)(2,1)S(1)} %get-tuple-element.15), channel_id=1, source_target_pairs={{0,2},{2,4},{4,6},{6,8},{8,10},{10,12},{12,14},{1,3},{3,5},{5,7},{... | collective-permute-start | bytes 393224 | tf_op jit(solution)/shard_map/ppermute | solution.py:14
  19.5 1.3 collective-permute-start.1
  20.9 1.7 %fusion.52 = f32[16,256,256]{2,1,0:T(8,128)S(1)} fusion(bf16[256,16,256]{2,1,0:T(8,128)(2,1)S(1)} %multiply_bitcast_fusion, bf16[3,3,256,256]{3,2,1,0:T(8,128)(2,1)S(1)} %copy-done.2), kind=kOutput, calls=%fused_computation.55 | convolution fusion | flops 536870912 | bytes 6422528 | tf_op jit(solution)/shard_map/oc,cyx->oyx/dot_general | solution.py:48
  22.6 2.3 %collective-permute-done.1 = bf16[256,1,256]{0,2,1:T(8,128)(2,1)S(1)} collective-permute-done((bf16[256,1,256]{0,2,1:T(8,128)(2,1)S(1)}, bf16[256,1,256]{0,2,1:T(8,128)(2,1)S(1)}, u32[]{:S(2)}, u32[]{:S(2)}) %collective-permute-start.1) | collective-permute-done | bytes 131104 | tf_op jit(solution)/shard_map/ppermute | solution.py:17
  26.5 2.8 %fusion.42 = f32[16,256,256]{2,1,0:T(8,128)} fusion(bf16[256,18,258]{0,2,1:T(8,128)(2,1)S(1)} %fusion.5, bf16[3,3,256,256]{3,2,1,0:T(8,128)(2,1)S(1)} %copy-done.2), kind=kOutput, calls=%fused_computation.44 | convolution fusion | flops 536870912 | bytes 6422528 | tf_op jit(solution)/shard_map/oc,cyx->oyx/dot_general | solution.py:48
  29.3 2.7 %fusion.44 = f32[16,256,256]{2,1,0:T(8,128)} fusion(bf16[256,18,258]{0,2,1:T(8,128)(2,1)S(1)} %fusion.5, bf16[3,3,256,256]{3,2,1,0:T(8,128)(2,1)S(1)} %copy-done.2), kind=kOutput, calls=%fused_computation.46 | convolution fusion | flops 536870912 | bytes 6422528 | tf_op jit(solution)/shard_map/oc,cyx->oyx/dot_general | solution.py:48
  32.0 2.7 %fusion.46 = f32[16,256,256]{2,1,0:T(8,128)} fusion(bf16[256,18,258]{0,2,1:T(8,128)(2,1)S(1)} %fusion.5, bf16[3,3,256,256]{3,2,1,0:T(8,128)(2,1)S(1)} %copy-done.2), kind=kOutput, calls=%fused_computation.48 | convolution fusion | flops 536870912 | bytes 6422528 | tf_op jit(solution)/shard_map/oc,cyx->oyx/dot_general | solution.py:48
  34.7 2.7 %fusion.48 = f32[16,256,256]{2,1,0:T(8,128)} fusion(bf16[256,18,258]{0,2,1:T(8,128)(2,1)S(1)} %fusion.5, bf16[3,3,256,256]{3,2,1,0:T(8,128)(2,1)S(1)} %copy-done.2), kind=kOutput, calls=%fused_computation.50 | convolution fusion | flops 536870912 | bytes 6422528 | tf_op jit(solution)/shard_map/oc,cyx->oyx/dot_general | solution.py:48
  37.4 2.8 %fusion.6 = f32[16,256,256]{2,1,0:T(8,128)} fusion(bf16[256,16,256]{0,2,1:T(8,128)(2,1)S(1)} %bitcast_multiply_fusion, bf16[256,1,256]{0,2,1:T(8,128)(2,1)S(1)} %collective-permute-done, bf16[3,3,256,256]{3,2,1,0:T(8,128)(2,1)S(1)} %copy-done.2), kind=kOutput, calls=%fused_computation.12 | convolution fusion | flops 541327360 | bytes 6553600 | tf_op jit(solution)/shard_map/oc,cyx->oyx/dot_general | solution.py:48
  40.2 2.7 %fusion.10 = f32[16,256,256]{2,1,0:T(8,128)} fusion(bf16[256,1,256]{0,2,1:T(8,128)(2,1)S(1)} %collective-permute-done.1, bf16[256,16,256]{0,2,1:T(8,128)(2,1)S(1)} %bitcast_multiply_fusion, bf16[3,3,256,256]{3,2,1,0:T(8,128)(2,1)S(1)} %copy-done.2), kind=kOutput, calls=%fused_computation.16 | convolution fusion | flops 541327360 | bytes 6553600 | tf_op jit(solution)/shard_map/oc,cyx->oyx/dot_general | solution.py:48
  42.8 9.7 %fusion.54 = bf16[256,16,256]{0,2,1:T(8,128)(2,1)S(1)} fusion(f32[16,256]{1,0:T(8,128)S(1)} %get-tuple-element.22, f32[256]{0:T(256)S(1)} %copy-done.5, bf16[256,18,258]{0,2,1:T(8,128)(2,1)S(1)} %fusion.5, f32[16,256,256]{2,1,0:T(8,128)} %fusion.10, f32[16,256,256]{2,1,0:T(8,128)S(1)} %fusion.40, f32[16,256,256]{2,1,0:T(8,128)} %fusion.42, ...), kind=kOutput, calls=%fused_computation.59 | convolution fusion | flops 549453824 | bytes 37897216 | tf_op jit(solution)/shard_map/oc,cyx->oyx/dot_general | solution.py:48
  52.6 5.4 %collective-permute-start.2 = (bf16[256,1,256]{0,2,1:T(8,128)(2,1)S(1)}, bf16[256,1,256]{0,2,1:T(8,128)(2,1)S(1)}, u32[]{:S(2)}, u32[]{:S(2)}) collective-permute-start(bf16[256,1,256]{0,2,1:T(8,128)(2,1)S(1)} %get-tuple-element.13), channel_id=1, source_target_pairs={{0,2},{2,4},{4,6},{6,8},{8,10},{10,12},{12,14},{1,3},{3,5},{5,7},{... | collective-permute-start | bytes 393224 | tf_op jit(solution)/shard_map/ppermute | solution.py:14
  58.1 1.5 %collective-permute-start.3 = (bf16[256,1,256]{0,2,1:T(8,128)(2,1)S(1)}, bf16[256,1,256]{0,2,1:T(8,128)(2,1)S(1)}, u32[]{:S(2)}, u32[]{:S(2)}) collective-permute-start(bf16[256,1,256]{0,2,1:T(8,128)(2,1)S(1)} %get-tuple-element.14), channel_id=1, source_target_pairs={{2,0},{4,2},{6,4},{8,6},{10,8},{12,10},{14,12},{3,1},{5,3},{7,5},{... | collective-permute-start | bytes 393224 | tf_op jit(solution)/shard_map/ppermute | solution.py:17
  59.5 3.6 %fusion.108 = f32[16,256,256]{2,1,0:T(8,128)} fusion(bf16[256,16,256]{0,2,1:T(8,128)(2,1)S(1)} %fusion.54, bf16[3,3,256,256]{3,2,1,0:T(8,128)(2,1)} %param.12), kind=kOutput, calls=%fused_computation.91 | convolution fusion | flops 536870912 | bytes 6422528 | tf_op jit(solution)/shard_map/oc,cyx->oyx/dot_general | solution.py:48
  63.1 0.9 select_maximum_fusion
  64.4 2.8 %fusion.26 = f32[16,256,256]{2,1,0:T(8,128)} fusion(bf16[256,18,258]{0,2,1:T(8,128)(2,1)S(1)} %select_maximum_fusion, bf16[3,3,256,256]{3,2,1,0:T(8,128)(2,1)S(1)} %copy-done.3), kind=kOutput, calls=%fused_computation.30 | convolution fusion | flops 536870912 | bytes 6422528 | tf_op jit(solution)/shard_map/oc,cyx->oyx/dot_general | solution.py:48
  67.2 2.7 %fusion.28 = f32[16,256,256]{2,1,0:T(8,128)} fusion(bf16[256,18,258]{0,2,1:T(8,128)(2,1)S(1)} %select_maximum_fusion, bf16[3,3,256,256]{3,2,1,0:T(8,128)(2,1)S(1)} %copy-done.3), kind=kOutput, calls=%fused_computation.32 | convolution fusion | flops 536870912 | bytes 6422528 | tf_op jit(solution)/shard_map/oc,cyx->oyx/dot_general | solution.py:48
  69.9 2.7 %fusion.30 = f32[16,256,256]{2,1,0:T(8,128)} fusion(bf16[256,18,258]{0,2,1:T(8,128)(2,1)S(1)} %select_maximum_fusion, bf16[3,3,256,256]{3,2,1,0:T(8,128)(2,1)S(1)} %copy-done.3), kind=kOutput, calls=%fused_computation.34 | convolution fusion | flops 536870912 | bytes 6422528 | tf_op jit(solution)/shard_map/oc,cyx->oyx/dot_general | solution.py:48
  72.6 2.8 %fusion.32 = f32[16,256,256]{2,1,0:T(8,128)} fusion(bf16[256,18,258]{0,2,1:T(8,128)(2,1)S(1)} %select_maximum_fusion, bf16[3,3,256,256]{3,2,1,0:T(8,128)(2,1)S(1)} %copy-done.3), kind=kOutput, calls=%fused_computation.36 | convolution fusion | flops 536870912 | bytes 6422528 | tf_op jit(solution)/shard_map/oc,cyx->oyx/dot_general | solution.py:48
  75.4 2.7 %fusion.34 = f32[16,256,256]{2,1,0:T(8,128)} fusion(bf16[256,18,258]{0,2,1:T(8,128)(2,1)S(1)} %select_maximum_fusion, bf16[3,3,256,256]{3,2,1,0:T(8,128)(2,1)S(1)} %copy-done.3), kind=kOutput, calls=%fused_computation.38 | convolution fusion | flops 536870912 | bytes 6422528 | tf_op jit(solution)/shard_map/oc,cyx->oyx/dot_general | solution.py:48
  78.1 2.7 %fusion.14 = f32[16,256,256]{2,1,0:T(8,128)} fusion(bf16[256,16,256]{0,2,1:T(8,128)(2,1)S(1)} %fusion.54, bf16[256,1,256]{0,2,1:T(8,128)(2,1)S(1)} %collective-permute-done.2, bf16[3,3,256,256]{3,2,1,0:T(8,128)(2,1)S(1)} %copy-done.3), kind=kOutput, calls=%fused_computation.20 | convolution fusion | flops 541327360 | bytes 6553600 | tf_op jit(solution)/shard_map/oc,cyx->oyx/dot_general | solution.py:48
  80.8 2.7 %fusion.18 = f32[16,256,256]{2,1,0:T(8,128)} fusion(bf16[256,1,256]{0,2,1:T(8,128)(2,1)S(1)} %collective-permute-done.3, bf16[256,16,256]{0,2,1:T(8,128)(2,1)S(1)} %fusion.54, bf16[3,3,256,256]{3,2,1,0:T(8,128)(2,1)S(1)} %copy-done.3), kind=kOutput, calls=%fused_computation.24 | convolution fusion | flops 541327360 | bytes 6553600 | tf_op jit(solution)/shard_map/oc,cyx->oyx/dot_general | solution.py:48
  83.5 13.2 %fusion.72 = bf16[19,16,256]{2,0,1:T(8,128)(2,1)S(1)} fusion(f32[16,256]{1,0:T(8,128)S(1)} %get-tuple-element.22, f32[256]{0:T(256)S(1)} %copy-done.6, bf16[256,18,258]{0,2,1:T(8,128)(2,1)S(1)} %select_maximum_fusion, f32[16,256,256]{2,1,0:T(8,128)} %fusion.18, f32[16,256,256]{2,1,0:T(8,128)} %fusion.26, f32[16,256,256]{2,1,0:T(8,128)} %fusion.28, ...), kind=kOutput, calls=%fused_computation.65 | convolution fusion | flops 589455360 | bytes 35968512 | tf_op jit(solution)/shard_map/kc,cyx->kyx/dot_general | solution.py:95
  103.7 18.8 %all-gather.2.cloned.1.call-done = bf16[19,128,256]{2,1,0:T(8,128)(2,1)} async-done(((bf16[19,16,256]{2,1,0:T(8,128)(2,1)}), bf16[19,128,256]{2,1,0:T(8,128)(2,1)}) %all-gather.2.cloned.1.call-update) | async-done | bytes 1245200 | tf_op jit(solution)/shard_map/all_gather | solution.py:103
  122.6 1.2 constant_dynamic-slice_fusion.1
  124.5 3.4 %all-to-all-start = ((bf16[2,19,10,256]{3,1,2,0:T(8,128)(2,1)}), bf16[2,19,10,256]{3,1,2,0:T(8,128)(2,1)S(1)}, u32[]{:S(2)}, u32[]{:S(2)}) async-start(bf16[2,19,10,256]{3,1,2,0:T(8,128)(2,1)} %pad_maximum_fusion), calls=%async_computation | async-start | bytes 491520 | tf_op jit(solution)/shard_map/all_to_all | solution.py:110
  128.0 5.6 %all-to-all-done = bf16[2,19,10,256]{3,1,2,0:T(8,128)(2,1)S(1)} async-done(((bf16[2,19,10,256]{3,1,2,0:T(8,128)(2,1)}), bf16[2,19,10,256]{3,1,2,0:T(8,128)(2,1)S(1)}, u32[]{:S(2)}, u32[]{:S(2)}) %all-to-all-start) | async-done | bytes 194592 | tf_op jit(solution)/shard_map/all_to_all | solution.py:110
  133.6 1.2 fusion.61
  134.9 2.7 %convolution_add_fusion = f32[32,19,1024]{2,0,1:T(8,128)} fusion(f32[32,19,1024]{2,0,1:T(8,128)S(1)} %fusion.61, f32[1024]{0:T(1024)S(1)} %get-tuple-element.35, s32[1024]{0:T(1024)S(1)} %get-tuple-element.38, f32[1024]{0:T(1024)S(1)} %get-tuple-element.36, s32[1024]{0:T(1024)S(1)} %get-tuple-element.37, ...), kind=kOutput, calls=%fused_computation.58 | convolution fusion | flops 114458816 | bytes 5094916 | tf_op jit(solution)/shard_map/iy,cyj->icj/dot_general | solution.py:125
  (40 shorter events, 4.5 us)
Async XLA Ops:
  6.5 76.9 %copy-start = (bf16[19,256]{1,0:T(8,128)(2,1)S(1)}, bf16[19,256]{1,0:T(8,128)(2,1)}, u32[]{:S(2)}) copy-start(bf16[19,256]{1,0:T(8,128)(2,1)} %param.14) | copy-start | bytes 29188
  6.5 116.0 %all-gather.2.cloned.1.call-start = ((), (), s32[]{:S(2)}) async-start(), calls=%async_computation.1 | async-start | bytes 1400832 | tf_op jit(solution)/shard_map/all_gather | solution.py:103
  14.8 6.0 %copy-start.1 = (bf16[1,256,16,256]{3,2,1,0:T(8,128)(2,1)S(1)}, bf16[1,256,16,256]{3,2,1,0:T(8,128)(2,1)}, u32[]{:S(2)}) copy-start(bf16[1,256,16,256]{3,2,1,0:T(8,128)(2,1)} %param.8) | copy-start | bytes 6291460
  16.9 4.0 %copy-start.2 = (bf16[3,3,256,256]{3,2,1,0:T(8,128)(2,1)S(1)}, bf16[3,3,256,256]{3,2,1,0:T(8,128)(2,1)}, u32[]{:S(2)}) copy-start(bf16[3,3,256,256]{3,2,1,0:T(8,128)(2,1)} %param.10) | copy-start | bytes 3538948
  17.0 5.6 %collective-permute-start = (bf16[256,1,256]{0,2,1:T(8,128)(2,1)S(1)}, bf16[256,1,256]{0,2,1:T(8,128)(2,1)S(1)}, u32[]{:S(2)}, u32[]{:S(2)}) collective-permute-start(bf16[256,1,256]{0,2,1:T(8,128)(2,1)S(1)} %get-tuple-element.15), channel_id=1, source_target_pairs={{0,2},{2,4},{4,6},{6,8},{8,10},{10,12},{12,14},{1,3},{3,5},{5,7},{... | collective-permute-start | bytes 393224 | tf_op jit(solution)/shard_map/ppermute | solution.py:14
  19.5 5.4 %collective-permute-start.1 = (bf16[256,1,256]{0,2,1:T(8,128)(2,1)S(1)}, bf16[256,1,256]{0,2,1:T(8,128)(2,1)S(1)}, u32[]{:S(2)}, u32[]{:S(2)}) collective-permute-start(bf16[256,1,256]{0,2,1:T(8,128)(2,1)S(1)} %get-tuple-element.16), channel_id=1, source_target_pairs={{2,0},{4,2},{6,4},{8,6},{10,8},{12,10},{14,12},{3,1},{5,3},{7,5},{... | collective-permute-start | bytes 393224 | tf_op jit(solution)/shard_map/ppermute | solution.py:17
  40.2 2.7 %copy-start.5 = (f32[256]{0:T(256)S(1)}, f32[256]{0:T(256)}, u32[]{:S(2)}) copy-start(f32[256]{0:T(256)} %param.11) | copy-start | bytes 3076
  52.6 10.5 %collective-permute-start.2 = (bf16[256,1,256]{0,2,1:T(8,128)(2,1)S(1)}, bf16[256,1,256]{0,2,1:T(8,128)(2,1)S(1)}, u32[]{:S(2)}, u32[]{:S(2)}) collective-permute-start(bf16[256,1,256]{0,2,1:T(8,128)(2,1)S(1)} %get-tuple-element.13), channel_id=1, source_target_pairs={{0,2},{2,4},{4,6},{6,8},{8,10},{10,12},{12,14},{1,3},{3,5},{5,7},{... | collective-permute-start | bytes 393224 | tf_op jit(solution)/shard_map/ppermute | solution.py:14
  58.1 5.1 %collective-permute-start.3 = (bf16[256,1,256]{0,2,1:T(8,128)(2,1)S(1)}, bf16[256,1,256]{0,2,1:T(8,128)(2,1)S(1)}, u32[]{:S(2)}, u32[]{:S(2)}) collective-permute-start(bf16[256,1,256]{0,2,1:T(8,128)(2,1)S(1)} %get-tuple-element.14), channel_id=1, source_target_pairs={{2,0},{4,2},{6,4},{8,6},{10,8},{12,10},{14,12},{3,1},{5,3},{7,5},{... | collective-permute-start | bytes 393224 | tf_op jit(solution)/shard_map/ppermute | solution.py:17
  63.1 1.3 copy-start.3
  80.8 2.7 %copy-start.6 = (f32[256]{0:T(256)S(1)}, f32[256]{0:T(256)}, u32[]{:S(2)}) copy-start(f32[256]{0:T(256)} %param.13) | copy-start | bytes 3076
  80.8 2.7 %copy-start.7 = (f32[19]{0:T(128)S(1)}, f32[19]{0:T(128)}, u32[]{:S(2)}) copy-start(f32[19]{0:T(128)} %param.15) | copy-start | bytes 232
  83.5 13.9 %copy-start.4 = (s32[2]{0:T(128)S(1)}, s32[2]{0:T(128)}, u32[]{:S(2)}) copy-start(s32[2]{0:T(128)} %param.9) | copy-start | bytes 28
  124.5 9.1 %all-to-all-start = ((bf16[2,19,10,256]{3,1,2,0:T(8,128)(2,1)}), bf16[2,19,10,256]{3,1,2,0:T(8,128)(2,1)S(1)}, u32[]{:S(2)}, u32[]{:S(2)}) async-start(bf16[2,19,10,256]{3,1,2,0:T(8,128)(2,1)} %pad_maximum_fusion), calls=%async_computation | async-start | bytes 491520 | tf_op jit(solution)/shard_map/all_to_all | solution.py:110
Sparse Core Ops, SparseCore 0:
  97.5 24.9 all-gather.1
where the time goes:
time: 145 us; the launch traced here: 144 us
  matrix products  68.2 us (47%)
  waiting for transfers between devices  26.8 us (18%)
  between operations  21.8 us (15%)
  starting transfers between devices  14.2 us (10%)
  local copies, waits for them, and re-layouts  7.31 us (5%)
  other arithmetic  6.15 us (4%)
    dot_general x17, matrix products, convolve(): jnp.einsum('oc,cyx->oyx', weights[row_tap, col_tap], window, preferred_el...  51.1 us
    all_gather x1, waiting for transfers between devices, shards(): gathered = lax.all_gather(logits, 'space', axis=1, tiled=True)  18.8 us
    dot_general x1, matrix products, shards(): jnp.einsum('kc,cyx->kyx', classify, second, preferred_element_type=jnp.fl...  13.2 us
    ppermute x2, starting transfers between devices, with_halo(): lax.ppermute(lax.slice_in_dim(block, block.shape[dim] - width, None, axis...  7.95 us
    all_to_all x1, waiting for transfers between devices, shards(): lax.all_to_all(outgoing, 'member', split_axis=0, concat_axis=0, tiled=True)  5.63 us
    unnamed x17, local copies, waits for them, and re-layouts  4.69 us
    dot_general x2, matrix products, shards(): jnp.einsum('iy,cyj->icj', row_part, widened, preferred_element_type=jnp.f...  3.89 us
    all_to_all x1, starting transfers between devices, shards(): lax.all_to_all(outgoing, 'member', split_axis=0, concat_axis=0, tiled=True)  3.44 us
  transfers between devices with their start and end apart: 6, of which 3 were waited for; matrix products, arithmetic and copies ran while one was open for 4% of the time, Pallas kernels for 0%

commit v1 on v0

--- a/solution.py
+++ b/solution.py
@@ -38,17 +38,16 @@
 
 
 def convolve(field, weights):
-    height, width = (field.shape[1], field.shape[2])
     padded = with_halo(field, (("space", 1),), 1)
-    padded = jnp.pad(padded, ((0, 0), (0, 0), (1, 1)))
-    total = jnp.zeros((weights.shape[2], height, width), jnp.float32)
-    for row_tap in range(3):
-        for col_tap in range(3):
-            window = padded[:, row_tap : row_tap + height, col_tap : col_tap + width]
-            total = total + jnp.einsum(
-                "oc,cyx->oyx", weights[row_tap, col_tap], window, preferred_element_type=jnp.float32
-            )
-    return total
+    out = lax.conv_general_dilated(
+        padded[None],
+        weights,
+        window_strides=(1, 1),
+        padding=((0, 0), (1, 1)),
+        dimension_numbers=("NCHW", "HWOI", "NCHW"),
+        preferred_element_type=jnp.float32,
+    )
+    return out[0]
 
 
 def window_start(numer, first_row, full_rows, out_rows, window_rows):

time: 145 us -> 125 us (0.86)
  matrix products: 68.2 us -> 19.4 us
  local copies, waits for them, and re-layouts: 7.31 us -> 24 us
  waiting for transfers between devices: 26.8 us -> 32.3 us
  other arithmetic: 6.15 us -> 11.6 us
    dot_general x17 -> x0, matrix products: 51.1 us -> none  [convolve(): jnp.einsum('oc,cyx->oyx', weights[row_tap, col_tap], window, preferred_el...]
    dot_general x1, matrix products: 13.2 us -> 1.34 us  [shards(): jnp.einsum('kc,cyx->kyx', classify, second, preferred_element_type=jnp.fl...]
    conv_general_dilated x0 -> x2, matrix products: none -> 11.5 us  [convolve(): lax.conv_general_dilated(padded[None], weights, window_strides=(1, 1), pa...]
    conv_general_dilated x0 -> x7, local copies, waits for them, and re-layouts: none -> 10.7 us  [convolve(): lax.conv_general_dilated(padded[None], weights, window_strides=(1, 1), pa...]
    broadcast_in_dim x0 -> x2, other arithmetic: none -> 6.86 us  [convolve(): padded[None]]
    ppermute x2, waiting for transfers between devices: 2.28 us -> 5.8 us  [with_halo(): lax.ppermute(lax.slice_in_dim(block, 0, width, axis=dim), axis, backward)]
    broadcast_in_dim x0 -> x2, local copies, waits for them, and re-layouts: none -> 2.94 us  [convolve(): padded[None]]
    dot_general x2, matrix products: 3.89 us -> 6.61 us  [shards(): jnp.einsum('iy,cyj->icj', row_part, widened, preferred_element_type=jnp.f...]
  transfers between devices with their start and end apart: 6 -> 6, of which waited for: 3 -> 4; matrix products, arithmetic and copies ran while one was open for 4% -> 1% of each run, Pallas kernels for 0% -> 0%
where the time goes in v1:
time: 125 us
  waiting for transfers between devices  32.3 us (26%)
  local copies, waits for them, and re-layouts  24 us (19%)
  between operations  22.1 us (18%)
  matrix products  19.4 us (16%)
  starting transfers between devices  15.3 us (12%)
  other arithmetic  11.6 us (9%)
    all_gather x1, waiting for transfers between devices, shards(): gathered = lax.all_gather(logits, 'space', axis=1, tiled=True)  20.8 us
    conv_general_dilated x2, matrix products, convolve(): lax.conv_general_dilated(padded[None], weights, window_strides=(1, 1), pa...  11.5 us
    conv_general_dilated x7, local copies, waits for them, and re-layouts, convolve(): lax.conv_general_dilated(padded[None], weights, window_strides=(1, 1), pa...  10.7 us
    ppermute x2, starting transfers between devices, with_halo(): lax.ppermute(lax.slice_in_dim(block, block.shape[dim] - width, None, axis...  9.02 us
    broadcast_in_dim x2, other arithmetic, convolve(): padded[None]  6.86 us
    dot_general x2, matrix products, shards(): jnp.einsum('iy,cyj->icj', row_part, widened, preferred_element_type=jnp.f...  6.61 us
    ppermute x2, waiting for transfers between devices, with_halo(): lax.ppermute(lax.slice_in_dim(block, 0, width, axis=dim), axis, backward)  5.8 us
    all_to_all x1, waiting for transfers between devices, shards(): lax.all_to_all(outgoing, 'member', split_axis=0, concat_axis=0, tiled=True)  5.63 us
  transfers between devices with their start and end apart: 6, of which 4 were waited for; matrix products, arithmetic and copies ran while one was open for 1% of the time, Pallas kernels for 0%

profile of v1, /device:TPU:0, one launch (start us, length us, event | category | flops | bytes accessed | tf_op | source)
XLA Modules:
  0.0 124.7 jit_solution(1669044014876538196)
XLA Ops:
  6.5 1.4 %fusion.95 = s32[]{:T(128)} fusion(s32[2]{0:T(128)} %param.9, s32[]{:T(128)S(6)} %axis_index.25), kind=kLoop, calls=%fused_computation.131 | loop fusion | flops 5 | bytes 16 | tf_op jit(solution)/shard_map/reduce_sum | solution.py:78
  10.7 1.7 %bitcast_multiply_fusion = bf16[256,16,256]{2,1,0:T(8,128)(2,1)S(1)} fusion(bf16[1,256,16,256]{3,2,1,0:T(8,128)(2,1)} %param.8, bf16[16,256]{1,0:T(8,128)(2,1)S(1)} %get-tuple-element.22), kind=kLoop, calls=%fused_computation.30 | loop fusion | flops 1048576 | bytes 4202496 | tf_op jit(solution)/shard_map/mul | solution.py:86
  12.4 1.2 fusion.108
  13.6 2.4 %collective-permute-start = (bf16[256,1,256]{2,1,0:T(2,128)(2,1)}, bf16[256,1,256]{2,1,0:T(2,128)(2,1)S(1)}, u32[]{:S(2)}, u32[]{:S(2)}) collective-permute-start(bf16[256,1,256]{2,1,0:T(2,128)(2,1)} %get-tuple-element.15), channel_id=1, source_target_pairs={{0,2},{2,4},{4,6},{6,8},{8,10},{10,12},{12,14},{1,3},{3,5},{5,7},{... | collective-permute-start | bytes 393224 | tf_op jit(solution)/shard_map/ppermute | solution.py:14
  16.0 1.3 %collective-permute-start.1 = (bf16[256,1,256]{2,1,0:T(2,128)(2,1)}, bf16[256,1,256]{2,1,0:T(2,128)(2,1)}, u32[]{:S(2)}, u32[]{:S(2)}) collective-permute-start(bf16[256,1,256]{2,1,0:T(2,128)(2,1)} %get-tuple-element.16), channel_id=1, source_target_pairs={{2,0},{4,2},{6,4},{8,6},{10,8},{12,10},{14,12},{3,1},{5,3},{7,5},{... | collective-permute-start | bytes 393224 | tf_op jit(solution)/shard_map/ppermute | solution.py:17
  17.3 0.7 copy.59
  18.1 3.9 %collective-permute-done.1 = bf16[256,1,256]{2,1,0:T(2,128)(2,1)} collective-permute-done((bf16[256,1,256]{2,1,0:T(2,128)(2,1)}, bf16[256,1,256]{2,1,0:T(2,128)(2,1)}, u32[]{:S(2)}, u32[]{:S(2)}) %collective-permute-start.1) | collective-permute-done | bytes 131104 | tf_op jit(solution)/shard_map/ppermute | solution.py:17
  21.9 4.8 %maximum_bitcast_fusion = bf16[256,18,1,256]{3,1,0,2:T(8,128)(2,1)} fusion(bf16[256,1,256]{2,1,0:T(2,128)(2,1)} %collective-permute-done.1, bf16[256,16,256]{2,1,0:T(8,128)(2,1)S(1)} %bitcast_multiply_fusion, bf16[256,1,256]{2,1,0:T(2,128)(2,1)S(1)} %collective-permute-done), kind=kLoop, calls=%fused_computation.13 | loop fusion | flops 7077888 | bytes 4718592 | tf_op jit(solution)/shard_map/broadcast_in_dim | solution.py:43
  26.8 3.6 %copy.76 = bf16[256,18,1,256]{0,3,1,2:T(8,128)(2,1)S(1)} copy(bf16[256,18,1,256]{3,1,0,2:T(8,128)(2,1)} %maximum_bitcast_fusion) | data formatting | bytes 4718592
  30.4 2.6 %pad.clone = bf16[256,18,1,264]{0,3,1,2:T(8,128)(2,1)} pad(bf16[256,18,1,256]{0,3,1,2:T(8,128)(2,1)S(1)} %copy.76, bf16[]{:T(256)} %constant.214), padding=0_0x0_0x0_0x1_7 | pad | bytes 4792322 | tf_op jit(solution)/shard_map/broadcast_in_dim | solution.py:43
  33.0 4.9 %reshape.243 = bf16[256,18,1,8,33]{0,4,3,1,2:T(8,128)(2,1)} reshape(bf16[256,18,1,264]{0,3,1,2:T(8,128)(2,1)} %pad.clone) | data formatting | bytes 4866048 | tf_op jit(solution)/shard_map/conv_general_dilated | solution.py:42
  37.9 2.4 %copy.57 = bf16[256,18,1,8,33]{0,3,4,1,2:T(8,128)(2,1)S(1)} copy(bf16[256,18,1,8,33]{0,4,3,1,2:T(8,128)(2,1)} %reshape.243) | data formatting | bytes 4866048 | tf_op jit(solution)/shard_map/conv_general_dilated | solution.py:42
  40.4 5.9 %broadcast_select_fusion.1 = f32[16,8,33,256]{3,1,2,0:T(8,128)S(1)} fusion(pred[8,33]{0,1:T(8,128)(4,1)S(1)} %copy-done.8, bf16[3,3,256,256]{3,2,1,0:T(8,128)(2,1)S(1)} %copy-done, bf16[256,18,1,7,2]{0,3,4,1,2:T(8,128)(2,1)S(1)} %slice.40, bf16[256,18,1,8,33]{0,3,4,1,2:T(8,128)(2,1)S(1)} %copy.57), kind=kOutput, calls=%fused_computation.28 | convolution fusion | flops 4991655936 | bytes 8067336 | tf_op jit(solution)/shard_map/conv_general_dilated | solution.py:42
  46.4 1.4 %copy.58 = f32[16,8,33,256]{3,0,2,1:T(8,128)S(1)} copy(f32[16,8,33,256]{3,1,2,0:T(8,128)S(1)} %broadcast_select_fusion.1) | data formatting | bytes 8650752 | tf_op jit(solution)/shard_map/conv_general_dilated | solution.py:42
  47.8 0.7 fusion.9
  48.9 6.7 %collective-permute-start.2 = (bf16[256,1,256]{0,1,2:T(2,128)(2,1)S(1)}, bf16[256,1,256]{0,1,2:T(2,128)(2,1)S(1)}, u32[]{:S(2)}, u32[]{:S(2)}) collective-permute-start(bf16[256,1,256]{0,1,2:T(2,128)(2,1)S(1)} %get-tuple-element.13), channel_id=1, source_target_pairs={{0,2},{2,4},{4,6},{6,8},{8,10},{10,12},{12,14},{1,3},{3,5},{5,7},{... | collective-permute-start | bytes 393224 | tf_op jit(solution)/shard_map/ppermute | solution.py:14
  55.6 1.5 %collective-permute-start.3 = (bf16[256,1,256]{0,1,2:T(2,128)(2,1)S(1)}, bf16[256,1,256]{0,1,2:T(2,128)(2,1)S(1)}, u32[]{:S(2)}, u32[]{:S(2)}) collective-permute-start(bf16[256,1,256]{0,1,2:T(2,128)(2,1)S(1)} %get-tuple-element.14), channel_id=1, source_target_pairs={{2,0},{4,2},{6,4},{8,6},{10,8},{12,10},{14,12},{3,1},{5,3},{7,5},{... | collective-permute-start | bytes 393224 | tf_op jit(solution)/shard_map/ppermute | solution.py:17
  57.1 1.9 %collective-permute-done.3 = bf16[256,1,256]{0,1,2:T(2,128)(2,1)S(1)} collective-permute-done((bf16[256,1,256]{0,1,2:T(2,128)(2,1)S(1)}, bf16[256,1,256]{0,1,2:T(2,128)(2,1)S(1)}, u32[]{:S(2)}, u32[]{:S(2)}) %collective-permute-start.3) | collective-permute-done | bytes 131104 | tf_op jit(solution)/shard_map/ppermute | solution.py:17
  59.0 2.0 %maximum_bitcast_fusion.1 = bf16[256,18,1,256]{0,1,3,2:T(8,128)(2,1)S(1)} fusion(bf16[256,1,256]{0,1,2:T(2,128)(2,1)S(1)} %collective-permute-done.3, bf16[256,16,256]{0,1,2:T(8,128)(2,1)S(1)} %fusion.9, bf16[256,1,256]{0,1,2:T(2,128)(2,1)S(1)} %collective-permute-done.2), kind=kLoop, calls=%fused_computation.14 | loop fusion | flops 7077888 | bytes 4718592 | tf_op jit(solution)/shard_map/broadcast_in_dim | solution.py:43
  62.0 0.7 copy-done.4
  62.7 5.5 %broadcast_select_fusion = f32[16,8,33,256]{3,1,2,0:T(8,128)S(1)} fusion(pred[8,33]{0,1:T(8,128)(4,1)S(1)} %copy-done.8, bf16[3,3,256,256]{3,2,1,0:T(8,128)(2,1)S(1)} %copy-done.4, bf16[256,18,1,7,2]{0,3,4,1,2:T(8,128)(2,1)S(1)} %slice.44, bf16[256,18,1,8,33]{0,3,4,1,2:T(8,128)(2,1)S(1)} %copy.62), kind=kOutput, calls=%fused_computation.27 | convolution fusion | flops 4991655936 | bytes 8067336 | tf_op jit(solution)/shard_map/conv_general_dilated | solution.py:42
  68.3 1.4 %copy.63 = f32[16,8,33,256]{3,0,2,1:T(8,128)S(1)} copy(f32[16,8,33,256]{3,1,2,0:T(8,128)S(1)} %broadcast_select_fusion) | data formatting | bytes 8650752 | tf_op jit(solution)/shard_map/conv_general_dilated | solution.py:42
  69.7 1.3 %fusion.35 = bf16[19,16,256]{0,1,2:T(8,128)(2,1)S(1)} fusion(f32[16,1,264,256]{3,0,2,1:T(8,128)S(1)} %bitcast.89, f32[256]{0:T(256)S(1)} %copy-done.6, f32[16,256]{0,1:T(8,128)S(1)} %copy-done.1, f32[19]{0:T(128)S(1)} %copy-done.7, bf16[19,256]{1,0:T(8,128)(2,1)S(1)} %copy-done.5), kind=kOutput, calls=%fused_computation.36 | convolution fusion | flops 44195840 | bytes 4494848 | tf_op jit(solution)/shard_map/kc,cyx->kyx/dot_general | solution.py:94
  71.0 1.7 %copy.64 = bf16[19,16,256]{2,1,0:T(8,128)(2,1)} copy(bf16[19,16,256]{0,1,2:T(8,128)(2,1)S(1)} %fusion.35) | data formatting | bytes 311296 | tf_op jit(solution)/shard_map/convert_element_type | solution.py:96
  72.8 0.6 fusion.110
  79.3 20.8 %all-gather.2.cloned.1.call-done = bf16[19,128,256]{2,1,0:T(8,128)(2,1)} async-done(((bf16[19,16,256]{2,1,0:T(8,128)(2,1)}), bf16[19,128,256]{2,1,0:T(8,128)(2,1)}) %all-gather.2.cloned.1.call-update) | async-done | bytes 1245200 | tf_op jit(solution)/shard_map/all_gather | solution.py:102
  100.1 1.2 constant_dynamic-slice_fusion.1
  101.4 0.7 pad_maximum_fusion
  102.1 3.4 %all-to-all-start = ((bf16[2,19,10,256]{3,1,2,0:T(8,128)(2,1)}), bf16[2,19,10,256]{3,1,2,0:T(8,128)(2,1)S(1)}, u32[]{:S(2)}, u32[]{:S(2)}) async-start(bf16[2,19,10,256]{3,1,2,0:T(8,128)(2,1)} %pad_maximum_fusion), calls=%async_computation | async-start | bytes 491520 | tf_op jit(solution)/shard_map/all_to_all | solution.py:109
  105.6 5.6 %all-to-all-done = bf16[2,19,10,256]{3,1,2,0:T(8,128)(2,1)S(1)} async-done(((bf16[2,19,10,256]{3,1,2,0:T(8,128)(2,1)}), bf16[2,19,10,256]{3,1,2,0:T(8,128)(2,1)S(1)}, u32[]{:S(2)}, u32[]{:S(2)}) %all-to-all-start) | async-done | bytes 194592 | tf_op jit(solution)/shard_map/all_to_all | solution.py:109
  111.2 2.7 %fusion.40 = f32[32,19,1024]{2,0,1:T(8,128)} fusion(f32[1024]{0:T(1024)S(1)} %get-tuple-element.31, s32[1024]{0:T(1024)S(1)} %get-tuple-element.34, f32[1024]{0:T(1024)S(1)} %get-tuple-element.32, s32[1024]{0:T(1024)S(1)} %get-tuple-element.33, bf16[1,19,10,256]{3,1,2,0:T(8,128)(2,1)S(1)} %get-tuple-element.20, f32[32]{0:T(128)S(1)} %get-tuple-element.26, ...), kind=kOutput, calls=%fused_computation.41 | convolution fusion | flops 113836224 | bytes 2604548 | tf_op jit(solution)/shard_map/iy,cyj->icj/dot_general | solution.py:124
  113.9 3.9 %convolution_add_fusion = f32[32,19,1024]{2,0,1:T(8,128)} fusion(f32[32,19,1024]{2,0,1:T(8,128)} %fusion.40, f32[1024]{0:T(1024)S(1)} %get-tuple-element.35, s32[1024]{0:T(1024)S(1)} %get-tuple-element.38, f32[1024]{0:T(1024)S(1)} %get-tuple-element.36, s32[1024]{0:T(1024)S(1)} %get-tuple-element.37, bf16[1,19,10,256]{3,1,2,0:T(8,128)(2,1)S(1)} %get-tuple-element.19, ...), kind=kOutput, calls=%fused_computation.35 | convolution fusion | flops 114458816 | bytes 5094916 | tf_op jit(solution)/shard_map/iy,cyj->icj/dot_general | solution.py:124
  (37 shorter events, 1.7 us)
Async XLA Ops:
  6.5 33.9 %copy-start = (bf16[3,3,256,256]{3,2,1,0:T(8,128)(2,1)S(1)}, bf16[3,3,256,256]{3,2,1,0:T(8,128)(2,1)}, u32[]{:S(2)}) copy-start(bf16[3,3,256,256]{3,2,1,0:T(8,128)(2,1)} %param.10) | copy-start | bytes 3538948
  6.5 93.6 %all-gather.2.cloned.1.call-start = ((), (), s32[]{:S(2)}) async-start(), calls=%async_computation.1 | async-start | bytes 1400832 | tf_op jit(solution)/shard_map/all_gather | solution.py:102
  13.6 4.4 %collective-permute-start = (bf16[256,1,256]{2,1,0:T(2,128)(2,1)}, bf16[256,1,256]{2,1,0:T(2,128)(2,1)S(1)}, u32[]{:S(2)}, u32[]{:S(2)}) collective-permute-start(bf16[256,1,256]{2,1,0:T(2,128)(2,1)} %get-tuple-element.15), channel_id=1, source_target_pairs={{0,2},{2,4},{4,6},{6,8},{8,10},{10,12},{12,14},{1,3},{3,5},{5,7},{... | collective-permute-start | bytes 393224 | tf_op jit(solution)/shard_map/ppermute | solution.py:14
  16.0 5.9 %collective-permute-start.1 = (bf16[256,1,256]{2,1,0:T(2,128)(2,1)}, bf16[256,1,256]{2,1,0:T(2,128)(2,1)}, u32[]{:S(2)}, u32[]{:S(2)}) collective-permute-start(bf16[256,1,256]{2,1,0:T(2,128)(2,1)} %get-tuple-element.16), channel_id=1, source_target_pairs={{2,0},{4,2},{6,4},{8,6},{10,8},{12,10},{14,12},{3,1},{5,3},{7,5},{... | collective-permute-start | bytes 393224 | tf_op jit(solution)/shard_map/ppermute | solution.py:17
  37.9 2.5 %copy-start.8 = (pred[8,33]{0,1:T(8,128)(4,1)S(1)}, pred[8,33]{0,1:T(8,128)(4,1)}, u32[]{:S(2)}) copy-start(pred[8,33]{0,1:T(8,128)(4,1)} %constant.222) | copy-start | bytes 796
  46.3 1.4 %copy-start.1 = (f32[16,256]{0,1:T(8,128)S(1)}, f32[16,256]{0,1:T(8,128)}, u32[]{:S(2)}) copy-start(f32[16,256]{0,1:T(8,128)} %copy.59) | copy-start | bytes 49156
  46.3 1.4 %copy-start.3 = (f32[256]{0:T(256)S(1)}, f32[256]{0:T(256)}, u32[]{:S(2)}) copy-start(f32[256]{0:T(256)} %param.11) | copy-start | bytes 3076
  48.9 8.2 %collective-permute-start.2 = (bf16[256,1,256]{0,1,2:T(2,128)(2,1)S(1)}, bf16[256,1,256]{0,1,2:T(2,128)(2,1)S(1)}, u32[]{:S(2)}, u32[]{:S(2)}) collective-permute-start(bf16[256,1,256]{0,1,2:T(2,128)(2,1)S(1)} %get-tuple-element.13), channel_id=1, source_target_pairs={{0,2},{2,4},{4,6},{6,8},{8,10},{10,12},{12,14},{1,3},{3,5},{5,7},{... | collective-permute-start | bytes 393224 | tf_op jit(solution)/shard_map/ppermute | solution.py:14
  55.6 3.4 %collective-permute-start.3 = (bf16[256,1,256]{0,1,2:T(2,128)(2,1)S(1)}, bf16[256,1,256]{0,1,2:T(2,128)(2,1)S(1)}, u32[]{:S(2)}, u32[]{:S(2)}) collective-permute-start(bf16[256,1,256]{0,1,2:T(2,128)(2,1)S(1)} %get-tuple-element.14), channel_id=1, source_target_pairs={{2,0},{4,2},{6,4},{8,6},{10,8},{12,10},{14,12},{3,1},{5,3},{7,5},{... | collective-permute-start | bytes 393224 | tf_op jit(solution)/shard_map/ppermute | solution.py:17
  61.4 1.3 %copy-start.4 = (bf16[3,3,256,256]{3,2,1,0:T(8,128)(2,1)S(1)}, bf16[3,3,256,256]{3,2,1,0:T(8,128)(2,1)}, u32[]{:S(2)}) copy-start(bf16[3,3,256,256]{3,2,1,0:T(8,128)(2,1)} %param.12) | copy-start | bytes 3538948
  68.2 1.4 %copy-start.5 = (bf16[19,256]{1,0:T(8,128)(2,1)S(1)}, bf16[19,256]{1,0:T(8,128)(2,1)}, u32[]{:S(2)}) copy-start(bf16[19,256]{1,0:T(8,128)(2,1)} %param.14) | copy-start | bytes 29188
  68.2 1.4 %copy-start.6 = (f32[256]{0:T(256)S(1)}, f32[256]{0:T(256)}, u32[]{:S(2)}) copy-start(f32[256]{0:T(256)} %param.13) | copy-start | bytes 3076
  68.2 1.4 %copy-start.7 = (f32[19]{0:T(128)S(1)}, f32[19]{0:T(128)}, u32[]{:S(2)}) copy-start(f32[19]{0:T(128)} %param.15) | copy-start | bytes 232
  69.7 3.1 %copy-start.2 = (s32[2]{0:T(128)S(1)}, s32[2]{0:T(128)}, u32[]{:S(2)}) copy-start(s32[2]{0:T(128)} %param.9) | copy-start | bytes 28
  102.1 9.1 %all-to-all-start = ((bf16[2,19,10,256]{3,1,2,0:T(8,128)(2,1)}), bf16[2,19,10,256]{3,1,2,0:T(8,128)(2,1)S(1)}, u32[]{:S(2)}, u32[]{:S(2)}) async-start(bf16[2,19,10,256]{3,1,2,0:T(8,128)(2,1)} %pad_maximum_fusion), calls=%async_computation | async-start | bytes 491520 | tf_op jit(solution)/shard_map/all_to_all | solution.py:109
Sparse Core Ops, SparseCore 0:
  72.9 27.1 all-gather.1

commit v2 on v1

--- a/solution.py
+++ b/solution.py
@@ -19,6 +19,22 @@
     return block
 
 
+def gather_rows(block, axis):
+    count = lax.axis_size(axis)
+    if count & (count - 1):
+        return lax.all_gather(block, axis, axis=0, tiled=True)
+    me = lax.axis_index(axis)
+    held = block[None]
+    bit = count // 2
+    while bit:
+        other = lax.ppermute(held, axis, [(i, i ^ bit) for i in range(count)])
+        upper = (me & bit) != 0
+        held = jnp.where(upper, jnp.stack([other, held], 1), jnp.stack([held, other], 1))
+        held = held.reshape((-1,) + block.shape)
+        bit //= 2
+    return held.reshape((count * block.shape[0],) + block.shape[1:])
+
+
 def resize_matrix(positions, out_len, valid, in_len):
     numer = (2 * positions + 1) * valid - out_len
     denom = 2 * out_len
@@ -38,13 +54,13 @@
 
 
 def convolve(field, weights):
-    padded = with_halo(field, (("space", 1),), 1)
+    padded = with_halo(field, (("space", 0),), 1)
     out = lax.conv_general_dilated(
         padded[None],
         weights,
         window_strides=(1, 1),
         padding=((0, 0), (1, 1)),
-        dimension_numbers=("NCHW", "HWOI", "NCHW"),
+        dimension_numbers=("NHWC", "HWOI", "NHWC"),
         preferred_element_type=jnp.float32,
     )
     return out[0]
@@ -83,46 +99,53 @@
     row_ok = row_ids < valid_rows
     col_ok = jnp.arange(cols, dtype=jnp.int32) < valid_cols
     mask = (row_ok[:, None] & col_ok[None, :]).astype(jnp.float32)
-    first = feat * mask.astype(jnp.bfloat16)
-    hidden = (jax.nn.relu(convolve(first, conv_first) + bias_first[:, None, None]) * mask).astype(
-        jnp.bfloat16
-    )
-    second = (
-        jax.nn.relu(convolve(hidden, conv_second) + bias_second[:, None, None]) * mask
-    ).astype(jnp.bfloat16)
+    first = jnp.transpose(feat * mask.astype(jnp.bfloat16), (1, 2, 0))
+    cell = mask[:, :, None]
+    hidden = (jax.nn.relu(convolve(first, conv_first) + bias_first) * cell).astype(jnp.bfloat16)
+    second = (jax.nn.relu(convolve(hidden, conv_second) + bias_second) * cell).astype(jnp.bfloat16)
     logits = (
-        jnp.einsum("kc,cyx->kyx", classify, second, preferred_element_type=jnp.float32)
-        + class_bias[:, None, None]
+        jnp.einsum("kc,yxc->ykx", classify, second, preferred_element_type=jnp.float32)
+        + class_bias[None, :, None]
     ).astype(jnp.bfloat16)
     out_rows = UP * full_rows
     out_cols = UP * cols
     own_rows = out_rows // spaces
     part_rows = own_rows // members
     window_rows = (part_rows - 1) // UP + 3
-    gathered = lax.all_gather(logits, "space", axis=1, tiled=True)
+    gathered = gather_rows(logits, "space")
     pieces = []
     for target in range(members):
         first_row = place * own_rows + target * part_rows
         begin = window_start(numer, first_row, full_rows, out_rows, window_rows)
-        pieces.append(lax.dynamic_slice_in_dim(gathered, begin, window_rows, 1))
+        pieces.append(lax.dynamic_slice_in_dim(gathered, begin, window_rows, 0))
     outgoing = jnp.stack(pieces, 0)
-    incoming = lax.all_to_all(outgoing, "member", split_axis=0, concat_axis=0, tiled=True)
     own_first = place * own_rows + member_index * part_rows
     positions = own_first + jnp.arange(part_rows, dtype=jnp.int32)
-    result = jnp.zeros((part_rows, logits.shape[0], out_cols), jnp.float32)
-    for source in range(members):
-        source_numer = views[source] // 2
-        source_flip = views[source] % 2
+    result = jnp.zeros((part_rows, logits.shape[1], out_cols), jnp.float32)
+    for shift in range(members):
+        if shift == 0:
+            arrived = lax.dynamic_index_in_dim(outgoing, member_index, 0, keepdims=False)
+        else:
+            send = lax.dynamic_index_in_dim(
+                outgoing, (member_index + shift) % members, 0, keepdims=False
+            )
+            arrived = lax.ppermute(
+                send, "member", [(i, (i + shift) % members) for i in range(members)]
+            )
+        source = (member_index - shift) % members
+        source_code = jnp.sum(jnp.where(jnp.arange(members) == source, views, 0))
+        source_numer = source_code // 2
+        source_flip = source_code % 2
         source_valid = full_rows * source_numer // 14
         begin = window_start(source_numer, own_first, full_rows, out_rows, window_rows)
         source_cols = column_table(source_numer, source_flip, cols, out_cols)
         row_table = resize_matrix(positions, out_rows, source_valid, full_rows)
         row_part = lax.dynamic_slice_in_dim(row_table, begin, window_rows, 1)
         widened = jnp.einsum(
-            "cyx,jx->cyj", incoming[source], source_cols, preferred_element_type=jnp.float32
+            "ycx,jx->ycj", arrived, source_cols, preferred_element_type=jnp.float32
         ).astype(jnp.bfloat16)
         result = result + jnp.einsum(
-            "iy,cyj->icj", row_part, widened, preferred_element_type=jnp.float32
+            "iy,ycj->icj", row_part, widened, preferred_element_type=jnp.float32
         )
     return result
 

time: 125 us -> 101 us (0.81)
  between operations: 22.1 us -> 8 us
  waiting for transfers between devices: 32.3 us -> 19.6 us
  starting transfers between devices: 15.3 us -> 19.6 us
  local copies, waits for them, and re-layouts: 24 us -> 22.6 us
    all_gather x1 -> x0, waiting for transfers between devices: 20.8 us -> none  [shards(): gathered = lax.all_gather(logits, 'space', axis=1, tiled=True)]
    ppermute x0 -> x4, waiting for transfers between devices: none -> 13.8 us  [the longest x3 11.9 us: gather_rows(): other = lax.ppermute(held, axis, [(i, i ^ bit) for i in range(count)])]
    ppermute x0 -> x4, starting transfers between devices: none -> 7.82 us  [the longest x3 6.25 us: gather_rows(): other = lax.ppermute(held, axis, [(i, i ^ bit) for i in range(count)])]
    all_to_all x1 -> x0, waiting for transfers between devices: 5.63 us -> none  [shards(): lax.all_to_all(outgoing, 'member', split_axis=0, concat_axis=0, tiled=True)]
    all_to_all x1 -> x0, starting transfers between devices: 3.44 us -> none  [shards(): lax.all_to_all(outgoing, 'member', split_axis=0, concat_axis=0, tiled=True)]
    mul x1 -> x0, other arithmetic: 1.73 us -> none  [shards(): first = feat * mask.astype(jnp.bfloat16)]
    transpose x0 -> x1, other arithmetic: none -> 1.73 us  [shards(): first = jnp.transpose(feat * mask.astype(jnp.bfloat16), (1, 2, 0))]
    convert_element_type x1 -> x0, local copies, waits for them, and re-layouts: 1.68 us -> none  [shards(): logits = (jnp.einsum('kc,cyx->kyx', classify, second, preferred_element_t...]
  transfers between devices with their start and end apart: 6 -> 8, of which waited for: 4 -> 6; matrix products, arithmetic and copies ran while one was open for 1% -> 5% of each run, Pallas kernels for 0% -> 0%
where the time goes in v2:
time: 101 us
  local copies, waits for them, and re-layouts  22.6 us (22%)
  starting transfers between devices  19.6 us (19%)
  waiting for transfers between devices  19.6 us (19%)
  matrix products  19.4 us (19%)
  other arithmetic  11.4 us (11%)
  between operations  8 us (8%)
    ppermute x3, waiting for transfers between devices, gather_rows(): other = lax.ppermute(held, axis, [(i, i ^ bit) for i in range(count)])  11.9 us
    conv_general_dilated x2, matrix products, convolve(): lax.conv_general_dilated(padded[None], weights, window_strides=(1, 1), pa...  11.5 us
    conv_general_dilated x7, local copies, waits for them, and re-layouts, convolve(): lax.conv_general_dilated(padded[None], weights, window_strides=(1, 1), pa...  10.7 us
    ppermute x2, starting transfers between devices, with_halo(): lax.ppermute(lax.slice_in_dim(block, block.shape[dim] - width, None, axis...  9.02 us
    broadcast_in_dim x2, other arithmetic, convolve(): padded[None]  6.88 us
    dot_general x2, matrix products, shards(): jnp.einsum('iy,ycj->icj', row_part, widened, preferred_element_type=jnp.f...  6.59 us
    ppermute x3, starting transfers between devices, gather_rows(): other = lax.ppermute(held, axis, [(i, i ^ bit) for i in range(count)])  6.25 us
    ppermute x2, waiting for transfers between devices, with_halo(): lax.ppermute(lax.slice_in_dim(block, 0, width, axis=dim), axis, backward)  5.79 us
  transfers between devices with their start and end apart: 8, of which 6 were waited for; matrix products, arithmetic and copies ran while one was open for 5% of the time, Pallas kernels for 0%

profile of v2, /device:TPU:0, one launch (start us, length us, event | category | flops | bytes accessed | tf_op | source)
XLA Modules:
  0.0 100.5 jit_solution(18119825801184095369)
XLA Ops:
  0.0 1.5 %fusion.103 = (s32[]{:T(128)}, s32[]{:T(128)}, s32[]{:T(128)}) fusion(s32[2]{0:T(128)} %param.9, s32[]{:T(128)S(6)} %select_n.540, s32[]{:T(128)S(6)} %select_n.493, s32[]{:T(128)S(6)} %axis_index.29), kind=kLoop, calls=%fused_computation.145 | loop fusion | flops 15 | bytes 32 | tf_op jit(solution)/shard_map/reduce_sum | solution.py:136
  4.2 1.7 %fusion.26 = bf16[16,256,256]{1,0,2:T(8,128)(2,1)S(1)} fusion(bf16[1,256,16,256]{3,2,1,0:T(8,128)(2,1)} %param.8, bf16[16,256]{1,0:T(8,128)(2,1)S(1)} %get-tuple-element.23), kind=kLoop, calls=%fused_computation.31 | loop fusion | flops 1048576 | bytes 4202496 | tf_op jit(solution)/shard_map/transpose | solution.py:102
  6.0 1.2 %fusion.118 = (bf16[1,256,256]{1,0,2:T(2,128)(2,1)}, bf16[1,256,256]{1,0,2:T(2,128)(2,1)}) fusion(bf16[16,256,256]{1,0,2:T(8,128)(2,1)S(1)} %fusion.26), kind=kLoop, calls=%fused_computation.167 | loop fusion | bytes 524288 | tf_op jit(solution)/shard_map/slice | solution.py:15
  7.2 2.4 %collective-permute-start = (bf16[1,256,256]{1,0,2:T(2,128)(2,1)}, bf16[1,256,256]{1,0,2:T(2,128)(2,1)S(1)}, u32[]{:S(2)}, u32[]{:S(2)}) collective-permute-start(bf16[1,256,256]{1,0,2:T(2,128)(2,1)} %get-tuple-element.18), channel_id=1, source_target_pairs={{0,2},{2,4},{4,6},{6,8},{8,10},{10,12},{12,14},{1,3},{3,5},{5,7},{... | collective-permute-start | bytes 393224 | tf_op jit(solution)/shard_map/ppermute | solution.py:14
  9.5 1.3 %collective-permute-start.1 = (bf16[1,256,256]{1,0,2:T(2,128)(2,1)}, bf16[1,256,256]{1,0,2:T(2,128)(2,1)}, u32[]{:S(2)}, u32[]{:S(2)}) collective-permute-start(bf16[1,256,256]{1,0,2:T(2,128)(2,1)} %get-tuple-element.19), channel_id=1, source_target_pairs={{2,0},{4,2},{6,4},{8,6},{10,8},{12,10},{14,12},{3,1},{5,3},{7,5},{... | collective-permute-start | bytes 393224 | tf_op jit(solution)/shard_map/ppermute | solution.py:17
  10.8 0.8 copy.38
  11.6 3.9 %collective-permute-done.1 = bf16[1,256,256]{1,0,2:T(2,128)(2,1)} collective-permute-done((bf16[1,256,256]{1,0,2:T(2,128)(2,1)}, bf16[1,256,256]{1,0,2:T(2,128)(2,1)}, u32[]{:S(2)}, u32[]{:S(2)}) %collective-permute-start.1) | collective-permute-done | bytes 131104 | tf_op jit(solution)/shard_map/ppermute | solution.py:17
  15.5 4.8 %maximum_bitcast_fusion = bf16[18,1,256,256]{2,0,3,1:T(8,128)(2,1)} fusion(bf16[1,256,256]{1,0,2:T(2,128)(2,1)} %collective-permute-done.1, bf16[16,256,256]{1,0,2:T(8,128)(2,1)S(1)} %fusion.26, bf16[1,256,256]{1,0,2:T(2,128)(2,1)S(1)} %collective-permute-done), kind=kLoop, calls=%fused_computation.13 | loop fusion | flops 7077888 | bytes 4718592 | tf_op jit(solution)/shard_map/broadcast_in_dim | solution.py:59
  20.3 3.6 %copy.55 = bf16[18,1,256,256]{3,2,0,1:T(8,128)(2,1)S(1)} copy(bf16[18,1,256,256]{2,0,3,1:T(8,128)(2,1)} %maximum_bitcast_fusion) | data formatting | bytes 4718592
  23.9 2.6 %pad.clone = bf16[18,1,264,256]{3,2,0,1:T(8,128)(2,1)} pad(bf16[18,1,256,256]{3,2,0,1:T(8,128)(2,1)S(1)} %copy.55, bf16[]{:T(256)} %constant.235), padding=0_0x0_0x1_7x0_0 | pad | bytes 4792322 | tf_op jit(solution)/shard_map/broadcast_in_dim | solution.py:59
  26.5 4.9 %reshape.354 = bf16[18,1,8,33,256]{4,3,2,0,1:T(8,128)(2,1)} reshape(bf16[18,1,264,256]{3,2,0,1:T(8,128)(2,1)} %pad.clone) | data formatting | bytes 4866048 | tf_op jit(solution)/shard_map/conv_general_dilated | solution.py:58
  31.4 2.4 %copy.36 = bf16[18,1,8,33,256]{4,2,3,0,1:T(8,128)(2,1)S(1)} copy(bf16[18,1,8,33,256]{4,3,2,0,1:T(8,128)(2,1)} %reshape.354) | data formatting | bytes 4866048 | tf_op jit(solution)/shard_map/conv_general_dilated | solution.py:58
  33.9 5.9 %broadcast_select_fusion.1 = f32[16,8,33,256]{3,1,2,0:T(8,128)S(1)} fusion(pred[8,33]{0,1:T(8,128)(4,1)S(1)} %copy-done.7, bf16[3,3,256,256]{3,2,1,0:T(8,128)(2,1)S(1)} %copy-done, bf16[18,1,7,2,256]{4,2,3,0,1:T(8,128)(2,1)S(1)} %slice.22, bf16[18,1,8,33,256]{4,2,3,0,1:T(8,128)(2,1)S(1)} %copy.36), kind=kOutput, calls=%fused_computation.28 | convolution fusion | flops 4991655936 | bytes 8067336 | tf_op jit(solution)/shard_map/conv_general_dilated | solution.py:58
  39.9 1.4 %copy.37 = f32[16,8,33,256]{3,0,2,1:T(8,128)S(1)} copy(f32[16,8,33,256]{3,1,2,0:T(8,128)S(1)} %broadcast_select_fusion.1) | data formatting | bytes 8650752 | tf_op jit(solution)/shard_map/conv_general_dilated | solution.py:58
  42.4 6.7 %collective-permute-start.2 = (bf16[1,256,256]{2,0,1:T(2,128)(2,1)S(1)}, bf16[1,256,256]{2,0,1:T(2,128)(2,1)S(1)}, u32[]{:S(2)}, u32[]{:S(2)}) collective-permute-start(bf16[1,256,256]{2,0,1:T(2,128)(2,1)S(1)} %get-tuple-element.16), channel_id=1, source_target_pairs={{0,2},{2,4},{4,6},{6,8},{8,10},{10,12},{12,14},{1,3},{3,5},{5,7},{... | collective-permute-start | bytes 393224 | tf_op jit(solution)/shard_map/ppermute | solution.py:14
  49.1 1.5 %collective-permute-start.3 = (bf16[1,256,256]{2,0,1:T(2,128)(2,1)S(1)}, bf16[1,256,256]{2,0,1:T(2,128)(2,1)S(1)}, u32[]{:S(2)}, u32[]{:S(2)}) collective-permute-start(bf16[1,256,256]{2,0,1:T(2,128)(2,1)S(1)} %get-tuple-element.17), channel_id=1, source_target_pairs={{2,0},{4,2},{6,4},{8,6},{10,8},{12,10},{14,12},{3,1},{5,3},{7,5},{... | collective-permute-start | bytes 393224 | tf_op jit(solution)/shard_map/ppermute | solution.py:17
  50.6 1.9 %collective-permute-done.3 = bf16[1,256,256]{2,0,1:T(2,128)(2,1)S(1)} collective-permute-done((bf16[1,256,256]{2,0,1:T(2,128)(2,1)S(1)}, bf16[1,256,256]{2,0,1:T(2,128)(2,1)S(1)}, u32[]{:S(2)}, u32[]{:S(2)}) %collective-permute-start.3) | collective-permute-done | bytes 131104 | tf_op jit(solution)/shard_map/ppermute | solution.py:17
  52.5 2.0 %maximum_bitcast_fusion.1 = bf16[18,1,256,256]{3,0,2,1:T(8,128)(2,1)S(1)} fusion(bf16[1,256,256]{2,0,1:T(2,128)(2,1)S(1)} %collective-permute-done.3, bf16[16,256,256]{2,0,1:T(8,128)(2,1)S(1)} %fusion.9, bf16[1,256,256]{2,0,1:T(2,128)(2,1)S(1)} %collective-permute-done.2), kind=kLoop, calls=%fused_computation.14 | loop fusion | flops 7077888 | bytes 4718592 | tf_op jit(solution)/shard_map/broadcast_in_dim | solution.py:59
  56.2 5.5 %broadcast_select_fusion = f32[16,8,33,256]{3,1,2,0:T(8,128)S(1)} fusion(pred[8,33]{0,1:T(8,128)(4,1)S(1)} %copy-done.7, bf16[3,3,256,256]{3,2,1,0:T(8,128)(2,1)S(1)} %copy-done.3, bf16[18,1,7,2,256]{4,2,3,0,1:T(8,128)(2,1)S(1)} %slice.26, bf16[18,1,8,33,256]{4,2,3,0,1:T(8,128)(2,1)S(1)} %copy.41), kind=kOutput, calls=%fused_computation.27 | convolution fusion | flops 4991655936 | bytes 8067336 | tf_op jit(solution)/shard_map/conv_general_dilated | solution.py:58
  61.8 1.4 %copy.42 = f32[16,8,33,256]{3,0,2,1:T(8,128)S(1)} copy(f32[16,8,33,256]{3,1,2,0:T(8,128)S(1)} %broadcast_select_fusion) | data formatting | bytes 8650752 | tf_op jit(solution)/shard_map/conv_general_dilated | solution.py:58
  63.2 1.3 %add_convert_fusion = bf16[16,256,19]{2,0,1:T(8,128)(2,1)S(1)} fusion(f32[16,1,264,256]{3,0,2,1:T(8,128)S(1)} %bitcast.96, f32[256]{0:T(256)S(1)} %copy-done.5, f32[16,256]{0,1:T(8,128)S(1)} %copy-done.1, f32[19]{0:T(128)S(1)} %copy-done.6, bf16[19,256]{1,0:T(8,128)(2,1)S(1)} %copy-done.4), kind=kOutput, calls=%fused_computation.32 | convolution fusion | flops 44195840 | bytes 4494848 | tf_op jit(solution)/shard_map/kc,yxc->ykx/dot_general | solution.py:107
  64.6 1.0 %copy.43 = bf16[1,16,19,256]{3,1,2,0:T(8,128)(2,1)S(1)} copy(bf16[1,16,19,256]{2,1,3,0:T(8,128)(2,1)S(1)} %bitcast.97) | data formatting | bytes 311296 | tf_op jit(solution)/shard_map/broadcast_in_dim | solution.py:27
  65.6 5.1 %collective-permute-start.4 = (bf16[1,16,19,256]{3,1,2,0:T(8,128)(2,1)S(1)}, bf16[1,16,19,256]{3,1,2,0:T(8,128)(2,1)S(1)}, u32[]{:S(2)}, u32[]{:S(2)}) collective-permute-start(bf16[1,16,19,256]{3,1,2,0:T(8,128)(2,1)S(1)} %copy.43), channel_id=1, source_target_pairs={{0,8},{2,10},{4,12},{6,14},{8,0},{10,2},{12,4},{14,6},{1,9},{3,11}... | collective-permute-start | bytes 466952 | tf_op jit(solution)/shard_map/ppermute | solution.py:30
  75.6 2.0 %collective-permute-done.4 = bf16[1,16,19,256]{3,1,2,0:T(8,128)(2,1)S(1)} collective-permute-done((bf16[1,16,19,256]{3,1,2,0:T(8,128)(2,1)S(1)}, bf16[1,16,19,256]{3,1,2,0:T(8,128)(2,1)S(1)}, u32[]{:S(2)}, u32[]{:S(2)}) %collective-permute-start.4) | collective-permute-done | bytes 155680 | tf_op jit(solution)/shard_map/ppermute | solution.py:30
  77.6 1.0 collective-permute-start.5
  78.7 1.0 %copy.46 = bf16[1,1,16,19,256]{4,2,3,1,0:T(8,128)(2,1)S(1)} copy(bf16[1,1,16,19,256]{3,2,4,1,0:T(8,128)(2,1)S(1)} %bitcast.98) | data formatting | bytes 311296 | tf_op jit(solution)/shard_map/stack | solution.py:32
  79.7 8.1 %collective-permute-done.5 = bf16[2,16,19,256]{3,1,2,0:T(8,128)(2,1)S(1)} collective-permute-done((bf16[2,16,19,256]{3,1,2,0:T(8,128)(2,1)S(1)}, bf16[2,16,19,256]{3,1,2,0:T(8,128)(2,1)S(1)}, u32[]{:S(2)}, u32[]{:S(2)}) %collective-permute-start.5) | collective-permute-done | bytes 311328 | tf_op jit(solution)/shard_map/ppermute | solution.py:30
  88.3 1.8 %collective-permute-done.6 = bf16[4,16,19,256]{3,1,0,2:T(8,128)(2,1)S(1)} collective-permute-done((bf16[4,16,19,256]{3,1,0,2:T(8,128)(2,1)S(1)}, bf16[4,16,19,256]{3,1,0,2:T(8,128)(2,1)S(1)}, u32[]{:S(2)}, u32[]{:S(2)}) %collective-permute-start.6) | collective-permute-done | bytes 622624 | tf_op jit(solution)/shard_map/ppermute | solution.py:30
  90.5 1.6 %collective-permute-start.7 = (bf16[10,19,256]{2,0,1:T(8,128)(2,1)S(1)}, bf16[10,19,256]{2,0,1:T(8,128)(2,1)S(1)}, u32[]{:S(2)}, u32[]{:S(2)}) collective-permute-start(bf16[10,19,256]{2,0,1:T(8,128)(2,1)S(1)} %fusion.66), channel_id=1, source_target_pairs={{0,1},{1,0},{2,3},{3,2},{4,5},{5,4},{6,7},{7,6},{8,9},{9,8},{10,11... | collective-permute-start | bytes 291848 | tf_op jit(solution)/shard_map/ppermute | solution.py:132
  92.0 2.6 %fusion.38 = f32[32,19,1024]{2,0,1:T(8,128)} fusion(f32[1024]{0:T(1024)S(1)} %get-tuple-element.24, s32[1024]{0:T(1024)S(1)} %get-tuple-element.27, f32[1024]{0:T(1024)S(1)} %get-tuple-element.25, s32[1024]{0:T(1024)S(1)} %get-tuple-element.26, s32[]{:T(128)S(6)} %select_n.528, bf16[1,10,19,256]{3,1,2,0:T(8,128)(2,1)S(1)} %get-tuple-element.21, ...), kind=kOutput, calls=%fused_computation.41 | convolution fusion | flops 113884864 | bytes 2701832 | tf_op jit(solution)/shard_map/iy,ycj->icj/dot_general | solution.py:147
  94.7 1.9 %collective-permute-done.7 = bf16[10,19,256]{2,0,1:T(8,128)(2,1)S(1)} collective-permute-done((bf16[10,19,256]{2,0,1:T(8,128)(2,1)S(1)}, bf16[10,19,256]{2,0,1:T(8,128)(2,1)S(1)}, u32[]{:S(2)}, u32[]{:S(2)}) %collective-permute-start.7) | collective-permute-done | bytes 97312 | tf_op jit(solution)/shard_map/ppermute | solution.py:132
  96.6 3.9 %convolution_add_fusion = f32[32,19,1024]{2,0,1:T(8,128)} fusion(f32[32,19,1024]{2,0,1:T(8,128)} %fusion.38, bf16[10,19,256]{2,0,1:T(8,128)(2,1)S(1)} %collective-permute-done.7, f32[1024]{0:T(1024)S(1)} %get-tuple-element.28, s32[1024]{0:T(1024)S(1)} %get-tuple-element.31, f32[1024]{0:T(1024)S(1)} %get-tuple-element.29, s32[1024]{0:T(1024)S(1)} %get-tuple-element.30, ...), kind=kOutput, calls=%fused_computation.36 | convolution fusion | flops 114458816 | bytes 5094916 | tf_op jit(solution)/shard_map/iy,ycj->icj/dot_general | solution.py:147
  (43 shorter events, 3.8 us)
Async XLA Ops:
  0.0 33.9 %copy-start = (bf16[3,3,256,256]{3,2,1,0:T(8,128)(2,1)S(1)}, bf16[3,3,256,256]{3,2,1,0:T(8,128)(2,1)}, u32[]{:S(2)}) copy-start(bf16[3,3,256,256]{3,2,1,0:T(8,128)(2,1)} %param.10) | copy-start | bytes 3538948
  7.2 4.4 %collective-permute-start = (bf16[1,256,256]{1,0,2:T(2,128)(2,1)}, bf16[1,256,256]{1,0,2:T(2,128)(2,1)S(1)}, u32[]{:S(2)}, u32[]{:S(2)}) collective-permute-start(bf16[1,256,256]{1,0,2:T(2,128)(2,1)} %get-tuple-element.18), channel_id=1, source_target_pairs={{0,2},{2,4},{4,6},{6,8},{8,10},{10,12},{12,14},{1,3},{3,5},{5,7},{... | collective-permute-start | bytes 393224 | tf_op jit(solution)/shard_map/ppermute | solution.py:14
  9.5 5.9 %collective-permute-start.1 = (bf16[1,256,256]{1,0,2:T(2,128)(2,1)}, bf16[1,256,256]{1,0,2:T(2,128)(2,1)}, u32[]{:S(2)}, u32[]{:S(2)}) collective-permute-start(bf16[1,256,256]{1,0,2:T(2,128)(2,1)} %get-tuple-element.19), channel_id=1, source_target_pairs={{2,0},{4,2},{6,4},{8,6},{10,8},{12,10},{14,12},{3,1},{5,3},{7,5},{... | collective-permute-start | bytes 393224 | tf_op jit(solution)/shard_map/ppermute | solution.py:17
  31.4 2.5 %copy-start.7 = (pred[8,33]{0,1:T(8,128)(4,1)S(1)}, pred[8,33]{0,1:T(8,128)(4,1)}, u32[]{:S(2)}) copy-start(pred[8,33]{0,1:T(8,128)(4,1)} %constant.243) | copy-start | bytes 796
  39.9 1.4 %copy-start.1 = (f32[16,256]{0,1:T(8,128)S(1)}, f32[16,256]{0,1:T(8,128)}, u32[]{:S(2)}) copy-start(f32[16,256]{0,1:T(8,128)} %copy.38) | copy-start | bytes 49156
  39.9 1.4 %copy-start.2 = (f32[256]{0:T(256)S(1)}, f32[256]{0:T(256)}, u32[]{:S(2)}) copy-start(f32[256]{0:T(256)} %param.11) | copy-start | bytes 3076
  42.4 8.2 %collective-permute-start.2 = (bf16[1,256,256]{2,0,1:T(2,128)(2,1)S(1)}, bf16[1,256,256]{2,0,1:T(2,128)(2,1)S(1)}, u32[]{:S(2)}, u32[]{:S(2)}) collective-permute-start(bf16[1,256,256]{2,0,1:T(2,128)(2,1)S(1)} %get-tuple-element.16), channel_id=1, source_target_pairs={{0,2},{2,4},{4,6},{6,8},{8,10},{10,12},{12,14},{1,3},{3,5},{5,7},{... | collective-permute-start | bytes 393224 | tf_op jit(solution)/shard_map/ppermute | solution.py:14
  49.1 3.4 %collective-permute-start.3 = (bf16[1,256,256]{2,0,1:T(2,128)(2,1)S(1)}, bf16[1,256,256]{2,0,1:T(2,128)(2,1)S(1)}, u32[]{:S(2)}, u32[]{:S(2)}) collective-permute-start(bf16[1,256,256]{2,0,1:T(2,128)(2,1)S(1)} %get-tuple-element.17), channel_id=1, source_target_pairs={{2,0},{4,2},{6,4},{8,6},{10,8},{12,10},{14,12},{3,1},{5,3},{7,5},{... | collective-permute-start | bytes 393224 | tf_op jit(solution)/shard_map/ppermute | solution.py:17
  54.9 1.3 %copy-start.3 = (bf16[3,3,256,256]{3,2,1,0:T(8,128)(2,1)S(1)}, bf16[3,3,256,256]{3,2,1,0:T(8,128)(2,1)}, u32[]{:S(2)}) copy-start(bf16[3,3,256,256]{3,2,1,0:T(8,128)(2,1)} %param.12) | copy-start | bytes 3538948
  61.7 1.4 %copy-start.4 = (bf16[19,256]{1,0:T(8,128)(2,1)S(1)}, bf16[19,256]{1,0:T(8,128)(2,1)}, u32[]{:S(2)}) copy-start(bf16[19,256]{1,0:T(8,128)(2,1)} %param.14) | copy-start | bytes 29188
  61.8 1.4 %copy-start.5 = (f32[256]{0:T(256)S(1)}, f32[256]{0:T(256)}, u32[]{:S(2)}) copy-start(f32[256]{0:T(256)} %param.13) | copy-start | bytes 3076
  61.8 1.4 %copy-start.6 = (f32[19]{0:T(128)S(1)}, f32[19]{0:T(128)}, u32[]{:S(2)}) copy-start(f32[19]{0:T(128)} %param.15) | copy-start | bytes 232
  65.6 12.0 %collective-permute-start.4 = (bf16[1,16,19,256]{3,1,2,0:T(8,128)(2,1)S(1)}, bf16[1,16,19,256]{3,1,2,0:T(8,128)(2,1)S(1)}, u32[]{:S(2)}, u32[]{:S(2)}) collective-permute-start(bf16[1,16,19,256]{3,1,2,0:T(8,128)(2,1)S(1)} %copy.43), channel_id=1, source_target_pairs={{0,8},{2,10},{4,12},{6,14},{8,0},{10,2},{12,4},{14,6},{1,9},{3,11}... | collective-permute-start | bytes 466952 | tf_op jit(solution)/shard_map/ppermute | solution.py:30
  77.6 10.2 %collective-permute-start.5 = (bf16[2,16,19,256]{3,1,2,0:T(8,128)(2,1)S(1)}, bf16[2,16,19,256]{3,1,2,0:T(8,128)(2,1)S(1)}, u32[]{:S(2)}, u32[]{:S(2)}) collective-permute-start(bf16[2,16,19,256]{3,1,2,0:T(8,128)(2,1)S(1)} %maximum_select_fusion.2), channel_id=1, source_target_pairs={{0,4},{2,6},{4,0},{6,2},{8,12},{10,14},{12,8},{14,10},{1,5},{3,7},... | collective-permute-start | bytes 933896 | tf_op jit(solution)/shard_map/ppermute | solution.py:30
  88.0 2.1 %collective-permute-start.6 = (bf16[4,16,19,256]{3,1,0,2:T(8,128)(2,1)S(1)}, bf16[4,16,19,256]{3,1,0,2:T(8,128)(2,1)S(1)}, u32[]{:S(2)}, u32[]{:S(2)}) collective-permute-start(bf16[4,16,19,256]{3,1,0,2:T(8,128)(2,1)S(1)} %bitcast.99), channel_id=1, source_target_pairs={{0,2},{2,0},{4,6},{6,4},{8,10},{10,8},{12,14},{14,12},{1,3},{3,1},... | collective-permute-start | bytes 1867784 | tf_op jit(solution)/shard_map/ppermute | solution.py:30
  90.5 6.1 %collective-permute-start.7 = (bf16[10,19,256]{2,0,1:T(8,128)(2,1)S(1)}, bf16[10,19,256]{2,0,1:T(8,128)(2,1)S(1)}, u32[]{:S(2)}, u32[]{:S(2)}) collective-permute-start(bf16[10,19,256]{2,0,1:T(8,128)(2,1)S(1)} %fusion.66), channel_id=1, source_target_pairs={{0,1},{1,0},{2,3},{3,2},{4,5},{5,4},{6,7},{7,6},{8,9},{9,8},{10,11... | collective-permute-start | bytes 291848 | tf_op jit(solution)/shard_map/ppermute | solution.py:132

commit v3 on v2

--- a/solution.py
+++ b/solution.py
@@ -1,6 +1,10 @@
+import functools
+
 import jax
 import jax.numpy as jnp
 from jax import lax
+from jax.experimental import pallas as pl
+from jax.experimental.pallas import tpu as pltpu
 from jax.sharding import PartitionSpec as P
 
 UP = 4
@@ -53,17 +57,56 @@
     return (first + second).astype(jnp.bfloat16)
 
 
-def convolve(field, weights):
-    padded = with_halo(field, (("space", 0),), 1)
-    out = lax.conv_general_dilated(
-        padded[None],
-        weights,
-        window_strides=(1, 1),
-        padding=((0, 0), (1, 1)),
-        dimension_numbers=("NHWC", "HWOI", "NHWC"),
-        preferred_element_type=jnp.float32,
+def conv_body(x_ref, w_ref, b_ref, s_ref, o_ref, *, block, width):
+    lo, hi, good_cols = s_ref[0], s_ref[1], s_ref[2]
+    chans = x_ref.shape[2]
+    flat = block * width
+    place = lax.broadcasted_iota(jnp.int32, (flat, 1), 0)
+    col = place % width
+    bias = b_ref[...]
+
+    def step(i, carry):
+        r0 = i * block
+        taps = []
+        for b in range(3):
+            acc = None
+            for a in range(3):
+                xs = x_ref[pl.ds(r0 + a, block), :, :].reshape(flat, chans)
+                d = lax.dot_general(
+                    xs, w_ref[a, b], (((1,), (1,)), ((), ())), preferred_element_type=jnp.float32
+                )
+                acc = d if acc is None else acc + d
+            taps.append(acc)
+        left = jnp.where(col == 0, 0.0, pltpu.roll(taps[0], 1, 0))
+        right = jnp.where(col == width - 1, 0.0, pltpu.roll(taps[2], flat - 1, 0))
+        total = jnp.maximum(taps[1] + left + right + bias, 0.0)
+        row = r0 + place // width
+        keep = (row >= lo) & (row < hi) & (col < good_cols)
+        out = jnp.where(keep, total, 0.0)
+        o_ref[pl.ds(r0, block), :, :] = out.reshape(block, width, -1).astype(o_ref.dtype)
+        return carry
+
+    lax.fori_loop(0, o_ref.shape[0] // block, step, 0)
+
+
+def conv_layer(x, weights, bias, limits):
+    rows_in, width, chans = x.shape
+    rows_out = rows_in - 2
+    outs = weights.shape[2]
+    block = next(k for k in (4, 3, 2, 1) if rows_out % k == 0)
+    vmem = pl.BlockSpec(memory_space=pltpu.VMEM)
+    cost = pl.CostEstimate(
+        flops=2 * 9 * rows_out * width * chans * outs,
+        bytes_accessed=2 * (x.size + weights.size + rows_out * width * outs),
+        transcendentals=0,
     )
-    return out[0]
+    return pl.pallas_call(
+        functools.partial(conv_body, block=block, width=width),
+        out_shape=jax.ShapeDtypeStruct((rows_out, width, outs), jnp.bfloat16),
+        in_specs=[vmem, vmem, vmem, pl.BlockSpec(memory_space=pltpu.SMEM)],
+        out_specs=vmem,
+        cost_estimate=cost,
+    )(x, weights, bias.reshape(1, -1), limits)
 
 
 def window_start(numer, first_row, full_rows, out_rows, window_rows):
@@ -98,11 +141,14 @@
     row_ids = place * rows_dev + jnp.arange(rows_dev, dtype=jnp.int32)
     row_ok = row_ids < valid_rows
     col_ok = jnp.arange(cols, dtype=jnp.int32) < valid_cols
-    mask = (row_ok[:, None] & col_ok[None, :]).astype(jnp.float32)
-    first = jnp.transpose(feat * mask.astype(jnp.bfloat16), (1, 2, 0))
-    cell = mask[:, :, None]
-    hidden = (jax.nn.relu(convolve(first, conv_first) + bias_first) * cell).astype(jnp.bfloat16)
-    second = (jax.nn.relu(convolve(hidden, conv_second) + bias_second) * cell).astype(jnp.bfloat16)
+    mask = (row_ok[:, None] & col_ok[None, :]).astype(jnp.bfloat16)
+    first = jnp.transpose(feat * mask, (1, 2, 0))
+    padded = with_halo(first, (("space", 0),), 2)
+    top = place * rows_dev
+    limits_first = jnp.stack([1 - top, valid_rows - top + 1, valid_cols]).astype(jnp.int32)
+    limits_second = jnp.stack([-top, valid_rows - top, valid_cols]).astype(jnp.int32)
+    hidden = conv_layer(padded, conv_first, bias_first, limits_first)
+    second = conv_layer(hidden, conv_second, bias_second, limits_second)
     logits = (
         jnp.einsum("kc,yxc->ykx", classify, second, preferred_element_type=jnp.float32)
         + class_bias[None, :, None]

time: 101 us -> 81.2 us (0.80)
  Pallas kernels: 0 us -> 20.5 us
  local copies, waits for them, and re-layouts: 22.6 us -> 4.71 us
  matrix products: 19.4 us -> 6.1 us
  starting transfers between devices: 19.6 us -> 11.9 us
  other arithmetic: 11.4 us -> 6.44 us
  waiting for transfers between devices: 19.6 us -> 23.2 us
    pallas_call x0 -> x2, Pallas kernels: none -> 20.5 us  [conv_layer(): pl.pallas_call(functools.partial(conv_body, block=block, width=width), ou...]
    conv_general_dilated x2 -> x0, matrix products: 11.5 us -> none  [convolve(): lax.conv_general_dilated(padded[None], weights, window_strides=(1, 1), pa...]
    conv_general_dilated x7 -> x0, local copies, waits for them, and re-layouts: 10.7 us -> none  [convolve(): lax.conv_general_dilated(padded[None], weights, window_strides=(1, 1), pa...]
    broadcast_in_dim x2 -> x0, other arithmetic: 6.88 us -> none  [convolve(): padded[None]]
    ppermute x2 -> x1, starting transfers between devices: 9.02 us -> 2.37 us  [with_halo(): lax.ppermute(lax.slice_in_dim(block, block.shape[dim] - width, None, axis...]
    ppermute x3, waiting for transfers between devices: 11.9 us -> 16.1 us  [gather_rows(): other = lax.ppermute(held, axis, [(i, i ^ bit) for i in range(count)])]
    broadcast_in_dim x3 -> x0, local copies, waits for them, and re-layouts: 3.94 us -> none  [the longest x2 2.94 us: convolve(): padded[None]]
    dot_general x2, matrix products: 6.59 us -> 3.86 us  [shards(): jnp.einsum('iy,ycj->icj', row_part, widened, preferred_element_type=jnp.f...]
  transfers between devices with their start and end apart: 8 -> 6, of which waited for: 6 -> 5; matrix products, arithmetic and copies ran while one was open for 5% -> 3% of each run, Pallas kernels for 0% -> 0%
where the time goes in v3:
time: 81.2 us; the launch traced here: 80.8 us
  waiting for transfers between devices  23.2 us (29%)
  Pallas kernels  20.5 us (25%)
  starting transfers between devices  11.9 us (15%)
  between operations  7.91 us (10%)
  other arithmetic  6.44 us (8%)
  matrix products  6.1 us (8%)
  local copies, waits for them, and re-layouts  4.71 us (6%)
    pallas_call x2, Pallas kernels, conv_layer(): pl.pallas_call(functools.partial(conv_body, block=block, width=width), ou...  20.5 us
    ppermute x3, waiting for transfers between devices, gather_rows(): other = lax.ppermute(held, axis, [(i, i ^ bit) for i in range(count)])  16.1 us
    ppermute x3, starting transfers between devices, gather_rows(): other = lax.ppermute(held, axis, [(i, i ^ bit) for i in range(count)])  6.73 us
    unnamed x5, local copies, waits for them, and re-layouts  4.28 us
    dot_general x2, matrix products, shards(): jnp.einsum('iy,ycj->icj', row_part, widened, preferred_element_type=jnp.f...  3.86 us
    ppermute x1, waiting for transfers between devices, with_halo(): lax.ppermute(lax.slice_in_dim(block, 0, width, axis=dim), axis, backward)  3.7 us
    ppermute x1, waiting for transfers between devices, shards(): lax.ppermute(send, 'member', [(i, (i + shift) % members) for i in range(m...  3.41 us
    ppermute x1, starting transfers between devices, with_halo(): lax.ppermute(lax.slice_in_dim(block, block.shape[dim] - width, None, axis...  2.37 us
  transfers between devices with their start and end apart: 6, of which 5 were waited for; matrix products, arithmetic and copies ran while one was open for 3% of the time, Pallas kernels for 0%

profile of v3, /device:TPU:0, one launch (start us, length us, event | category | flops | bytes accessed | tf_op | source)
XLA Modules:
  0.0 80.8 jit_solution(7387113940101491266)
XLA Ops:
  0.0 1.3 %fusion.66 = (s32[]{:T(128)}, s32[]{:T(128)}, s32[]{:T(128)}) fusion(s32[2]{0:T(128)} %param.9, s32[]{:T(128)S(6)} %select_n.540, s32[]{:T(128)S(6)} %select_n.493, s32[]{:T(128)S(6)} %axis_index.29), kind=kLoop, calls=%fused_computation.111 | loop fusion | flops 15 | bytes 32 | tf_op jit(solution)/shard_map/reduce_sum | solution.py:182
  4.0 4.3 %copy.10 = bf16[1,256,16,256]{1,3,2,0:T(8,128)(2,1)} copy(bf16[1,256,16,256]{3,2,1,0:T(8,128)(2,1)} %param.8) | data formatting | bytes 4194304 | tf_op args[0]
  8.3 0.1 and_convert_fusion
  8.4 1.9 %fusion = bf16[16,256,256]{2,1,0:T(8,128)(2,1)S(1)} fusion(bf16[1,256,16,256]{1,3,2,0:T(8,128)(2,1)} %copy.10, bf16[16,256]{1,0:T(8,128)(2,1)S(1)} %and_convert_fusion), kind=kLoop, calls=%fused_computation.2 | loop fusion | flops 1048576 | bytes 4202496 | tf_op jit(solution)/shard_map/transpose | solution.py:145
  10.3 2.4 %collective-permute-start = (bf16[2,256,256]{2,1,0:T(8,128)(2,1)S(1)}, bf16[2,256,256]{2,1,0:T(8,128)(2,1)S(1)}, u32[]{:S(2)}, u32[]{:S(2)}) collective-permute-start(bf16[2,256,256]{2,1,0:T(8,128)(2,1)S(1)} %get-tuple-element.16), channel_id=1, source_target_pairs={{0,2},{2,4},{4,6},{6,8},{8,10},{10,12},{12,14},{1,3},{3,5},{5,7},{... | collective-permute-start | bytes 786440 | tf_op jit(solution)/shard_map/ppermute | solution.py:18
  12.7 1.3 %collective-permute-start.1 = (bf16[2,256,256]{2,1,0:T(8,128)(2,1)S(1)}, bf16[2,256,256]{2,1,0:T(8,128)(2,1)S(1)}, u32[]{:S(2)}, u32[]{:S(2)}) collective-permute-start(bf16[2,256,256]{2,1,0:T(8,128)(2,1)S(1)} %get-tuple-element.17), channel_id=1, source_target_pairs={{2,0},{4,2},{6,4},{8,6},{10,8},{12,10},{14,12},{3,1},{5,3},{7,5},{... | collective-permute-start | bytes 786440 | tf_op jit(solution)/shard_map/ppermute | solution.py:21
  14.0 0.6 add_add_fusion
  14.6 0.0 collective-permute-done
  14.6 3.7 %collective-permute-done.1 = bf16[2,256,256]{2,1,0:T(8,128)(2,1)S(1)} collective-permute-done((bf16[2,256,256]{2,1,0:T(8,128)(2,1)S(1)}, bf16[2,256,256]{2,1,0:T(8,128)(2,1)S(1)}, u32[]{:S(2)}, u32[]{:S(2)}) %collective-permute-start.1) | collective-permute-done | bytes 262176 | tf_op jit(solution)/shard_map/ppermute | solution.py:21
  18.3 1.8 %pad_maximum_fusion.x_ref = bf16[20,256,256]{2,1,0:T(8,128)(2,1)} fusion(bf16[2,256,256]{2,1,0:T(8,128)(2,1)S(1)} %collective-permute-done.1, bf16[16,256,256]{2,1,0:T(8,128)(2,1)S(1)} %fusion, bf16[2,256,256]{2,1,0:T(8,128)(2,1)S(1)} %collective-permute-done), kind=kLoop, calls=%fused_computation | loop fusion | flops 2621440 | bytes 5242880 | tf_op jit(solution)/shard_map/concatenate | solution.py:22
  20.2 10.8 %shard_map.82.x_ref = bf16[18,256,256]{2,1,0:T(8,128)(2,1)} custom-call(bf16[20,256,256]{2,1,0:T(8,128)(2,1)} %pad_maximum_fusion.x_ref, bf16[3,3,256,256]{3,2,1,0:T(8,128)(2,1)} %w_ref.2, f32[1,256]{1,0:T(1,128)} %bitcast.62, s32[3]{0:T(128)} %get-tuple-element.20.s_ref), custom_call_target="tpu_custom_call" | custom-call | flops 5435817984 | bytes 6160384 | tf_op jit(solution)/shard_map/pallas_call | solution.py:103
  31.0 9.7 %shard_map.83 = bf16[16,256,256]{2,1,0:T(8,128)(2,1)} custom-call(bf16[18,256,256]{2,1,0:T(8,128)(2,1)} %shard_map.82.x_ref, bf16[3,3,256,256]{3,2,1,0:T(8,128)(2,1)} %w_ref.3, f32[1,256]{1,0:T(1,128)} %bitcast.63, s32[3]{0:T(128)} %get-tuple-element.21.s_ref), custom_call_target="tpu_custom_call" | custom-call | flops 4831838208 | bytes 5636096 | tf_op jit(solution)/shard_map/pallas_call | solution.py:103
  40.6 0.0 copy-done.1
  40.6 2.2 %fusion.2 = bf16[16,256,19]{1,2,0:T(8,128)(2,1)S(1)} fusion(bf16[16,256,256]{2,1,0:T(8,128)(2,1)} %shard_map.83, f32[19]{0:T(128)S(1)} %copy-done.1, bf16[19,256]{1,0:T(8,128)(2,1)S(1)} %copy-done), kind=kOutput, calls=%fused_computation.9 | convolution fusion | flops 40001536 | bytes 2262604 | tf_op jit(solution)/shard_map/kc,yxc->ykx/dot_general | solution.py:153
  42.9 5.6 %collective-permute-start.2 = (bf16[1,16,19,256]{3,2,1,0:T(8,128)(2,1)S(1)}, bf16[1,16,19,256]{3,2,1,0:T(8,128)(2,1)S(1)}, u32[]{:S(2)}, u32[]{:S(2)}) collective-permute-start(bf16[1,16,19,256]{3,2,1,0:T(8,128)(2,1)S(1)} %bitcast.56), channel_id=1, source_target_pairs={{0,8},{2,10},{4,12},{6,14},{8,0},{10,2},{12,4},{14,6},{1,9},{3,11}... | collective-permute-start | bytes 466952 | tf_op jit(solution)/shard_map/ppermute | solution.py:34
  53.6 3.6 %collective-permute-done.2 = bf16[1,16,19,256]{3,2,1,0:T(8,128)(2,1)S(1)} collective-permute-done((bf16[1,16,19,256]{3,2,1,0:T(8,128)(2,1)S(1)}, bf16[1,16,19,256]{3,2,1,0:T(8,128)(2,1)S(1)}, u32[]{:S(2)}, u32[]{:S(2)}) %collective-permute-start.2) | collective-permute-done | bytes 155680 | tf_op jit(solution)/shard_map/ppermute | solution.py:34
  57.2 0.1 maximum_select_fusion.2
  57.2 1.0 %collective-permute-start.3 = (bf16[2,16,19,256]{3,2,1,0:T(8,128)(2,1)S(1)}, bf16[2,16,19,256]{3,2,1,0:T(8,128)(2,1)S(1)}, u32[]{:S(2)}, u32[]{:S(2)}) collective-permute-start(bf16[2,16,19,256]{3,2,1,0:T(8,128)(2,1)S(1)} %maximum_select_fusion.2), channel_id=1, source_target_pairs={{0,4},{2,6},{4,0},{6,2},{8,12},{10,14},{12,8},{14,10},{1,5},{3,7},... | collective-permute-start | bytes 933896 | tf_op jit(solution)/shard_map/ppermute | solution.py:34
  58.3 0.1 maximum_select_fusion.3
  58.4 10.9 %collective-permute-done.3 = bf16[2,16,19,256]{3,2,1,0:T(8,128)(2,1)S(1)} collective-permute-done((bf16[2,16,19,256]{3,2,1,0:T(8,128)(2,1)S(1)}, bf16[2,16,19,256]{3,2,1,0:T(8,128)(2,1)S(1)}, u32[]{:S(2)}, u32[]{:S(2)}) %collective-permute-start.3) | collective-permute-done | bytes 311328 | tf_op jit(solution)/shard_map/ppermute | solution.py:34
  69.2 0.1 maximum_select_fusion.1
  69.4 0.1 copy.11
  69.5 0.2 collective-permute-start.4
  69.8 0.1 copy.12
  70.0 1.6 %collective-permute-done.4 = bf16[4,16,19,256]{3,1,0,2:T(8,128)(2,1)S(1)} collective-permute-done((bf16[4,16,19,256]{3,1,0,2:T(8,128)(2,1)S(1)}, bf16[4,16,19,256]{3,1,0,2:T(8,128)(2,1)S(1)}, u32[]{:S(2)}, u32[]{:S(2)}) %collective-permute-start.4) | collective-permute-done | bytes 622624 | tf_op jit(solution)/shard_map/ppermute | solution.py:34
  71.6 0.1 maximum_select_fusion
  71.7 0.1 dynamic-slice_bitcast_fusion
  71.9 0.1 fusion.30
  72.0 1.5 %collective-permute-start.5 = (bf16[10,19,256]{2,0,1:T(8,128)(2,1)S(1)}, bf16[10,19,256]{2,0,1:T(8,128)(2,1)S(1)}, u32[]{:S(2)}, u32[]{:S(2)}) collective-permute-start(bf16[10,19,256]{2,0,1:T(8,128)(2,1)S(1)} %fusion.30), channel_id=1, source_target_pairs={{0,1},{1,0},{2,3},{3,2},{4,5},{5,4},{6,7},{7,6},{8,9},{9,8},{10,11... | collective-permute-start | bytes 291848 | tf_op jit(solution)/shard_map/ppermute | solution.py:178
  73.5 1.2 %fusion.1 = f32[32,19,1024]{2,0,1:T(8,128)S(1)} fusion(f32[1024]{0:T(1024)S(1)} %get-tuple-element.22, s32[1024]{0:T(1024)S(1)} %get-tuple-element.25, f32[1024]{0:T(1024)S(1)} %get-tuple-element.23, s32[1024]{0:T(1024)S(1)} %get-tuple-element.24, s32[]{:T(128)S(6)} %select_n.528, bf16[1,10,19,256]{3,1,2,0:T(8,128)(2,1)S(1)} %get-tuple-element.19, ...), kind=kOutput, calls=%fused_computation.6 | convolution fusion | flops 113884864 | bytes 2701832 | tf_op jit(solution)/shard_map/iy,ycj->icj/dot_general | solution.py:193
  74.7 3.4 %collective-permute-done.5 = bf16[10,19,256]{2,0,1:T(8,128)(2,1)S(1)} collective-permute-done((bf16[10,19,256]{2,0,1:T(8,128)(2,1)S(1)}, bf16[10,19,256]{2,0,1:T(8,128)(2,1)S(1)}, u32[]{:S(2)}, u32[]{:S(2)}) %collective-permute-start.5) | collective-permute-done | bytes 97312 | tf_op jit(solution)/shard_map/ppermute | solution.py:178
  78.1 2.7 %convolution_add_fusion = f32[32,19,1024]{2,0,1:T(8,128)} fusion(f32[32,19,1024]{2,0,1:T(8,128)S(1)} %fusion.1, bf16[10,19,256]{2,0,1:T(8,128)(2,1)S(1)} %collective-permute-done.5, f32[1024]{0:T(1024)S(1)} %get-tuple-element.26, s32[1024]{0:T(1024)S(1)} %get-tuple-element.29, f32[1024]{0:T(1024)S(1)} %get-tuple-element.27, s32[1024]{0:T(1024)S(1)} %get-tuple-element.28, ...), kind=kOutput, calls=%fused_computation.3 | convolution fusion | flops 114458816 | bytes 5094916 | tf_op jit(solution)/shard_map/iy,ycj->icj/dot_general | solution.py:193
  (14 shorter events, 0.2 us)
Async XLA Ops:
  0.0 40.6 %copy-start = (bf16[19,256]{1,0:T(8,128)(2,1)S(1)}, bf16[19,256]{1,0:T(8,128)(2,1)}, u32[]{:S(2)}) copy-start(bf16[19,256]{1,0:T(8,128)(2,1)} %param.14) | copy-start | bytes 29188
  10.3 4.3 %collective-permute-start = (bf16[2,256,256]{2,1,0:T(8,128)(2,1)S(1)}, bf16[2,256,256]{2,1,0:T(8,128)(2,1)S(1)}, u32[]{:S(2)}, u32[]{:S(2)}) collective-permute-start(bf16[2,256,256]{2,1,0:T(8,128)(2,1)S(1)} %get-tuple-element.16), channel_id=1, source_target_pairs={{0,2},{2,4},{4,6},{6,8},{8,10},{10,12},{12,14},{1,3},{3,5},{5,7},{... | collective-permute-start | bytes 786440 | tf_op jit(solution)/shard_map/ppermute | solution.py:18
  12.7 5.6 %collective-permute-start.1 = (bf16[2,256,256]{2,1,0:T(8,128)(2,1)S(1)}, bf16[2,256,256]{2,1,0:T(8,128)(2,1)S(1)}, u32[]{:S(2)}, u32[]{:S(2)}) collective-permute-start(bf16[2,256,256]{2,1,0:T(8,128)(2,1)S(1)} %get-tuple-element.17), channel_id=1, source_target_pairs={{2,0},{4,2},{6,4},{8,6},{10,8},{12,10},{14,12},{3,1},{5,3},{7,5},{... | collective-permute-start | bytes 786440 | tf_op jit(solution)/shard_map/ppermute | solution.py:21
  31.0 9.7 %copy-start.1 = (f32[19]{0:T(128)S(1)}, f32[19]{0:T(128)}, u32[]{:S(2)}) copy-start(f32[19]{0:T(128)} %param.15) | copy-start | bytes 232
  42.9 14.3 %collective-permute-start.2 = (bf16[1,16,19,256]{3,2,1,0:T(8,128)(2,1)S(1)}, bf16[1,16,19,256]{3,2,1,0:T(8,128)(2,1)S(1)}, u32[]{:S(2)}, u32[]{:S(2)}) collective-permute-start(bf16[1,16,19,256]{3,2,1,0:T(8,128)(2,1)S(1)} %bitcast.56), channel_id=1, source_target_pairs={{0,8},{2,10},{4,12},{6,14},{8,0},{10,2},{12,4},{14,6},{1,9},{3,11}... | collective-permute-start | bytes 466952 | tf_op jit(solution)/shard_map/ppermute | solution.py:34
  57.2 12.0 %collective-permute-start.3 = (bf16[2,16,19,256]{3,2,1,0:T(8,128)(2,1)S(1)}, bf16[2,16,19,256]{3,2,1,0:T(8,128)(2,1)S(1)}, u32[]{:S(2)}, u32[]{:S(2)}) collective-permute-start(bf16[2,16,19,256]{3,2,1,0:T(8,128)(2,1)S(1)} %maximum_select_fusion.2), channel_id=1, source_target_pairs={{0,4},{2,6},{4,0},{6,2},{8,12},{10,14},{12,8},{14,10},{1,5},{3,7},... | collective-permute-start | bytes 933896 | tf_op jit(solution)/shard_map/ppermute | solution.py:34
  69.5 2.1 %collective-permute-start.4 = (bf16[4,16,19,256]{3,1,0,2:T(8,128)(2,1)S(1)}, bf16[4,16,19,256]{3,1,0,2:T(8,128)(2,1)S(1)}, u32[]{:S(2)}, u32[]{:S(2)}) collective-permute-start(bf16[4,16,19,256]{3,1,0,2:T(8,128)(2,1)S(1)} %copy.11), channel_id=1, source_target_pairs={{0,2},{2,0},{4,6},{6,4},{8,10},{10,8},{12,14},{14,12},{1,3},{3,1},... | collective-permute-start | bytes 1867784 | tf_op jit(solution)/shard_map/ppermute | solution.py:34
  72.0 6.1 %collective-permute-start.5 = (bf16[10,19,256]{2,0,1:T(8,128)(2,1)S(1)}, bf16[10,19,256]{2,0,1:T(8,128)(2,1)S(1)}, u32[]{:S(2)}, u32[]{:S(2)}) collective-permute-start(bf16[10,19,256]{2,0,1:T(8,128)(2,1)S(1)} %fusion.30), channel_id=1, source_target_pairs={{0,1},{1,0},{2,3},{3,2},{4,5},{5,4},{6,7},{7,6},{8,9},{9,8},{10,11... | collective-permute-start | bytes 291848 | tf_op jit(solution)/shard_map/ppermute | solution.py:178

commit v4 on v3

--- a/solution.py
+++ b/solution.py
@@ -26,17 +26,18 @@
 def gather_rows(block, axis):
     count = lax.axis_size(axis)
     if count & (count - 1):
-        return lax.all_gather(block, axis, axis=0, tiled=True)
+        return lax.all_gather(block, axis, axis=1, tiled=True)
     me = lax.axis_index(axis)
-    held = block[None]
+    lead, rows, rest = block.shape[0], block.shape[1], block.shape[2:]
+    held = block[:, None]
     bit = count // 2
     while bit:
         other = lax.ppermute(held, axis, [(i, i ^ bit) for i in range(count)])
         upper = (me & bit) != 0
-        held = jnp.where(upper, jnp.stack([other, held], 1), jnp.stack([held, other], 1))
-        held = held.reshape((-1,) + block.shape)
+        held = jnp.where(upper, jnp.stack([other, held], 2), jnp.stack([held, other], 2))
+        held = held.reshape((lead, -1, rows) + rest)
         bit //= 2
-    return held.reshape((count * block.shape[0],) + block.shape[1:])
+    return held.reshape((lead, count * rows) + rest)
 
 
 def resize_matrix(positions, out_len, valid, in_len):
@@ -57,11 +58,14 @@
     return (first + second).astype(jnp.bfloat16)
 
 
-def conv_body(x_ref, w_ref, b_ref, s_ref, o_ref, *, block, width):
+def conv_body(*refs, block, width, project):
+    if project:
+        x_ref, w_ref, b_ref, k_ref, kb_ref, s_ref, o_ref = refs
+    else:
+        x_ref, w_ref, b_ref, s_ref, o_ref = refs
     lo, hi, good_cols = s_ref[0], s_ref[1], s_ref[2]
-    chans = x_ref.shape[2]
     flat = block * width
-    place = lax.broadcasted_iota(jnp.int32, (flat, 1), 0)
+    place = lax.broadcasted_iota(jnp.int32, (1, flat), 1)
     col = place % width
     bias = b_ref[...]
 
@@ -71,42 +75,51 @@
         for b in range(3):
             acc = None
             for a in range(3):
-                xs = x_ref[pl.ds(r0 + a, block), :, :].reshape(flat, chans)
-                d = lax.dot_general(
-                    xs, w_ref[a, b], (((1,), (1,)), ((), ())), preferred_element_type=jnp.float32
-                )
+                start = pl.multiple_of((r0 + a) * width, width)
+                xs = x_ref[:, pl.ds(start, flat)]
+                d = jnp.dot(w_ref[a, b], xs, preferred_element_type=jnp.float32)
                 acc = d if acc is None else acc + d
             taps.append(acc)
-        left = jnp.where(col == 0, 0.0, pltpu.roll(taps[0], 1, 0))
-        right = jnp.where(col == width - 1, 0.0, pltpu.roll(taps[2], flat - 1, 0))
+        left = jnp.where(col == 0, 0.0, pltpu.roll(taps[0], 1, 1))
+        right = jnp.where(col == width - 1, 0.0, pltpu.roll(taps[2], flat - 1, 1))
         total = jnp.maximum(taps[1] + left + right + bias, 0.0)
         row = r0 + place // width
         keep = (row >= lo) & (row < hi) & (col < good_cols)
-        out = jnp.where(keep, total, 0.0)
-        o_ref[pl.ds(r0, block), :, :] = out.reshape(block, width, -1).astype(o_ref.dtype)
+        out = jnp.where(keep, total, 0.0).astype(jnp.bfloat16)
+        if project:
+            out = jnp.dot(k_ref[...], out, preferred_element_type=jnp.float32) + kb_ref[...]
+        o_ref[:, pl.ds(pl.multiple_of(r0 * width, width), flat)] = out.astype(o_ref.dtype)
         return carry
 
-    lax.fori_loop(0, o_ref.shape[0] // block, step, 0)
-
-
-def conv_layer(x, weights, bias, limits):
-    rows_in, width, chans = x.shape
+    lax.fori_loop(0, o_ref.shape[1] // flat, step, 0)
+
+
+def conv_layer(x, weights, bias, limits, head=None):
+    chans, rows_in, width = x.shape
     rows_out = rows_in - 2
     outs = weights.shape[2]
     block = next(k for k in (4, 3, 2, 1) if rows_out % k == 0)
     vmem = pl.BlockSpec(memory_space=pltpu.VMEM)
+    args = [x.reshape(chans, rows_in * width), weights, bias.reshape(-1, 1)]
+    flops = 2 * 9 * rows_out * width * chans * outs
+    final = outs
+    if head is not None:
+        args += [head[0], head[1].reshape(-1, 1)]
+        final = head[0].shape[0]
+        flops += 2 * rows_out * width * outs * final
     cost = pl.CostEstimate(
-        flops=2 * 9 * rows_out * width * chans * outs,
-        bytes_accessed=2 * (x.size + weights.size + rows_out * width * outs),
+        flops=flops,
+        bytes_accessed=2 * (x.size + weights.size + rows_out * width * final),
         transcendentals=0,
     )
-    return pl.pallas_call(
-        functools.partial(conv_body, block=block, width=width),
-        out_shape=jax.ShapeDtypeStruct((rows_out, width, outs), jnp.bfloat16),
-        in_specs=[vmem, vmem, vmem, pl.BlockSpec(memory_space=pltpu.SMEM)],
+    out = pl.pallas_call(
+        functools.partial(conv_body, block=block, width=width, project=head is not None),
+        out_shape=jax.ShapeDtypeStruct((final, rows_out * width), jnp.bfloat16),
+        in_specs=[vmem] * len(args) + [pl.BlockSpec(memory_space=pltpu.SMEM)],
         out_specs=vmem,
         cost_estimate=cost,
-    )(x, weights, bias.reshape(1, -1), limits)
+    )(*args, limits)
+    return out.reshape(final, rows_out, width)
 
 
 def window_start(numer, first_row, full_rows, out_rows, window_rows):
@@ -142,17 +155,13 @@
     row_ok = row_ids < valid_rows
     col_ok = jnp.arange(cols, dtype=jnp.int32) < valid_cols
     mask = (row_ok[:, None] & col_ok[None, :]).astype(jnp.bfloat16)
-    first = jnp.transpose(feat * mask, (1, 2, 0))
-    padded = with_halo(first, (("space", 0),), 2)
+    first = feat * mask
+    padded = with_halo(first, (("space", 1),), 2)
     top = place * rows_dev
     limits_first = jnp.stack([1 - top, valid_rows - top + 1, valid_cols]).astype(jnp.int32)
     limits_second = jnp.stack([-top, valid_rows - top, valid_cols]).astype(jnp.int32)
     hidden = conv_layer(padded, conv_first, bias_first, limits_first)
-    second = conv_layer(hidden, conv_second, bias_second, limits_second)
-    logits = (
-        jnp.einsum("kc,yxc->ykx", classify, second, preferred_element_type=jnp.float32)
-        + class_bias[None, :, None]
-    ).astype(jnp.bfloat16)
+    logits = conv_layer(hidden, conv_second, bias_second, limits_second, (classify, class_bias))
     out_rows = UP * full_rows
     out_cols = UP * cols
     own_rows = out_rows // spaces
@@ -163,11 +172,11 @@
     for target in range(members):
         first_row = place * own_rows + target * part_rows
         begin = window_start(numer, first_row, full_rows, out_rows, window_rows)
-        pieces.append(lax.dynamic_slice_in_dim(gathered, begin, window_rows, 0))
+        pieces.append(lax.dynamic_slice_in_dim(gathered, begin, window_rows, 1))
     outgoing = jnp.stack(pieces, 0)
     own_first = place * own_rows + member_index * part_rows
     positions = own_first + jnp.arange(part_rows, dtype=jnp.int32)
-    result = jnp.zeros((part_rows, logits.shape[1], out_cols), jnp.float32)
+    result = jnp.zeros((part_rows, logits.shape[0], out_cols), jnp.float32)
     for shift in range(members):
         if shift == 0:
             arrived = lax.dynamic_index_in_dim(outgoing, member_index, 0, keepdims=False)
@@ -188,10 +197,10 @@
         row_table = resize_matrix(positions, out_rows, source_valid, full_rows)
         row_part = lax.dynamic_slice_in_dim(row_table, begin, window_rows, 1)
         widened = jnp.einsum(
-            "ycx,jx->ycj", arrived, source_cols, preferred_element_type=jnp.float32
+            "cyx,jx->cyj", arrived, source_cols, preferred_element_type=jnp.float32
         ).astype(jnp.bfloat16)
         result = result + jnp.einsum(
-            "iy,ycj->icj", row_part, widened, preferred_element_type=jnp.float32
+            "iy,cyj->icj", row_part, widened, preferred_element_type=jnp.float32
         )
     return result
 

time: 81.2 us -> 81 us (level)
  local copies, waits for them, and re-layouts: 4.71 us -> 12.2 us
  waiting for transfers between devices: 23.2 us -> 17.1 us
  matrix products: 6.1 us -> 3.86 us
    reshape x0 -> x4, local copies, waits for them, and re-layouts: none -> 6.71 us  [the longest x3 6.02 us: conv_layer(): args = [x.reshape(chans, rows_in * width), weights, bias.reshape(-1, 1)]]
    ppermute x3, waiting for transfers between devices: 16.1 us -> 12.4 us  [gather_rows(): other = lax.ppermute(held, axis, [(i, i ^ bit) for i in range(count)])]
    ppermute x1, waiting for transfers between devices: 3.7 us -> 1.35 us  [with_halo(): lax.ppermute(lax.slice_in_dim(block, 0, width, axis=dim), axis, backward)]
    dot_general x3 -> x2, matrix products: 6.1 us -> 3.86 us  [shards(): jnp.einsum('iy,cyj->icj', row_part, widened, preferred_element_type=jnp.f...]
    mul x0 -> x1, other arithmetic: none -> 1.96 us  [shards(): first = feat * mask]
    transpose x1 -> x0, other arithmetic: 1.92 us -> none  [shards(): first = jnp.transpose(feat * mask, (1, 2, 0))]
    unnamed x5 -> x8, local copies, waits for them, and re-layouts: 4.28 us -> 5.25 us
  transfers between devices with their start and end apart: 6 -> 6, of which waited for: 5 -> 5; matrix products, arithmetic and copies ran while one was open for 3% -> 5% of each run, Pallas kernels for 0% -> 0%
where the time goes in v4:
time: 81 us; the launch traced here: 80.5 us
  Pallas kernels  20.6 us (25%)
  waiting for transfers between devices  17.1 us (21%)
  local copies, waits for them, and re-layouts  12.2 us (15%)
  starting transfers between devices  12 us (15%)
  between operations  8.29 us (10%)
  other arithmetic  6.41 us (8%)
  matrix products  3.86 us (5%)
    pallas_call x2, Pallas kernels, conv_layer(): pl.pallas_call(functools.partial(conv_body, block=block, width=width, pro...  20.6 us
    ppermute x3, waiting for transfers between devices, gather_rows(): other = lax.ppermute(held, axis, [(i, i ^ bit) for i in range(count)])  12.4 us
    ppermute x3, starting transfers between devices, gather_rows(): other = lax.ppermute(held, axis, [(i, i ^ bit) for i in range(count)])  6.74 us
    reshape x3, local copies, waits for them, and re-layouts, conv_layer(): args = [x.reshape(chans, rows_in * width), weights, bias.reshape(-1, 1)]  6.02 us
    unnamed x8, local copies, waits for them, and re-layouts  5.25 us
    dot_general x2, matrix products, shards(): jnp.einsum('iy,cyj->icj', row_part, widened, preferred_element_type=jnp.f...  3.86 us
    ppermute x1, waiting for transfers between devices, shards(): lax.ppermute(send, 'member', [(i, (i + shift) % members) for i in range(m...  3.34 us
    ppermute x1, starting transfers between devices, with_halo(): lax.ppermute(lax.slice_in_dim(block, block.shape[dim] - width, None, axis...  2.37 us
  transfers between devices with their start and end apart: 6, of which 5 were waited for; matrix products, arithmetic and copies ran while one was open for 5% of the time, Pallas kernels for 0%

profile of v4, /device:TPU:0, one launch (start us, length us, event | category | flops | bytes accessed | tf_op | source)
XLA Modules:
  0.0 80.5 jit_solution(11674090262502565248)
XLA Ops:
  0.0 1.4 %fusion.63 = (s32[]{:T(128)}, s32[]{:T(128)}, s32[]{:T(128)}) fusion(s32[2]{0:T(128)} %param.9, s32[]{:T(128)S(6)} %select_n.540, s32[]{:T(128)S(6)} %select_n.493, s32[]{:T(128)S(6)} %axis_index.29), kind=kLoop, calls=%fused_computation.109 | loop fusion | flops 15 | bytes 32 | tf_op jit(solution)/shard_map/reduce_sum | solution.py:191
  4.0 4.3 %copy.10 = bf16[1,256,16,256]{1,3,2,0:T(8,128)(2,1)} copy(bf16[1,256,16,256]{3,2,1,0:T(8,128)(2,1)} %param.8) | data formatting | bytes 4194304 | tf_op args[0]
  8.3 0.1 and_convert_fusion
  8.4 2.0 %bitcast_multiply_fusion = bf16[256,16,256]{0,2,1:T(8,128)(2,1)S(1)} fusion(bf16[1,256,16,256]{1,3,2,0:T(8,128)(2,1)} %copy.10, bf16[16,256]{1,0:T(8,128)(2,1)S(1)} %and_convert_fusion), kind=kLoop, calls=%fused_computation.1 | loop fusion | flops 1048576 | bytes 4202496 | tf_op jit(solution)/shard_map/mul | solution.py:158
  10.4 2.4 %collective-permute-start = (bf16[256,2,256]{0,2,1:T(8,128)(2,1)S(1)}, bf16[256,2,256]{0,2,1:T(8,128)(2,1)S(1)}, u32[]{:S(2)}, u32[]{:S(2)}) collective-permute-start(bf16[256,2,256]{0,2,1:T(8,128)(2,1)S(1)} %get-tuple-element.16), channel_id=1, source_target_pairs={{0,2},{2,4},{4,6},{6,8},{8,10},{10,12},{12,14},{1,3},{3,5},{5,7},{... | collective-permute-start | bytes 786440 | tf_op jit(solution)/shard_map/ppermute | solution.py:18
  12.8 1.3 %collective-permute-start.1 = (bf16[256,2,256]{0,2,1:T(8,128)(2,1)S(1)}, bf16[256,2,256]{0,2,1:T(8,128)(2,1)S(1)}, u32[]{:S(2)}, u32[]{:S(2)}) collective-permute-start(bf16[256,2,256]{0,2,1:T(8,128)(2,1)S(1)} %get-tuple-element.17), channel_id=1, source_target_pairs={{2,0},{4,2},{6,4},{8,6},{10,8},{12,10},{14,12},{3,1},{5,3},{7,5},{... | collective-permute-start | bytes 786440 | tf_op jit(solution)/shard_map/ppermute | solution.py:21
  14.1 0.8 copy.12.refs_2_
  14.9 0.8 copy.13.refs_2_
  15.7 0.7 copy.14.refs_4_
  16.4 0.6 add_add_fusion
  17.1 0.0 collective-permute-done
  17.1 1.4 %collective-permute-done.1 = bf16[256,2,256]{0,2,1:T(8,128)(2,1)S(1)} collective-permute-done((bf16[256,2,256]{0,2,1:T(8,128)(2,1)S(1)}, bf16[256,2,256]{0,2,1:T(8,128)(2,1)S(1)}, u32[]{:S(2)}, u32[]{:S(2)}) %collective-permute-start.1) | collective-permute-done | bytes 262176 | tf_op jit(solution)/shard_map/ppermute | solution.py:21
  18.4 1.8 %pad_maximum_fusion = bf16[256,20,256]{0,2,1:T(8,128)(2,1)} fusion(bf16[256,2,256]{0,2,1:T(8,128)(2,1)S(1)} %collective-permute-done.1, bf16[256,16,256]{0,2,1:T(8,128)(2,1)S(1)} %bitcast_multiply_fusion, bf16[256,2,256]{0,2,1:T(8,128)(2,1)S(1)} %collective-permute-done), kind=kLoop, calls=%fused_computation | loop fusion | flops 2621440 | bytes 5242880 | tf_op jit(solution)/shard_map/concatenate | solution.py:22
  20.3 4.4 %copy.11.refs_0_ = bf16[256,5120]{1,0:T(8,128)(2,1)} copy(bf16[256,5120]{0,1:T(8,128)(2,1)} %bitcast.54) | data formatting | bytes 5242880 | tf_op jit(solution)/shard_map/reshape | solution.py:103
  24.7 11.0 %shard_map.82.refs_0_ = bf16[256,4608]{1,0:T(8,128)(2,1)} custom-call(bf16[256,5120]{1,0:T(8,128)(2,1)} %copy.11.refs_0_, bf16[3,3,256,256]{3,2,1,0:T(8,128)(2,1)} %refs_1_.2, f32[256,1]{1,0:T(8,128)} %copy.12.refs_2_, s32[3]{0:T(128)} %get-tuple-element.22.refs_3_), custom_call_target="tpu_custom_call" | custom-call | flops 5435817984 | bytes 6160384 | tf_op jit(solution)/shard_map/pallas_call | solution.py:115
  35.7 9.7 %shard_map.83 = bf16[19,4096]{1,0:T(8,128)(2,1)} custom-call(bf16[256,4608]{1,0:T(8,128)(2,1)} %shard_map.82.refs_0_, bf16[3,3,256,256]{3,2,1,0:T(8,128)(2,1)} %refs_1_.3, f32[256,1]{1,0:T(8,128)} %copy.13.refs_2_, bf16[19,256]{1,0:T(8,128)(2,1)} %refs_3_.1, f32[19,1]{1,0:T(8,128)} %copy.14.refs_4_, s32[3]{0:T(128)} %get-tuple-element.23.refs_5_), custom_call_target="tpu_custom_call" | custom-call | flops 4871684096 | bytes 3694592 | tf_op jit(solution)/shard_map/pallas_call | solution.py:115
  45.3 1.0 %copy.17 = bf16[3,8,16,256]{3,2,1,0:T(8,128)(2,1)S(1)} copy(bf16[3,8,16,256]{3,1,2,0:T(8,128)(2,1)} %bitcast.62) | data formatting | bytes 393216
  46.3 5.6 %collective-permute-start.2 = (bf16[19,1,16,256]{3,2,0,1:T(8,128)(2,1)S(1)}, bf16[19,1,16,256]{3,2,0,1:T(8,128)(2,1)S(1)}, u32[]{:S(2)}, u32[]{:S(2)}) collective-permute-start(bf16[19,1,16,256]{3,2,0,1:T(8,128)(2,1)S(1)} %get-tuple-element.20), channel_id=1, source_target_pairs={{0,8},{2,10},{4,12},{6,14},{8,0},{10,2},{12,4},{14,6},{1,9},{3,11}... | collective-permute-start | bytes 466952 | tf_op jit(solution)/shard_map/ppermute | solution.py:35
  57.4 1.5 %collective-permute-done.2 = bf16[19,1,16,256]{3,2,0,1:T(8,128)(2,1)S(1)} collective-permute-done((bf16[19,1,16,256]{3,2,0,1:T(8,128)(2,1)S(1)}, bf16[19,1,16,256]{3,2,0,1:T(8,128)(2,1)S(1)}, u32[]{:S(2)}, u32[]{:S(2)}) %collective-permute-start.2) | collective-permute-done | bytes 155680 | tf_op jit(solution)/shard_map/ppermute | solution.py:35
  58.9 1.0 %collective-permute-start.3 = (bf16[19,2,16,256]{3,2,0,1:T(8,128)(2,1)S(1)}, bf16[19,2,16,256]{3,2,0,1:T(8,128)(2,1)S(1)}, u32[]{:S(2)}, u32[]{:S(2)}) collective-permute-start(bf16[19,2,16,256]{3,2,0,1:T(8,128)(2,1)S(1)} %maximum_select_fusion.2), channel_id=1, source_target_pairs={{0,4},{2,6},{4,0},{6,2},{8,12},{10,14},{12,8},{14,10},{1,5},{3,7},... | collective-permute-start | bytes 933896 | tf_op jit(solution)/shard_map/ppermute | solution.py:35
  60.0 9.1 %collective-permute-done.3 = bf16[19,2,16,256]{3,2,0,1:T(8,128)(2,1)S(1)} collective-permute-done((bf16[19,2,16,256]{3,2,0,1:T(8,128)(2,1)S(1)}, bf16[19,2,16,256]{3,2,0,1:T(8,128)(2,1)S(1)}, u32[]{:S(2)}, u32[]{:S(2)}) %collective-permute-start.3) | collective-permute-done | bytes 311328 | tf_op jit(solution)/shard_map/ppermute | solution.py:35
  69.1 0.1 maximum_select_fusion.1
  69.1 0.1 copy.15
  69.2 0.2 collective-permute-start.4
  69.6 1.8 %collective-permute-done.4 = bf16[19,4,16,256]{3,2,1,0:T(8,128)(2,1)S(1)} collective-permute-done((bf16[19,4,16,256]{3,2,1,0:T(8,128)(2,1)S(1)}, bf16[19,4,16,256]{3,2,1,0:T(8,128)(2,1)S(1)}, u32[]{:S(2)}, u32[]{:S(2)}) %collective-permute-start.4) | collective-permute-done | bytes 622624 | tf_op jit(solution)/shard_map/ppermute | solution.py:35
  71.3 0.1 maximum_select_fusion
  71.5 0.1 dynamic-slice_bitcast_fusion
  71.6 0.1 fusion.28
  71.7 1.6 %collective-permute-start.5 = (bf16[19,10,256]{2,1,0:T(8,128)(2,1)S(1)}, bf16[19,10,256]{2,1,0:T(8,128)(2,1)S(1)}, u32[]{:S(2)}, u32[]{:S(2)}) collective-permute-start(bf16[19,10,256]{2,1,0:T(8,128)(2,1)S(1)} %fusion.28), channel_id=1, source_target_pairs={{0,1},{1,0},{2,3},{3,2},{4,5},{5,4},{6,7},{7,6},{8,9},{9,8},{10,11... | collective-permute-start | bytes 291848 | tf_op jit(solution)/shard_map/ppermute | solution.py:187
  73.3 1.2 %fusion = f32[32,19,1024]{2,0,1:T(8,128)S(1)} fusion(f32[1024]{0:T(1024)S(1)} %get-tuple-element.24, s32[1024]{0:T(1024)S(1)} %get-tuple-element.27, f32[1024]{0:T(1024)S(1)} %get-tuple-element.25, s32[1024]{0:T(1024)S(1)} %get-tuple-element.26, s32[]{:T(128)S(6)} %select_n.528, bf16[1,19,10,256]{3,2,1,0:T(8,128)(2,1)S(1)} %get-tuple-element.19, ...), kind=kOutput, calls=%fused_computation.5 | convolution fusion | flops 113884864 | bytes 2701832 | tf_op jit(solution)/shard_map/iy,cyj->icj/dot_general | solution.py:202
  74.5 3.3 %collective-permute-done.5 = bf16[19,10,256]{2,1,0:T(8,128)(2,1)S(1)} collective-permute-done((bf16[19,10,256]{2,1,0:T(8,128)(2,1)S(1)}, bf16[19,10,256]{2,1,0:T(8,128)(2,1)S(1)}, u32[]{:S(2)}, u32[]{:S(2)}) %collective-permute-start.5) | collective-permute-done | bytes 97312 | tf_op jit(solution)/shard_map/ppermute | solution.py:187
  77.8 2.7 %convolution_add_fusion = f32[32,19,1024]{2,0,1:T(8,128)} fusion(f32[32,19,1024]{2,0,1:T(8,128)S(1)} %fusion, bf16[19,10,256]{2,1,0:T(8,128)(2,1)S(1)} %collective-permute-done.5, f32[1024]{0:T(1024)S(1)} %get-tuple-element.28, s32[1024]{0:T(1024)S(1)} %get-tuple-element.31, f32[1024]{0:T(1024)S(1)} %get-tuple-element.29, s32[1024]{0:T(1024)S(1)} %get-tuple-element.30, ...), kind=kOutput, calls=%fused_computation.2 | convolution fusion | flops 114458816 | bytes 5094916 | tf_op jit(solution)/shard_map/iy,cyj->icj/dot_general | solution.py:202
  (20 shorter events, 0.3 us)
Async XLA Ops:
  8.4 5.7 %copy-start = (f32[256]{0:T(256)S(1)}, f32[256]{0:T(256)}, u32[]{:S(2)}) copy-start(f32[256]{0:T(256)} %param.11) | copy-start | bytes 3076
  8.4 6.5 %copy-start.1 = (f32[256]{0:T(256)S(1)}, f32[256]{0:T(256)}, u32[]{:S(2)}) copy-start(f32[256]{0:T(256)} %param.13) | copy-start | bytes 3076
  8.4 7.3 %copy-start.2 = (f32[19]{0:T(128)S(1)}, f32[19]{0:T(128)}, u32[]{:S(2)}) copy-start(f32[19]{0:T(128)} %param.15) | copy-start | bytes 232
  10.4 6.6 %collective-permute-start = (bf16[256,2,256]{0,2,1:T(8,128)(2,1)S(1)}, bf16[256,2,256]{0,2,1:T(8,128)(2,1)S(1)}, u32[]{:S(2)}, u32[]{:S(2)}) collective-permute-start(bf16[256,2,256]{0,2,1:T(8,128)(2,1)S(1)} %get-tuple-element.16), channel_id=1, source_target_pairs={{0,2},{2,4},{4,6},{6,8},{8,10},{10,12},{12,14},{1,3},{3,5},{5,7},{... | collective-permute-start | bytes 786440 | tf_op jit(solution)/shard_map/ppermute | solution.py:18
  12.8 5.6 %collective-permute-start.1 = (bf16[256,2,256]{0,2,1:T(8,128)(2,1)S(1)}, bf16[256,2,256]{0,2,1:T(8,128)(2,1)S(1)}, u32[]{:S(2)}, u32[]{:S(2)}) collective-permute-start(bf16[256,2,256]{0,2,1:T(8,128)(2,1)S(1)} %get-tuple-element.17), channel_id=1, source_target_pairs={{2,0},{4,2},{6,4},{8,6},{10,8},{12,10},{14,12},{3,1},{5,3},{7,5},{... | collective-permute-start | bytes 786440 | tf_op jit(solution)/shard_map/ppermute | solution.py:21
  46.3 12.5 %collective-permute-start.2 = (bf16[19,1,16,256]{3,2,0,1:T(8,128)(2,1)S(1)}, bf16[19,1,16,256]{3,2,0,1:T(8,128)(2,1)S(1)}, u32[]{:S(2)}, u32[]{:S(2)}) collective-permute-start(bf16[19,1,16,256]{3,2,0,1:T(8,128)(2,1)S(1)} %get-tuple-element.20), channel_id=1, source_target_pairs={{0,8},{2,10},{4,12},{6,14},{8,0},{10,2},{12,4},{14,6},{1,9},{3,11}... | collective-permute-start | bytes 466952 | tf_op jit(solution)/shard_map/ppermute | solution.py:35
  58.9 10.2 %collective-permute-start.3 = (bf16[19,2,16,256]{3,2,0,1:T(8,128)(2,1)S(1)}, bf16[19,2,16,256]{3,2,0,1:T(8,128)(2,1)S(1)}, u32[]{:S(2)}, u32[]{:S(2)}) collective-permute-start(bf16[19,2,16,256]{3,2,0,1:T(8,128)(2,1)S(1)} %maximum_select_fusion.2), channel_id=1, source_target_pairs={{0,4},{2,6},{4,0},{6,2},{8,12},{10,14},{12,8},{14,10},{1,5},{3,7},... | collective-permute-start | bytes 933896 | tf_op jit(solution)/shard_map/ppermute | solution.py:35
  69.2 2.1 %collective-permute-start.4 = (bf16[19,4,16,256]{3,2,1,0:T(8,128)(2,1)S(1)}, bf16[19,4,16,256]{3,2,1,0:T(8,128)(2,1)S(1)}, u32[]{:S(2)}, u32[]{:S(2)}) collective-permute-start(bf16[19,4,16,256]{3,2,1,0:T(8,128)(2,1)S(1)} %bitcast.55), channel_id=1, source_target_pairs={{0,2},{2,0},{4,6},{6,4},{8,10},{10,8},{12,14},{14,12},{1,3},{3,1},... | collective-permute-start | bytes 1867784 | tf_op jit(solution)/shard_map/ppermute | solution.py:35
  71.7 6.1 %collective-permute-start.5 = (bf16[19,10,256]{2,1,0:T(8,128)(2,1)S(1)}, bf16[19,10,256]{2,1,0:T(8,128)(2,1)S(1)}, u32[]{:S(2)}, u32[]{:S(2)}) collective-permute-start(bf16[19,10,256]{2,1,0:T(8,128)(2,1)S(1)} %fusion.28), channel_id=1, source_target_pairs={{0,1},{1,0},{2,3},{3,2},{4,5},{5,4},{6,7},{7,6},{8,9},{9,8},{10,11... | collective-permute-start | bytes 291848 | tf_op jit(solution)/shard_map/ppermute | solution.py:187

commit v5 on v4

--- a/solution.py
+++ b/solution.py
@@ -58,16 +58,10 @@
     return (first + second).astype(jnp.bfloat16)
 
 
-def conv_body(*refs, block, width, project):
-    if project:
-        x_ref, w_ref, b_ref, k_ref, kb_ref, s_ref, o_ref = refs
-    else:
-        x_ref, w_ref, b_ref, s_ref, o_ref = refs
-    lo, hi, good_cols = s_ref[0], s_ref[1], s_ref[2]
+def run_conv(x_ref, w_ref, bias, lo, hi, good_cols, o_ref, width, block, head=None):
     flat = block * width
     place = lax.broadcasted_iota(jnp.int32, (1, flat), 1)
     col = place % width
-    bias = b_ref[...]
 
     def step(i, carry):
         r0 = i * block
@@ -86,40 +80,102 @@
         row = r0 + place // width
         keep = (row >= lo) & (row < hi) & (col < good_cols)
         out = jnp.where(keep, total, 0.0).astype(jnp.bfloat16)
-        if project:
-            out = jnp.dot(k_ref[...], out, preferred_element_type=jnp.float32) + kb_ref[...]
+        if head is not None:
+            out = jnp.dot(head[0], out, preferred_element_type=jnp.float32) + head[1]
         o_ref[:, pl.ds(pl.multiple_of(r0 * width, width), flat)] = out.astype(o_ref.dtype)
         return carry
 
     lax.fori_loop(0, o_ref.shape[1] // flat, step, 0)
 
 
-def conv_layer(x, weights, bias, limits, head=None):
-    chans, rows_in, width = x.shape
+def first_body(main_ref, top_ref, low_ref, w_ref, b_ref, s_ref, o_ref, x_ref, *, width, block, halo):
+    lo_in, hi_in, good_cols, lo, hi = s_ref[0], s_ref[1], s_ref[2], s_ref[3], s_ref[4]
+    chans = main_ref.shape[0]
+    rows_main = main_ref.shape[1] // width
+
+    def put(src, offset, rows):
+        place = lax.broadcasted_iota(jnp.int32, (1, rows * width), 1)
+        row = offset + place // width
+        keep = (row >= lo_in) & (row < hi_in) & (place % width < good_cols)
+        x_ref[:, pl.ds(pl.multiple_of(offset * width, width), rows * width)] = jnp.where(
+            keep, src, jnp.zeros_like(src)
+        )
+
+    put(top_ref[...], 0, halo)
+    put(low_ref[...], halo + rows_main, halo)
+
+    def chunk(i, carry):
+        start = pl.multiple_of(i * 2 * width, width)
+        put(main_ref[:, pl.ds(start, 2 * width)], halo + 2 * i, 2)
+        return carry
+
+    lax.fori_loop(0, rows_main // 2, chunk, 0)
+    run_conv(x_ref, w_ref, b_ref[pl.ds(0, chans), :], lo, hi, good_cols, o_ref, width, block)
+
+
+def second_body(x_ref, w_ref, b_ref, k_ref, s_ref, o_ref, *, width, block):
+    chans = x_ref.shape[0]
+    classes = k_ref.shape[0]
+    head = (k_ref[...], b_ref[pl.ds(2 * chans, classes), :])
+    lo, hi, good_cols = s_ref[3], s_ref[4], s_ref[2]
+    run_conv(x_ref, w_ref, b_ref[pl.ds(chans, chans), :], lo, hi, good_cols, o_ref, width, block, head)
+
+
+def pick_block(rows):
+    return next(k for k in (4, 3, 2, 1) if rows % k == 0)
+
+
+def conv_first_layer(feat, top, low, weights, biases, limits):
+    chans, rows_main, width = feat.shape
+    halo = top.shape[1]
+    rows_in = rows_main + 2 * halo
     rows_out = rows_in - 2
     outs = weights.shape[2]
-    block = next(k for k in (4, 3, 2, 1) if rows_out % k == 0)
+    block = pick_block(rows_out)
     vmem = pl.BlockSpec(memory_space=pltpu.VMEM)
-    args = [x.reshape(chans, rows_in * width), weights, bias.reshape(-1, 1)]
-    flops = 2 * 9 * rows_out * width * chans * outs
-    final = outs
-    if head is not None:
-        args += [head[0], head[1].reshape(-1, 1)]
-        final = head[0].shape[0]
-        flops += 2 * rows_out * width * outs * final
     cost = pl.CostEstimate(
-        flops=flops,
-        bytes_accessed=2 * (x.size + weights.size + rows_out * width * final),
+        flops=2 * 9 * rows_out * width * chans * outs,
+        bytes_accessed=2 * (chans * rows_in * width + weights.size + rows_out * width * outs),
         transcendentals=0,
     )
     out = pl.pallas_call(
-        functools.partial(conv_body, block=block, width=width, project=head is not None),
-        out_shape=jax.ShapeDtypeStruct((final, rows_out * width), jnp.bfloat16),
-        in_specs=[vmem] * len(args) + [pl.BlockSpec(memory_space=pltpu.SMEM)],
+        functools.partial(first_body, width=width, block=block, halo=halo),
+        out_shape=jax.ShapeDtypeStruct((outs, rows_out * width), jnp.bfloat16),
+        in_specs=[vmem] * 5 + [pl.BlockSpec(memory_space=pltpu.SMEM)],
+        out_specs=vmem,
+        scratch_shapes=[pltpu.VMEM((chans, rows_in * width), jnp.bfloat16)],
+        cost_estimate=cost,
+    )(
+        feat.reshape(chans, rows_main * width),
+        top.reshape(chans, halo * width),
+        low.reshape(chans, halo * width),
+        weights,
+        biases,
+        limits,
+    )
+    return out
+
+
+def conv_second_layer(x, width, weights, biases, head, limits):
+    chans, flat_in = x.shape
+    rows_out = flat_in // width - 2
+    outs = weights.shape[2]
+    classes = head.shape[0]
+    block = pick_block(rows_out)
+    vmem = pl.BlockSpec(memory_space=pltpu.VMEM)
+    cost = pl.CostEstimate(
+        flops=2 * 9 * rows_out * width * chans * outs + 2 * rows_out * width * outs * classes,
+        bytes_accessed=2 * (x.size + weights.size + rows_out * width * classes),
+        transcendentals=0,
+    )
+    out = pl.pallas_call(
+        functools.partial(second_body, width=width, block=block),
+        out_shape=jax.ShapeDtypeStruct((classes, rows_out * width), jnp.bfloat16),
+        in_specs=[vmem] * 4 + [pl.BlockSpec(memory_space=pltpu.SMEM)],
         out_specs=vmem,
         cost_estimate=cost,
-    )(*args, limits)
-    return out.reshape(final, rows_out, width)
+    )(x, weights, biases, head, limits)
+    return out.reshape(classes, rows_out, width)
 
 
 def window_start(numer, first_row, full_rows, out_rows, window_rows):
@@ -151,17 +207,20 @@
     numer = code // 2
     valid_rows = full_rows * numer // 14
     valid_cols = cols * numer // 14
-    row_ids = place * rows_dev + jnp.arange(rows_dev, dtype=jnp.int32)
-    row_ok = row_ids < valid_rows
-    col_ok = jnp.arange(cols, dtype=jnp.int32) < valid_cols
-    mask = (row_ok[:, None] & col_ok[None, :]).astype(jnp.bfloat16)
-    first = feat * mask
-    padded = with_halo(first, (("space", 1),), 2)
+    count = lax.axis_size("space")
+    halo = 2
+    forward = [(i, i + 1) for i in range(count - 1)]
+    backward = [(target, source) for source, target in forward]
+    top_rows = lax.ppermute(lax.slice_in_dim(feat, rows_dev - halo, None, axis=1), "space", forward)
+    low_rows = lax.ppermute(lax.slice_in_dim(feat, 0, halo, axis=1), "space", backward)
     top = place * rows_dev
-    limits_first = jnp.stack([1 - top, valid_rows - top + 1, valid_cols]).astype(jnp.int32)
-    limits_second = jnp.stack([-top, valid_rows - top, valid_cols]).astype(jnp.int32)
-    hidden = conv_layer(padded, conv_first, bias_first, limits_first)
-    logits = conv_layer(hidden, conv_second, bias_second, limits_second, (classify, class_bias))
+    limits = jnp.stack(
+        [halo - top, valid_rows - top + halo, valid_cols, 1 - top, valid_rows - top + 1, -top, valid_rows - top]
+    ).astype(jnp.int32)
+    limits_second = limits[jnp.array([0, 1, 2, 5, 6])]
+    biases = jnp.concatenate([bias_first, bias_second, class_bias]).reshape(-1, 1)
+    hidden = conv_first_layer(feat, top_rows, low_rows, conv_first, biases, limits[:5])
+    logits = conv_second_layer(hidden, cols, conv_second, biases, classify, limits_second)
     out_rows = UP * full_rows
     out_cols = UP * cols
     own_rows = out_rows // spaces

time: 81 us -> 74.6 us (0.921)
  other arithmetic: 6.41 us -> 2.6 us
  waiting for transfers between devices: 17.1 us -> 16.1 us
  local copies, waits for them, and re-layouts: 12.2 us -> 11.3 us
    reshape x4 -> x1, local copies, waits for them, and re-layouts: 6.71 us -> 0.84 us  [shards(): jnp.concatenate([bias_first, bias_second, class_bias]).reshape(-1, 1)]
    mul x1 -> x0, other arithmetic: 1.96 us -> none  [shards(): first = feat * mask]
    slice x1, local copies, waits for them, and re-layouts: 0.04 us -> 1.95 us  [shards(): lax.slice_in_dim(feat, 0, halo, axis=1)]
    ppermute x2, waiting for transfers between devices: 1.36 us -> 0.01 us  [the longest x1 0.01 us: shards(): lax.ppermute(lax.slice_in_dim(feat, 0, halo, axis=1), 'space', backward)]
    gather x0 -> x1, local copies, waits for them, and re-layouts: none -> 1.23 us  [shards(): limits_second = limits[jnp.array([0, 1, 2, 5, 6])]]
    concatenate x1, other arithmetic: 1.84 us -> 0.72 us  [shards(): jnp.concatenate([bias_first, bias_second, class_bias]).reshape(-1, 1)]
    unnamed x8 -> x6, local copies, waits for them, and re-layouts: 5.25 us -> 6.3 us
  transfers between devices with their start and end apart: 6 -> 6, of which waited for: 5 -> 4; matrix products, arithmetic and copies ran while one was open for 5% -> 15% of each run, Pallas kernels for 0% -> 0%
where the time goes in v5:
time: 74.6 us; the launch traced here: 74.2 us
  Pallas kernels  20.9 us (28%)
  waiting for transfers between devices  16.1 us (22%)
  starting transfers between devices  11.4 us (15%)
  local copies, waits for them, and re-layouts  11.3 us (15%)
  between operations  8.14 us (11%)
  matrix products  3.85 us (5%)
  other arithmetic  2.6 us (3%)
    ppermute x3, waiting for transfers between devices, gather_rows(): other = lax.ppermute(held, axis, [(i, i ^ bit) for i in range(count)])  12.7 us
    pallas_call x1, Pallas kernels, conv_first_layer(): pl.pallas_call(functools.partial(first_body, width=width, block=block, ha...  11.2 us
    pallas_call x1, Pallas kernels, conv_second_layer(): pl.pallas_call(functools.partial(second_body, width=width, block=block),...  9.66 us
    unnamed x6, local copies, waits for them, and re-layouts  6.3 us
    ppermute x3, starting transfers between devices, gather_rows(): other = lax.ppermute(held, axis, [(i, i ^ bit) for i in range(count)])  6.14 us
    dot_general x2, matrix products, shards(): jnp.einsum('iy,cyj->icj', row_part, widened, preferred_element_type=jnp.f...  3.85 us
    ppermute x1, waiting for transfers between devices, shards(): lax.ppermute(send, 'member', [(i, (i + shift) % members) for i in range(m...  3.38 us
    ppermute x1, starting transfers between devices, shards(): lax.ppermute(lax.slice_in_dim(feat, rows_dev - halo, None, axis=1), 'spac...  2.37 us
  transfers between devices with their start and end apart: 6, of which 4 were waited for; matrix products, arithmetic and copies ran while one was open for 15% of the time, Pallas kernels for 0%

profile of v5, /device:TPU:0, one launch (start us, length us, event | category | flops | bytes accessed | tf_op | source)
XLA Modules:
  0.0 74.2 jit_solution(13959680583420228135)
XLA Ops:
  0.0 1.9 %fusion.70 = (bf16[256,2,256]{2,1,0:T(2,128)(2,1)S(1)}, bf16[256,2,256]{2,1,0:T(2,128)(2,1)S(1)}) fusion(bf16[256,16,256]{2,1,0:T(8,128)(2,1)} %bitcast.58), kind=kLoop, calls=%fused_computation.121 | loop fusion | bytes 1048576 | tf_op jit(solution)/shard_map/slice | solution.py:215
  2.0 2.4 %collective-permute-start = (bf16[256,2,256]{2,1,0:T(2,128)(2,1)S(1)}, bf16[256,2,256]{2,1,0:T(2,128)(2,1)S(1)}, u32[]{:S(2)}, u32[]{:S(2)}) collective-permute-start(bf16[256,2,256]{2,1,0:T(2,128)(2,1)S(1)} %get-tuple-element.17), channel_id=1, source_target_pairs={{0,2},{2,4},{4,6},{6,8},{8,10},{10,12},{12,14},{1,3},{3,5},{5,7},{... | collective-permute-start | bytes 786440 | tf_op jit(solution)/shard_map/ppermute | solution.py:214
  4.3 1.3 %collective-permute-start.1 = (bf16[256,2,256]{2,1,0:T(2,128)(2,1)S(1)}, bf16[256,2,256]{2,1,0:T(2,128)(2,1)S(1)}, u32[]{:S(2)}, u32[]{:S(2)}) collective-permute-start(bf16[256,2,256]{2,1,0:T(2,128)(2,1)S(1)} %get-tuple-element.16), channel_id=1, source_target_pairs={{2,0},{4,2},{6,4},{8,6},{10,8},{12,10},{14,12},{3,1},{5,3},{7,5},{... | collective-permute-start | bytes 786440 | tf_op jit(solution)/shard_map/ppermute | solution.py:215
  5.7 1.4 %fusion.63 = (s32[]{:T(128)}, s32[]{:T(128)}, s32[]{:T(128)}) fusion(s32[2]{0:T(128)} %param.10, s32[]{:T(128)S(6)} %select_n.544, s32[]{:T(128)S(6)} %select_n.496, s32[]{:T(128)S(6)} %axis_index.29), kind=kLoop, calls=%fused_computation.108 | loop fusion | flops 15 | bytes 32 | tf_op jit(solution)/shard_map/reduce_sum | solution.py:250
  9.7 0.7 pad_maximum_fusion
  10.4 0.8 %reshape.307.b_ref = f32[531,1]{1,0:T(8,128)} reshape(f32[531]{0:T(1024)S(1)} %pad_maximum_fusion) | data formatting | bytes 4248 | tf_op jit(solution)/shard_map/reshape | solution.py:221
  11.3 3.9 %copy.14 = bf16[32,8,16,256]{3,1,2,0:T(8,128)(2,1)} copy(bf16[32,8,16,256]{3,2,1,0:T(8,128)(2,1)} %bitcast.59) | data formatting | bytes 4194304
  15.1 0.7 stack.76.s_ref
  15.8 0.1 stack.79
  15.9 1.2 %gather_fusion = s32[5]{0:T(128)} fusion(s32[7]{0:T(128)S(1)} %stack.79, s32[1024]{0:T(1024)S(1)} %pad_clamp_fusion), kind=kCustom, calls=%fused_computation | custom fusion | bytes 60 | tf_op jit(solution)/shard_map/gather | solution.py:220
  17.1 0.0 collective-permute-done
  17.1 0.7 copy.15
  17.9 0.0 collective-permute-done.1
  17.9 0.7 copy.16
  18.6 11.2 %shard_map.91.x_ref = bf16[256,4608]{1,0:T(8,128)(2,1)} custom-call(bf16[256,4096]{1,0:T(8,128)(2,1)} %bitcast.62, bf16[256,512]{1,0:T(8,128)(2,1)} %bitcast.70, bf16[256,512]{1,0:T(8,128)(2,1)} %bitcast.71, bf16[3,3,256,256]{3,2,1,0:T(8,128)(2,1)} %w_ref.2, f32[531,1]{1,0:T(8,128)} %reshape.307.b_ref, s32[5]{0:T(128)} %stack.76.s_ref), custom_call_target="tpu_custom_call" | custom-call | flops 5435817984 | bytes 6160384 | tf_op jit(solution)/shard_map/pallas_call | solution.py:141
  29.8 9.7 %shard_map.92 = bf16[19,4096]{1,0:T(8,128)(2,1)} custom-call(bf16[256,4608]{1,0:T(8,128)(2,1)} %shard_map.91.x_ref, bf16[3,3,256,256]{3,2,1,0:T(8,128)(2,1)} %w_ref.3, f32[531,1]{1,0:T(8,128)} %reshape.307.b_ref, bf16[19,256]{1,0:T(8,128)(2,1)} %k_ref.1, s32[5]{0:T(128)} %gather_fusion), custom_call_target="tpu_custom_call" | custom-call | flops 4871684096 | bytes 3694592 | tf_op jit(solution)/shard_map/pallas_call | solution.py:171
  39.5 1.0 %copy.17 = bf16[3,8,16,256]{3,2,1,0:T(8,128)(2,1)S(1)} copy(bf16[3,8,16,256]{3,1,2,0:T(8,128)(2,1)} %bitcast.72) | data formatting | bytes 393216
  40.5 6.0 %collective-permute-start.2 = (bf16[19,1,16,256]{3,2,0,1:T(8,128)(2,1)S(1)}, bf16[19,1,16,256]{3,2,0,1:T(8,128)(2,1)S(1)}, u32[]{:S(2)}, u32[]{:S(2)}) collective-permute-start(bf16[19,1,16,256]{3,2,0,1:T(8,128)(2,1)S(1)} %get-tuple-element.20), channel_id=1, source_target_pairs={{0,8},{2,10},{4,12},{6,14},{8,0},{10,2},{12,4},{14,6},{1,9},{3,11}... | collective-permute-start | bytes 466952 | tf_op jit(solution)/shard_map/ppermute | solution.py:35
  51.8 2.2 %collective-permute-done.2 = bf16[19,1,16,256]{3,2,0,1:T(8,128)(2,1)S(1)} collective-permute-done((bf16[19,1,16,256]{3,2,0,1:T(8,128)(2,1)S(1)}, bf16[19,1,16,256]{3,2,0,1:T(8,128)(2,1)S(1)}, u32[]{:S(2)}, u32[]{:S(2)}) %collective-permute-start.2) | collective-permute-done | bytes 155680 | tf_op jit(solution)/shard_map/ppermute | solution.py:35
  54.0 0.1 collective-permute-start.3
  54.2 8.6 %collective-permute-done.3 = bf16[19,2,16,256]{3,2,0,1:T(8,128)(2,1)S(1)} collective-permute-done((bf16[19,2,16,256]{3,2,0,1:T(8,128)(2,1)S(1)}, bf16[19,2,16,256]{3,2,0,1:T(8,128)(2,1)S(1)}, u32[]{:S(2)}, u32[]{:S(2)}) %collective-permute-start.3) | collective-permute-done | bytes 311328 | tf_op jit(solution)/shard_map/ppermute | solution.py:35
  62.8 0.1 maximum_select_fusion.1
  62.9 0.1 copy.12
  63.0 0.1 collective-permute-start.4
  63.2 1.9 %collective-permute-done.4 = bf16[19,4,16,256]{3,2,1,0:T(8,128)(2,1)S(1)} collective-permute-done((bf16[19,4,16,256]{3,2,1,0:T(8,128)(2,1)S(1)}, bf16[19,4,16,256]{3,2,1,0:T(8,128)(2,1)S(1)}, u32[]{:S(2)}, u32[]{:S(2)}) %collective-permute-start.4) | collective-permute-done | bytes 622624 | tf_op jit(solution)/shard_map/ppermute | solution.py:35
  65.1 0.1 maximum_select_fusion
  65.2 0.1 dynamic-slice_bitcast_fusion
  65.4 0.1 fusion.28
  65.5 1.6 %collective-permute-start.5 = (bf16[19,10,256]{2,1,0:T(8,128)(2,1)S(1)}, bf16[19,10,256]{2,1,0:T(8,128)(2,1)S(1)}, u32[]{:S(2)}, u32[]{:S(2)}) collective-permute-start(bf16[19,10,256]{2,1,0:T(8,128)(2,1)S(1)} %fusion.28), channel_id=1, source_target_pairs={{0,1},{1,0},{2,3},{3,2},{4,5},{5,4},{6,7},{7,6},{8,9},{9,8},{10,11... | collective-permute-start | bytes 291848 | tf_op jit(solution)/shard_map/ppermute | solution.py:246
  67.0 1.2 %fusion = f32[32,19,1024]{2,0,1:T(8,128)S(1)} fusion(f32[1024]{0:T(1024)S(1)} %get-tuple-element.22, s32[1024]{0:T(1024)S(1)} %get-tuple-element.25, f32[1024]{0:T(1024)S(1)} %get-tuple-element.23, s32[1024]{0:T(1024)S(1)} %get-tuple-element.24, s32[]{:T(128)S(6)} %select_n.532, bf16[1,19,10,256]{3,2,1,0:T(8,128)(2,1)S(1)} %get-tuple-element.19, ...), kind=kOutput, calls=%fused_computation.4 | convolution fusion | flops 113884864 | bytes 2701832 | tf_op jit(solution)/shard_map/iy,cyj->icj/dot_general | solution.py:261
  68.2 3.4 %collective-permute-done.5 = bf16[19,10,256]{2,1,0:T(8,128)(2,1)S(1)} collective-permute-done((bf16[19,10,256]{2,1,0:T(8,128)(2,1)S(1)}, bf16[19,10,256]{2,1,0:T(8,128)(2,1)S(1)}, u32[]{:S(2)}, u32[]{:S(2)}) %collective-permute-start.5) | collective-permute-done | bytes 97312 | tf_op jit(solution)/shard_map/ppermute | solution.py:246
  71.6 2.7 %convolution_add_fusion = f32[32,19,1024]{2,0,1:T(8,128)} fusion(f32[32,19,1024]{2,0,1:T(8,128)S(1)} %fusion, bf16[19,10,256]{2,1,0:T(8,128)(2,1)S(1)} %collective-permute-done.5, f32[1024]{0:T(1024)S(1)} %get-tuple-element.26, s32[1024]{0:T(1024)S(1)} %get-tuple-element.29, f32[1024]{0:T(1024)S(1)} %get-tuple-element.27, s32[1024]{0:T(1024)S(1)} %get-tuple-element.28, ...), kind=kOutput, calls=%fused_computation.1 | convolution fusion | flops 114458816 | bytes 5094916 | tf_op jit(solution)/shard_map/iy,cyj->icj/dot_general | solution.py:261
  (14 shorter events, 0.3 us)
Async XLA Ops:
  2.0 15.2 %collective-permute-start = (bf16[256,2,256]{2,1,0:T(2,128)(2,1)S(1)}, bf16[256,2,256]{2,1,0:T(2,128)(2,1)S(1)}, u32[]{:S(2)}, u32[]{:S(2)}) collective-permute-start(bf16[256,2,256]{2,1,0:T(2,128)(2,1)S(1)} %get-tuple-element.17), channel_id=1, source_target_pairs={{0,2},{2,4},{4,6},{6,8},{8,10},{10,12},{12,14},{1,3},{3,5},{5,7},{... | collective-permute-start | bytes 786440 | tf_op jit(solution)/shard_map/ppermute | solution.py:214
  4.3 13.5 %collective-permute-start.1 = (bf16[256,2,256]{2,1,0:T(2,128)(2,1)S(1)}, bf16[256,2,256]{2,1,0:T(2,128)(2,1)S(1)}, u32[]{:S(2)}, u32[]{:S(2)}) collective-permute-start(bf16[256,2,256]{2,1,0:T(2,128)(2,1)S(1)} %get-tuple-element.16), channel_id=1, source_target_pairs={{2,0},{4,2},{6,4},{8,6},{10,8},{12,10},{14,12},{3,1},{5,3},{7,5},{... | collective-permute-start | bytes 786440 | tf_op jit(solution)/shard_map/ppermute | solution.py:215
  11.2 4.6 %copy-start = (s32[5]{0:T(128)S(1)}, s32[5]{0:T(128)}, u32[]{:S(2)}) copy-start(s32[5]{0:T(128)} %constant.242) | copy-start | bytes 64
  40.5 13.5 %collective-permute-start.2 = (bf16[19,1,16,256]{3,2,0,1:T(8,128)(2,1)S(1)}, bf16[19,1,16,256]{3,2,0,1:T(8,128)(2,1)S(1)}, u32[]{:S(2)}, u32[]{:S(2)}) collective-permute-start(bf16[19,1,16,256]{3,2,0,1:T(8,128)(2,1)S(1)} %get-tuple-element.20), channel_id=1, source_target_pairs={{0,8},{2,10},{4,12},{6,14},{8,0},{10,2},{12,4},{14,6},{1,9},{3,11}... | collective-permute-start | bytes 466952 | tf_op jit(solution)/shard_map/ppermute | solution.py:35
  54.0 8.8 %collective-permute-start.3 = (bf16[19,2,16,256]{3,2,0,1:T(8,128)(2,1)S(1)}, bf16[19,2,16,256]{3,2,0,1:T(8,128)(2,1)S(1)}, u32[]{:S(2)}, u32[]{:S(2)}) collective-permute-start(bf16[19,2,16,256]{3,2,0,1:T(8,128)(2,1)S(1)} %maximum_select_fusion.2), channel_id=1, source_target_pairs={{0,4},{2,6},{4,0},{6,2},{8,12},{10,14},{12,8},{14,10},{1,5},{3,7},... | collective-permute-start | bytes 933896 | tf_op jit(solution)/shard_map/ppermute | solution.py:35
  63.0 2.1 %collective-permute-start.4 = (bf16[19,4,16,256]{3,2,1,0:T(8,128)(2,1)S(1)}, bf16[19,4,16,256]{3,2,1,0:T(8,128)(2,1)S(1)}, u32[]{:S(2)}, u32[]{:S(2)}) collective-permute-start(bf16[19,4,16,256]{3,2,1,0:T(8,128)(2,1)S(1)} %bitcast.60), channel_id=1, source_target_pairs={{0,2},{2,0},{4,6},{6,4},{8,10},{10,8},{12,14},{14,12},{1,3},{3,1},... | collective-permute-start | bytes 1867784 | tf_op jit(solution)/shard_map/ppermute | solution.py:35
  65.5 6.1 %collective-permute-start.5 = (bf16[19,10,256]{2,1,0:T(8,128)(2,1)S(1)}, bf16[19,10,256]{2,1,0:T(8,128)(2,1)S(1)}, u32[]{:S(2)}, u32[]{:S(2)}) collective-permute-start(bf16[19,10,256]{2,1,0:T(8,128)(2,1)S(1)} %fusion.28), channel_id=1, source_target_pairs={{0,1},{1,0},{2,3},{3,2},{4,5},{5,4},{6,7},{7,6},{8,9},{9,8},{10,11... | collective-permute-start | bytes 291848 | tf_op jit(solution)/shard_map/ppermute | solution.py:246

commit v6 on v5

--- a/solution.py
+++ b/solution.py
@@ -60,20 +60,21 @@
 
 def run_conv(x_ref, w_ref, bias, lo, hi, good_cols, o_ref, width, block, head=None):
     flat = block * width
+    outs = w_ref.shape[2]
     place = lax.broadcasted_iota(jnp.int32, (1, flat), 1)
     col = place % width
+    stacked = jnp.concatenate(
+        [jnp.concatenate([w_ref[a, b] for a in range(3)], axis=1) for b in range(3)], axis=0
+    )
 
     def step(i, carry):
         r0 = i * block
-        taps = []
-        for b in range(3):
-            acc = None
-            for a in range(3):
-                start = pl.multiple_of((r0 + a) * width, width)
-                xs = x_ref[:, pl.ds(start, flat)]
-                d = jnp.dot(w_ref[a, b], xs, preferred_element_type=jnp.float32)
-                acc = d if acc is None else acc + d
-            taps.append(acc)
+        rhs = jnp.concatenate(
+            [x_ref[:, pl.ds(pl.multiple_of((r0 + a) * width, width), flat)] for a in range(3)],
+            axis=0,
+        )
+        res = jnp.dot(stacked, rhs, preferred_element_type=jnp.float32)
+        taps = [res[b * outs:(b + 1) * outs] for b in range(3)]
         left = jnp.where(col == 0, 0.0, pltpu.roll(taps[0], 1, 1))
         right = jnp.where(col == width - 1, 0.0, pltpu.roll(taps[2], flat - 1, 1))
         total = jnp.maximum(taps[1] + left + right + bias, 0.0)

time: 74.6 us -> 74.8 us (level)
  no operation moved by 1% of the time
where the time goes in v6:
time: 74.8 us; the launch traced here: 74.4 us
  Pallas kernels  21 us (28%)
  waiting for transfers between devices  16.1 us (22%)
  local copies, waits for them, and re-layouts  11.3 us (15%)
  starting transfers between devices  11.3 us (15%)
  between operations  8.13 us (11%)
  matrix products  3.87 us (5%)
  other arithmetic  2.6 us (3%)
    ppermute x3, waiting for transfers between devices, gather_rows(): other = lax.ppermute(held, axis, [(i, i ^ bit) for i in range(count)])  12.7 us
    pallas_call x1, Pallas kernels, conv_first_layer(): pl.pallas_call(functools.partial(first_body, width=width, block=block, ha...  11.5 us
    pallas_call x1, Pallas kernels, conv_second_layer(): pl.pallas_call(functools.partial(second_body, width=width, block=block),...  9.51 us
    unnamed x6, local copies, waits for them, and re-layouts  6.3 us
    ppermute x3, starting transfers between devices, gather_rows(): other = lax.ppermute(held, axis, [(i, i ^ bit) for i in range(count)])  6.14 us
    dot_general x2, matrix products, shards(): jnp.einsum('iy,cyj->icj', row_part, widened, preferred_element_type=jnp.f...  3.87 us
    ppermute x1, waiting for transfers between devices, shards(): lax.ppermute(send, 'member', [(i, (i + shift) % members) for i in range(m...  3.39 us
    ppermute x1, starting transfers between devices, shards(): lax.ppermute(lax.slice_in_dim(feat, rows_dev - halo, None, axis=1), 'spac...  2.37 us
  transfers between devices with their start and end apart: 6, of which 4 were waited for; matrix products, arithmetic and copies ran while one was open for 15% of the time, Pallas kernels for 0%

profile of v6, /device:TPU:0, one launch (start us, length us, event | category | flops | bytes accessed | tf_op | source)
XLA Modules:
  0.0 74.4 jit_solution(10667343342210316452)
XLA Ops:
  0.0 1.9 %fusion.70 = (bf16[256,2,256]{2,1,0:T(2,128)(2,1)S(1)}, bf16[256,2,256]{2,1,0:T(2,128)(2,1)S(1)}) fusion(bf16[256,16,256]{2,1,0:T(8,128)(2,1)} %bitcast.58), kind=kLoop, calls=%fused_computation.121 | loop fusion | bytes 1048576 | tf_op jit(solution)/shard_map/slice | solution.py:216
  2.0 2.4 %collective-permute-start = (bf16[256,2,256]{2,1,0:T(2,128)(2,1)S(1)}, bf16[256,2,256]{2,1,0:T(2,128)(2,1)S(1)}, u32[]{:S(2)}, u32[]{:S(2)}) collective-permute-start(bf16[256,2,256]{2,1,0:T(2,128)(2,1)S(1)} %get-tuple-element.17), channel_id=1, source_target_pairs={{0,2},{2,4},{4,6},{6,8},{8,10},{10,12},{12,14},{1,3},{3,5},{5,7},{... | collective-permute-start | bytes 786440 | tf_op jit(solution)/shard_map/ppermute | solution.py:215
  4.3 1.3 %collective-permute-start.1 = (bf16[256,2,256]{2,1,0:T(2,128)(2,1)S(1)}, bf16[256,2,256]{2,1,0:T(2,128)(2,1)S(1)}, u32[]{:S(2)}, u32[]{:S(2)}) collective-permute-start(bf16[256,2,256]{2,1,0:T(2,128)(2,1)S(1)} %get-tuple-element.16), channel_id=1, source_target_pairs={{2,0},{4,2},{6,4},{8,6},{10,8},{12,10},{14,12},{3,1},{5,3},{7,5},{... | collective-permute-start | bytes 786440 | tf_op jit(solution)/shard_map/ppermute | solution.py:216
  5.7 1.4 %fusion.63 = (s32[]{:T(128)}, s32[]{:T(128)}, s32[]{:T(128)}) fusion(s32[2]{0:T(128)} %param.10, s32[]{:T(128)S(6)} %select_n.544, s32[]{:T(128)S(6)} %select_n.496, s32[]{:T(128)S(6)} %axis_index.29), kind=kLoop, calls=%fused_computation.108 | loop fusion | flops 15 | bytes 32 | tf_op jit(solution)/shard_map/reduce_sum | solution.py:251
  9.7 0.7 pad_maximum_fusion
  10.4 0.8 %reshape.307.b_ref = f32[531,1]{1,0:T(8,128)} reshape(f32[531]{0:T(1024)S(1)} %pad_maximum_fusion) | data formatting | bytes 4248 | tf_op jit(solution)/shard_map/reshape | solution.py:222
  11.3 3.9 %copy.14 = bf16[32,8,16,256]{3,1,2,0:T(8,128)(2,1)} copy(bf16[32,8,16,256]{3,2,1,0:T(8,128)(2,1)} %bitcast.59) | data formatting | bytes 4194304
  15.1 0.7 stack.76.s_ref
  15.8 0.1 stack.79
  15.9 1.2 %gather_fusion = s32[5]{0:T(128)} fusion(s32[7]{0:T(128)S(1)} %stack.79, s32[1024]{0:T(1024)S(1)} %pad_clamp_fusion), kind=kCustom, calls=%fused_computation | custom fusion | bytes 60 | tf_op jit(solution)/shard_map/gather | solution.py:221
  17.1 0.0 collective-permute-done
  17.1 0.7 copy.15
  17.9 0.0 collective-permute-done.1
  17.9 0.7 copy.16
  18.6 11.5 %shard_map.91.x_ref = bf16[256,4608]{1,0:T(8,128)(2,1)} custom-call(bf16[256,4096]{1,0:T(8,128)(2,1)} %bitcast.62, bf16[256,512]{1,0:T(8,128)(2,1)} %bitcast.70, bf16[256,512]{1,0:T(8,128)(2,1)} %bitcast.71, bf16[3,3,256,256]{3,2,1,0:T(8,128)(2,1)} %w_ref.2, f32[531,1]{1,0:T(8,128)} %reshape.307.b_ref, s32[5]{0:T(128)} %stack.76.s_ref), custom_call_target="tpu_custom_call" | custom-call | flops 5435817984 | bytes 6160384 | tf_op jit(solution)/shard_map/pallas_call | solution.py:142
  30.1 9.5 %shard_map.92 = bf16[19,4096]{1,0:T(8,128)(2,1)} custom-call(bf16[256,4608]{1,0:T(8,128)(2,1)} %shard_map.91.x_ref, bf16[3,3,256,256]{3,2,1,0:T(8,128)(2,1)} %w_ref.3, f32[531,1]{1,0:T(8,128)} %reshape.307.b_ref, bf16[19,256]{1,0:T(8,128)(2,1)} %k_ref.1, s32[5]{0:T(128)} %gather_fusion), custom_call_target="tpu_custom_call" | custom-call | flops 4871684096 | bytes 3694592 | tf_op jit(solution)/shard_map/pallas_call | solution.py:172
  39.6 1.0 %copy.17 = bf16[3,8,16,256]{3,2,1,0:T(8,128)(2,1)S(1)} copy(bf16[3,8,16,256]{3,1,2,0:T(8,128)(2,1)} %bitcast.72) | data formatting | bytes 393216
  40.6 6.0 %collective-permute-start.2 = (bf16[19,1,16,256]{3,2,0,1:T(8,128)(2,1)S(1)}, bf16[19,1,16,256]{3,2,0,1:T(8,128)(2,1)S(1)}, u32[]{:S(2)}, u32[]{:S(2)}) collective-permute-start(bf16[19,1,16,256]{3,2,0,1:T(8,128)(2,1)S(1)} %get-tuple-element.20), channel_id=1, source_target_pairs={{0,8},{2,10},{4,12},{6,14},{8,0},{10,2},{12,4},{14,6},{1,9},{3,11}... | collective-permute-start | bytes 466952 | tf_op jit(solution)/shard_map/ppermute | solution.py:35
  51.9 2.2 %collective-permute-done.2 = bf16[19,1,16,256]{3,2,0,1:T(8,128)(2,1)S(1)} collective-permute-done((bf16[19,1,16,256]{3,2,0,1:T(8,128)(2,1)S(1)}, bf16[19,1,16,256]{3,2,0,1:T(8,128)(2,1)S(1)}, u32[]{:S(2)}, u32[]{:S(2)}) %collective-permute-start.2) | collective-permute-done | bytes 155680 | tf_op jit(solution)/shard_map/ppermute | solution.py:35
  54.2 0.1 collective-permute-start.3
  54.3 8.6 %collective-permute-done.3 = bf16[19,2,16,256]{3,2,0,1:T(8,128)(2,1)S(1)} collective-permute-done((bf16[19,2,16,256]{3,2,0,1:T(8,128)(2,1)S(1)}, bf16[19,2,16,256]{3,2,0,1:T(8,128)(2,1)S(1)}, u32[]{:S(2)}, u32[]{:S(2)}) %collective-permute-start.3) | collective-permute-done | bytes 311328 | tf_op jit(solution)/shard_map/ppermute | solution.py:35
  63.0 0.1 maximum_select_fusion.1
  63.0 0.1 copy.12
  63.1 0.1 collective-permute-start.4
  63.3 1.9 %collective-permute-done.4 = bf16[19,4,16,256]{3,2,1,0:T(8,128)(2,1)S(1)} collective-permute-done((bf16[19,4,16,256]{3,2,1,0:T(8,128)(2,1)S(1)}, bf16[19,4,16,256]{3,2,1,0:T(8,128)(2,1)S(1)}, u32[]{:S(2)}, u32[]{:S(2)}) %collective-permute-start.4) | collective-permute-done | bytes 622624 | tf_op jit(solution)/shard_map/ppermute | solution.py:35
  65.2 0.1 maximum_select_fusion
  65.3 0.1 dynamic-slice_bitcast_fusion
  65.5 0.1 fusion.28
  65.6 1.5 %collective-permute-start.5 = (bf16[19,10,256]{2,1,0:T(8,128)(2,1)S(1)}, bf16[19,10,256]{2,1,0:T(8,128)(2,1)S(1)}, u32[]{:S(2)}, u32[]{:S(2)}) collective-permute-start(bf16[19,10,256]{2,1,0:T(8,128)(2,1)S(1)} %fusion.28), channel_id=1, source_target_pairs={{0,1},{1,0},{2,3},{3,2},{4,5},{5,4},{6,7},{7,6},{8,9},{9,8},{10,11... | collective-permute-start | bytes 291848 | tf_op jit(solution)/shard_map/ppermute | solution.py:247
  67.1 1.2 %fusion = f32[32,19,1024]{2,0,1:T(8,128)S(1)} fusion(f32[1024]{0:T(1024)S(1)} %get-tuple-element.22, s32[1024]{0:T(1024)S(1)} %get-tuple-element.25, f32[1024]{0:T(1024)S(1)} %get-tuple-element.23, s32[1024]{0:T(1024)S(1)} %get-tuple-element.24, s32[]{:T(128)S(6)} %select_n.532, bf16[1,19,10,256]{3,2,1,0:T(8,128)(2,1)S(1)} %get-tuple-element.19, ...), kind=kOutput, calls=%fused_computation.4 | convolution fusion | flops 113884864 | bytes 2701832 | tf_op jit(solution)/shard_map/iy,cyj->icj/dot_general | solution.py:262
  68.3 3.4 %collective-permute-done.5 = bf16[19,10,256]{2,1,0:T(8,128)(2,1)S(1)} collective-permute-done((bf16[19,10,256]{2,1,0:T(8,128)(2,1)S(1)}, bf16[19,10,256]{2,1,0:T(8,128)(2,1)S(1)}, u32[]{:S(2)}, u32[]{:S(2)}) %collective-permute-start.5) | collective-permute-done | bytes 97312 | tf_op jit(solution)/shard_map/ppermute | solution.py:247
  71.7 2.7 %convolution_add_fusion = f32[32,19,1024]{2,0,1:T(8,128)} fusion(f32[32,19,1024]{2,0,1:T(8,128)S(1)} %fusion, bf16[19,10,256]{2,1,0:T(8,128)(2,1)S(1)} %collective-permute-done.5, f32[1024]{0:T(1024)S(1)} %get-tuple-element.26, s32[1024]{0:T(1024)S(1)} %get-tuple-element.29, f32[1024]{0:T(1024)S(1)} %get-tuple-element.27, s32[1024]{0:T(1024)S(1)} %get-tuple-element.28, ...), kind=kOutput, calls=%fused_computation.1 | convolution fusion | flops 114458816 | bytes 5094916 | tf_op jit(solution)/shard_map/iy,cyj->icj/dot_general | solution.py:262
  (14 shorter events, 0.3 us)
Async XLA Ops:
  2.0 15.2 %collective-permute-start = (bf16[256,2,256]{2,1,0:T(2,128)(2,1)S(1)}, bf16[256,2,256]{2,1,0:T(2,128)(2,1)S(1)}, u32[]{:S(2)}, u32[]{:S(2)}) collective-permute-start(bf16[256,2,256]{2,1,0:T(2,128)(2,1)S(1)} %get-tuple-element.17), channel_id=1, source_target_pairs={{0,2},{2,4},{4,6},{6,8},{8,10},{10,12},{12,14},{1,3},{3,5},{5,7},{... | collective-permute-start | bytes 786440 | tf_op jit(solution)/shard_map/ppermute | solution.py:215
  4.3 13.5 %collective-permute-start.1 = (bf16[256,2,256]{2,1,0:T(2,128)(2,1)S(1)}, bf16[256,2,256]{2,1,0:T(2,128)(2,1)S(1)}, u32[]{:S(2)}, u32[]{:S(2)}) collective-permute-start(bf16[256,2,256]{2,1,0:T(2,128)(2,1)S(1)} %get-tuple-element.16), channel_id=1, source_target_pairs={{2,0},{4,2},{6,4},{8,6},{10,8},{12,10},{14,12},{3,1},{5,3},{7,5},{... | collective-permute-start | bytes 786440 | tf_op jit(solution)/shard_map/ppermute | solution.py:216
  11.2 4.6 %copy-start = (s32[5]{0:T(128)S(1)}, s32[5]{0:T(128)}, u32[]{:S(2)}) copy-start(s32[5]{0:T(128)} %constant.242) | copy-start | bytes 64
  40.6 13.5 %collective-permute-start.2 = (bf16[19,1,16,256]{3,2,0,1:T(8,128)(2,1)S(1)}, bf16[19,1,16,256]{3,2,0,1:T(8,128)(2,1)S(1)}, u32[]{:S(2)}, u32[]{:S(2)}) collective-permute-start(bf16[19,1,16,256]{3,2,0,1:T(8,128)(2,1)S(1)} %get-tuple-element.20), channel_id=1, source_target_pairs={{0,8},{2,10},{4,12},{6,14},{8,0},{10,2},{12,4},{14,6},{1,9},{3,11}... | collective-permute-start | bytes 466952 | tf_op jit(solution)/shard_map/ppermute | solution.py:35
  54.2 8.8 %collective-permute-start.3 = (bf16[19,2,16,256]{3,2,0,1:T(8,128)(2,1)S(1)}, bf16[19,2,16,256]{3,2,0,1:T(8,128)(2,1)S(1)}, u32[]{:S(2)}, u32[]{:S(2)}) collective-permute-start(bf16[19,2,16,256]{3,2,0,1:T(8,128)(2,1)S(1)} %maximum_select_fusion.2), channel_id=1, source_target_pairs={{0,4},{2,6},{4,0},{6,2},{8,12},{10,14},{12,8},{14,10},{1,5},{3,7},... | collective-permute-start | bytes 933896 | tf_op jit(solution)/shard_map/ppermute | solution.py:35
  63.1 2.1 %collective-permute-start.4 = (bf16[19,4,16,256]{3,2,1,0:T(8,128)(2,1)S(1)}, bf16[19,4,16,256]{3,2,1,0:T(8,128)(2,1)S(1)}, u32[]{:S(2)}, u32[]{:S(2)}) collective-permute-start(bf16[19,4,16,256]{3,2,1,0:T(8,128)(2,1)S(1)} %bitcast.60), channel_id=1, source_target_pairs={{0,2},{2,0},{4,6},{6,4},{8,10},{10,8},{12,14},{14,12},{1,3},{3,1},... | collective-permute-start | bytes 1867784 | tf_op jit(solution)/shard_map/ppermute | solution.py:35
  65.6 6.1 %collective-permute-start.5 = (bf16[19,10,256]{2,1,0:T(8,128)(2,1)S(1)}, bf16[19,10,256]{2,1,0:T(8,128)(2,1)S(1)}, u32[]{:S(2)}, u32[]{:S(2)}) collective-permute-start(bf16[19,10,256]{2,1,0:T(8,128)(2,1)S(1)} %fusion.28), channel_id=1, source_target_pairs={{0,1},{1,0},{2,3},{3,2},{4,5},{5,4},{6,7},{7,6},{8,9},{9,8},{10,11... | collective-permute-start | bytes 291848 | tf_op jit(solution)/shard_map/ppermute | solution.py:247

commit v7 on v6

--- a/solution.py
+++ b/solution.py
@@ -86,7 +86,7 @@
         o_ref[:, pl.ds(pl.multiple_of(r0 * width, width), flat)] = out.astype(o_ref.dtype)
         return carry
 
-    lax.fori_loop(0, o_ref.shape[1] // flat, step, 0)
+    lax.fori_loop(0, o_ref.shape[1] // flat, step, 0, unroll=True)
 
 
 def first_body(main_ref, top_ref, low_ref, w_ref, b_ref, s_ref, o_ref, x_ref, *, width, block, halo):

time: 74.8 us -> 72.5 us (0.969)
  Pallas kernels: 21 us -> 18.7 us
    pallas_call x1, Pallas kernels: 11.5 us -> 9.74 us  [conv_first_layer(): pl.pallas_call(functools.partial(first_body, width=width, block=block, ha...]
where the time goes in v7:
time: 72.5 us; the launch traced here: 72.1 us
  Pallas kernels  18.7 us (26%)
  waiting for transfers between devices  16.1 us (22%)
  starting transfers between devices  11.4 us (16%)
  local copies, waits for them, and re-layouts  11.3 us (16%)
  between operations  8.14 us (11%)
  matrix products  3.87 us (5%)
  other arithmetic  2.6 us (4%)
    ppermute x3, waiting for transfers between devices, gather_rows(): other = lax.ppermute(held, axis, [(i, i ^ bit) for i in range(count)])  12.7 us
    pallas_call x1, Pallas kernels, conv_first_layer(): pl.pallas_call(functools.partial(first_body, width=width, block=block, ha...  9.74 us
    pallas_call x1, Pallas kernels, conv_second_layer(): pl.pallas_call(functools.partial(second_body, width=width, block=block),...  9.01 us
    unnamed x6, local copies, waits for them, and re-layouts  6.3 us
    ppermute x3, starting transfers between devices, gather_rows(): other = lax.ppermute(held, axis, [(i, i ^ bit) for i in range(count)])  6.14 us
    dot_general x2, matrix products, shards(): jnp.einsum('iy,cyj->icj', row_part, widened, preferred_element_type=jnp.f...  3.87 us
    ppermute x1, waiting for transfers between devices, shards(): lax.ppermute(send, 'member', [(i, (i + shift) % members) for i in range(m...  3.38 us
    ppermute x1, starting transfers between devices, shards(): lax.ppermute(lax.slice_in_dim(feat, rows_dev - halo, None, axis=1), 'spac...  2.37 us
  transfers between devices with their start and end apart: 6, of which 4 were waited for; matrix products, arithmetic and copies ran while one was open for 15% of the time, Pallas kernels for 0%

profile of v7, /device:TPU:0, one launch (start us, length us, event | category | flops | bytes accessed | tf_op | source)
XLA Modules:
  0.0 72.1 jit_solution(5058003180942582647)
XLA Ops:
  0.0 1.9 %fusion.70 = (bf16[256,2,256]{2,1,0:T(2,128)(2,1)S(1)}, bf16[256,2,256]{2,1,0:T(2,128)(2,1)S(1)}) fusion(bf16[256,16,256]{2,1,0:T(8,128)(2,1)} %bitcast.58), kind=kLoop, calls=%fused_computation.121 | loop fusion | bytes 1048576 | tf_op jit(solution)/shard_map/slice | solution.py:216
  2.0 2.4 %collective-permute-start = (bf16[256,2,256]{2,1,0:T(2,128)(2,1)S(1)}, bf16[256,2,256]{2,1,0:T(2,128)(2,1)S(1)}, u32[]{:S(2)}, u32[]{:S(2)}) collective-permute-start(bf16[256,2,256]{2,1,0:T(2,128)(2,1)S(1)} %get-tuple-element.17), channel_id=1, source_target_pairs={{0,2},{2,4},{4,6},{6,8},{8,10},{10,12},{12,14},{1,3},{3,5},{5,7},{... | collective-permute-start | bytes 786440 | tf_op jit(solution)/shard_map/ppermute | solution.py:215
  4.3 1.3 %collective-permute-start.1 = (bf16[256,2,256]{2,1,0:T(2,128)(2,1)S(1)}, bf16[256,2,256]{2,1,0:T(2,128)(2,1)S(1)}, u32[]{:S(2)}, u32[]{:S(2)}) collective-permute-start(bf16[256,2,256]{2,1,0:T(2,128)(2,1)S(1)} %get-tuple-element.16), channel_id=1, source_target_pairs={{2,0},{4,2},{6,4},{8,6},{10,8},{12,10},{14,12},{3,1},{5,3},{7,5},{... | collective-permute-start | bytes 786440 | tf_op jit(solution)/shard_map/ppermute | solution.py:216
  5.7 1.4 %fusion.63 = (s32[]{:T(128)}, s32[]{:T(128)}, s32[]{:T(128)}) fusion(s32[2]{0:T(128)} %param.10, s32[]{:T(128)S(6)} %select_n.544, s32[]{:T(128)S(6)} %select_n.496, s32[]{:T(128)S(6)} %axis_index.29), kind=kLoop, calls=%fused_computation.108 | loop fusion | flops 15 | bytes 32 | tf_op jit(solution)/shard_map/reduce_sum | solution.py:251
  9.7 0.7 %pad_maximum_fusion = f32[531]{0:T(1024)S(1)} fusion(f32[19]{0:T(128)} %param.16, f32[256]{0:T(256)} %param.14, f32[256]{0:T(256)} %param.12), kind=kLoop, calls=%fused_computation.76 | loop fusion | flops 1062 | bytes 4248 | tf_op jit(solution)/shard_map/concatenate | solution.py:222
  10.4 0.8 %reshape.307.b_ref = f32[531,1]{1,0:T(8,128)} reshape(f32[531]{0:T(1024)S(1)} %pad_maximum_fusion) | data formatting | bytes 4248 | tf_op jit(solution)/shard_map/reshape | solution.py:222
  11.3 3.9 %copy.14 = bf16[32,8,16,256]{3,1,2,0:T(8,128)(2,1)} copy(bf16[32,8,16,256]{3,2,1,0:T(8,128)(2,1)} %bitcast.59) | data formatting | bytes 4194304
  15.1 0.7 stack.76.s_ref
  15.8 0.1 stack.79
  15.9 1.2 %gather_fusion = s32[5]{0:T(128)} fusion(s32[7]{0:T(128)S(1)} %stack.79, s32[1024]{0:T(1024)S(1)} %pad_clamp_fusion), kind=kCustom, calls=%fused_computation | custom fusion | bytes 60 | tf_op jit(solution)/shard_map/gather | solution.py:221
  17.1 0.0 collective-permute-done
  17.1 0.7 %copy.15 = bf16[32,8,2,256]{3,1,2,0:T(8,128)(2,1)} copy(bf16[32,8,2,256]{3,2,1,0:T(2,128)(2,1)S(1)} %bitcast.69) | data formatting | bytes 524288
  17.9 0.0 collective-permute-done.1
  17.9 0.7 %copy.16 = bf16[32,8,2,256]{3,1,2,0:T(8,128)(2,1)} copy(bf16[32,8,2,256]{3,2,1,0:T(2,128)(2,1)S(1)} %bitcast.68) | data formatting | bytes 524288
  18.6 9.7 %shard_map.91.x_ref = bf16[256,4608]{1,0:T(8,128)(2,1)} custom-call(bf16[256,4096]{1,0:T(8,128)(2,1)} %bitcast.62, bf16[256,512]{1,0:T(8,128)(2,1)} %bitcast.70, bf16[256,512]{1,0:T(8,128)(2,1)} %bitcast.71, bf16[3,3,256,256]{3,2,1,0:T(8,128)(2,1)} %w_ref.2, f32[531,1]{1,0:T(8,128)} %reshape.307.b_ref, s32[5]{0:T(128)} %stack.76.s_ref), custom_call_target="tpu_custom_call" | custom-call | flops 5435817984 | bytes 6160384 | tf_op jit(solution)/shard_map/pallas_call | solution.py:142
  28.3 9.0 %shard_map.92 = bf16[19,4096]{1,0:T(8,128)(2,1)} custom-call(bf16[256,4608]{1,0:T(8,128)(2,1)} %shard_map.91.x_ref, bf16[3,3,256,256]{3,2,1,0:T(8,128)(2,1)} %w_ref.3, f32[531,1]{1,0:T(8,128)} %reshape.307.b_ref, bf16[19,256]{1,0:T(8,128)(2,1)} %k_ref.1, s32[5]{0:T(128)} %gather_fusion), custom_call_target="tpu_custom_call" | custom-call | flops 4871684096 | bytes 3694592 | tf_op jit(solution)/shard_map/pallas_call | solution.py:172
  37.3 1.0 %copy.17 = bf16[3,8,16,256]{3,2,1,0:T(8,128)(2,1)S(1)} copy(bf16[3,8,16,256]{3,1,2,0:T(8,128)(2,1)} %bitcast.72) | data formatting | bytes 393216
  38.3 6.0 %collective-permute-start.2 = (bf16[19,1,16,256]{3,2,0,1:T(8,128)(2,1)S(1)}, bf16[19,1,16,256]{3,2,0,1:T(8,128)(2,1)S(1)}, u32[]{:S(2)}, u32[]{:S(2)}) collective-permute-start(bf16[19,1,16,256]{3,2,0,1:T(8,128)(2,1)S(1)} %get-tuple-element.20), channel_id=1, source_target_pairs={{0,8},{2,10},{4,12},{6,14},{8,0},{10,2},{12,4},{14,6},{1,9},{3,11}... | collective-permute-start | bytes 466952 | tf_op jit(solution)/shard_map/ppermute | solution.py:35
  49.7 2.2 %collective-permute-done.2 = bf16[19,1,16,256]{3,2,0,1:T(8,128)(2,1)S(1)} collective-permute-done((bf16[19,1,16,256]{3,2,0,1:T(8,128)(2,1)S(1)}, bf16[19,1,16,256]{3,2,0,1:T(8,128)(2,1)S(1)}, u32[]{:S(2)}, u32[]{:S(2)}) %collective-permute-start.2) | collective-permute-done | bytes 155680 | tf_op jit(solution)/shard_map/ppermute | solution.py:35
  51.9 0.1 collective-permute-start.3
  52.1 8.6 %collective-permute-done.3 = bf16[19,2,16,256]{3,2,0,1:T(8,128)(2,1)S(1)} collective-permute-done((bf16[19,2,16,256]{3,2,0,1:T(8,128)(2,1)S(1)}, bf16[19,2,16,256]{3,2,0,1:T(8,128)(2,1)S(1)}, u32[]{:S(2)}, u32[]{:S(2)}) %collective-permute-start.3) | collective-permute-done | bytes 311328 | tf_op jit(solution)/shard_map/ppermute | solution.py:35
  60.7 0.1 maximum_select_fusion.1
  60.8 0.1 copy.12
  60.8 0.1 collective-permute-start.4
  61.1 1.9 %collective-permute-done.4 = bf16[19,4,16,256]{3,2,1,0:T(8,128)(2,1)S(1)} collective-permute-done((bf16[19,4,16,256]{3,2,1,0:T(8,128)(2,1)S(1)}, bf16[19,4,16,256]{3,2,1,0:T(8,128)(2,1)S(1)}, u32[]{:S(2)}, u32[]{:S(2)}) %collective-permute-start.4) | collective-permute-done | bytes 622624 | tf_op jit(solution)/shard_map/ppermute | solution.py:35
  63.0 0.1 maximum_select_fusion
  63.1 0.1 dynamic-slice_bitcast_fusion
  63.2 0.1 fusion.28
  63.3 1.6 %collective-permute-start.5 = (bf16[19,10,256]{2,1,0:T(8,128)(2,1)S(1)}, bf16[19,10,256]{2,1,0:T(8,128)(2,1)S(1)}, u32[]{:S(2)}, u32[]{:S(2)}) collective-permute-start(bf16[19,10,256]{2,1,0:T(8,128)(2,1)S(1)} %fusion.28), channel_id=1, source_target_pairs={{0,1},{1,0},{2,3},{3,2},{4,5},{5,4},{6,7},{7,6},{8,9},{9,8},{10,11... | collective-permute-start | bytes 291848 | tf_op jit(solution)/shard_map/ppermute | solution.py:247
  64.9 1.2 %fusion = f32[32,19,1024]{2,0,1:T(8,128)S(1)} fusion(f32[1024]{0:T(1024)S(1)} %get-tuple-element.22, s32[1024]{0:T(1024)S(1)} %get-tuple-element.25, f32[1024]{0:T(1024)S(1)} %get-tuple-element.23, s32[1024]{0:T(1024)S(1)} %get-tuple-element.24, s32[]{:T(128)S(6)} %select_n.532, bf16[1,19,10,256]{3,2,1,0:T(8,128)(2,1)S(1)} %get-tuple-element.19, ...), kind=kOutput, calls=%fused_computation.4 | convolution fusion | flops 113884864 | bytes 2701832 | tf_op jit(solution)/shard_map/iy,cyj->icj/dot_general | solution.py:262
  66.1 3.4 %collective-permute-done.5 = bf16[19,10,256]{2,1,0:T(8,128)(2,1)S(1)} collective-permute-done((bf16[19,10,256]{2,1,0:T(8,128)(2,1)S(1)}, bf16[19,10,256]{2,1,0:T(8,128)(2,1)S(1)}, u32[]{:S(2)}, u32[]{:S(2)}) %collective-permute-start.5) | collective-permute-done | bytes 97312 | tf_op jit(solution)/shard_map/ppermute | solution.py:247
  69.4 2.7 %convolution_add_fusion = f32[32,19,1024]{2,0,1:T(8,128)} fusion(f32[32,19,1024]{2,0,1:T(8,128)S(1)} %fusion, bf16[19,10,256]{2,1,0:T(8,128)(2,1)S(1)} %collective-permute-done.5, f32[1024]{0:T(1024)S(1)} %get-tuple-element.26, s32[1024]{0:T(1024)S(1)} %get-tuple-element.29, f32[1024]{0:T(1024)S(1)} %get-tuple-element.27, s32[1024]{0:T(1024)S(1)} %get-tuple-element.28, ...), kind=kOutput, calls=%fused_computation.1 | convolution fusion | flops 114458816 | bytes 5094916 | tf_op jit(solution)/shard_map/iy,cyj->icj/dot_general | solution.py:262
  (14 shorter events, 0.3 us)
Async XLA Ops:
  2.0 15.2 %collective-permute-start = (bf16[256,2,256]{2,1,0:T(2,128)(2,1)S(1)}, bf16[256,2,256]{2,1,0:T(2,128)(2,1)S(1)}, u32[]{:S(2)}, u32[]{:S(2)}) collective-permute-start(bf16[256,2,256]{2,1,0:T(2,128)(2,1)S(1)} %get-tuple-element.17), channel_id=1, source_target_pairs={{0,2},{2,4},{4,6},{6,8},{8,10},{10,12},{12,14},{1,3},{3,5},{5,7},{... | collective-permute-start | bytes 786440 | tf_op jit(solution)/shard_map/ppermute | solution.py:215
  4.3 13.5 %collective-permute-start.1 = (bf16[256,2,256]{2,1,0:T(2,128)(2,1)S(1)}, bf16[256,2,256]{2,1,0:T(2,128)(2,1)S(1)}, u32[]{:S(2)}, u32[]{:S(2)}) collective-permute-start(bf16[256,2,256]{2,1,0:T(2,128)(2,1)S(1)} %get-tuple-element.16), channel_id=1, source_target_pairs={{2,0},{4,2},{6,4},{8,6},{10,8},{12,10},{14,12},{3,1},{5,3},{7,5},{... | collective-permute-start | bytes 786440 | tf_op jit(solution)/shard_map/ppermute | solution.py:216
  11.2 4.6 %copy-start = (s32[5]{0:T(128)S(1)}, s32[5]{0:T(128)}, u32[]{:S(2)}) copy-start(s32[5]{0:T(128)} %constant.242) | copy-start | bytes 64
  38.3 13.5 %collective-permute-start.2 = (bf16[19,1,16,256]{3,2,0,1:T(8,128)(2,1)S(1)}, bf16[19,1,16,256]{3,2,0,1:T(8,128)(2,1)S(1)}, u32[]{:S(2)}, u32[]{:S(2)}) collective-permute-start(bf16[19,1,16,256]{3,2,0,1:T(8,128)(2,1)S(1)} %get-tuple-element.20), channel_id=1, source_target_pairs={{0,8},{2,10},{4,12},{6,14},{8,0},{10,2},{12,4},{14,6},{1,9},{3,11}... | collective-permute-start | bytes 466952 | tf_op jit(solution)/shard_map/ppermute | solution.py:35
  51.9 8.8 %collective-permute-start.3 = (bf16[19,2,16,256]{3,2,0,1:T(8,128)(2,1)S(1)}, bf16[19,2,16,256]{3,2,0,1:T(8,128)(2,1)S(1)}, u32[]{:S(2)}, u32[]{:S(2)}) collective-permute-start(bf16[19,2,16,256]{3,2,0,1:T(8,128)(2,1)S(1)} %maximum_select_fusion.2), channel_id=1, source_target_pairs={{0,4},{2,6},{4,0},{6,2},{8,12},{10,14},{12,8},{14,10},{1,5},{3,7},... | collective-permute-start | bytes 933896 | tf_op jit(solution)/shard_map/ppermute | solution.py:35
  60.8 2.1 %collective-permute-start.4 = (bf16[19,4,16,256]{3,2,1,0:T(8,128)(2,1)S(1)}, bf16[19,4,16,256]{3,2,1,0:T(8,128)(2,1)S(1)}, u32[]{:S(2)}, u32[]{:S(2)}) collective-permute-start(bf16[19,4,16,256]{3,2,1,0:T(8,128)(2,1)S(1)} %bitcast.60), channel_id=1, source_target_pairs={{0,2},{2,0},{4,6},{6,4},{8,10},{10,8},{12,14},{14,12},{1,3},{3,1},... | collective-permute-start | bytes 1867784 | tf_op jit(solution)/shard_map/ppermute | solution.py:35
  63.3 6.1 %collective-permute-start.5 = (bf16[19,10,256]{2,1,0:T(8,128)(2,1)S(1)}, bf16[19,10,256]{2,1,0:T(8,128)(2,1)S(1)}, u32[]{:S(2)}, u32[]{:S(2)}) collective-permute-start(bf16[19,10,256]{2,1,0:T(8,128)(2,1)S(1)} %fusion.28), channel_id=1, source_target_pairs={{0,1},{1,0},{2,3},{3,2},{4,5},{5,4},{6,7},{7,6},{8,9},{9,8},{10,11... | collective-permute-start | bytes 291848 | tf_op jit(solution)/shard_map/ppermute | solution.py:247

commit v8 on v7

--- a/solution.py
+++ b/solution.py
@@ -118,7 +118,7 @@
     chans = x_ref.shape[0]
     classes = k_ref.shape[0]
     head = (k_ref[...], b_ref[pl.ds(2 * chans, classes), :])
-    lo, hi, good_cols = s_ref[3], s_ref[4], s_ref[2]
+    lo, hi, good_cols = s_ref[5], s_ref[6], s_ref[2]
     run_conv(x_ref, w_ref, b_ref[pl.ds(chans, chans), :], lo, hi, good_cols, o_ref, width, block, head)
 
 
@@ -126,9 +126,10 @@
     return next(k for k in (4, 3, 2, 1) if rows % k == 0)
 
 
-def conv_first_layer(feat, top, low, weights, biases, limits):
-    chans, rows_main, width = feat.shape
-    halo = top.shape[1]
+def conv_first_layer(feat, top, low, width, weights, biases, limits):
+    chans = feat.shape[0]
+    rows_main = feat.shape[1] // width
+    halo = top.shape[1] // width
     rows_in = rows_main + 2 * halo
     rows_out = rows_in - 2
     outs = weights.shape[2]
@@ -147,9 +148,9 @@
         scratch_shapes=[pltpu.VMEM((chans, rows_in * width), jnp.bfloat16)],
         cost_estimate=cost,
     )(
-        feat.reshape(chans, rows_main * width),
-        top.reshape(chans, halo * width),
-        low.reshape(chans, halo * width),
+        feat,
+        top,
+        low,
         weights,
         biases,
         limits,
@@ -212,16 +213,16 @@
     halo = 2
     forward = [(i, i + 1) for i in range(count - 1)]
     backward = [(target, source) for source, target in forward]
-    top_rows = lax.ppermute(lax.slice_in_dim(feat, rows_dev - halo, None, axis=1), "space", forward)
-    low_rows = lax.ppermute(lax.slice_in_dim(feat, 0, halo, axis=1), "space", backward)
+    flat_feat = feat.reshape(feat.shape[0], rows_dev * cols)
+    top_rows = lax.ppermute(flat_feat[:, (rows_dev - halo) * cols:], "space", forward)
+    low_rows = lax.ppermute(flat_feat[:, : halo * cols], "space", backward)
     top = place * rows_dev
     limits = jnp.stack(
         [halo - top, valid_rows - top + halo, valid_cols, 1 - top, valid_rows - top + 1, -top, valid_rows - top]
     ).astype(jnp.int32)
-    limits_second = limits[jnp.array([0, 1, 2, 5, 6])]
     biases = jnp.concatenate([bias_first, bias_second, class_bias]).reshape(-1, 1)
-    hidden = conv_first_layer(feat, top_rows, low_rows, conv_first, biases, limits[:5])
-    logits = conv_second_layer(hidden, cols, conv_second, biases, classify, limits_second)
+    hidden = conv_first_layer(flat_feat, top_rows, low_rows, cols, conv_first, biases, limits)
+    logits = conv_second_layer(hidden, cols, conv_second, biases, classify, limits)
     out_rows = UP * full_rows
     out_cols = UP * cols
     own_rows = out_rows // spaces

time: 72.5 us -> 66.9 us (0.923)
  local copies, waits for them, and re-layouts: 11.3 us -> 6.67 us
  other arithmetic: 2.6 us -> 1.23 us
    slice x1, local copies, waits for them, and re-layouts: 1.95 us -> 0.04 us  [shards(): low_rows = lax.ppermute(flat_feat[:, :halo * cols], 'space', backward)]
    unnamed x6 -> x16, local copies, waits for them, and re-layouts: 6.3 us -> 4.98 us
    gather x1 -> x0, local copies, waits for them, and re-layouts: 1.23 us -> none  [shards(): limits_second = limits[jnp.array([0, 1, 2, 5, 6])]]
  transfers between devices with their start and end apart: 6 -> 6, of which waited for: 4 -> 4; matrix products, arithmetic and copies ran while one was open for 15% -> 5% of each run, Pallas kernels for 0% -> 0%
where the time goes in v8:
time: 66.9 us; the launch traced here: 66.5 us
  Pallas kernels  18.7 us (28%)
  waiting for transfers between devices  16.4 us (25%)
  starting transfers between devices  11.4 us (17%)
  between operations  8.26 us (12%)
  local copies, waits for them, and re-layouts  6.67 us (10%)
  matrix products  3.86 us (6%)
  other arithmetic  1.23 us (2%)
    ppermute x3, waiting for transfers between devices, gather_rows(): other = lax.ppermute(held, axis, [(i, i ^ bit) for i in range(count)])  13 us
    pallas_call x1, Pallas kernels, conv_first_layer(): pl.pallas_call(functools.partial(first_body, width=width, block=block, ha...  9.74 us
    pallas_call x1, Pallas kernels, conv_second_layer(): pl.pallas_call(functools.partial(second_body, width=width, block=block),...  9.01 us
    ppermute x3, starting transfers between devices, gather_rows(): other = lax.ppermute(held, axis, [(i, i ^ bit) for i in range(count)])  6.14 us
    unnamed x16, local copies, waits for them, and re-layouts  4.98 us
    dot_general x2, matrix products, shards(): jnp.einsum('iy,cyj->icj', row_part, widened, preferred_element_type=jnp.f...  3.86 us
    ppermute x1, waiting for transfers between devices, shards(): lax.ppermute(send, 'member', [(i, (i + shift) % members) for i in range(m...  3.38 us
    ppermute x1, starting transfers between devices, shards(): lax.ppermute(flat_feat[:, (rows_dev - halo) * cols:], 'space', forward)  2.37 us
  transfers between devices with their start and end apart: 6, of which 4 were waited for; matrix products, arithmetic and copies ran while one was open for 5% of the time, Pallas kernels for 0%

profile of v8, /device:TPU:0, one launch (start us, length us, event | category | flops | bytes accessed | tf_op | source)
XLA Modules:
  0.0 66.5 jit_solution(16447081675587534254)
XLA Ops:
  0.0 2.6 %copy.13 = bf16[32,8,16,256]{3,1,2,0:T(8,128)(2,1)S(1)} copy(bf16[32,8,16,256]{3,2,1,0:T(8,128)(2,1)} %bitcast.57) | data formatting | bytes 4194304
  2.6 0.0 copy-start
  2.6 2.4 %collective-permute-start = (bf16[256,512]{1,0:T(8,128)(2,1)S(1)}, bf16[256,512]{1,0:T(8,128)(2,1)S(1)}, u32[]{:S(2)}, u32[]{:S(2)}) collective-permute-start(bf16[256,512]{1,0:T(8,128)(2,1)S(1)} %get-tuple-element.17), channel_id=1, source_target_pairs={{0,2},{2,4},{4,6},{6,8},{8,10},{10,12},{12,14},{1,3},{3,5},{5,7},{... | collective-permute-start | bytes 786440 | tf_op jit(solution)/shard_map/ppermute | solution.py:217
  5.0 1.3 %collective-permute-start.1 = (bf16[256,512]{1,0:T(8,128)(2,1)S(1)}, bf16[256,512]{1,0:T(8,128)(2,1)S(1)}, u32[]{:S(2)}, u32[]{:S(2)}) collective-permute-start(bf16[256,512]{1,0:T(8,128)(2,1)S(1)} %get-tuple-element.16), channel_id=1, source_target_pairs={{2,0},{4,2},{6,4},{8,6},{10,8},{12,10},{14,12},{3,1},{5,3},{7,5},{... | collective-permute-start | bytes 786440 | tf_op jit(solution)/shard_map/ppermute | solution.py:218
  6.4 0.0 copy-done.3
  6.4 0.7 %fusion.63 = (s32[]{:T(128)}, s32[]{:T(128)}, s32[]{:T(128)}) fusion(s32[2]{0:T(128)S(1)} %copy-done.3, s32[]{:T(128)S(6)} %select_n.540, s32[]{:T(128)S(6)} %select_n.493, s32[]{:T(128)S(6)} %axis_index.29), kind=kLoop, calls=%fused_computation.106 | loop fusion | flops 15 | bytes 32 | tf_op jit(solution)/shard_map/reduce_sum | solution.py:252
  9.7 0.0 copy-done.1
  9.7 0.0 copy-done.2
  9.8 0.9 %reshape.291.b_ref = f32[531,1]{1,0:T(8,128)} reshape(f32[531]{0:T(1024)S(1)} %pad_maximum_fusion) | data formatting | bytes 4248 | tf_op jit(solution)/shard_map/reshape | solution.py:223
  10.6 0.6 stack.76.s_ref
  11.2 0.0 collective-permute-done.top_ref
  11.2 0.0 collective-permute-done.1.low_ref
  11.2 0.7 %copy-done.5 = bf16[256,512]{1,0:T(8,128)(2,1)} copy-done((bf16[256,512]{1,0:T(8,128)(2,1)}, bf16[256,512]{1,0:T(8,128)(2,1)S(1)}, u32[]{:S(2)}) %copy-start.5) | copy-done | bytes 262168
  11.9 0.7 %copy-done.6 = bf16[256,512]{1,0:T(8,128)(2,1)} copy-done((bf16[256,512]{1,0:T(8,128)(2,1)}, bf16[256,512]{1,0:T(8,128)(2,1)S(1)}, u32[]{:S(2)}) %copy-start.6) | copy-done | bytes 262168
  12.6 9.7 %shard_map.82.x_ref = bf16[256,4608]{1,0:T(8,128)(2,1)} custom-call(bf16[256,4096]{1,0:T(8,128)(2,1)} %bitcast.54, bf16[256,512]{1,0:T(8,128)(2,1)} %copy-done.5, bf16[256,512]{1,0:T(8,128)(2,1)} %copy-done.6, bf16[3,3,256,256]{3,2,1,0:T(8,128)(2,1)} %w_ref.2, f32[531,1]{1,0:T(8,128)} %reshape.291.b_ref, s32[7]{0:T(128)} %stack.76.s_ref), custom_call_target="tpu_custom_call" | custom-call | flops 5435817984 | bytes 6160384 | tf_op jit(solution)/shard_map/pallas_call | solution.py:143
  22.4 9.0 %shard_map.83 = bf16[19,4096]{1,0:T(8,128)(2,1)} custom-call(bf16[256,4608]{1,0:T(8,128)(2,1)} %shard_map.82.x_ref, bf16[3,3,256,256]{3,2,1,0:T(8,128)(2,1)} %w_ref.3, f32[531,1]{1,0:T(8,128)} %reshape.291.b_ref, bf16[19,256]{1,0:T(8,128)(2,1)} %k_ref.1, s32[7]{0:T(128)} %stack.76.s_ref), custom_call_target="tpu_custom_call" | custom-call | flops 4871684096 | bytes 3694592 | tf_op jit(solution)/shard_map/pallas_call | solution.py:173
  31.4 1.0 %copy.14 = bf16[3,8,16,256]{3,2,1,0:T(8,128)(2,1)S(1)} copy(bf16[3,8,16,256]{3,1,2,0:T(8,128)(2,1)} %bitcast.63) | data formatting | bytes 393216
  32.4 6.0 %collective-permute-start.2 = (bf16[19,1,16,256]{3,2,0,1:T(8,128)(2,1)S(1)}, bf16[19,1,16,256]{3,2,0,1:T(8,128)(2,1)S(1)}, u32[]{:S(2)}, u32[]{:S(2)}) collective-permute-start(bf16[19,1,16,256]{3,2,0,1:T(8,128)(2,1)S(1)} %get-tuple-element.20), channel_id=1, source_target_pairs={{0,8},{2,10},{4,12},{6,14},{8,0},{10,2},{12,4},{14,6},{1,9},{3,11}... | collective-permute-start | bytes 466952 | tf_op jit(solution)/shard_map/ppermute | solution.py:35
  43.8 2.3 %collective-permute-done.2 = bf16[19,1,16,256]{3,2,0,1:T(8,128)(2,1)S(1)} collective-permute-done((bf16[19,1,16,256]{3,2,0,1:T(8,128)(2,1)S(1)}, bf16[19,1,16,256]{3,2,0,1:T(8,128)(2,1)S(1)}, u32[]{:S(2)}, u32[]{:S(2)}) %collective-permute-start.2) | collective-permute-done | bytes 155680 | tf_op jit(solution)/shard_map/ppermute | solution.py:35
  46.1 0.1 collective-permute-start.3
  46.3 8.8 %collective-permute-done.3 = bf16[19,2,16,256]{3,2,0,1:T(8,128)(2,1)S(1)} collective-permute-done((bf16[19,2,16,256]{3,2,0,1:T(8,128)(2,1)S(1)}, bf16[19,2,16,256]{3,2,0,1:T(8,128)(2,1)S(1)}, u32[]{:S(2)}, u32[]{:S(2)}) %collective-permute-start.3) | collective-permute-done | bytes 311328 | tf_op jit(solution)/shard_map/ppermute | solution.py:35
  55.1 0.1 maximum_select_fusion.1
  55.2 0.1 copy.11
  55.3 0.1 collective-permute-start.4
  55.5 1.9 %collective-permute-done.4 = bf16[19,4,16,256]{3,2,1,0:T(8,128)(2,1)S(1)} collective-permute-done((bf16[19,4,16,256]{3,2,1,0:T(8,128)(2,1)S(1)}, bf16[19,4,16,256]{3,2,1,0:T(8,128)(2,1)S(1)}, u32[]{:S(2)}, u32[]{:S(2)}) %collective-permute-start.4) | collective-permute-done | bytes 622624 | tf_op jit(solution)/shard_map/ppermute | solution.py:35
  57.4 0.1 maximum_select_fusion
  57.5 0.1 dynamic-slice_bitcast_fusion
  57.7 0.1 fusion.28
  57.7 1.6 %collective-permute-start.5 = (bf16[19,10,256]{2,1,0:T(8,128)(2,1)S(1)}, bf16[19,10,256]{2,1,0:T(8,128)(2,1)S(1)}, u32[]{:S(2)}, u32[]{:S(2)}) collective-permute-start(bf16[19,10,256]{2,1,0:T(8,128)(2,1)S(1)} %fusion.28), channel_id=1, source_target_pairs={{0,1},{1,0},{2,3},{3,2},{4,5},{5,4},{6,7},{7,6},{8,9},{9,8},{10,11... | collective-permute-start | bytes 291848 | tf_op jit(solution)/shard_map/ppermute | solution.py:248
  59.3 1.2 %fusion = f32[32,19,1024]{2,0,1:T(8,128)S(1)} fusion(f32[1024]{0:T(1024)S(1)} %get-tuple-element.22, s32[1024]{0:T(1024)S(1)} %get-tuple-element.25, f32[1024]{0:T(1024)S(1)} %get-tuple-element.23, s32[1024]{0:T(1024)S(1)} %get-tuple-element.24, s32[]{:T(128)S(6)} %select_n.528, bf16[1,19,10,256]{3,2,1,0:T(8,128)(2,1)S(1)} %get-tuple-element.19, ...), kind=kOutput, calls=%fused_computation.3 | convolution fusion | flops 113884864 | bytes 2701832 | tf_op jit(solution)/shard_map/iy,cyj->icj/dot_general | solution.py:263
  60.5 3.4 %collective-permute-done.5 = bf16[19,10,256]{2,1,0:T(8,128)(2,1)S(1)} collective-permute-done((bf16[19,10,256]{2,1,0:T(8,128)(2,1)S(1)}, bf16[19,10,256]{2,1,0:T(8,128)(2,1)S(1)}, u32[]{:S(2)}, u32[]{:S(2)}) %collective-permute-start.5) | collective-permute-done | bytes 97312 | tf_op jit(solution)/shard_map/ppermute | solution.py:248
  63.9 2.7 %convolution_add_fusion = f32[32,19,1024]{2,0,1:T(8,128)} fusion(f32[32,19,1024]{2,0,1:T(8,128)S(1)} %fusion, bf16[19,10,256]{2,1,0:T(8,128)(2,1)S(1)} %collective-permute-done.5, f32[1024]{0:T(1024)S(1)} %get-tuple-element.26, s32[1024]{0:T(1024)S(1)} %get-tuple-element.29, f32[1024]{0:T(1024)S(1)} %get-tuple-element.27, s32[1024]{0:T(1024)S(1)} %get-tuple-element.28, ...), kind=kOutput, calls=%fused_computation | convolution fusion | flops 114458816 | bytes 5094916 | tf_op jit(solution)/shard_map/iy,cyj->icj/dot_general | solution.py:263
  (21 shorter events, 0.3 us)
Async XLA Ops:
  0.0 6.4 %copy-start.3 = (s32[2]{0:T(128)S(1)}, s32[2]{0:T(128)}, u32[]{:S(2)}) copy-start(s32[2]{0:T(128)} %param.9) | copy-start | bytes 28
  0.0 9.7 %copy-start.1 = (f32[256]{0:T(256)S(1)}, f32[256]{0:T(256)}, u32[]{:S(2)}) copy-start(f32[256]{0:T(256)} %param.13) | copy-start | bytes 3076
  0.0 9.7 %copy-start.2 = (f32[256]{0:T(256)S(1)}, f32[256]{0:T(256)}, u32[]{:S(2)}) copy-start(f32[256]{0:T(256)} %param.11) | copy-start | bytes 3076
  0.0 9.8 %copy-start.4 = (f32[19]{0:T(128)S(1)}, f32[19]{0:T(128)}, u32[]{:S(2)}) copy-start(f32[19]{0:T(128)} %param.15) | copy-start | bytes 232
  2.6 8.6 %copy-start = (bf16[32,8,16,256]{3,1,2,0:T(8,128)(2,1)}, bf16[32,8,16,256]{3,1,2,0:T(8,128)(2,1)S(1)}, u32[]{:S(2)}) copy-start(bf16[32,8,16,256]{3,1,2,0:T(8,128)(2,1)S(1)} %copy.13) | copy-start | bytes 6291460
  2.6 8.6 %collective-permute-start = (bf16[256,512]{1,0:T(8,128)(2,1)S(1)}, bf16[256,512]{1,0:T(8,128)(2,1)S(1)}, u32[]{:S(2)}, u32[]{:S(2)}) collective-permute-start(bf16[256,512]{1,0:T(8,128)(2,1)S(1)} %get-tuple-element.17), channel_id=1, source_target_pairs={{0,2},{2,4},{4,6},{6,8},{8,10},{10,12},{12,14},{1,3},{3,5},{5,7},{... | collective-permute-start | bytes 786440 | tf_op jit(solution)/shard_map/ppermute | solution.py:217
  5.0 6.2 %collective-permute-start.1 = (bf16[256,512]{1,0:T(8,128)(2,1)S(1)}, bf16[256,512]{1,0:T(8,128)(2,1)S(1)}, u32[]{:S(2)}, u32[]{:S(2)}) collective-permute-start(bf16[256,512]{1,0:T(8,128)(2,1)S(1)} %get-tuple-element.16), channel_id=1, source_target_pairs={{2,0},{4,2},{6,4},{8,6},{10,8},{12,10},{14,12},{3,1},{5,3},{7,5},{... | collective-permute-start | bytes 786440 | tf_op jit(solution)/shard_map/ppermute | solution.py:218
  11.2 0.7 %copy-start.5 = (bf16[256,512]{1,0:T(8,128)(2,1)}, bf16[256,512]{1,0:T(8,128)(2,1)S(1)}, u32[]{:S(2)}) copy-start(bf16[256,512]{1,0:T(8,128)(2,1)S(1)} %collective-permute-done.top_ref) | copy-start | bytes 786436
  11.9 0.7 %copy-start.6 = (bf16[256,512]{1,0:T(8,128)(2,1)}, bf16[256,512]{1,0:T(8,128)(2,1)S(1)}, u32[]{:S(2)}) copy-start(bf16[256,512]{1,0:T(8,128)(2,1)S(1)} %collective-permute-done.1.low_ref) | copy-start | bytes 786436
  32.4 13.7 %collective-permute-start.2 = (bf16[19,1,16,256]{3,2,0,1:T(8,128)(2,1)S(1)}, bf16[19,1,16,256]{3,2,0,1:T(8,128)(2,1)S(1)}, u32[]{:S(2)}, u32[]{:S(2)}) collective-permute-start(bf16[19,1,16,256]{3,2,0,1:T(8,128)(2,1)S(1)} %get-tuple-element.20), channel_id=1, source_target_pairs={{0,8},{2,10},{4,12},{6,14},{8,0},{10,2},{12,4},{14,6},{1,9},{3,11}... | collective-permute-start | bytes 466952 | tf_op jit(solution)/shard_map/ppermute | solution.py:35
  46.1 9.0 %collective-permute-start.3 = (bf16[19,2,16,256]{3,2,0,1:T(8,128)(2,1)S(1)}, bf16[19,2,16,256]{3,2,0,1:T(8,128)(2,1)S(1)}, u32[]{:S(2)}, u32[]{:S(2)}) collective-permute-start(bf16[19,2,16,256]{3,2,0,1:T(8,128)(2,1)S(1)} %maximum_select_fusion.2), channel_id=1, source_target_pairs={{0,4},{2,6},{4,0},{6,2},{8,12},{10,14},{12,8},{14,10},{1,5},{3,7},... | collective-permute-start | bytes 933896 | tf_op jit(solution)/shard_map/ppermute | solution.py:35
  55.3 2.1 %collective-permute-start.4 = (bf16[19,4,16,256]{3,2,1,0:T(8,128)(2,1)S(1)}, bf16[19,4,16,256]{3,2,1,0:T(8,128)(2,1)S(1)}, u32[]{:S(2)}, u32[]{:S(2)}) collective-permute-start(bf16[19,4,16,256]{3,2,1,0:T(8,128)(2,1)S(1)} %bitcast.55), channel_id=1, source_target_pairs={{0,2},{2,0},{4,6},{6,4},{8,10},{10,8},{12,14},{14,12},{1,3},{3,1},... | collective-permute-start | bytes 1867784 | tf_op jit(solution)/shard_map/ppermute | solution.py:35
  57.7 6.1 %collective-permute-start.5 = (bf16[19,10,256]{2,1,0:T(8,128)(2,1)S(1)}, bf16[19,10,256]{2,1,0:T(8,128)(2,1)S(1)}, u32[]{:S(2)}, u32[]{:S(2)}) collective-permute-start(bf16[19,10,256]{2,1,0:T(8,128)(2,1)S(1)} %fusion.28), channel_id=1, source_target_pairs={{0,1},{1,0},{2,3},{3,2},{4,5},{5,4},{6,7},{7,6},{8,9},{9,8},{10,11... | collective-permute-start | bytes 291848 | tf_op jit(solution)/shard_map/ppermute | solution.py:248

commit v9 on v8

--- a/solution.py
+++ b/solution.py
@@ -8,6 +8,8 @@
 from jax.sharding import PartitionSpec as P
 
 UP = 4
+LOW_CODE = 8
+HIGH_CODE = 29
 
 
 def with_halo(block, sides, width):
@@ -23,7 +25,7 @@
     return block
 
 
-def gather_rows(block, axis):
+def gather_rows(block, axis, need):
     count = lax.axis_size(axis)
     if count & (count - 1):
         return lax.all_gather(block, axis, axis=1, tiled=True)
@@ -32,12 +34,52 @@
     held = block[:, None]
     bit = count // 2
     while bit:
-        other = lax.ppermute(held, axis, [(i, i ^ bit) for i in range(count)])
+        span = 2 * bit
+        routes = {}
+        for p in range(held.shape[1]):
+            pairs = []
+            for i in range(count):
+                j = i ^ bit
+                source = p * span + i % span
+                if any(source in need[g] for g in range(count) if g // bit == j // bit):
+                    pairs.append((i, j))
+            routes.setdefault(tuple(pairs), []).append(p)
+        parts = [None] * held.shape[1]
+        for pairs, places in routes.items():
+            if not pairs:
+                continue
+            sent = lax.ppermute(held[:, jnp.array(places)] if len(places) > 1 else held[:, places[0]:places[0] + 1], axis, list(pairs))
+            for n, p in enumerate(places):
+                parts[p] = sent[:, n:n + 1]
+        empty = jnp.zeros_like(held[:, :1])
+        other = jnp.concatenate([empty if x is None else x for x in parts], 1)
         upper = (me & bit) != 0
         held = jnp.where(upper, jnp.stack([other, held], 2), jnp.stack([held, other], 2))
         held = held.reshape((lead, -1, rows) + rest)
         bit //= 2
     return held.reshape((lead, count * rows) + rest)
+
+
+def block_needs(spaces, members, rows_dev, low_code, high_code):
+    full_rows = rows_dev * spaces
+    out_rows = UP * full_rows
+    own_rows = out_rows // spaces
+    part_rows = own_rows // members
+    window_rows = (part_rows - 1) // UP + 3
+    need = []
+    for place in range(spaces):
+        blocks = set()
+        for numer in range(low_code // 2, high_code // 2 + 1):
+            valid = full_rows * numer // 14
+            for target in range(members):
+                first_row = place * own_rows + target * part_rows
+                pos = (2 * first_row + 1) * valid - out_rows
+                lower = 0 if pos < 0 else pos // (2 * out_rows)
+                lower = valid - 1 if lower >= valid - 1 else lower
+                begin = min(max(lower, 0), full_rows - window_rows)
+                blocks |= set(range(begin // rows_dev, (begin + window_rows - 1) // rows_dev + 1))
+        need.append(blocks)
+    return need
 
 
 def resize_matrix(positions, out_len, valid, in_len):
@@ -228,7 +270,8 @@
     own_rows = out_rows // spaces
     part_rows = own_rows // members
     window_rows = (part_rows - 1) // UP + 3
-    gathered = gather_rows(logits, "space")
+    need = block_needs(spaces, members, rows_dev, LOW_CODE, HIGH_CODE)
+    gathered = gather_rows(logits, "space", need)
     pieces = []
     for target in range(members):
         first_row = place * own_rows + target * part_rows

time: 66.9 us -> 74.7 us (1.12)
  the two profiles are of different devices: /device:TPU:0 before, /device:TPU:30 now
where the time goes in v9:
time: 74.7 us; the launch traced here: 74.2 us
  starting transfers between devices  19.5 us (26%)
  Pallas kernels  18.7 us (25%)
  waiting for transfers between devices  16 us (21%)
  between operations  8.05 us (11%)
  local copies, waits for them, and re-layouts  6.76 us (9%)
  matrix products  3.86 us (5%)
  other arithmetic  1.32 us (2%)
    ppermute x7, starting transfers between devices, gather_rows(): lax.ppermute(held[:, jnp.array(places)] if len(places) > 1 else held[:, p...  13.4 us
    ppermute x7, waiting for transfers between devices, gather_rows(): lax.ppermute(held[:, jnp.array(places)] if len(places) > 1 else held[:, p...  11.4 us
    pallas_call x1, Pallas kernels, conv_first_layer(): pl.pallas_call(functools.partial(first_body, width=width, block=block, ha...  9.74 us
    pallas_call x1, Pallas kernels, conv_second_layer(): pl.pallas_call(functools.partial(second_body, width=width, block=block),...  9 us
    unnamed x16, local copies, waits for them, and re-layouts  4.94 us
    ppermute x1, waiting for transfers between devices, shards(): lax.ppermute(send, 'member', [(i, (i + shift) % members) for i in range(m...  4.56 us
    dot_general x2, matrix products, shards(): jnp.einsum('iy,cyj->icj', row_part, widened, preferred_element_type=jnp.f...  3.86 us
    ppermute x1, starting transfers between devices, shards(): low_rows = lax.ppermute(flat_feat[:, :halo * cols], 'space', backward)  3.64 us
  transfers between devices with their start and end apart: 10, of which 5 were waited for; matrix products, arithmetic and copies ran while one was open for 5% of the time, Pallas kernels for 0%

profile of v9, /device:TPU:30, one launch (start us, length us, event | category | flops | bytes accessed | tf_op | source)
XLA Modules:
  0.0 74.2 jit_solution(15642749851239141492)
XLA Ops:
  0.0 2.6 %copy.13 = bf16[32,8,16,256]{3,1,2,0:T(8,128)(2,1)S(1)} copy(bf16[32,8,16,256]{3,2,1,0:T(8,128)(2,1)} %bitcast.59) | data formatting | bytes 4194304
  2.6 1.9 %collective-permute-start = (bf16[256,512]{1,0:T(8,128)(2,1)S(1)}, bf16[256,512]{1,0:T(8,128)(2,1)S(1)}, u32[]{:S(2)}, u32[]{:S(2)}) collective-permute-start(bf16[256,512]{1,0:T(8,128)(2,1)S(1)} %get-tuple-element.17), channel_id=1, source_target_pairs={{0,2},{2,4},{4,6},{6,8},{8,10},{10,12},{12,14},{1,3},{3,5},{5,7},{... | collective-permute-start | bytes 786440 | tf_op jit(solution)/shard_map/ppermute | solution.py:259
  4.6 3.6 %collective-permute-start.1 = (bf16[256,512]{1,0:T(8,128)(2,1)S(1)}, bf16[256,512]{1,0:T(8,128)(2,1)S(1)}, u32[]{:S(2)}, u32[]{:S(2)}) collective-permute-start(bf16[256,512]{1,0:T(8,128)(2,1)S(1)} %get-tuple-element.16), channel_id=1, source_target_pairs={{2,0},{4,2},{6,4},{8,6},{10,8},{12,10},{14,12},{3,1},{5,3},{7,5},{... | collective-permute-start | bytes 786440 | tf_op jit(solution)/shard_map/ppermute | solution.py:260
  8.3 0.7 fusion.63
  14.2 0.8 %reshape.291.b_ref = f32[531,1]{1,0:T(8,128)} reshape(f32[531]{0:T(1024)S(1)} %pad_maximum_fusion) | data formatting | bytes 4248 | tf_op jit(solution)/shard_map/reshape | solution.py:265
  15.1 0.6 stack.76.s_ref
  15.8 0.7 copy-done.5
  16.5 0.7 copy-done.6
  17.2 9.7 %shard_map.82.x_ref = bf16[256,4608]{1,0:T(8,128)(2,1)} custom-call(bf16[256,4096]{1,0:T(8,128)(2,1)} %bitcast.58, bf16[256,512]{1,0:T(8,128)(2,1)} %copy-done.5, bf16[256,512]{1,0:T(8,128)(2,1)} %copy-done.6, bf16[3,3,256,256]{3,2,1,0:T(8,128)(2,1)} %w_ref.2, f32[531,1]{1,0:T(8,128)} %reshape.291.b_ref, s32[7]{0:T(128)} %stack.76.s_ref), custom_call_target="tpu_custom_call" | custom-call | flops 5435817984 | bytes 6160384 | tf_op jit(solution)/shard_map/pallas_call | solution.py:185
  26.9 9.0 %shard_map.83 = bf16[19,4096]{1,0:T(8,128)(2,1)} custom-call(bf16[256,4608]{1,0:T(8,128)(2,1)} %shard_map.82.x_ref, bf16[3,3,256,256]{3,2,1,0:T(8,128)(2,1)} %w_ref.3, f32[531,1]{1,0:T(8,128)} %reshape.291.b_ref, bf16[19,256]{1,0:T(8,128)(2,1)} %k_ref.1, s32[7]{0:T(128)} %stack.76.s_ref), custom_call_target="tpu_custom_call" | custom-call | flops 4871684096 | bytes 3694592 | tf_op jit(solution)/shard_map/pallas_call | solution.py:215
  35.9 1.0 %copy.14 = bf16[3,8,16,256]{3,2,1,0:T(8,128)(2,1)S(1)} copy(bf16[3,8,16,256]{3,1,2,0:T(8,128)(2,1)} %bitcast.63) | data formatting | bytes 393216
  36.9 1.3 %collective-permute-start.2 = (bf16[19,1,16,256]{3,2,0,1:T(8,128)(2,1)S(1)}, bf16[19,1,16,256]{3,2,0,1:T(8,128)(2,1)S(1)}, u32[]{:S(2)}, u32[]{:S(2)}) collective-permute-start(bf16[19,1,16,256]{3,2,0,1:T(8,128)(2,1)S(1)} %get-tuple-element.26), channel_id=1, source_target_pairs={{2,10},{4,12},{6,14},{8,0},{3,11},{5,13},{7,15},{9,1},{18,26},{20,... | collective-permute-start | bytes 466952 | tf_op jit(solution)/shard_map/ppermute | solution.py:51
  40.6 5.5 %collective-permute-done.2 = bf16[19,1,16,256]{3,2,0,1:T(8,128)(2,1)S(1)} collective-permute-done((bf16[19,1,16,256]{3,2,0,1:T(8,128)(2,1)S(1)}, bf16[19,1,16,256]{3,2,0,1:T(8,128)(2,1)S(1)}, u32[]{:S(2)}, u32[]{:S(2)}) %collective-permute-start.2) | collective-permute-done | bytes 155680 | tf_op jit(solution)/shard_map/ppermute | solution.py:51
  46.2 1.3 %collective-permute-start.3 = (bf16[19,1,16,256]{3,2,0,1:T(8,128)(2,1)S(1)}, bf16[19,1,16,256]{3,2,0,1:T(8,128)(2,1)S(1)}, u32[]{:S(2)}, u32[]{:S(2)}) collective-permute-start(bf16[19,1,16,256]{3,2,0,1:T(8,128)(2,1)S(1)} %get-tuple-element.24), channel_id=1, source_target_pairs={{0,4},{2,6},{4,0},{10,14},{12,8},{14,10},{1,5},{3,7},{5,1},{11,15}... | collective-permute-start | bytes 466952 | tf_op jit(solution)/shard_map/ppermute | solution.py:51
  47.5 2.1 %collective-permute-start.4 = (bf16[19,1,16,256]{3,2,0,1:T(8,128)(2,1)S(1)}, bf16[19,1,16,256]{3,2,0,1:T(8,128)(2,1)S(1)}, u32[]{:S(2)}, u32[]{:S(2)}) collective-permute-start(bf16[19,1,16,256]{3,2,0,1:T(8,128)(2,1)S(1)} %get-tuple-element.25), channel_id=1, source_target_pairs={{0,4},{8,12},{10,14},{12,8},{1,5},{9,13},{11,15},{13,9},{16,20},{2... | collective-permute-start | bytes 466952 | tf_op jit(solution)/shard_map/ppermute | solution.py:51
  49.7 1.0 %collective-permute-done.3 = bf16[19,1,16,256]{3,2,0,1:T(8,128)(2,1)S(1)} collective-permute-done((bf16[19,1,16,256]{3,2,0,1:T(8,128)(2,1)S(1)}, bf16[19,1,16,256]{3,2,0,1:T(8,128)(2,1)S(1)}, u32[]{:S(2)}, u32[]{:S(2)}) %collective-permute-start.3) | collective-permute-done | bytes 155680 | tf_op jit(solution)/shard_map/ppermute | solution.py:51
  50.7 4.1 %collective-permute-done.4 = bf16[19,1,16,256]{3,2,0,1:T(8,128)(2,1)S(1)} collective-permute-done((bf16[19,1,16,256]{3,2,0,1:T(8,128)(2,1)S(1)}, bf16[19,1,16,256]{3,2,0,1:T(8,128)(2,1)S(1)}, u32[]{:S(2)}, u32[]{:S(2)}) %collective-permute-start.4) | collective-permute-done | bytes 155680 | tf_op jit(solution)/shard_map/ppermute | solution.py:51
  54.9 0.1 maximum_select_fusion.1
  54.9 0.1 copy.11
  55.1 1.3 %collective-permute-start.5 = (bf16[19,1,16,256]{3,2,1,0:T(8,128)(2,1)S(1)}, bf16[19,1,16,256]{3,2,1,0:T(8,128)(2,1)S(1)}, u32[]{:S(2)}, u32[]{:S(2)}) collective-permute-start(bf16[19,1,16,256]{3,2,1,0:T(8,128)(2,1)S(1)} %get-tuple-element.20), channel_id=1, source_target_pairs={{0,2},{2,0},{4,6},{6,4},{10,8},{14,12},{1,3},{3,1},{5,7},{7,5},{11... | collective-permute-start | bytes 466952 | tf_op jit(solution)/shard_map/ppermute | solution.py:51
  56.4 3.0 %collective-permute-start.6 = (bf16[19,1,16,256]{3,2,1,0:T(8,128)(2,1)S(1)}, bf16[19,1,16,256]{3,2,1,0:T(8,128)(2,1)S(1)}, u32[]{:S(2)}, u32[]{:S(2)}) collective-permute-start(bf16[19,1,16,256]{3,2,1,0:T(8,128)(2,1)S(1)} %get-tuple-element.23), channel_id=1, source_target_pairs={{0,2},{4,6},{6,4},{8,10},{10,8},{12,14},{14,12},{1,3},{5,7},{7,5},... | collective-permute-start | bytes 466952 | tf_op jit(solution)/shard_map/ppermute | solution.py:51
  59.4 1.9 %collective-permute-start.7 = (bf16[19,1,16,256]{3,2,1,0:T(8,128)(2,1)S(1)}, bf16[19,1,16,256]{3,2,1,0:T(8,128)(2,1)S(1)}, u32[]{:S(2)}, u32[]{:S(2)}) collective-permute-start(bf16[19,1,16,256]{3,2,1,0:T(8,128)(2,1)S(1)} %get-tuple-element.22), channel_id=1, source_target_pairs={{4,6},{8,10},{10,8},{12,14},{14,12},{5,7},{9,11},{11,9},{13,15},{1... | collective-permute-start | bytes 466952 | tf_op jit(solution)/shard_map/ppermute | solution.py:51
  61.3 2.4 %collective-permute-start.8 = (bf16[19,1,16,256]{3,2,1,0:T(8,128)(2,1)S(1)}, bf16[19,1,16,256]{3,2,1,0:T(8,128)(2,1)S(1)}, u32[]{:S(2)}, u32[]{:S(2)}) collective-permute-start(bf16[19,1,16,256]{3,2,1,0:T(8,128)(2,1)S(1)} %get-tuple-element.21), channel_id=1, source_target_pairs={{8,10},{12,14},{14,12},{9,11},{13,15},{15,13},{24,26},{28,30},{30,... | collective-permute-start | bytes 466952 | tf_op jit(solution)/shard_map/ppermute | solution.py:51
  64.0 0.8 %collective-permute-done.8 = bf16[19,1,16,256]{3,2,1,0:T(8,128)(2,1)S(1)} collective-permute-done((bf16[19,1,16,256]{3,2,1,0:T(8,128)(2,1)S(1)}, bf16[19,1,16,256]{3,2,1,0:T(8,128)(2,1)S(1)}, u32[]{:S(2)}, u32[]{:S(2)}) %collective-permute-start.8) | collective-permute-done | bytes 155680 | tf_op jit(solution)/shard_map/ppermute | solution.py:51
  64.8 0.1 maximum_bitcast_fusion
  64.8 0.1 maximum_select_fusion
  65.0 0.1 dynamic-slice_bitcast_fusion
  65.1 0.1 fusion.28
  65.2 0.6 collective-permute-start.9
  65.8 1.2 %fusion = f32[32,19,1024]{2,0,1:T(8,128)S(1)} fusion(f32[1024]{0:T(1024)S(1)} %get-tuple-element.28, s32[1024]{0:T(1024)S(1)} %get-tuple-element.31, f32[1024]{0:T(1024)S(1)} %get-tuple-element.29, s32[1024]{0:T(1024)S(1)} %get-tuple-element.30, s32[]{:T(128)S(6)} %select_n.528, bf16[1,19,10,256]{3,2,1,0:T(8,128)(2,1)S(1)} %get-tuple-element.19, ...), kind=kOutput, calls=%fused_computation.3 | convolution fusion | flops 113884864 | bytes 2701832 | tf_op jit(solution)/shard_map/iy,cyj->icj/dot_general | solution.py:306
  67.0 4.6 %collective-permute-done.9 = bf16[19,10,256]{2,1,0:T(8,128)(2,1)S(1)} collective-permute-done((bf16[19,10,256]{2,1,0:T(8,128)(2,1)S(1)}, bf16[19,10,256]{2,1,0:T(8,128)(2,1)S(1)}, u32[]{:S(2)}, u32[]{:S(2)}) %collective-permute-start.9) | collective-permute-done | bytes 97312 | tf_op jit(solution)/shard_map/ppermute | solution.py:291
  71.6 2.7 %convolution_add_fusion = f32[32,19,1024]{2,0,1:T(8,128)} fusion(f32[32,19,1024]{2,0,1:T(8,128)S(1)} %fusion, bf16[19,10,256]{2,1,0:T(8,128)(2,1)S(1)} %collective-permute-done.9, f32[1024]{0:T(1024)S(1)} %get-tuple-element.32, s32[1024]{0:T(1024)S(1)} %get-tuple-element.35, f32[1024]{0:T(1024)S(1)} %get-tuple-element.33, s32[1024]{0:T(1024)S(1)} %get-tuple-element.34, ...), kind=kOutput, calls=%fused_computation | convolution fusion | flops 114458816 | bytes 5094916 | tf_op jit(solution)/shard_map/iy,cyj->icj/dot_general | solution.py:306
  (33 shorter events, 0.5 us)
Async XLA Ops:
  0.0 8.3 %copy-start.3 = (s32[2]{0:T(128)S(1)}, s32[2]{0:T(128)}, u32[]{:S(2)}) copy-start(s32[2]{0:T(128)} %param.9) | copy-start | bytes 28
  0.0 11.6 %copy-start.1 = (f32[256]{0:T(256)S(1)}, f32[256]{0:T(256)}, u32[]{:S(2)}) copy-start(f32[256]{0:T(256)} %param.13) | copy-start | bytes 3076
  0.0 11.6 %copy-start.2 = (f32[256]{0:T(256)S(1)}, f32[256]{0:T(256)}, u32[]{:S(2)}) copy-start(f32[256]{0:T(256)} %param.11) | copy-start | bytes 3076
  0.0 11.6 %copy-start.4 = (f32[19]{0:T(128)S(1)}, f32[19]{0:T(128)}, u32[]{:S(2)}) copy-start(f32[19]{0:T(128)} %param.15) | copy-start | bytes 232
  2.6 13.2 %copy-start = (bf16[32,8,16,256]{3,1,2,0:T(8,128)(2,1)}, bf16[32,8,16,256]{3,1,2,0:T(8,128)(2,1)S(1)}, u32[]{:S(2)}) copy-start(bf16[32,8,16,256]{3,1,2,0:T(8,128)(2,1)S(1)} %copy.13) | copy-start | bytes 6291460
  2.6 13.1 %collective-permute-start = (bf16[256,512]{1,0:T(8,128)(2,1)S(1)}, bf16[256,512]{1,0:T(8,128)(2,1)S(1)}, u32[]{:S(2)}, u32[]{:S(2)}) collective-permute-start(bf16[256,512]{1,0:T(8,128)(2,1)S(1)} %get-tuple-element.17), channel_id=1, source_target_pairs={{0,2},{2,4},{4,6},{6,8},{8,10},{10,12},{12,14},{1,3},{3,5},{5,7},{... | collective-permute-start | bytes 786440 | tf_op jit(solution)/shard_map/ppermute | solution.py:259
  4.6 11.2 %collective-permute-start.1 = (bf16[256,512]{1,0:T(8,128)(2,1)S(1)}, bf16[256,512]{1,0:T(8,128)(2,1)S(1)}, u32[]{:S(2)}, u32[]{:S(2)}) collective-permute-start(bf16[256,512]{1,0:T(8,128)(2,1)S(1)} %get-tuple-element.16), channel_id=1, source_target_pairs={{2,0},{4,2},{6,4},{8,6},{10,8},{12,10},{14,12},{3,1},{5,3},{7,5},{... | collective-permute-start | bytes 786440 | tf_op jit(solution)/shard_map/ppermute | solution.py:260
  15.8 0.7 copy-start.5
  16.5 0.7 copy-start.6
  36.9 9.2 %collective-permute-start.2 = (bf16[19,1,16,256]{3,2,0,1:T(8,128)(2,1)S(1)}, bf16[19,1,16,256]{3,2,0,1:T(8,128)(2,1)S(1)}, u32[]{:S(2)}, u32[]{:S(2)}) collective-permute-start(bf16[19,1,16,256]{3,2,0,1:T(8,128)(2,1)S(1)} %get-tuple-element.26), channel_id=1, source_target_pairs={{2,10},{4,12},{6,14},{8,0},{3,11},{5,13},{7,15},{9,1},{18,26},{20,... | collective-permute-start | bytes 466952 | tf_op jit(solution)/shard_map/ppermute | solution.py:51
  46.2 4.5 %collective-permute-start.3 = (bf16[19,1,16,256]{3,2,0,1:T(8,128)(2,1)S(1)}, bf16[19,1,16,256]{3,2,0,1:T(8,128)(2,1)S(1)}, u32[]{:S(2)}, u32[]{:S(2)}) collective-permute-start(bf16[19,1,16,256]{3,2,0,1:T(8,128)(2,1)S(1)} %get-tuple-element.24), channel_id=1, source_target_pairs={{0,4},{2,6},{4,0},{10,14},{12,8},{14,10},{1,5},{3,7},{5,1},{11,15}... | collective-permute-start | bytes 466952 | tf_op jit(solution)/shard_map/ppermute | solution.py:51
  47.5 7.3 %collective-permute-start.4 = (bf16[19,1,16,256]{3,2,0,1:T(8,128)(2,1)S(1)}, bf16[19,1,16,256]{3,2,0,1:T(8,128)(2,1)S(1)}, u32[]{:S(2)}, u32[]{:S(2)}) collective-permute-start(bf16[19,1,16,256]{3,2,0,1:T(8,128)(2,1)S(1)} %get-tuple-element.25), channel_id=1, source_target_pairs={{0,4},{8,12},{10,14},{12,8},{1,5},{9,13},{11,15},{13,9},{16,20},{2... | collective-permute-start | bytes 466952 | tf_op jit(solution)/shard_map/ppermute | solution.py:51
  55.1 8.9 %collective-permute-start.5 = (bf16[19,1,16,256]{3,2,1,0:T(8,128)(2,1)S(1)}, bf16[19,1,16,256]{3,2,1,0:T(8,128)(2,1)S(1)}, u32[]{:S(2)}, u32[]{:S(2)}) collective-permute-start(bf16[19,1,16,256]{3,2,1,0:T(8,128)(2,1)S(1)} %get-tuple-element.20), channel_id=1, source_target_pairs={{0,2},{2,0},{4,6},{6,4},{10,8},{14,12},{1,3},{3,1},{5,7},{7,5},{11... | collective-permute-start | bytes 466952 | tf_op jit(solution)/shard_map/ppermute | solution.py:51
  56.4 7.6 %collective-permute-start.6 = (bf16[19,1,16,256]{3,2,1,0:T(8,128)(2,1)S(1)}, bf16[19,1,16,256]{3,2,1,0:T(8,128)(2,1)S(1)}, u32[]{:S(2)}, u32[]{:S(2)}) collective-permute-start(bf16[19,1,16,256]{3,2,1,0:T(8,128)(2,1)S(1)} %get-tuple-element.23), channel_id=1, source_target_pairs={{0,2},{4,6},{6,4},{8,10},{10,8},{12,14},{14,12},{1,3},{5,7},{7,5},... | collective-permute-start | bytes 466952 | tf_op jit(solution)/shard_map/ppermute | solution.py:51
  59.4 4.6 %collective-permute-start.7 = (bf16[19,1,16,256]{3,2,1,0:T(8,128)(2,1)S(1)}, bf16[19,1,16,256]{3,2,1,0:T(8,128)(2,1)S(1)}, u32[]{:S(2)}, u32[]{:S(2)}) collective-permute-start(bf16[19,1,16,256]{3,2,1,0:T(8,128)(2,1)S(1)} %get-tuple-element.22), channel_id=1, source_target_pairs={{4,6},{8,10},{10,8},{12,14},{14,12},{5,7},{9,11},{11,9},{13,15},{1... | collective-permute-start | bytes 466952 | tf_op jit(solution)/shard_map/ppermute | solution.py:51
  61.3 3.4 %collective-permute-start.8 = (bf16[19,1,16,256]{3,2,1,0:T(8,128)(2,1)S(1)}, bf16[19,1,16,256]{3,2,1,0:T(8,128)(2,1)S(1)}, u32[]{:S(2)}, u32[]{:S(2)}) collective-permute-start(bf16[19,1,16,256]{3,2,1,0:T(8,128)(2,1)S(1)} %get-tuple-element.21), channel_id=1, source_target_pairs={{8,10},{12,14},{14,12},{9,11},{13,15},{15,13},{24,26},{28,30},{30,... | collective-permute-start | bytes 466952 | tf_op jit(solution)/shard_map/ppermute | solution.py:51
  65.2 6.4 %collective-permute-start.9 = (bf16[19,10,256]{2,1,0:T(8,128)(2,1)S(1)}, bf16[19,10,256]{2,1,0:T(8,128)(2,1)S(1)}, u32[]{:S(2)}, u32[]{:S(2)}) collective-permute-start(bf16[19,10,256]{2,1,0:T(8,128)(2,1)S(1)} %fusion.28), channel_id=1, source_target_pairs={{0,1},{1,0},{2,3},{3,2},{4,5},{5,4},{6,7},{7,6},{8,9},{9,8},{10,11... | collective-permute-start | bytes 291848 | tf_op jit(solution)/shard_map/ppermute | solution.py:291

commit v10 on v9

--- a/solution.py
+++ b/solution.py
@@ -35,24 +35,13 @@
     bit = count // 2
     while bit:
         span = 2 * bit
-        routes = {}
-        for p in range(held.shape[1]):
-            pairs = []
-            for i in range(count):
-                j = i ^ bit
-                source = p * span + i % span
-                if any(source in need[g] for g in range(count) if g // bit == j // bit):
-                    pairs.append((i, j))
-            routes.setdefault(tuple(pairs), []).append(p)
-        parts = [None] * held.shape[1]
-        for pairs, places in routes.items():
-            if not pairs:
-                continue
-            sent = lax.ppermute(held[:, jnp.array(places)] if len(places) > 1 else held[:, places[0]:places[0] + 1], axis, list(pairs))
-            for n, p in enumerate(places):
-                parts[p] = sent[:, n:n + 1]
-        empty = jnp.zeros_like(held[:, :1])
-        other = jnp.concatenate([empty if x is None else x for x in parts], 1)
+        pairs = []
+        for i in range(count):
+            j = i ^ bit
+            wanted = set().union(*[need[g] for g in range(count) if g // bit == j // bit])
+            if any(p * span + i % span in wanted for p in range(held.shape[1])):
+                pairs.append((i, j))
+        other = lax.ppermute(held, axis, pairs)
         upper = (me & bit) != 0
         held = jnp.where(upper, jnp.stack([other, held], 2), jnp.stack([held, other], 2))
         held = held.reshape((lead, -1, rows) + rest)

time: 74.7 us -> 66.2 us (0.89)
  the two profiles are of different devices: /device:TPU:30 before, /device:TPU:0 now
where the time goes in v10:
time: 66.2 us; the launch traced here: 65.8 us
  Pallas kernels  18.7 us (28%)
  waiting for transfers between devices  14 us (21%)
  starting transfers between devices  13.1 us (20%)
  between operations  8.25 us (12%)
  local copies, waits for them, and re-layouts  6.67 us (10%)
  matrix products  3.86 us (6%)
  other arithmetic  1.23 us (2%)
    ppermute x3, waiting for transfers between devices, gather_rows(): other = lax.ppermute(held, axis, pairs)  10.6 us
    pallas_call x1, Pallas kernels, conv_first_layer(): pl.pallas_call(functools.partial(first_body, width=width, block=block, ha...  9.74 us
    pallas_call x1, Pallas kernels, conv_second_layer(): pl.pallas_call(functools.partial(second_body, width=width, block=block),...  9.01 us
    ppermute x3, starting transfers between devices, gather_rows(): other = lax.ppermute(held, axis, pairs)  7.86 us
    unnamed x16, local copies, waits for them, and re-layouts  4.98 us
    dot_general x2, matrix products, shards(): jnp.einsum('iy,cyj->icj', row_part, widened, preferred_element_type=jnp.f...  3.86 us
    ppermute x1, waiting for transfers between devices, shards(): lax.ppermute(send, 'member', [(i, (i + shift) % members) for i in range(m...  3.37 us
    ppermute x1, starting transfers between devices, shards(): lax.ppermute(flat_feat[:, (rows_dev - halo) * cols:], 'space', forward)  2.37 us
  transfers between devices with their start and end apart: 6, of which 4 were waited for; matrix products, arithmetic and copies ran while one was open for 5% of the time, Pallas kernels for 0%

profile of v10, /device:TPU:0, one launch (start us, length us, event | category | flops | bytes accessed | tf_op | source)
XLA Modules:
  0.0 65.8 jit_solution(17042902587662788641)
XLA Ops:
  0.0 2.6 %copy.13 = bf16[32,8,16,256]{3,1,2,0:T(8,128)(2,1)S(1)} copy(bf16[32,8,16,256]{3,2,1,0:T(8,128)(2,1)} %bitcast.57) | data formatting | bytes 4194304
  2.6 0.0 copy-start
  2.6 2.4 %collective-permute-start = (bf16[256,512]{1,0:T(8,128)(2,1)S(1)}, bf16[256,512]{1,0:T(8,128)(2,1)S(1)}, u32[]{:S(2)}, u32[]{:S(2)}) collective-permute-start(bf16[256,512]{1,0:T(8,128)(2,1)S(1)} %get-tuple-element.17), channel_id=1, source_target_pairs={{0,2},{2,4},{4,6},{6,8},{8,10},{10,12},{12,14},{1,3},{3,5},{5,7},{... | collective-permute-start | bytes 786440 | tf_op jit(solution)/shard_map/ppermute | solution.py:248
  5.0 1.3 %collective-permute-start.1 = (bf16[256,512]{1,0:T(8,128)(2,1)S(1)}, bf16[256,512]{1,0:T(8,128)(2,1)S(1)}, u32[]{:S(2)}, u32[]{:S(2)}) collective-permute-start(bf16[256,512]{1,0:T(8,128)(2,1)S(1)} %get-tuple-element.16), channel_id=1, source_target_pairs={{2,0},{4,2},{6,4},{8,6},{10,8},{12,10},{14,12},{3,1},{5,3},{7,5},{... | collective-permute-start | bytes 786440 | tf_op jit(solution)/shard_map/ppermute | solution.py:249
  6.4 0.0 copy-done.3
  6.4 0.7 %fusion.63 = (s32[]{:T(128)}, s32[]{:T(128)}, s32[]{:T(128)}) fusion(s32[2]{0:T(128)S(1)} %copy-done.3, s32[]{:T(128)S(6)} %select_n.540, s32[]{:T(128)S(6)} %select_n.493, s32[]{:T(128)S(6)} %axis_index.29), kind=kLoop, calls=%fused_computation.106 | loop fusion | flops 15 | bytes 32 | tf_op jit(solution)/shard_map/reduce_sum | solution.py:284
  9.7 0.0 copy-done.1
  9.7 0.0 copy-done.2
  9.8 0.9 %reshape.291.b_ref = f32[531,1]{1,0:T(8,128)} reshape(f32[531]{0:T(1024)S(1)} %pad_maximum_fusion) | data formatting | bytes 4248 | tf_op jit(solution)/shard_map/reshape | solution.py:254
  10.6 0.6 stack.76.s_ref
  11.2 0.0 collective-permute-done.top_ref
  11.2 0.0 collective-permute-done.1.low_ref
  11.2 0.7 %copy-done.5 = bf16[256,512]{1,0:T(8,128)(2,1)} copy-done((bf16[256,512]{1,0:T(8,128)(2,1)}, bf16[256,512]{1,0:T(8,128)(2,1)S(1)}, u32[]{:S(2)}) %copy-start.5) | copy-done | bytes 262168
  11.9 0.7 %copy-done.6 = bf16[256,512]{1,0:T(8,128)(2,1)} copy-done((bf16[256,512]{1,0:T(8,128)(2,1)}, bf16[256,512]{1,0:T(8,128)(2,1)S(1)}, u32[]{:S(2)}) %copy-start.6) | copy-done | bytes 262168
  12.6 9.7 %shard_map.82.x_ref = bf16[256,4608]{1,0:T(8,128)(2,1)} custom-call(bf16[256,4096]{1,0:T(8,128)(2,1)} %bitcast.54, bf16[256,512]{1,0:T(8,128)(2,1)} %copy-done.5, bf16[256,512]{1,0:T(8,128)(2,1)} %copy-done.6, bf16[3,3,256,256]{3,2,1,0:T(8,128)(2,1)} %w_ref.2, f32[531,1]{1,0:T(8,128)} %reshape.291.b_ref, s32[7]{0:T(128)} %stack.76.s_ref), custom_call_target="tpu_custom_call" | custom-call | flops 5435817984 | bytes 6160384 | tf_op jit(solution)/shard_map/pallas_call | solution.py:174
  22.4 9.0 %shard_map.83 = bf16[19,4096]{1,0:T(8,128)(2,1)} custom-call(bf16[256,4608]{1,0:T(8,128)(2,1)} %shard_map.82.x_ref, bf16[3,3,256,256]{3,2,1,0:T(8,128)(2,1)} %w_ref.3, f32[531,1]{1,0:T(8,128)} %reshape.291.b_ref, bf16[19,256]{1,0:T(8,128)(2,1)} %k_ref.1, s32[7]{0:T(128)} %stack.76.s_ref), custom_call_target="tpu_custom_call" | custom-call | flops 4871684096 | bytes 3694592 | tf_op jit(solution)/shard_map/pallas_call | solution.py:204
  31.4 1.0 %copy.14 = bf16[3,8,16,256]{3,2,1,0:T(8,128)(2,1)S(1)} copy(bf16[3,8,16,256]{3,1,2,0:T(8,128)(2,1)} %bitcast.63) | data formatting | bytes 393216
  32.4 1.3 %collective-permute-start.2 = (bf16[19,1,16,256]{3,2,0,1:T(8,128)(2,1)S(1)}, bf16[19,1,16,256]{3,2,0,1:T(8,128)(2,1)S(1)}, u32[]{:S(2)}, u32[]{:S(2)}) collective-permute-start(bf16[19,1,16,256]{3,2,0,1:T(8,128)(2,1)S(1)} %get-tuple-element.20), channel_id=1, source_target_pairs={{2,10},{4,12},{6,14},{8,0},{3,11},{5,13},{7,15},{9,1},{18,26},{20,... | collective-permute-start | bytes 466952 | tf_op jit(solution)/shard_map/ppermute | solution.py:44
  39.1 3.7 %collective-permute-done.2 = bf16[19,1,16,256]{3,2,0,1:T(8,128)(2,1)S(1)} collective-permute-done((bf16[19,1,16,256]{3,2,0,1:T(8,128)(2,1)S(1)}, bf16[19,1,16,256]{3,2,0,1:T(8,128)(2,1)S(1)}, u32[]{:S(2)}, u32[]{:S(2)}) %collective-permute-start.2) | collective-permute-done | bytes 155680 | tf_op jit(solution)/shard_map/ppermute | solution.py:44
  42.8 6.5 %collective-permute-start.3 = (bf16[19,2,16,256]{3,2,0,1:T(8,128)(2,1)S(1)}, bf16[19,2,16,256]{3,2,0,1:T(8,128)(2,1)S(1)}, u32[]{:S(2)}, u32[]{:S(2)}) collective-permute-start(bf16[19,2,16,256]{3,2,0,1:T(8,128)(2,1)S(1)} %maximum_select_fusion.2), channel_id=1, source_target_pairs={{0,4},{2,6},{4,0},{8,12},{10,14},{12,8},{14,10},{1,5},{3,7},{5,1},... | collective-permute-start | bytes 933896 | tf_op jit(solution)/shard_map/ppermute | solution.py:44
  49.4 5.0 %collective-permute-done.3 = bf16[19,2,16,256]{3,2,0,1:T(8,128)(2,1)S(1)} collective-permute-done((bf16[19,2,16,256]{3,2,0,1:T(8,128)(2,1)S(1)}, bf16[19,2,16,256]{3,2,0,1:T(8,128)(2,1)S(1)}, u32[]{:S(2)}, u32[]{:S(2)}) %collective-permute-start.3) | collective-permute-done | bytes 311328 | tf_op jit(solution)/shard_map/ppermute | solution.py:44
  54.4 0.1 maximum_select_fusion.1
  54.5 0.1 copy.11
  54.6 0.1 collective-permute-start.4
  54.8 1.9 %collective-permute-done.4 = bf16[19,4,16,256]{3,2,1,0:T(8,128)(2,1)S(1)} collective-permute-done((bf16[19,4,16,256]{3,2,1,0:T(8,128)(2,1)S(1)}, bf16[19,4,16,256]{3,2,1,0:T(8,128)(2,1)S(1)}, u32[]{:S(2)}, u32[]{:S(2)}) %collective-permute-start.4) | collective-permute-done | bytes 622624 | tf_op jit(solution)/shard_map/ppermute | solution.py:44
  56.7 0.1 maximum_select_fusion
  56.8 0.1 dynamic-slice_bitcast_fusion
  57.0 0.1 fusion.28
  57.0 1.6 %collective-permute-start.5 = (bf16[19,10,256]{2,1,0:T(8,128)(2,1)S(1)}, bf16[19,10,256]{2,1,0:T(8,128)(2,1)S(1)}, u32[]{:S(2)}, u32[]{:S(2)}) collective-permute-start(bf16[19,10,256]{2,1,0:T(8,128)(2,1)S(1)} %fusion.28), channel_id=1, source_target_pairs={{0,1},{1,0},{2,3},{3,2},{4,5},{5,4},{6,7},{7,6},{8,9},{9,8},{10,11... | collective-permute-start | bytes 291848 | tf_op jit(solution)/shard_map/ppermute | solution.py:280
  58.6 1.2 %fusion = f32[32,19,1024]{2,0,1:T(8,128)S(1)} fusion(f32[1024]{0:T(1024)S(1)} %get-tuple-element.22, s32[1024]{0:T(1024)S(1)} %get-tuple-element.25, f32[1024]{0:T(1024)S(1)} %get-tuple-element.23, s32[1024]{0:T(1024)S(1)} %get-tuple-element.24, s32[]{:T(128)S(6)} %select_n.528, bf16[1,19,10,256]{3,2,1,0:T(8,128)(2,1)S(1)} %get-tuple-element.19, ...), kind=kOutput, calls=%fused_computation.3 | convolution fusion | flops 113884864 | bytes 2701832 | tf_op jit(solution)/shard_map/iy,cyj->icj/dot_general | solution.py:295
  59.8 3.4 %collective-permute-done.5 = bf16[19,10,256]{2,1,0:T(8,128)(2,1)S(1)} collective-permute-done((bf16[19,10,256]{2,1,0:T(8,128)(2,1)S(1)}, bf16[19,10,256]{2,1,0:T(8,128)(2,1)S(1)}, u32[]{:S(2)}, u32[]{:S(2)}) %collective-permute-start.5) | collective-permute-done | bytes 97312 | tf_op jit(solution)/shard_map/ppermute | solution.py:280
  63.2 2.7 %convolution_add_fusion = f32[32,19,1024]{2,0,1:T(8,128)} fusion(f32[32,19,1024]{2,0,1:T(8,128)S(1)} %fusion, bf16[19,10,256]{2,1,0:T(8,128)(2,1)S(1)} %collective-permute-done.5, f32[1024]{0:T(1024)S(1)} %get-tuple-element.26, s32[1024]{0:T(1024)S(1)} %get-tuple-element.29, f32[1024]{0:T(1024)S(1)} %get-tuple-element.27, s32[1024]{0:T(1024)S(1)} %get-tuple-element.28, ...), kind=kOutput, calls=%fused_computation | convolution fusion | flops 114458816 | bytes 5094916 | tf_op jit(solution)/shard_map/iy,cyj->icj/dot_general | solution.py:295
  (21 shorter events, 0.3 us)
Async XLA Ops:
  0.0 6.4 %copy-start.3 = (s32[2]{0:T(128)S(1)}, s32[2]{0:T(128)}, u32[]{:S(2)}) copy-start(s32[2]{0:T(128)} %param.9) | copy-start | bytes 28
  0.0 9.7 %copy-start.1 = (f32[256]{0:T(256)S(1)}, f32[256]{0:T(256)}, u32[]{:S(2)}) copy-start(f32[256]{0:T(256)} %param.13) | copy-start | bytes 3076
  0.0 9.7 %copy-start.2 = (f32[256]{0:T(256)S(1)}, f32[256]{0:T(256)}, u32[]{:S(2)}) copy-start(f32[256]{0:T(256)} %param.11) | copy-start | bytes 3076
  0.0 9.8 %copy-start.4 = (f32[19]{0:T(128)S(1)}, f32[19]{0:T(128)}, u32[]{:S(2)}) copy-start(f32[19]{0:T(128)} %param.15) | copy-start | bytes 232
  2.6 8.6 %copy-start = (bf16[32,8,16,256]{3,1,2,0:T(8,128)(2,1)}, bf16[32,8,16,256]{3,1,2,0:T(8,128)(2,1)S(1)}, u32[]{:S(2)}) copy-start(bf16[32,8,16,256]{3,1,2,0:T(8,128)(2,1)S(1)} %copy.13) | copy-start | bytes 6291460
  2.6 8.6 %collective-permute-start = (bf16[256,512]{1,0:T(8,128)(2,1)S(1)}, bf16[256,512]{1,0:T(8,128)(2,1)S(1)}, u32[]{:S(2)}, u32[]{:S(2)}) collective-permute-start(bf16[256,512]{1,0:T(8,128)(2,1)S(1)} %get-tuple-element.17), channel_id=1, source_target_pairs={{0,2},{2,4},{4,6},{6,8},{8,10},{10,12},{12,14},{1,3},{3,5},{5,7},{... | collective-permute-start | bytes 786440 | tf_op jit(solution)/shard_map/ppermute | solution.py:248
  5.0 6.2 %collective-permute-start.1 = (bf16[256,512]{1,0:T(8,128)(2,1)S(1)}, bf16[256,512]{1,0:T(8,128)(2,1)S(1)}, u32[]{:S(2)}, u32[]{:S(2)}) collective-permute-start(bf16[256,512]{1,0:T(8,128)(2,1)S(1)} %get-tuple-element.16), channel_id=1, source_target_pairs={{2,0},{4,2},{6,4},{8,6},{10,8},{12,10},{14,12},{3,1},{5,3},{7,5},{... | collective-permute-start | bytes 786440 | tf_op jit(solution)/shard_map/ppermute | solution.py:249
  11.2 0.7 %copy-start.5 = (bf16[256,512]{1,0:T(8,128)(2,1)}, bf16[256,512]{1,0:T(8,128)(2,1)S(1)}, u32[]{:S(2)}) copy-start(bf16[256,512]{1,0:T(8,128)(2,1)S(1)} %collective-permute-done.top_ref) | copy-start | bytes 786436
  11.9 0.7 %copy-start.6 = (bf16[256,512]{1,0:T(8,128)(2,1)}, bf16[256,512]{1,0:T(8,128)(2,1)S(1)}, u32[]{:S(2)}) copy-start(bf16[256,512]{1,0:T(8,128)(2,1)S(1)} %collective-permute-done.1.low_ref) | copy-start | bytes 786436
  32.4 10.4 %collective-permute-start.2 = (bf16[19,1,16,256]{3,2,0,1:T(8,128)(2,1)S(1)}, bf16[19,1,16,256]{3,2,0,1:T(8,128)(2,1)S(1)}, u32[]{:S(2)}, u32[]{:S(2)}) collective-permute-start(bf16[19,1,16,256]{3,2,0,1:T(8,128)(2,1)S(1)} %get-tuple-element.20), channel_id=1, source_target_pairs={{2,10},{4,12},{6,14},{8,0},{3,11},{5,13},{7,15},{9,1},{18,26},{20,... | collective-permute-start | bytes 466952 | tf_op jit(solution)/shard_map/ppermute | solution.py:44
  42.8 11.6 %collective-permute-start.3 = (bf16[19,2,16,256]{3,2,0,1:T(8,128)(2,1)S(1)}, bf16[19,2,16,256]{3,2,0,1:T(8,128)(2,1)S(1)}, u32[]{:S(2)}, u32[]{:S(2)}) collective-permute-start(bf16[19,2,16,256]{3,2,0,1:T(8,128)(2,1)S(1)} %maximum_select_fusion.2), channel_id=1, source_target_pairs={{0,4},{2,6},{4,0},{8,12},{10,14},{12,8},{14,10},{1,5},{3,7},{5,1},... | collective-permute-start | bytes 933896 | tf_op jit(solution)/shard_map/ppermute | solution.py:44
  54.6 2.1 %collective-permute-start.4 = (bf16[19,4,16,256]{3,2,1,0:T(8,128)(2,1)S(1)}, bf16[19,4,16,256]{3,2,1,0:T(8,128)(2,1)S(1)}, u32[]{:S(2)}, u32[]{:S(2)}) collective-permute-start(bf16[19,4,16,256]{3,2,1,0:T(8,128)(2,1)S(1)} %bitcast.55), channel_id=1, source_target_pairs={{0,2},{2,0},{4,6},{6,4},{8,10},{10,8},{12,14},{14,12},{1,3},{3,1},... | collective-permute-start | bytes 1867784 | tf_op jit(solution)/shard_map/ppermute | solution.py:44
  57.0 6.1 %collective-permute-start.5 = (bf16[19,10,256]{2,1,0:T(8,128)(2,1)S(1)}, bf16[19,10,256]{2,1,0:T(8,128)(2,1)S(1)}, u32[]{:S(2)}, u32[]{:S(2)}) collective-permute-start(bf16[19,10,256]{2,1,0:T(8,128)(2,1)S(1)} %fusion.28), channel_id=1, source_target_pairs={{0,1},{1,0},{2,3},{3,2},{4,5},{5,4},{6,7},{7,6},{8,9},{9,8},{10,11... | collective-permute-start | bytes 291848 | tf_op jit(solution)/shard_map/ppermute | solution.py:280

commit v11 on v9

--- a/solution.py
+++ b/solution.py
@@ -40,19 +40,21 @@
             pairs = []
             for i in range(count):
                 j = i ^ bit
-                source = p * span + i % span
-                if any(source in need[g] for g in range(count) if g // bit == j // bit):
+                wanted = set().union(*[need[g] for g in range(count) if g // bit == j // bit])
+                if p * span + i % span in wanted:
                     pairs.append((i, j))
             routes.setdefault(tuple(pairs), []).append(p)
-        parts = [None] * held.shape[1]
-        for pairs, places in routes.items():
-            if not pairs:
-                continue
-            sent = lax.ppermute(held[:, jnp.array(places)] if len(places) > 1 else held[:, places[0]:places[0] + 1], axis, list(pairs))
-            for n, p in enumerate(places):
-                parts[p] = sent[:, n:n + 1]
-        empty = jnp.zeros_like(held[:, :1])
-        other = jnp.concatenate([empty if x is None else x for x in parts], 1)
+        if bit == 1 or len(routes) == 1:
+            pairs = sorted(set().union(*[set(r) for r in routes]))
+            other = lax.ppermute(held, axis, pairs)
+        else:
+            parts = [None] * held.shape[1]
+            for pairs, places in routes.items():
+                if pairs:
+                    for p in places:
+                        parts[p] = lax.ppermute(held[:, p:p + 1], axis, list(pairs))
+            empty = jnp.zeros_like(held[:, :1])
+            other = jnp.concatenate([empty if x is None else x for x in parts], 1)
         upper = (me & bit) != 0
         held = jnp.where(upper, jnp.stack([other, held], 2), jnp.stack([held, other], 2))
         held = held.reshape((lead, -1, rows) + rest)

time: 74.7 us -> 64.3 us (0.86)
  the two profiles are of different devices: /device:TPU:30 before, /device:TPU:0 now
where the time goes in v11:
time: 64.3 us; the launch traced here: 63.9 us
  Pallas kernels  18.8 us (29%)
  starting transfers between devices  13.5 us (21%)
  waiting for transfers between devices  11.6 us (18%)
  between operations  8.13 us (13%)
  local copies, waits for them, and re-layouts  6.78 us (11%)
  matrix products  3.86 us (6%)
  other arithmetic  1.25 us (2%)
    pallas_call x1, Pallas kernels, conv_first_layer(): pl.pallas_call(functools.partial(first_body, width=width, block=block, ha...  9.74 us
    pallas_call x1, Pallas kernels, conv_second_layer(): pl.pallas_call(functools.partial(second_body, width=width, block=block),...  9.02 us
    ppermute x2, waiting for transfers between devices, gather_rows(): other = lax.ppermute(held, axis, pairs)  8.25 us
    ppermute x2, starting transfers between devices, gather_rows(): parts[p] = lax.ppermute(held[:, p:p + 1], axis, list(pairs))  6.9 us
    unnamed x16, local copies, waits for them, and re-layouts  4.97 us
    dot_general x2, matrix products, shards(): jnp.einsum('iy,cyj->icj', row_part, widened, preferred_element_type=jnp.f...  3.86 us
    ppermute x1, waiting for transfers between devices, shards(): lax.ppermute(send, 'member', [(i, (i + shift) % members) for i in range(m...  3.37 us
    ppermute x1, starting transfers between devices, shards(): lax.ppermute(flat_feat[:, (rows_dev - halo) * cols:], 'space', forward)  2.37 us
  transfers between devices with their start and end apart: 7, of which 3 were waited for; matrix products, arithmetic and copies ran while one was open for 6% of the time, Pallas kernels for 0%

profile of v11, /device:TPU:0, one launch (start us, length us, event | category | flops | bytes accessed | tf_op | source)
XLA Modules:
  0.0 63.9 jit_solution(16290624681448681895)
XLA Ops:
  0.0 2.6 %copy.13 = bf16[32,8,16,256]{3,1,2,0:T(8,128)(2,1)S(1)} copy(bf16[32,8,16,256]{3,2,1,0:T(8,128)(2,1)} %bitcast.58) | data formatting | bytes 4194304
  2.6 0.0 copy-start
  2.6 2.4 %collective-permute-start = (bf16[256,512]{1,0:T(8,128)(2,1)S(1)}, bf16[256,512]{1,0:T(8,128)(2,1)S(1)}, u32[]{:S(2)}, u32[]{:S(2)}) collective-permute-start(bf16[256,512]{1,0:T(8,128)(2,1)S(1)} %get-tuple-element.17), channel_id=1, source_target_pairs={{0,2},{2,4},{4,6},{6,8},{8,10},{10,12},{12,14},{1,3},{3,5},{5,7},{... | collective-permute-start | bytes 786440 | tf_op jit(solution)/shard_map/ppermute | solution.py:261
  5.0 1.3 %collective-permute-start.1 = (bf16[256,512]{1,0:T(8,128)(2,1)S(1)}, bf16[256,512]{1,0:T(8,128)(2,1)S(1)}, u32[]{:S(2)}, u32[]{:S(2)}) collective-permute-start(bf16[256,512]{1,0:T(8,128)(2,1)S(1)} %get-tuple-element.16), channel_id=1, source_target_pairs={{2,0},{4,2},{6,4},{8,6},{10,8},{12,10},{14,12},{3,1},{5,3},{7,5},{... | collective-permute-start | bytes 786440 | tf_op jit(solution)/shard_map/ppermute | solution.py:262
  6.4 0.0 copy-done.3
  6.4 0.7 %fusion.63 = (s32[]{:T(128)}, s32[]{:T(128)}, s32[]{:T(128)}) fusion(s32[2]{0:T(128)S(1)} %copy-done.3, s32[]{:T(128)S(6)} %select_n.540, s32[]{:T(128)S(6)} %select_n.493, s32[]{:T(128)S(6)} %axis_index.29), kind=kLoop, calls=%fused_computation.107 | loop fusion | flops 15 | bytes 32 | tf_op jit(solution)/shard_map/reduce_sum | solution.py:297
  9.8 0.8 %reshape.291.b_ref = f32[531,1]{1,0:T(8,128)} reshape(f32[531]{0:T(1024)S(1)} %pad_maximum_fusion) | data formatting | bytes 4248 | tf_op jit(solution)/shard_map/reshape | solution.py:267
  10.6 0.7 %stack.76.s_ref = s32[7]{0:T(128)} concatenate(s32[1]{0:T(128)} %bitcast.1, s32[1]{0:T(128)} %bitcast.2, s32[1]{0:T(128)} %bitcast.3, s32[1]{0:T(128)} %bitcast.4, s32[1]{0:T(128)} %bitcast.5, s32[1]{0:T(128)} %bitcast.6, s32[1]{0:T(128)} %bitcast.7), dimensions={0} | concatenate | bytes 56 | tf_op jit(solution)/shard_map/stack | solution.py:264
  11.3 0.0 collective-permute-done.top_ref
  11.3 0.0 collective-permute-done.1.low_ref
  11.3 0.7 %copy-done.5 = bf16[256,512]{1,0:T(8,128)(2,1)} copy-done((bf16[256,512]{1,0:T(8,128)(2,1)}, bf16[256,512]{1,0:T(8,128)(2,1)S(1)}, u32[]{:S(2)}) %copy-start.5) | copy-done | bytes 262168
  12.0 0.7 %copy-done.6 = bf16[256,512]{1,0:T(8,128)(2,1)} copy-done((bf16[256,512]{1,0:T(8,128)(2,1)}, bf16[256,512]{1,0:T(8,128)(2,1)S(1)}, u32[]{:S(2)}) %copy-start.6) | copy-done | bytes 262168
  12.7 9.7 %shard_map.82.x_ref = bf16[256,4608]{1,0:T(8,128)(2,1)} custom-call(bf16[256,4096]{1,0:T(8,128)(2,1)} %bitcast.55, bf16[256,512]{1,0:T(8,128)(2,1)} %copy-done.5, bf16[256,512]{1,0:T(8,128)(2,1)} %copy-done.6, bf16[3,3,256,256]{3,2,1,0:T(8,128)(2,1)} %w_ref.2, f32[531,1]{1,0:T(8,128)} %reshape.291.b_ref, s32[7]{0:T(128)} %stack.76.s_ref), custom_call_target="tpu_custom_call" | custom-call | flops 5435817984 | bytes 6160384 | tf_op jit(solution)/shard_map/pallas_call | solution.py:187
  22.5 9.0 %shard_map.83 = bf16[19,4096]{1,0:T(8,128)(2,1)} custom-call(bf16[256,4608]{1,0:T(8,128)(2,1)} %shard_map.82.x_ref, bf16[3,3,256,256]{3,2,1,0:T(8,128)(2,1)} %w_ref.3, f32[531,1]{1,0:T(8,128)} %reshape.291.b_ref, bf16[19,256]{1,0:T(8,128)(2,1)} %k_ref.1, s32[7]{0:T(128)} %stack.76.s_ref), custom_call_target="tpu_custom_call" | custom-call | flops 4871684096 | bytes 3694592 | tf_op jit(solution)/shard_map/pallas_call | solution.py:217
  31.5 1.0 %copy.14 = bf16[3,8,16,256]{3,2,1,0:T(8,128)(2,1)S(1)} copy(bf16[3,8,16,256]{3,1,2,0:T(8,128)(2,1)} %bitcast.63) | data formatting | bytes 393216
  32.5 1.3 %collective-permute-start.2 = (bf16[19,1,16,256]{3,2,0,1:T(8,128)(2,1)S(1)}, bf16[19,1,16,256]{3,2,0,1:T(8,128)(2,1)S(1)}, u32[]{:S(2)}, u32[]{:S(2)}) collective-permute-start(bf16[19,1,16,256]{3,2,0,1:T(8,128)(2,1)S(1)} %get-tuple-element.22), channel_id=1, source_target_pairs={{2,10},{4,12},{6,14},{8,0},{3,11},{5,13},{7,15},{9,1},{18,26},{20,... | collective-permute-start | bytes 466952 | tf_op jit(solution)/shard_map/ppermute | solution.py:49
  36.5 6.4 %collective-permute-done.2 = bf16[19,1,16,256]{3,2,0,1:T(8,128)(2,1)S(1)} collective-permute-done((bf16[19,1,16,256]{3,2,0,1:T(8,128)(2,1)S(1)}, bf16[19,1,16,256]{3,2,0,1:T(8,128)(2,1)S(1)}, u32[]{:S(2)}, u32[]{:S(2)}) %collective-permute-start.2) | collective-permute-done | bytes 155680 | tf_op jit(solution)/shard_map/ppermute | solution.py:49
  43.0 4.8 %collective-permute-start.3 = (bf16[19,1,16,256]{3,2,0,1:T(8,128)(2,1)S(1)}, bf16[19,1,16,256]{3,2,0,1:T(8,128)(2,1)S(1)}, u32[]{:S(2)}, u32[]{:S(2)}) collective-permute-start(bf16[19,1,16,256]{3,2,0,1:T(8,128)(2,1)S(1)} %get-tuple-element.20), channel_id=1, source_target_pairs={{0,4},{2,6},{4,0},{10,14},{12,8},{14,10},{1,5},{3,7},{5,1},{11,15}... | collective-permute-start | bytes 466952 | tf_op jit(solution)/shard_map/ppermute | solution.py:55
  47.8 2.1 %collective-permute-start.4 = (bf16[19,1,16,256]{3,2,0,1:T(8,128)(2,1)S(1)}, bf16[19,1,16,256]{3,2,0,1:T(8,128)(2,1)S(1)}, u32[]{:S(2)}, u32[]{:S(2)}) collective-permute-start(bf16[19,1,16,256]{3,2,0,1:T(8,128)(2,1)S(1)} %get-tuple-element.21), channel_id=1, source_target_pairs={{0,4},{8,12},{10,14},{12,8},{1,5},{9,13},{11,15},{13,9},{16,20},{2... | collective-permute-start | bytes 466952 | tf_op jit(solution)/shard_map/ppermute | solution.py:55
  52.4 0.0 collective-permute-done.3
  52.4 0.0 collective-permute-done.4
  52.5 0.1 maximum_select_fusion.1
  52.6 0.1 copy.11
  52.6 0.1 collective-permute-start.5
  52.9 1.9 %collective-permute-done.5 = bf16[19,4,16,256]{3,2,1,0:T(8,128)(2,1)S(1)} collective-permute-done((bf16[19,4,16,256]{3,2,1,0:T(8,128)(2,1)S(1)}, bf16[19,4,16,256]{3,2,1,0:T(8,128)(2,1)S(1)}, u32[]{:S(2)}, u32[]{:S(2)}) %collective-permute-start.5) | collective-permute-done | bytes 622624 | tf_op jit(solution)/shard_map/ppermute | solution.py:49
  54.8 0.1 maximum_select_fusion
  54.9 0.1 dynamic-slice_bitcast_fusion
  55.0 0.1 fusion.28
  55.1 1.6 %collective-permute-start.6 = (bf16[19,10,256]{2,1,0:T(8,128)(2,1)S(1)}, bf16[19,10,256]{2,1,0:T(8,128)(2,1)S(1)}, u32[]{:S(2)}, u32[]{:S(2)}) collective-permute-start(bf16[19,10,256]{2,1,0:T(8,128)(2,1)S(1)} %fusion.28), channel_id=1, source_target_pairs={{0,1},{1,0},{2,3},{3,2},{4,5},{5,4},{6,7},{7,6},{8,9},{9,8},{10,11... | collective-permute-start | bytes 291848 | tf_op jit(solution)/shard_map/ppermute | solution.py:293
  56.7 1.2 %fusion = f32[32,19,1024]{2,0,1:T(8,128)S(1)} fusion(f32[1024]{0:T(1024)S(1)} %get-tuple-element.24, s32[1024]{0:T(1024)S(1)} %get-tuple-element.27, f32[1024]{0:T(1024)S(1)} %get-tuple-element.25, s32[1024]{0:T(1024)S(1)} %get-tuple-element.26, s32[]{:T(128)S(6)} %select_n.528, bf16[1,19,10,256]{3,2,1,0:T(8,128)(2,1)S(1)} %get-tuple-element.19, ...), kind=kOutput, calls=%fused_computation.3 | convolution fusion | flops 113884864 | bytes 2701832 | tf_op jit(solution)/shard_map/iy,cyj->icj/dot_general | solution.py:308
  57.9 3.4 %collective-permute-done.6 = bf16[19,10,256]{2,1,0:T(8,128)(2,1)S(1)} collective-permute-done((bf16[19,10,256]{2,1,0:T(8,128)(2,1)S(1)}, bf16[19,10,256]{2,1,0:T(8,128)(2,1)S(1)}, u32[]{:S(2)}, u32[]{:S(2)}) %collective-permute-start.6) | collective-permute-done | bytes 97312 | tf_op jit(solution)/shard_map/ppermute | solution.py:293
  61.2 2.7 %convolution_add_fusion = f32[32,19,1024]{2,0,1:T(8,128)} fusion(f32[32,19,1024]{2,0,1:T(8,128)S(1)} %fusion, bf16[19,10,256]{2,1,0:T(8,128)(2,1)S(1)} %collective-permute-done.6, f32[1024]{0:T(1024)S(1)} %get-tuple-element.28, s32[1024]{0:T(1024)S(1)} %get-tuple-element.31, f32[1024]{0:T(1024)S(1)} %get-tuple-element.29, s32[1024]{0:T(1024)S(1)} %get-tuple-element.30, ...), kind=kOutput, calls=%fused_computation | convolution fusion | flops 114458816 | bytes 5094916 | tf_op jit(solution)/shard_map/iy,cyj->icj/dot_general | solution.py:308
  (25 shorter events, 0.4 us)
Async XLA Ops:
  0.0 6.4 %copy-start.3 = (s32[2]{0:T(128)S(1)}, s32[2]{0:T(128)}, u32[]{:S(2)}) copy-start(s32[2]{0:T(128)} %param.9) | copy-start | bytes 28
  0.0 9.7 %copy-start.1 = (f32[256]{0:T(256)S(1)}, f32[256]{0:T(256)}, u32[]{:S(2)}) copy-start(f32[256]{0:T(256)} %param.13) | copy-start | bytes 3076
  0.0 9.7 %copy-start.2 = (f32[256]{0:T(256)S(1)}, f32[256]{0:T(256)}, u32[]{:S(2)}) copy-start(f32[256]{0:T(256)} %param.11) | copy-start | bytes 3076
  0.0 9.7 %copy-start.4 = (f32[19]{0:T(128)S(1)}, f32[19]{0:T(128)}, u32[]{:S(2)}) copy-start(f32[19]{0:T(128)} %param.15) | copy-start | bytes 232
  2.6 8.7 %copy-start = (bf16[32,8,16,256]{3,1,2,0:T(8,128)(2,1)}, bf16[32,8,16,256]{3,1,2,0:T(8,128)(2,1)S(1)}, u32[]{:S(2)}) copy-start(bf16[32,8,16,256]{3,1,2,0:T(8,128)(2,1)S(1)} %copy.13) | copy-start | bytes 6291460
  2.6 8.6 %collective-permute-start = (bf16[256,512]{1,0:T(8,128)(2,1)S(1)}, bf16[256,512]{1,0:T(8,128)(2,1)S(1)}, u32[]{:S(2)}, u32[]{:S(2)}) collective-permute-start(bf16[256,512]{1,0:T(8,128)(2,1)S(1)} %get-tuple-element.17), channel_id=1, source_target_pairs={{0,2},{2,4},{4,6},{6,8},{8,10},{10,12},{12,14},{1,3},{3,5},{5,7},{... | collective-permute-start | bytes 786440 | tf_op jit(solution)/shard_map/ppermute | solution.py:261
  5.0 6.3 %collective-permute-start.1 = (bf16[256,512]{1,0:T(8,128)(2,1)S(1)}, bf16[256,512]{1,0:T(8,128)(2,1)S(1)}, u32[]{:S(2)}, u32[]{:S(2)}) collective-permute-start(bf16[256,512]{1,0:T(8,128)(2,1)S(1)} %get-tuple-element.16), channel_id=1, source_target_pairs={{2,0},{4,2},{6,4},{8,6},{10,8},{12,10},{14,12},{3,1},{5,3},{7,5},{... | collective-permute-start | bytes 786440 | tf_op jit(solution)/shard_map/ppermute | solution.py:262
  11.3 0.7 %copy-start.5 = (bf16[256,512]{1,0:T(8,128)(2,1)}, bf16[256,512]{1,0:T(8,128)(2,1)S(1)}, u32[]{:S(2)}) copy-start(bf16[256,512]{1,0:T(8,128)(2,1)S(1)} %collective-permute-done.top_ref) | copy-start | bytes 786436
  12.0 0.7 %copy-start.6 = (bf16[256,512]{1,0:T(8,128)(2,1)}, bf16[256,512]{1,0:T(8,128)(2,1)S(1)}, u32[]{:S(2)}) copy-start(bf16[256,512]{1,0:T(8,128)(2,1)S(1)} %collective-permute-done.1.low_ref) | copy-start | bytes 786436
  32.5 10.4 %collective-permute-start.2 = (bf16[19,1,16,256]{3,2,0,1:T(8,128)(2,1)S(1)}, bf16[19,1,16,256]{3,2,0,1:T(8,128)(2,1)S(1)}, u32[]{:S(2)}, u32[]{:S(2)}) collective-permute-start(bf16[19,1,16,256]{3,2,0,1:T(8,128)(2,1)S(1)} %get-tuple-element.22), channel_id=1, source_target_pairs={{2,10},{4,12},{6,14},{8,0},{3,11},{5,13},{7,15},{9,1},{18,26},{20,... | collective-permute-start | bytes 466952 | tf_op jit(solution)/shard_map/ppermute | solution.py:49
  43.0 9.5 %collective-permute-start.3 = (bf16[19,1,16,256]{3,2,0,1:T(8,128)(2,1)S(1)}, bf16[19,1,16,256]{3,2,0,1:T(8,128)(2,1)S(1)}, u32[]{:S(2)}, u32[]{:S(2)}) collective-permute-start(bf16[19,1,16,256]{3,2,0,1:T(8,128)(2,1)S(1)} %get-tuple-element.20), channel_id=1, source_target_pairs={{0,4},{2,6},{4,0},{10,14},{12,8},{14,10},{1,5},{3,7},{5,1},{11,15}... | collective-permute-start | bytes 466952 | tf_op jit(solution)/shard_map/ppermute | solution.py:55
  47.8 4.7 %collective-permute-start.4 = (bf16[19,1,16,256]{3,2,0,1:T(8,128)(2,1)S(1)}, bf16[19,1,16,256]{3,2,0,1:T(8,128)(2,1)S(1)}, u32[]{:S(2)}, u32[]{:S(2)}) collective-permute-start(bf16[19,1,16,256]{3,2,0,1:T(8,128)(2,1)S(1)} %get-tuple-element.21), channel_id=1, source_target_pairs={{0,4},{8,12},{10,14},{12,8},{1,5},{9,13},{11,15},{13,9},{16,20},{2... | collective-permute-start | bytes 466952 | tf_op jit(solution)/shard_map/ppermute | solution.py:55
  52.6 2.1 %collective-permute-start.5 = (bf16[19,4,16,256]{3,2,1,0:T(8,128)(2,1)S(1)}, bf16[19,4,16,256]{3,2,1,0:T(8,128)(2,1)S(1)}, u32[]{:S(2)}, u32[]{:S(2)}) collective-permute-start(bf16[19,4,16,256]{3,2,1,0:T(8,128)(2,1)S(1)} %bitcast.56), channel_id=1, source_target_pairs={{0,2},{2,0},{4,6},{6,4},{8,10},{10,8},{12,14},{14,12},{1,3},{3,1},... | collective-permute-start | bytes 1867784 | tf_op jit(solution)/shard_map/ppermute | solution.py:49
  55.1 6.1 %collective-permute-start.6 = (bf16[19,10,256]{2,1,0:T(8,128)(2,1)S(1)}, bf16[19,10,256]{2,1,0:T(8,128)(2,1)S(1)}, u32[]{:S(2)}, u32[]{:S(2)}) collective-permute-start(bf16[19,10,256]{2,1,0:T(8,128)(2,1)S(1)} %fusion.28), channel_id=1, source_target_pairs={{0,1},{1,0},{2,3},{3,2},{4,5},{5,4},{6,7},{7,6},{8,9},{9,8},{10,11... | collective-permute-start | bytes 291848 | tf_op jit(solution)/shard_map/ppermute | solution.py:293

commit v12 on v11

--- a/solution.py
+++ b/solution.py
@@ -125,12 +125,18 @@
         row = r0 + place // width
         keep = (row >= lo) & (row < hi) & (col < good_cols)
         out = jnp.where(keep, total, 0.0).astype(jnp.bfloat16)
-        if head is not None:
+        if head is None:
+            o_ref[:, pl.ds(r0 * width, flat)] = out.astype(o_ref.dtype)
+        else:
             out = jnp.dot(head[0], out, preferred_element_type=jnp.float32) + head[1]
-        o_ref[:, pl.ds(pl.multiple_of(r0 * width, width), flat)] = out.astype(o_ref.dtype)
+            out = out.astype(o_ref.dtype)
+            for r in range(block):
+                o_ref[:, r0 + r, :] = out[:, r * width:(r + 1) * width]
         return carry
 
-    lax.fori_loop(0, o_ref.shape[1] // flat, step, 0, unroll=True)
+    rows_out = o_ref.shape[1] // width if head is None else o_ref.shape[1]
+    for i in range(rows_out // block):
+        step(i, 0)
 
 
 def first_body(main_ref, top_ref, low_ref, w_ref, b_ref, s_ref, o_ref, x_ref, *, width, block, halo):
@@ -216,12 +222,12 @@
     )
     out = pl.pallas_call(
         functools.partial(second_body, width=width, block=block),
-        out_shape=jax.ShapeDtypeStruct((classes, rows_out * width), jnp.bfloat16),
+        out_shape=jax.ShapeDtypeStruct((classes, rows_out, width), jnp.bfloat16),
         in_specs=[vmem] * 4 + [pl.BlockSpec(memory_space=pltpu.SMEM)],
         out_specs=vmem,
         cost_estimate=cost,
     )(x, weights, biases, head, limits)
-    return out.reshape(classes, rows_out, width)
+    return out
 
 
 def window_start(numer, first_row, full_rows, out_rows, window_rows):

time: 64.3 us -> 66.4 us (1.033)
  other arithmetic: 1.25 us -> 3.74 us
  local copies, waits for them, and re-layouts: 6.78 us -> 5.78 us
  waiting for transfers between devices: 11.6 us -> 12.3 us
    select_n x4, other arithmetic: 0.25 us -> 2.77 us  [gather_rows(): jnp.where(upper, jnp.stack([other, held], 2), jnp.stack([held, other], 2))]
    unnamed x16 -> x15, local copies, waits for them, and re-layouts: 4.97 us -> 4.01 us
    ppermute x2, waiting for transfers between devices: 8.25 us -> 8.95 us  [gather_rows(): other = lax.ppermute(held, axis, pairs)]
  transfers between devices with their start and end apart: 7 -> 7, of which waited for: 3 -> 3; matrix products, arithmetic and copies ran while one was open for 6% -> 7% of each run, Pallas kernels for 0% -> 0%
where the time goes in v12:
time: 66.4 us; the launch traced here: 66 us
  Pallas kernels  18.9 us (28%)
  starting transfers between devices  13.6 us (20%)
  waiting for transfers between devices  12.3 us (19%)
  between operations  7.74 us (12%)
  local copies, waits for them, and re-layouts  5.78 us (9%)
  matrix products  3.85 us (6%)
  other arithmetic  3.74 us (6%)
    pallas_call x1, Pallas kernels, conv_first_layer(): pl.pallas_call(functools.partial(first_body, width=width, block=block, ha...  9.74 us
    pallas_call x1, Pallas kernels, conv_second_layer(): pl.pallas_call(functools.partial(second_body, width=width, block=block),...  9.19 us
    ppermute x2, waiting for transfers between devices, gather_rows(): other = lax.ppermute(held, axis, pairs)  8.95 us
    ppermute x2, starting transfers between devices, gather_rows(): parts[p] = lax.ppermute(held[:, p:p + 1], axis, list(pairs))  7 us
    unnamed x15, local copies, waits for them, and re-layouts  4.01 us
    dot_general x2, matrix products, shards(): jnp.einsum('iy,cyj->icj', row_part, widened, preferred_element_type=jnp.f...  3.85 us
    ppermute x1, waiting for transfers between devices, shards(): lax.ppermute(send, 'member', [(i, (i + shift) % members) for i in range(m...  3.37 us
    select_n x4, other arithmetic, gather_rows(): jnp.where(upper, jnp.stack([other, held], 2), jnp.stack([held, other], 2))  2.77 us
  transfers between devices with their start and end apart: 7, of which 3 were waited for; matrix products, arithmetic and copies ran while one was open for 7% of the time, Pallas kernels for 0%

profile of v12, /device:TPU:0, one launch (start us, length us, event | category | flops | bytes accessed | tf_op | source)
XLA Modules:
  0.0 66.0 jit_solution(11930231551321946817)
XLA Ops:
  0.0 2.6 %copy.14 = bf16[32,8,16,256]{3,1,2,0:T(8,128)(2,1)S(1)} copy(bf16[32,8,16,256]{3,2,1,0:T(8,128)(2,1)} %bitcast.50) | data formatting | bytes 4194304
  2.6 0.0 copy-start
  2.6 2.4 %collective-permute-start = (bf16[256,512]{1,0:T(8,128)(2,1)S(1)}, bf16[256,512]{1,0:T(8,128)(2,1)S(1)}, u32[]{:S(2)}, u32[]{:S(2)}) collective-permute-start(bf16[256,512]{1,0:T(8,128)(2,1)S(1)} %get-tuple-element.17), channel_id=1, source_target_pairs={{0,2},{2,4},{4,6},{6,8},{8,10},{10,12},{12,14},{1,3},{3,5},{5,7},{... | collective-permute-start | bytes 786440 | tf_op jit(solution)/shard_map/ppermute | solution.py:267
  5.0 1.3 %collective-permute-start.1 = (bf16[256,512]{1,0:T(8,128)(2,1)S(1)}, bf16[256,512]{1,0:T(8,128)(2,1)S(1)}, u32[]{:S(2)}, u32[]{:S(2)}) collective-permute-start(bf16[256,512]{1,0:T(8,128)(2,1)S(1)} %get-tuple-element.16), channel_id=1, source_target_pairs={{2,0},{4,2},{6,4},{8,6},{10,8},{12,10},{14,12},{3,1},{5,3},{7,5},{... | collective-permute-start | bytes 786440 | tf_op jit(solution)/shard_map/ppermute | solution.py:268
  6.4 0.7 %fusion.63 = (s32[]{:T(128)}, s32[]{:T(128)}, s32[]{:T(128)}) fusion(s32[2]{0:T(128)S(1)} %copy-done.3, s32[]{:T(128)S(6)} %select_n.540, s32[]{:T(128)S(6)} %select_n.493, s32[]{:T(128)S(6)} %axis_index.29), kind=kLoop, calls=%fused_computation.105 | loop fusion | flops 15 | bytes 32 | tf_op jit(solution)/shard_map/reduce_sum | solution.py:303
  9.7 0.8 %reshape.291.b_ref = f32[531,1]{1,0:T(8,128)} reshape(f32[531]{0:T(1024)S(1)} %pad_maximum_fusion) | data formatting | bytes 4248 | tf_op jit(solution)/shard_map/reshape | solution.py:273
  10.6 0.7 %stack.76.s_ref = s32[7]{0:T(128)} concatenate(s32[1]{0:T(128)} %bitcast.1, s32[1]{0:T(128)} %bitcast.2, s32[1]{0:T(128)} %bitcast.3, s32[1]{0:T(128)} %bitcast.4, s32[1]{0:T(128)} %bitcast.5, s32[1]{0:T(128)} %bitcast.6, s32[1]{0:T(128)} %bitcast.7), dimensions={0} | concatenate | bytes 56 | tf_op jit(solution)/shard_map/stack | solution.py:270
  11.2 0.0 collective-permute-done.top_ref
  11.3 0.0 collective-permute-done.1.low_ref
  11.3 0.7 %copy-done.5 = bf16[256,512]{1,0:T(8,128)(2,1)} copy-done((bf16[256,512]{1,0:T(8,128)(2,1)}, bf16[256,512]{1,0:T(8,128)(2,1)S(1)}, u32[]{:S(2)}) %copy-start.5) | copy-done | bytes 262168
  12.0 0.7 %copy-done.6 = bf16[256,512]{1,0:T(8,128)(2,1)} copy-done((bf16[256,512]{1,0:T(8,128)(2,1)}, bf16[256,512]{1,0:T(8,128)(2,1)S(1)}, u32[]{:S(2)}) %copy-start.6) | copy-done | bytes 262168
  12.7 9.7 %shard_map.82.x_ref = bf16[256,4608]{1,0:T(8,128)(2,1)} custom-call(bf16[256,4096]{1,0:T(8,128)(2,1)} %bitcast.49, bf16[256,512]{1,0:T(8,128)(2,1)} %copy-done.5, bf16[256,512]{1,0:T(8,128)(2,1)} %copy-done.6, bf16[3,3,256,256]{3,2,1,0:T(8,128)(2,1)} %w_ref.2, f32[531,1]{1,0:T(8,128)} %reshape.291.b_ref, s32[7]{0:T(128)} %stack.76.s_ref), custom_call_target="tpu_custom_call" | custom-call | flops 5435817984 | bytes 6160384 | tf_op jit(solution)/shard_map/pallas_call | solution.py:193
  22.4 9.2 %shard_map.83 = bf16[19,16,256]{2,1,0:T(8,128)(2,1)} custom-call(bf16[256,4608]{1,0:T(8,128)(2,1)} %shard_map.82.x_ref, bf16[3,3,256,256]{3,2,1,0:T(8,128)(2,1)} %w_ref.3, f32[531,1]{1,0:T(8,128)} %reshape.291.b_ref, bf16[19,256]{1,0:T(8,128)(2,1)} %k_ref.1, s32[7]{0:T(128)} %stack.76.s_ref), custom_call_target="tpu_custom_call" | custom-call | flops 4871684096 | bytes 3694592 | tf_op jit(solution)/shard_map/pallas_call | solution.py:223
  31.6 1.3 %collective-permute-start.2 = (bf16[19,1,16,256]{3,2,0,1:T(8,128)(2,1)}, bf16[19,1,16,256]{3,2,0,1:T(8,128)(2,1)S(1)}, u32[]{:S(2)}, u32[]{:S(2)}) collective-permute-start(bf16[19,1,16,256]{3,2,0,1:T(8,128)(2,1)} %bitcast.53), channel_id=1, source_target_pairs={{2,10},{4,12},{6,14},{8,0},{3,11},{5,13},{7,15},{9,1},{18,26},{20,... | collective-permute-start | bytes 466952 | tf_op jit(solution)/shard_map/ppermute | solution.py:49
  35.2 7.1 %collective-permute-done.2 = bf16[19,1,16,256]{3,2,0,1:T(8,128)(2,1)S(1)} collective-permute-done((bf16[19,1,16,256]{3,2,0,1:T(8,128)(2,1)}, bf16[19,1,16,256]{3,2,0,1:T(8,128)(2,1)S(1)}, u32[]{:S(2)}, u32[]{:S(2)}) %collective-permute-start.2) | collective-permute-done | bytes 155680 | tf_op jit(solution)/shard_map/ppermute | solution.py:49
  42.2 1.0 %maximum_select_fusion.2 = bf16[19,2,16,256]{3,2,0,1:T(8,128)(2,1)S(1)} fusion(bf16[19,1,16,256]{3,2,0,1:T(8,128)(2,1)} %bitcast.54, bf16[19,1,16,256]{3,2,0,1:T(8,128)(2,1)S(1)} %collective-permute-done.2, pred[]{:T(512)S(6)} %ne.270), kind=kLoop, calls=%fused_computation.28 | loop fusion | flops 466944 | bytes 622593 | tf_op jit(solution)/shard_map/jit(_where)/select_n | solution.py:59
  43.3 4.9 %collective-permute-start.3 = (bf16[19,1,16,256]{3,2,0,1:T(8,128)(2,1)S(1)}, bf16[19,1,16,256]{3,2,0,1:T(8,128)(2,1)S(1)}, u32[]{:S(2)}, u32[]{:S(2)}) collective-permute-start(bf16[19,1,16,256]{3,2,0,1:T(8,128)(2,1)S(1)} %get-tuple-element.20), channel_id=1, source_target_pairs={{0,4},{2,6},{4,0},{10,14},{12,8},{14,10},{1,5},{3,7},{5,1},{11,15}... | collective-permute-start | bytes 466952 | tf_op jit(solution)/shard_map/ppermute | solution.py:55
  48.2 2.1 %collective-permute-start.4 = (bf16[19,1,16,256]{3,2,0,1:T(8,128)(2,1)S(1)}, bf16[19,1,16,256]{3,2,0,1:T(8,128)(2,1)S(1)}, u32[]{:S(2)}, u32[]{:S(2)}) collective-permute-start(bf16[19,1,16,256]{3,2,0,1:T(8,128)(2,1)S(1)} %get-tuple-element.21), channel_id=1, source_target_pairs={{0,4},{8,12},{10,14},{12,8},{1,5},{9,13},{11,15},{13,9},{16,20},{2... | collective-permute-start | bytes 466952 | tf_op jit(solution)/shard_map/ppermute | solution.py:55
  52.9 1.0 %maximum_select_fusion.3 = bf16[19,2,1,16,256]{4,3,0,2,1:T(8,128)(2,1)S(1)} fusion(bf16[19,1,1,16,256]{4,3,0,2,1:T(8,128)(2,1)} %bitcast.55, bf16[19,1,1,16,256]{4,3,0,2,1:T(8,128)(2,1)S(1)} %bitcast.56, pred[]{:T(512)S(6)} %ne.270), kind=kLoop, calls=%fused_computation.30 | loop fusion | flops 466944 | bytes 622593 | tf_op jit(solution)/shard_map/jit(_where)/select_n | solution.py:59
  54.0 0.0 collective-permute-done.3
  54.0 0.0 collective-permute-done.4
  54.0 0.1 maximum_select_fusion.1
  54.1 0.1 copy.11
  54.2 0.1 collective-permute-start.5
  54.4 1.9 %collective-permute-done.5 = bf16[19,4,16,256]{3,2,1,0:T(8,128)(2,1)S(1)} collective-permute-done((bf16[19,4,16,256]{3,2,1,0:T(8,128)(2,1)S(1)}, bf16[19,4,16,256]{3,2,1,0:T(8,128)(2,1)S(1)}, u32[]{:S(2)}, u32[]{:S(2)}) %collective-permute-start.5) | collective-permute-done | bytes 622624 | tf_op jit(solution)/shard_map/ppermute | solution.py:49
  56.3 0.6 maximum_select_fusion
  56.9 0.1 dynamic-slice_bitcast_fusion
  57.1 0.1 fusion.28
  57.2 1.6 %collective-permute-start.6 = (bf16[19,10,256]{2,1,0:T(8,128)(2,1)S(1)}, bf16[19,10,256]{2,1,0:T(8,128)(2,1)S(1)}, u32[]{:S(2)}, u32[]{:S(2)}) collective-permute-start(bf16[19,10,256]{2,1,0:T(8,128)(2,1)S(1)} %fusion.28), channel_id=1, source_target_pairs={{0,1},{1,0},{2,3},{3,2},{4,5},{5,4},{6,7},{7,6},{8,9},{9,8},{10,11... | collective-permute-start | bytes 291848 | tf_op jit(solution)/shard_map/ppermute | solution.py:299
  58.7 1.2 %fusion = f32[32,19,1024]{2,0,1:T(8,128)S(1)} fusion(f32[1024]{0:T(1024)S(1)} %get-tuple-element.22, s32[1024]{0:T(1024)S(1)} %get-tuple-element.25, f32[1024]{0:T(1024)S(1)} %get-tuple-element.23, s32[1024]{0:T(1024)S(1)} %get-tuple-element.24, s32[]{:T(128)S(6)} %select_n.528, bf16[1,19,10,256]{3,2,1,0:T(8,128)(2,1)S(1)} %get-tuple-element.19, ...), kind=kOutput, calls=%fused_computation.3 | convolution fusion | flops 113884864 | bytes 2701832 | tf_op jit(solution)/shard_map/iy,cyj->icj/dot_general | solution.py:314
  59.9 3.4 %collective-permute-done.6 = bf16[19,10,256]{2,1,0:T(8,128)(2,1)S(1)} collective-permute-done((bf16[19,10,256]{2,1,0:T(8,128)(2,1)S(1)}, bf16[19,10,256]{2,1,0:T(8,128)(2,1)S(1)}, u32[]{:S(2)}, u32[]{:S(2)}) %collective-permute-start.6) | collective-permute-done | bytes 97312 | tf_op jit(solution)/shard_map/ppermute | solution.py:299
  63.3 2.7 %convolution_add_fusion = f32[32,19,1024]{2,0,1:T(8,128)} fusion(f32[32,19,1024]{2,0,1:T(8,128)S(1)} %fusion, bf16[19,10,256]{2,1,0:T(8,128)(2,1)S(1)} %collective-permute-done.6, f32[1024]{0:T(1024)S(1)} %get-tuple-element.26, s32[1024]{0:T(1024)S(1)} %get-tuple-element.29, f32[1024]{0:T(1024)S(1)} %get-tuple-element.27, s32[1024]{0:T(1024)S(1)} %get-tuple-element.28, ...), kind=kOutput, calls=%fused_computation | convolution fusion | flops 114458816 | bytes 5094916 | tf_op jit(solution)/shard_map/iy,cyj->icj/dot_general | solution.py:314
  (23 shorter events, 0.3 us)
Async XLA Ops:
  0.0 6.4 %copy-start.3 = (s32[2]{0:T(128)S(1)}, s32[2]{0:T(128)}, u32[]{:S(2)}) copy-start(s32[2]{0:T(128)} %param.9) | copy-start | bytes 28
  0.0 9.7 %copy-start.1 = (f32[256]{0:T(256)S(1)}, f32[256]{0:T(256)}, u32[]{:S(2)}) copy-start(f32[256]{0:T(256)} %param.13) | copy-start | bytes 3076
  0.0 9.7 %copy-start.2 = (f32[256]{0:T(256)S(1)}, f32[256]{0:T(256)}, u32[]{:S(2)}) copy-start(f32[256]{0:T(256)} %param.11) | copy-start | bytes 3076
  0.0 9.7 %copy-start.4 = (f32[19]{0:T(128)S(1)}, f32[19]{0:T(128)}, u32[]{:S(2)}) copy-start(f32[19]{0:T(128)} %param.15) | copy-start | bytes 232
  2.6 8.7 %copy-start = (bf16[32,8,16,256]{3,1,2,0:T(8,128)(2,1)}, bf16[32,8,16,256]{3,1,2,0:T(8,128)(2,1)S(1)}, u32[]{:S(2)}) copy-start(bf16[32,8,16,256]{3,1,2,0:T(8,128)(2,1)S(1)} %copy.14) | copy-start | bytes 6291460
  2.6 8.6 %collective-permute-start = (bf16[256,512]{1,0:T(8,128)(2,1)S(1)}, bf16[256,512]{1,0:T(8,128)(2,1)S(1)}, u32[]{:S(2)}, u32[]{:S(2)}) collective-permute-start(bf16[256,512]{1,0:T(8,128)(2,1)S(1)} %get-tuple-element.17), channel_id=1, source_target_pairs={{0,2},{2,4},{4,6},{6,8},{8,10},{10,12},{12,14},{1,3},{3,5},{5,7},{... | collective-permute-start | bytes 786440 | tf_op jit(solution)/shard_map/ppermute | solution.py:267
  5.0 6.2 %collective-permute-start.1 = (bf16[256,512]{1,0:T(8,128)(2,1)S(1)}, bf16[256,512]{1,0:T(8,128)(2,1)S(1)}, u32[]{:S(2)}, u32[]{:S(2)}) collective-permute-start(bf16[256,512]{1,0:T(8,128)(2,1)S(1)} %get-tuple-element.16), channel_id=1, source_target_pairs={{2,0},{4,2},{6,4},{8,6},{10,8},{12,10},{14,12},{3,1},{5,3},{7,5},{... | collective-permute-start | bytes 786440 | tf_op jit(solution)/shard_map/ppermute | solution.py:268
  11.2 0.7 %copy-start.5 = (bf16[256,512]{1,0:T(8,128)(2,1)}, bf16[256,512]{1,0:T(8,128)(2,1)S(1)}, u32[]{:S(2)}) copy-start(bf16[256,512]{1,0:T(8,128)(2,1)S(1)} %collective-permute-done.top_ref) | copy-start | bytes 786436
  12.0 0.7 %copy-start.6 = (bf16[256,512]{1,0:T(8,128)(2,1)}, bf16[256,512]{1,0:T(8,128)(2,1)S(1)}, u32[]{:S(2)}) copy-start(bf16[256,512]{1,0:T(8,128)(2,1)S(1)} %collective-permute-done.1.low_ref) | copy-start | bytes 786436
  31.6 10.6 %collective-permute-start.2 = (bf16[19,1,16,256]{3,2,0,1:T(8,128)(2,1)}, bf16[19,1,16,256]{3,2,0,1:T(8,128)(2,1)S(1)}, u32[]{:S(2)}, u32[]{:S(2)}) collective-permute-start(bf16[19,1,16,256]{3,2,0,1:T(8,128)(2,1)} %bitcast.53), channel_id=1, source_target_pairs={{2,10},{4,12},{6,14},{8,0},{3,11},{5,13},{7,15},{9,1},{18,26},{20,... | collective-permute-start | bytes 466952 | tf_op jit(solution)/shard_map/ppermute | solution.py:49
  43.3 10.7 %collective-permute-start.3 = (bf16[19,1,16,256]{3,2,0,1:T(8,128)(2,1)S(1)}, bf16[19,1,16,256]{3,2,0,1:T(8,128)(2,1)S(1)}, u32[]{:S(2)}, u32[]{:S(2)}) collective-permute-start(bf16[19,1,16,256]{3,2,0,1:T(8,128)(2,1)S(1)} %get-tuple-element.20), channel_id=1, source_target_pairs={{0,4},{2,6},{4,0},{10,14},{12,8},{14,10},{1,5},{3,7},{5,1},{11,15}... | collective-permute-start | bytes 466952 | tf_op jit(solution)/shard_map/ppermute | solution.py:55
  48.2 5.8 %collective-permute-start.4 = (bf16[19,1,16,256]{3,2,0,1:T(8,128)(2,1)S(1)}, bf16[19,1,16,256]{3,2,0,1:T(8,128)(2,1)S(1)}, u32[]{:S(2)}, u32[]{:S(2)}) collective-permute-start(bf16[19,1,16,256]{3,2,0,1:T(8,128)(2,1)S(1)} %get-tuple-element.21), channel_id=1, source_target_pairs={{0,4},{8,12},{10,14},{12,8},{1,5},{9,13},{11,15},{13,9},{16,20},{2... | collective-permute-start | bytes 466952 | tf_op jit(solution)/shard_map/ppermute | solution.py:55
  54.2 2.1 %collective-permute-start.5 = (bf16[19,4,16,256]{3,2,1,0:T(8,128)(2,1)S(1)}, bf16[19,4,16,256]{3,2,1,0:T(8,128)(2,1)S(1)}, u32[]{:S(2)}, u32[]{:S(2)}) collective-permute-start(bf16[19,4,16,256]{3,2,1,0:T(8,128)(2,1)S(1)} %copy.11), channel_id=1, source_target_pairs={{0,2},{2,0},{4,6},{6,4},{8,10},{10,8},{12,14},{14,12},{1,3},{3,1},... | collective-permute-start | bytes 1867784 | tf_op jit(solution)/shard_map/ppermute | solution.py:49
  57.2 6.1 %collective-permute-start.6 = (bf16[19,10,256]{2,1,0:T(8,128)(2,1)S(1)}, bf16[19,10,256]{2,1,0:T(8,128)(2,1)S(1)}, u32[]{:S(2)}, u32[]{:S(2)}) collective-permute-start(bf16[19,10,256]{2,1,0:T(8,128)(2,1)S(1)} %fusion.28), channel_id=1, source_target_pairs={{0,1},{1,0},{2,3},{3,2},{4,5},{5,4},{6,7},{7,6},{8,9},{9,8},{10,11... | collective-permute-start | bytes 291848 | tf_op jit(solution)/shard_map/ppermute | solution.py:299

commit v13 on v11

--- a/solution.py
+++ b/solution.py
@@ -167,7 +167,7 @@
 
 
 def pick_block(rows):
-    return next(k for k in (4, 3, 2, 1) if rows % k == 0)
+    return next(k for k in (2, 1) if rows % k == 0)
 
 
 def conv_first_layer(feat, top, low, width, weights, biases, limits):

time: 64.3 us -> 65.3 us (1.016)
  Pallas kernels: 18.8 us -> 19.8 us
    pallas_call x1, Pallas kernels: 9.02 us -> 10.2 us  [conv_second_layer(): pl.pallas_call(functools.partial(second_body, width=width, block=block),...]
  transfers between devices with their start and end apart: 7 -> 7, of which waited for: 3 -> 4; matrix products, arithmetic and copies ran while one was open for 6% -> 6% of each run, Pallas kernels for 0% -> 0%
where the time goes in v13:
time: 65.3 us; the launch traced here: 64.9 us
  Pallas kernels  19.8 us (30%)
  starting transfers between devices  13.5 us (21%)
  waiting for transfers between devices  11.6 us (18%)
  between operations  8.12 us (12%)
  local copies, waits for them, and re-layouts  6.78 us (10%)
  matrix products  3.85 us (6%)
  other arithmetic  1.25 us (2%)
    pallas_call x1, Pallas kernels, conv_second_layer(): pl.pallas_call(functools.partial(second_body, width=width, block=block),...  10.2 us
    pallas_call x1, Pallas kernels, conv_first_layer(): pl.pallas_call(functools.partial(first_body, width=width, block=block, ha...  9.56 us
    ppermute x2, waiting for transfers between devices, gather_rows(): other = lax.ppermute(held, axis, pairs)  8.07 us
    ppermute x2, starting transfers between devices, gather_rows(): parts[p] = lax.ppermute(held[:, p:p + 1], axis, list(pairs))  6.72 us
    unnamed x16, local copies, waits for them, and re-layouts  4.97 us
    dot_general x2, matrix products, shards(): jnp.einsum('iy,cyj->icj', row_part, widened, preferred_element_type=jnp.f...  3.85 us
    ppermute x1, waiting for transfers between devices, shards(): lax.ppermute(send, 'member', [(i, (i + shift) % members) for i in range(m...  3.37 us
    ppermute x1, starting transfers between devices, shards(): lax.ppermute(flat_feat[:, (rows_dev - halo) * cols:], 'space', forward)  2.37 us
  transfers between devices with their start and end apart: 7, of which 4 were waited for; matrix products, arithmetic and copies ran while one was open for 6% of the time, Pallas kernels for 0%

profile of v13, /device:TPU:0, one launch (start us, length us, event | category | flops | bytes accessed | tf_op | source)
XLA Modules:
  0.0 64.9 jit_solution(13030028303971520531)
XLA Ops:
  0.0 2.6 %copy.13 = bf16[32,8,16,256]{3,1,2,0:T(8,128)(2,1)S(1)} copy(bf16[32,8,16,256]{3,2,1,0:T(8,128)(2,1)} %bitcast.58) | data formatting | bytes 4194304
  2.6 0.0 copy-start
  2.6 2.4 %collective-permute-start = (bf16[256,512]{1,0:T(8,128)(2,1)S(1)}, bf16[256,512]{1,0:T(8,128)(2,1)S(1)}, u32[]{:S(2)}, u32[]{:S(2)}) collective-permute-start(bf16[256,512]{1,0:T(8,128)(2,1)S(1)} %get-tuple-element.17), channel_id=1, source_target_pairs={{0,2},{2,4},{4,6},{6,8},{8,10},{10,12},{12,14},{1,3},{3,5},{5,7},{... | collective-permute-start | bytes 786440 | tf_op jit(solution)/shard_map/ppermute | solution.py:261
  5.0 1.3 %collective-permute-start.1 = (bf16[256,512]{1,0:T(8,128)(2,1)S(1)}, bf16[256,512]{1,0:T(8,128)(2,1)S(1)}, u32[]{:S(2)}, u32[]{:S(2)}) collective-permute-start(bf16[256,512]{1,0:T(8,128)(2,1)S(1)} %get-tuple-element.16), channel_id=1, source_target_pairs={{2,0},{4,2},{6,4},{8,6},{10,8},{12,10},{14,12},{3,1},{5,3},{7,5},{... | collective-permute-start | bytes 786440 | tf_op jit(solution)/shard_map/ppermute | solution.py:262
  6.4 0.0 copy-done.3
  6.4 0.7 %fusion.63 = (s32[]{:T(128)}, s32[]{:T(128)}, s32[]{:T(128)}) fusion(s32[2]{0:T(128)S(1)} %copy-done.3, s32[]{:T(128)S(6)} %select_n.540, s32[]{:T(128)S(6)} %select_n.493, s32[]{:T(128)S(6)} %axis_index.29), kind=kLoop, calls=%fused_computation.107 | loop fusion | flops 15 | bytes 32 | tf_op jit(solution)/shard_map/reduce_sum | solution.py:297
  9.8 0.8 %reshape.291.b_ref = f32[531,1]{1,0:T(8,128)} reshape(f32[531]{0:T(1024)S(1)} %pad_maximum_fusion) | data formatting | bytes 4248 | tf_op jit(solution)/shard_map/reshape | solution.py:267
  10.6 0.7 %stack.76.s_ref = s32[7]{0:T(128)} concatenate(s32[1]{0:T(128)} %bitcast.1, s32[1]{0:T(128)} %bitcast.2, s32[1]{0:T(128)} %bitcast.3, s32[1]{0:T(128)} %bitcast.4, s32[1]{0:T(128)} %bitcast.5, s32[1]{0:T(128)} %bitcast.6, s32[1]{0:T(128)} %bitcast.7), dimensions={0} | concatenate | bytes 56 | tf_op jit(solution)/shard_map/stack | solution.py:264
  11.3 0.0 collective-permute-done.top_ref
  11.3 0.0 collective-permute-done.1.low_ref
  11.3 0.7 %copy-done.5 = bf16[256,512]{1,0:T(8,128)(2,1)} copy-done((bf16[256,512]{1,0:T(8,128)(2,1)}, bf16[256,512]{1,0:T(8,128)(2,1)S(1)}, u32[]{:S(2)}) %copy-start.5) | copy-done | bytes 262168
  12.0 0.7 %copy-done.6 = bf16[256,512]{1,0:T(8,128)(2,1)} copy-done((bf16[256,512]{1,0:T(8,128)(2,1)}, bf16[256,512]{1,0:T(8,128)(2,1)S(1)}, u32[]{:S(2)}) %copy-start.6) | copy-done | bytes 262168
  12.7 9.6 %shard_map.82.x_ref = bf16[256,4608]{1,0:T(8,128)(2,1)} custom-call(bf16[256,4096]{1,0:T(8,128)(2,1)} %bitcast.55, bf16[256,512]{1,0:T(8,128)(2,1)} %copy-done.5, bf16[256,512]{1,0:T(8,128)(2,1)} %copy-done.6, bf16[3,3,256,256]{3,2,1,0:T(8,128)(2,1)} %w_ref.2, f32[531,1]{1,0:T(8,128)} %reshape.291.b_ref, s32[7]{0:T(128)} %stack.76.s_ref), custom_call_target="tpu_custom_call" | custom-call | flops 5435817984 | bytes 6160384 | tf_op jit(solution)/shard_map/pallas_call | solution.py:187
  22.3 10.2 %shard_map.83 = bf16[19,4096]{1,0:T(8,128)(2,1)} custom-call(bf16[256,4608]{1,0:T(8,128)(2,1)} %shard_map.82.x_ref, bf16[3,3,256,256]{3,2,1,0:T(8,128)(2,1)} %w_ref.3, f32[531,1]{1,0:T(8,128)} %reshape.291.b_ref, bf16[19,256]{1,0:T(8,128)(2,1)} %k_ref.1, s32[7]{0:T(128)} %stack.76.s_ref), custom_call_target="tpu_custom_call" | custom-call | flops 4871684096 | bytes 3694592 | tf_op jit(solution)/shard_map/pallas_call | solution.py:217
  32.5 1.0 %copy.14 = bf16[3,8,16,256]{3,2,1,0:T(8,128)(2,1)S(1)} copy(bf16[3,8,16,256]{3,1,2,0:T(8,128)(2,1)} %bitcast.63) | data formatting | bytes 393216
  33.5 1.5 %collective-permute-start.2 = (bf16[19,1,16,256]{3,2,0,1:T(8,128)(2,1)S(1)}, bf16[19,1,16,256]{3,2,0,1:T(8,128)(2,1)S(1)}, u32[]{:S(2)}, u32[]{:S(2)}) collective-permute-start(bf16[19,1,16,256]{3,2,0,1:T(8,128)(2,1)S(1)} %get-tuple-element.22), channel_id=1, source_target_pairs={{2,10},{4,12},{6,14},{8,0},{3,11},{5,13},{7,15},{9,1},{18,26},{20,... | collective-permute-start | bytes 466952 | tf_op jit(solution)/shard_map/ppermute | solution.py:49
  37.7 6.2 %collective-permute-done.2 = bf16[19,1,16,256]{3,2,0,1:T(8,128)(2,1)S(1)} collective-permute-done((bf16[19,1,16,256]{3,2,0,1:T(8,128)(2,1)S(1)}, bf16[19,1,16,256]{3,2,0,1:T(8,128)(2,1)S(1)}, u32[]{:S(2)}, u32[]{:S(2)}) %collective-permute-start.2) | collective-permute-done | bytes 155680 | tf_op jit(solution)/shard_map/ppermute | solution.py:49
  44.0 4.8 %collective-permute-start.3 = (bf16[19,1,16,256]{3,2,0,1:T(8,128)(2,1)S(1)}, bf16[19,1,16,256]{3,2,0,1:T(8,128)(2,1)S(1)}, u32[]{:S(2)}, u32[]{:S(2)}) collective-permute-start(bf16[19,1,16,256]{3,2,0,1:T(8,128)(2,1)S(1)} %get-tuple-element.20), channel_id=1, source_target_pairs={{0,4},{2,6},{4,0},{10,14},{12,8},{14,10},{1,5},{3,7},{5,1},{11,15}... | collective-permute-start | bytes 466952 | tf_op jit(solution)/shard_map/ppermute | solution.py:55
  48.8 1.9 %collective-permute-start.4 = (bf16[19,1,16,256]{3,2,0,1:T(8,128)(2,1)S(1)}, bf16[19,1,16,256]{3,2,0,1:T(8,128)(2,1)S(1)}, u32[]{:S(2)}, u32[]{:S(2)}) collective-permute-start(bf16[19,1,16,256]{3,2,0,1:T(8,128)(2,1)S(1)} %get-tuple-element.21), channel_id=1, source_target_pairs={{0,4},{8,12},{10,14},{12,8},{1,5},{9,13},{11,15},{13,9},{16,20},{2... | collective-permute-start | bytes 466952 | tf_op jit(solution)/shard_map/ppermute | solution.py:55
  53.3 0.0 collective-permute-done.3
  53.3 0.2 collective-permute-done.4
  53.5 0.1 maximum_select_fusion.1
  53.5 0.1 copy.11
  53.6 0.1 collective-permute-start.5
  53.9 1.9 %collective-permute-done.5 = bf16[19,4,16,256]{3,2,1,0:T(8,128)(2,1)S(1)} collective-permute-done((bf16[19,4,16,256]{3,2,1,0:T(8,128)(2,1)S(1)}, bf16[19,4,16,256]{3,2,1,0:T(8,128)(2,1)S(1)}, u32[]{:S(2)}, u32[]{:S(2)}) %collective-permute-start.5) | collective-permute-done | bytes 622624 | tf_op jit(solution)/shard_map/ppermute | solution.py:49
  55.7 0.1 maximum_select_fusion
  55.9 0.1 dynamic-slice_bitcast_fusion
  56.0 0.1 fusion.28
  56.1 1.6 %collective-permute-start.6 = (bf16[19,10,256]{2,1,0:T(8,128)(2,1)S(1)}, bf16[19,10,256]{2,1,0:T(8,128)(2,1)S(1)}, u32[]{:S(2)}, u32[]{:S(2)}) collective-permute-start(bf16[19,10,256]{2,1,0:T(8,128)(2,1)S(1)} %fusion.28), channel_id=1, source_target_pairs={{0,1},{1,0},{2,3},{3,2},{4,5},{5,4},{6,7},{7,6},{8,9},{9,8},{10,11... | collective-permute-start | bytes 291848 | tf_op jit(solution)/shard_map/ppermute | solution.py:293
  57.7 1.2 %fusion = f32[32,19,1024]{2,0,1:T(8,128)S(1)} fusion(f32[1024]{0:T(1024)S(1)} %get-tuple-element.24, s32[1024]{0:T(1024)S(1)} %get-tuple-element.27, f32[1024]{0:T(1024)S(1)} %get-tuple-element.25, s32[1024]{0:T(1024)S(1)} %get-tuple-element.26, s32[]{:T(128)S(6)} %select_n.528, bf16[1,19,10,256]{3,2,1,0:T(8,128)(2,1)S(1)} %get-tuple-element.19, ...), kind=kOutput, calls=%fused_computation.3 | convolution fusion | flops 113884864 | bytes 2701832 | tf_op jit(solution)/shard_map/iy,cyj->icj/dot_general | solution.py:308
  58.9 3.4 %collective-permute-done.6 = bf16[19,10,256]{2,1,0:T(8,128)(2,1)S(1)} collective-permute-done((bf16[19,10,256]{2,1,0:T(8,128)(2,1)S(1)}, bf16[19,10,256]{2,1,0:T(8,128)(2,1)S(1)}, u32[]{:S(2)}, u32[]{:S(2)}) %collective-permute-start.6) | collective-permute-done | bytes 97312 | tf_op jit(solution)/shard_map/ppermute | solution.py:293
  62.2 2.7 %convolution_add_fusion = f32[32,19,1024]{2,0,1:T(8,128)} fusion(f32[32,19,1024]{2,0,1:T(8,128)S(1)} %fusion, bf16[19,10,256]{2,1,0:T(8,128)(2,1)S(1)} %collective-permute-done.6, f32[1024]{0:T(1024)S(1)} %get-tuple-element.28, s32[1024]{0:T(1024)S(1)} %get-tuple-element.31, f32[1024]{0:T(1024)S(1)} %get-tuple-element.29, s32[1024]{0:T(1024)S(1)} %get-tuple-element.30, ...), kind=kOutput, calls=%fused_computation | convolution fusion | flops 114458816 | bytes 5094916 | tf_op jit(solution)/shard_map/iy,cyj->icj/dot_general | solution.py:308
  (25 shorter events, 0.4 us)
Async XLA Ops:
  0.0 6.4 %copy-start.3 = (s32[2]{0:T(128)S(1)}, s32[2]{0:T(128)}, u32[]{:S(2)}) copy-start(s32[2]{0:T(128)} %param.9) | copy-start | bytes 28
  0.0 9.7 %copy-start.1 = (f32[256]{0:T(256)S(1)}, f32[256]{0:T(256)}, u32[]{:S(2)}) copy-start(f32[256]{0:T(256)} %param.13) | copy-start | bytes 3076
  0.0 9.7 %copy-start.2 = (f32[256]{0:T(256)S(1)}, f32[256]{0:T(256)}, u32[]{:S(2)}) copy-start(f32[256]{0:T(256)} %param.11) | copy-start | bytes 3076
  0.0 9.7 %copy-start.4 = (f32[19]{0:T(128)S(1)}, f32[19]{0:T(128)}, u32[]{:S(2)}) copy-start(f32[19]{0:T(128)} %param.15) | copy-start | bytes 232
  2.6 8.7 %copy-start = (bf16[32,8,16,256]{3,1,2,0:T(8,128)(2,1)}, bf16[32,8,16,256]{3,1,2,0:T(8,128)(2,1)S(1)}, u32[]{:S(2)}) copy-start(bf16[32,8,16,256]{3,1,2,0:T(8,128)(2,1)S(1)} %copy.13) | copy-start | bytes 6291460
  2.6 8.6 %collective-permute-start = (bf16[256,512]{1,0:T(8,128)(2,1)S(1)}, bf16[256,512]{1,0:T(8,128)(2,1)S(1)}, u32[]{:S(2)}, u32[]{:S(2)}) collective-permute-start(bf16[256,512]{1,0:T(8,128)(2,1)S(1)} %get-tuple-element.17), channel_id=1, source_target_pairs={{0,2},{2,4},{4,6},{6,8},{8,10},{10,12},{12,14},{1,3},{3,5},{5,7},{... | collective-permute-start | bytes 786440 | tf_op jit(solution)/shard_map/ppermute | solution.py:261
  5.0 6.3 %collective-permute-start.1 = (bf16[256,512]{1,0:T(8,128)(2,1)S(1)}, bf16[256,512]{1,0:T(8,128)(2,1)S(1)}, u32[]{:S(2)}, u32[]{:S(2)}) collective-permute-start(bf16[256,512]{1,0:T(8,128)(2,1)S(1)} %get-tuple-element.16), channel_id=1, source_target_pairs={{2,0},{4,2},{6,4},{8,6},{10,8},{12,10},{14,12},{3,1},{5,3},{7,5},{... | collective-permute-start | bytes 786440 | tf_op jit(solution)/shard_map/ppermute | solution.py:262
  11.3 0.7 %copy-start.5 = (bf16[256,512]{1,0:T(8,128)(2,1)}, bf16[256,512]{1,0:T(8,128)(2,1)S(1)}, u32[]{:S(2)}) copy-start(bf16[256,512]{1,0:T(8,128)(2,1)S(1)} %collective-permute-done.top_ref) | copy-start | bytes 786436
  12.0 0.7 %copy-start.6 = (bf16[256,512]{1,0:T(8,128)(2,1)}, bf16[256,512]{1,0:T(8,128)(2,1)S(1)}, u32[]{:S(2)}) copy-start(bf16[256,512]{1,0:T(8,128)(2,1)S(1)} %collective-permute-done.1.low_ref) | copy-start | bytes 786436
  33.5 10.4 %collective-permute-start.2 = (bf16[19,1,16,256]{3,2,0,1:T(8,128)(2,1)S(1)}, bf16[19,1,16,256]{3,2,0,1:T(8,128)(2,1)S(1)}, u32[]{:S(2)}, u32[]{:S(2)}) collective-permute-start(bf16[19,1,16,256]{3,2,0,1:T(8,128)(2,1)S(1)} %get-tuple-element.22), channel_id=1, source_target_pairs={{2,10},{4,12},{6,14},{8,0},{3,11},{5,13},{7,15},{9,1},{18,26},{20,... | collective-permute-start | bytes 466952 | tf_op jit(solution)/shard_map/ppermute | solution.py:49
  44.0 9.3 %collective-permute-start.3 = (bf16[19,1,16,256]{3,2,0,1:T(8,128)(2,1)S(1)}, bf16[19,1,16,256]{3,2,0,1:T(8,128)(2,1)S(1)}, u32[]{:S(2)}, u32[]{:S(2)}) collective-permute-start(bf16[19,1,16,256]{3,2,0,1:T(8,128)(2,1)S(1)} %get-tuple-element.20), channel_id=1, source_target_pairs={{0,4},{2,6},{4,0},{10,14},{12,8},{14,10},{1,5},{3,7},{5,1},{11,15}... | collective-permute-start | bytes 466952 | tf_op jit(solution)/shard_map/ppermute | solution.py:55
  48.8 4.7 %collective-permute-start.4 = (bf16[19,1,16,256]{3,2,0,1:T(8,128)(2,1)S(1)}, bf16[19,1,16,256]{3,2,0,1:T(8,128)(2,1)S(1)}, u32[]{:S(2)}, u32[]{:S(2)}) collective-permute-start(bf16[19,1,16,256]{3,2,0,1:T(8,128)(2,1)S(1)} %get-tuple-element.21), channel_id=1, source_target_pairs={{0,4},{8,12},{10,14},{12,8},{1,5},{9,13},{11,15},{13,9},{16,20},{2... | collective-permute-start | bytes 466952 | tf_op jit(solution)/shard_map/ppermute | solution.py:55
  53.6 2.1 %collective-permute-start.5 = (bf16[19,4,16,256]{3,2,1,0:T(8,128)(2,1)S(1)}, bf16[19,4,16,256]{3,2,1,0:T(8,128)(2,1)S(1)}, u32[]{:S(2)}, u32[]{:S(2)}) collective-permute-start(bf16[19,4,16,256]{3,2,1,0:T(8,128)(2,1)S(1)} %bitcast.56), channel_id=1, source_target_pairs={{0,2},{2,0},{4,6},{6,4},{8,10},{10,8},{12,14},{14,12},{1,3},{3,1},... | collective-permute-start | bytes 1867784 | tf_op jit(solution)/shard_map/ppermute | solution.py:49
  56.1 6.1 %collective-permute-start.6 = (bf16[19,10,256]{2,1,0:T(8,128)(2,1)S(1)}, bf16[19,10,256]{2,1,0:T(8,128)(2,1)S(1)}, u32[]{:S(2)}, u32[]{:S(2)}) collective-permute-start(bf16[19,10,256]{2,1,0:T(8,128)(2,1)S(1)} %fusion.28), channel_id=1, source_target_pairs={{0,1},{1,0},{2,3},{3,2},{4,5},{5,4},{6,7},{7,6},{8,9},{9,8},{10,11... | collective-permute-start | bytes 291848 | tf_op jit(solution)/shard_map/ppermute | solution.py:293

commit v14 on v11

--- a/solution.py
+++ b/solution.py
@@ -102,7 +102,7 @@
     return (first + second).astype(jnp.bfloat16)
 
 
-def run_conv(x_ref, w_ref, bias, lo, hi, good_cols, o_ref, width, block, head=None):
+def run_conv(x_ref, w_ref, bias, lo, hi, good_cols, o_ref, width, block, head=None, skip=0):
     flat = block * width
     outs = w_ref.shape[2]
     place = lax.broadcasted_iota(jnp.int32, (1, flat), 1)
@@ -114,7 +114,7 @@
     def step(i, carry):
         r0 = i * block
         rhs = jnp.concatenate(
-            [x_ref[:, pl.ds(pl.multiple_of((r0 + a) * width, width), flat)] for a in range(3)],
+            [x_ref[:, pl.ds(pl.multiple_of((skip + r0 + a) * width, width), flat)] for a in range(3)],
             axis=0,
         )
         res = jnp.dot(stacked, rhs, preferred_element_type=jnp.float32)
@@ -122,7 +122,7 @@
         left = jnp.where(col == 0, 0.0, pltpu.roll(taps[0], 1, 1))
         right = jnp.where(col == width - 1, 0.0, pltpu.roll(taps[2], flat - 1, 1))
         total = jnp.maximum(taps[1] + left + right + bias, 0.0)
-        row = r0 + place // width
+        row = skip + r0 + place // width
         keep = (row >= lo) & (row < hi) & (col < good_cols)
         out = jnp.where(keep, total, 0.0).astype(jnp.bfloat16)
         if head is not None:
@@ -158,12 +158,12 @@
     run_conv(x_ref, w_ref, b_ref[pl.ds(0, chans), :], lo, hi, good_cols, o_ref, width, block)
 
 
-def second_body(x_ref, w_ref, b_ref, k_ref, s_ref, o_ref, *, width, block):
+def second_body(x_ref, w_ref, b_ref, k_ref, s_ref, o_ref, *, width, block, skip):
     chans = x_ref.shape[0]
     classes = k_ref.shape[0]
     head = (k_ref[...], b_ref[pl.ds(2 * chans, classes), :])
     lo, hi, good_cols = s_ref[5], s_ref[6], s_ref[2]
-    run_conv(x_ref, w_ref, b_ref[pl.ds(chans, chans), :], lo, hi, good_cols, o_ref, width, block, head)
+    run_conv(x_ref, w_ref, b_ref[pl.ds(chans, chans), :], lo, hi, good_cols, o_ref, width, block, head, skip)
 
 
 def pick_block(rows):
@@ -202,9 +202,8 @@
     return out
 
 
-def conv_second_layer(x, width, weights, biases, head, limits):
+def conv_second_layer(x, width, weights, biases, head, limits, skip, rows_out):
     chans, flat_in = x.shape
-    rows_out = flat_in // width - 2
     outs = weights.shape[2]
     classes = head.shape[0]
     block = pick_block(rows_out)
@@ -215,7 +214,7 @@
         transcendentals=0,
     )
     out = pl.pallas_call(
-        functools.partial(second_body, width=width, block=block),
+        functools.partial(second_body, width=width, block=block, skip=skip),
         out_shape=jax.ShapeDtypeStruct((classes, rows_out * width), jnp.bfloat16),
         in_specs=[vmem] * 4 + [pl.BlockSpec(memory_space=pltpu.SMEM)],
         out_specs=vmem,
@@ -266,14 +265,20 @@
     ).astype(jnp.int32)
     biases = jnp.concatenate([bias_first, bias_second, class_bias]).reshape(-1, 1)
     hidden = conv_first_layer(flat_feat, top_rows, low_rows, cols, conv_first, biases, limits)
-    logits = conv_second_layer(hidden, cols, conv_second, biases, classify, limits)
+    half = rows_dev // 2 if rows_dev % 4 == 0 else rows_dev
+    logit_parts = [
+        conv_second_layer(hidden, cols, conv_second, biases, classify, limits, skip, half)
+        for skip in range(0, rows_dev, half)
+    ]
     out_rows = UP * full_rows
     out_cols = UP * cols
     own_rows = out_rows // spaces
     part_rows = own_rows // members
     window_rows = (part_rows - 1) // UP + 3
     need = block_needs(spaces, members, rows_dev, LOW_CODE, HIGH_CODE)
-    gathered = gather_rows(logits, "space", need)
+    gathered = jnp.stack(
+        [gather_rows(x, "space", need).reshape(x.shape[0], spaces, half, cols) for x in logit_parts], 2
+    ).reshape(classify.shape[0], full_rows, cols)
     pieces = []
     for target in range(members):
         first_row = place * own_rows + target * part_rows
@@ -282,7 +287,7 @@
     outgoing = jnp.stack(pieces, 0)
     own_first = place * own_rows + member_index * part_rows
     positions = own_first + jnp.arange(part_rows, dtype=jnp.int32)
-    result = jnp.zeros((part_rows, logits.shape[0], out_cols), jnp.float32)
+    result = jnp.zeros((part_rows, classify.shape[0], out_cols), jnp.float32)
     for shift in range(members):
         if shift == 0:
             arrived = lax.dynamic_index_in_dim(outgoing, member_index, 0, keepdims=False)

time: 64.3 us -> 77.1 us (1.20)
  starting transfers between devices: 13.5 us -> 19.8 us
  waiting for transfers between devices: 11.6 us -> 14.8 us
  Pallas kernels: 18.8 us -> 21.5 us
    ppermute x2 -> x4, starting transfers between devices: 6.9 us -> 11.9 us  [gather_rows(): parts[p] = lax.ppermute(held[:, p:p + 1], axis, list(pairs))]
    pallas_call x1 -> x2, Pallas kernels: 9.02 us -> 11.8 us  [conv_second_layer(): pl.pallas_call(functools.partial(second_body, width=width, block=block, s...]
    ppermute x2 -> x4, waiting for transfers between devices: 0.01 us -> 1.79 us  [gather_rows(): parts[p] = lax.ppermute(held[:, p:p + 1], axis, list(pairs))]
    ppermute x2 -> x4, waiting for transfers between devices: 8.25 us -> 9.64 us  [gather_rows(): other = lax.ppermute(held, axis, pairs)]
    ppermute x2 -> x4, starting transfers between devices: 1.36 us -> 2.73 us  [gather_rows(): other = lax.ppermute(held, axis, pairs)]
    unnamed x16 -> x19, local copies, waits for them, and re-layouts: 4.97 us -> 4.93 us
  transfers between devices with their start and end apart: 7 -> 11, of which waited for: 3 -> 6; matrix products, arithmetic and copies ran while one was open for 6% -> 6% of each run, Pallas kernels for 0% -> 0%
where the time goes in v14:
time: 77.1 us; the launch traced here: 76.6 us
  Pallas kernels  21.5 us (28%)
  starting transfers between devices  19.8 us (26%)
  waiting for transfers between devices  14.8 us (19%)
  between operations  8.31 us (11%)
  local copies, waits for them, and re-layouts  6.88 us (9%)
  matrix products  3.85 us (5%)
  other arithmetic  1.46 us (2%)
    ppermute x4, starting transfers between devices, gather_rows(): parts[p] = lax.ppermute(held[:, p:p + 1], axis, list(pairs))  11.9 us
    pallas_call x2, Pallas kernels, conv_second_layer(): pl.pallas_call(functools.partial(second_body, width=width, block=block, s...  11.8 us
    pallas_call x1, Pallas kernels, conv_first_layer(): pl.pallas_call(functools.partial(first_body, width=width, block=block, ha...  9.74 us
    ppermute x4, waiting for transfers between devices, gather_rows(): other = lax.ppermute(held, axis, pairs)  9.64 us
    unnamed x19, local copies, waits for them, and re-layouts  4.93 us
    dot_general x2, matrix products, shards(): jnp.einsum('iy,cyj->icj', row_part, widened, preferred_element_type=jnp.f...  3.85 us
    ppermute x1, waiting for transfers between devices, shards(): lax.ppermute(send, 'member', [(i, (i + shift) % members) for i in range(m...  3.38 us
    ppermute x4, starting transfers between devices, gather_rows(): other = lax.ppermute(held, axis, pairs)  2.73 us
  transfers between devices with their start and end apart: 11, of which 6 were waited for; matrix products, arithmetic and copies ran while one was open for 6% of the time, Pallas kernels for 0%

profile of v14, /device:TPU:0, one launch (start us, length us, event | category | flops | bytes accessed | tf_op | source)
XLA Modules:
  0.0 76.6 jit_solution(11873700097260174756)
XLA Ops:
  0.0 2.6 %copy.42 = bf16[32,8,16,256]{3,1,2,0:T(8,128)(2,1)S(1)} copy(bf16[32,8,16,256]{3,2,1,0:T(8,128)(2,1)} %bitcast.84) | data formatting | bytes 4194304
  2.6 2.4 %collective-permute-start = (bf16[256,512]{1,0:T(8,128)(2,1)S(1)}, bf16[256,512]{1,0:T(8,128)(2,1)S(1)}, u32[]{:S(2)}, u32[]{:S(2)}) collective-permute-start(bf16[256,512]{1,0:T(8,128)(2,1)S(1)} %get-tuple-element.17), channel_id=1, source_target_pairs={{0,2},{2,4},{4,6},{6,8},{8,10},{10,12},{12,14},{1,3},{3,5},{5,7},{... | collective-permute-start | bytes 786440 | tf_op jit(solution)/shard_map/ppermute | solution.py:260
  5.0 1.3 %collective-permute-start.1 = (bf16[256,512]{1,0:T(8,128)(2,1)S(1)}, bf16[256,512]{1,0:T(8,128)(2,1)S(1)}, u32[]{:S(2)}, u32[]{:S(2)}) collective-permute-start(bf16[256,512]{1,0:T(8,128)(2,1)S(1)} %get-tuple-element.16), channel_id=1, source_target_pairs={{2,0},{4,2},{6,4},{8,6},{10,8},{12,10},{14,12},{3,1},{5,3},{7,5},{... | collective-permute-start | bytes 786440 | tf_op jit(solution)/shard_map/ppermute | solution.py:261
  6.4 0.7 fusion.63
  15.1 0.8 %reshape.434.b_ref = f32[531,1]{1,0:T(8,128)} reshape(f32[531]{0:T(1024)S(1)} %pad_maximum_fusion.2) | data formatting | bytes 4248 | tf_op jit(solution)/shard_map/reshape | solution.py:266
  16.0 0.7 stack.115.s_ref
  16.7 0.7 copy-done.6
  17.4 0.7 copy-done.7
  18.1 9.7 %shard_map.82.x_ref = bf16[256,4608]{1,0:T(8,128)(2,1)} custom-call(bf16[256,4096]{1,0:T(8,128)(2,1)} %bitcast.81, bf16[256,512]{1,0:T(8,128)(2,1)} %copy-done.6, bf16[256,512]{1,0:T(8,128)(2,1)} %copy-done.7, bf16[3,3,256,256]{3,2,1,0:T(8,128)(2,1)} %w_ref.3, f32[531,1]{1,0:T(8,128)} %reshape.434.b_ref, s32[7]{0:T(128)} %stack.115.s_ref), custom_call_target="tpu_custom_call" | custom-call | flops 5435817984 | bytes 6160384 | tf_op jit(solution)/shard_map/pallas_call | solution.py:187
  27.8 5.9 %shard_map.83 = bf16[19,2048]{1,0:T(8,128)(2,1)} custom-call(bf16[256,4608]{1,0:T(8,128)(2,1)} %shard_map.82.x_ref, bf16[3,3,256,256]{3,2,1,0:T(8,128)(2,1)} %w_ref.5, f32[531,1]{1,0:T(8,128)} %reshape.434.b_ref, bf16[19,256]{1,0:T(8,128)(2,1)} %k_ref.3, s32[7]{0:T(128)} %stack.115.s_ref), custom_call_target="tpu_custom_call" | custom-call | flops 2435842048 | bytes 3616768 | tf_op jit(solution)/shard_map/pallas_call | solution.py:216
  33.7 5.9 %shard_map.84 = bf16[19,2048]{1,0:T(8,128)(2,1)} custom-call(bf16[256,4608]{1,0:T(8,128)(2,1)} %shard_map.82.x_ref, bf16[3,3,256,256]{3,2,1,0:T(8,128)(2,1)} %w_ref.5, f32[531,1]{1,0:T(8,128)} %reshape.434.b_ref, bf16[19,256]{1,0:T(8,128)(2,1)} %k_ref.3, s32[7]{0:T(128)} %stack.115.s_ref), custom_call_target="tpu_custom_call" | custom-call | flops 2435842048 | bytes 3616768 | tf_op jit(solution)/shard_map/pallas_call | solution.py:216
  39.7 1.3 %collective-permute-start.2 = (bf16[19,1,8,256]{3,2,0,1:T(8,128)(2,1)S(1)}, bf16[19,1,8,256]{3,2,0,1:T(8,128)(2,1)S(1)}, u32[]{:S(2)}, u32[]{:S(2)}) collective-permute-start(bf16[19,1,8,256]{3,2,0,1:T(8,128)(2,1)S(1)} %get-tuple-element.24), channel_id=1, source_target_pairs={{2,10},{4,12},{6,14},{8,0},{3,11},{5,13},{7,15},{9,1},{18,26},{20,... | collective-permute-start | bytes 233480 | tf_op jit(solution)/shard_map/ppermute | solution.py:49
  41.0 0.9 %copy.45 = bf16[3,8,8,256]{3,2,1,0:T(8,128)(2,1)S(1)} copy(bf16[3,8,8,256]{3,1,2,0:T(8,128)(2,1)} %bitcast.96) | data formatting | bytes 196608
  41.9 1.3 %collective-permute-start.6 = (bf16[19,1,8,256]{3,2,0,1:T(8,128)(2,1)S(1)}, bf16[19,1,8,256]{3,2,0,1:T(8,128)(2,1)S(1)}, u32[]{:S(2)}, u32[]{:S(2)}) collective-permute-start(bf16[19,1,8,256]{3,2,0,1:T(8,128)(2,1)S(1)} %get-tuple-element.26), channel_id=1, source_target_pairs={{2,10},{4,12},{6,14},{8,0},{3,11},{5,13},{7,15},{9,1},{18,26},{20,... | collective-permute-start | bytes 233480 | tf_op jit(solution)/shard_map/ppermute | solution.py:49
  43.2 6.0 %collective-permute-done.2 = bf16[19,1,8,256]{3,2,0,1:T(8,128)(2,1)S(1)} collective-permute-done((bf16[19,1,8,256]{3,2,0,1:T(8,128)(2,1)S(1)}, bf16[19,1,8,256]{3,2,0,1:T(8,128)(2,1)S(1)}, u32[]{:S(2)}, u32[]{:S(2)}) %collective-permute-start.2) | collective-permute-done | bytes 77856 | tf_op jit(solution)/shard_map/ppermute | solution.py:49
  49.2 2.2 %collective-permute-done.6 = bf16[19,1,8,256]{3,2,0,1:T(8,128)(2,1)S(1)} collective-permute-done((bf16[19,1,8,256]{3,2,0,1:T(8,128)(2,1)S(1)}, bf16[19,1,8,256]{3,2,0,1:T(8,128)(2,1)S(1)}, u32[]{:S(2)}, u32[]{:S(2)}) %collective-permute-start.6) | collective-permute-done | bytes 77856 | tf_op jit(solution)/shard_map/ppermute | solution.py:49
  51.5 3.9 %collective-permute-start.3 = (bf16[19,1,8,256]{3,2,0,1:T(8,128)(2,1)S(1)}, bf16[19,1,8,256]{3,2,0,1:T(8,128)(2,1)S(1)}, u32[]{:S(2)}, u32[]{:S(2)}) collective-permute-start(bf16[19,1,8,256]{3,2,0,1:T(8,128)(2,1)S(1)} %get-tuple-element.20), channel_id=1, source_target_pairs={{0,4},{2,6},{4,0},{10,14},{12,8},{14,10},{1,5},{3,7},{5,1},{11,15}... | collective-permute-start | bytes 233480 | tf_op jit(solution)/shard_map/ppermute | solution.py:55
  55.5 2.1 %collective-permute-start.4 = (bf16[19,1,8,256]{3,2,0,1:T(8,128)(2,1)S(1)}, bf16[19,1,8,256]{3,2,0,1:T(8,128)(2,1)S(1)}, u32[]{:S(2)}, u32[]{:S(2)}) collective-permute-start(bf16[19,1,8,256]{3,2,0,1:T(8,128)(2,1)S(1)} %get-tuple-element.21), channel_id=1, source_target_pairs={{0,4},{8,12},{10,14},{12,8},{1,5},{9,13},{11,15},{13,9},{16,20},{2... | collective-permute-start | bytes 233480 | tf_op jit(solution)/shard_map/ppermute | solution.py:55
  57.6 1.9 %collective-permute-start.7 = (bf16[19,1,8,256]{3,2,0,1:T(8,128)(2,1)S(1)}, bf16[19,1,8,256]{3,2,0,1:T(8,128)(2,1)S(1)}, u32[]{:S(2)}, u32[]{:S(2)}) collective-permute-start(bf16[19,1,8,256]{3,2,0,1:T(8,128)(2,1)S(1)} %get-tuple-element.22), channel_id=1, source_target_pairs={{0,4},{2,6},{4,0},{10,14},{12,8},{14,10},{1,5},{3,7},{5,1},{11,15}... | collective-permute-start | bytes 233480 | tf_op jit(solution)/shard_map/ppermute | solution.py:55
  59.5 3.9 %collective-permute-start.8 = (bf16[19,1,8,256]{3,2,0,1:T(8,128)(2,1)S(1)}, bf16[19,1,8,256]{3,2,0,1:T(8,128)(2,1)S(1)}, u32[]{:S(2)}, u32[]{:S(2)}) collective-permute-start(bf16[19,1,8,256]{3,2,0,1:T(8,128)(2,1)S(1)} %get-tuple-element.23), channel_id=1, source_target_pairs={{0,4},{8,12},{10,14},{12,8},{1,5},{9,13},{11,15},{13,9},{16,20},{2... | collective-permute-start | bytes 233480 | tf_op jit(solution)/shard_map/ppermute | solution.py:55
  63.7 0.2 collective-permute-done.7
  63.9 1.6 %collective-permute-done.8 = bf16[19,1,8,256]{3,2,0,1:T(8,128)(2,1)S(1)} collective-permute-done((bf16[19,1,8,256]{3,2,0,1:T(8,128)(2,1)S(1)}, bf16[19,1,8,256]{3,2,0,1:T(8,128)(2,1)S(1)}, u32[]{:S(2)}, u32[]{:S(2)}) %collective-permute-start.8) | collective-permute-done | bytes 77856 | tf_op jit(solution)/shard_map/ppermute | solution.py:55
  65.7 0.1 maximum_select_fusion
  65.8 1.4 %collective-permute-done.9 = bf16[19,4,8,256]{3,2,1,0:T(8,128)(2,1)S(1)} collective-permute-done((bf16[19,4,8,256]{3,2,1,0:T(8,128)(2,1)S(1)}, bf16[19,4,8,256]{3,2,1,0:T(8,128)(2,1)S(1)}, u32[]{:S(2)}, u32[]{:S(2)}) %collective-permute-start.9) | collective-permute-done | bytes 311328 | tf_op jit(solution)/shard_map/ppermute | solution.py:49
  67.2 0.1 maximum_select_fusion.1
  67.4 0.1 pad_maximum_fusion
  67.5 0.1 copy.41
  67.6 0.1 dynamic-slice_bitcast_fusion
  67.8 1.6 %collective-permute-start.10 = (bf16[19,10,256]{2,1,0:T(8,128)(2,1)S(1)}, bf16[19,10,256]{2,1,0:T(8,128)(2,1)S(1)}, u32[]{:S(2)}, u32[]{:S(2)}) collective-permute-start(bf16[19,10,256]{2,1,0:T(8,128)(2,1)S(1)} %fusion.28), channel_id=1, source_target_pairs={{0,1},{1,0},{2,3},{3,2},{4,5},{5,4},{6,7},{7,6},{8,9},{9,8},{10,11... | collective-permute-start | bytes 291848 | tf_op jit(solution)/shard_map/ppermute | solution.py:298
  69.4 1.2 %fusion = f32[32,19,1024]{2,0,1:T(8,128)S(1)} fusion(f32[1024]{0:T(1024)S(1)} %get-tuple-element.30, s32[1024]{0:T(1024)S(1)} %get-tuple-element.33, f32[1024]{0:T(1024)S(1)} %get-tuple-element.31, s32[1024]{0:T(1024)S(1)} %get-tuple-element.32, s32[]{:T(128)S(6)} %select_n.589, bf16[1,19,10,256]{3,2,1,0:T(8,128)(2,1)S(1)} %get-tuple-element.19, ...), kind=kOutput, calls=%fused_computation.3 | convolution fusion | flops 113884864 | bytes 2701832 | tf_op jit(solution)/shard_map/iy,cyj->icj/dot_general | solution.py:313
  70.6 3.4 %collective-permute-done.10 = bf16[19,10,256]{2,1,0:T(8,128)(2,1)S(1)} collective-permute-done((bf16[19,10,256]{2,1,0:T(8,128)(2,1)S(1)}, bf16[19,10,256]{2,1,0:T(8,128)(2,1)S(1)}, u32[]{:S(2)}, u32[]{:S(2)}) %collective-permute-start.10) | collective-permute-done | bytes 97312 | tf_op jit(solution)/shard_map/ppermute | solution.py:298
  74.0 2.7 %convolution_add_fusion = f32[32,19,1024]{2,0,1:T(8,128)} fusion(f32[32,19,1024]{2,0,1:T(8,128)S(1)} %fusion, bf16[19,10,256]{2,1,0:T(8,128)(2,1)S(1)} %collective-permute-done.10, f32[1024]{0:T(1024)S(1)} %get-tuple-element.34, s32[1024]{0:T(1024)S(1)} %get-tuple-element.37, f32[1024]{0:T(1024)S(1)} %get-tuple-element.35, s32[1024]{0:T(1024)S(1)} %get-tuple-element.36, ...), kind=kOutput, calls=%fused_computation | convolution fusion | flops 114458816 | bytes 5094916 | tf_op jit(solution)/shard_map/iy,cyj->icj/dot_general | solution.py:313
  (47 shorter events, 0.8 us)
Async XLA Ops:
  0.0 6.4 %copy-start.4 = (s32[2]{0:T(128)S(1)}, s32[2]{0:T(128)}, u32[]{:S(2)}) copy-start(s32[2]{0:T(128)} %param.9) | copy-start | bytes 28
  0.0 9.7 %copy-start.2 = (f32[256]{0:T(256)S(1)}, f32[256]{0:T(256)}, u32[]{:S(2)}) copy-start(f32[256]{0:T(256)} %param.13) | copy-start | bytes 3076
  0.0 9.8 %copy-start.3 = (f32[256]{0:T(256)S(1)}, f32[256]{0:T(256)}, u32[]{:S(2)}) copy-start(f32[256]{0:T(256)} %param.11) | copy-start | bytes 3076
  0.0 9.8 %copy-start.5 = (f32[19]{0:T(128)S(1)}, f32[19]{0:T(128)}, u32[]{:S(2)}) copy-start(f32[19]{0:T(128)} %param.15) | copy-start | bytes 232
  2.6 14.1 %copy-start = (bf16[32,8,16,256]{3,1,2,0:T(8,128)(2,1)}, bf16[32,8,16,256]{3,1,2,0:T(8,128)(2,1)S(1)}, u32[]{:S(2)}) copy-start(bf16[32,8,16,256]{3,1,2,0:T(8,128)(2,1)S(1)} %copy.42) | copy-start | bytes 6291460
  2.6 14.0 %collective-permute-start = (bf16[256,512]{1,0:T(8,128)(2,1)S(1)}, bf16[256,512]{1,0:T(8,128)(2,1)S(1)}, u32[]{:S(2)}, u32[]{:S(2)}) collective-permute-start(bf16[256,512]{1,0:T(8,128)(2,1)S(1)} %get-tuple-element.17), channel_id=1, source_target_pairs={{0,2},{2,4},{4,6},{6,8},{8,10},{10,12},{12,14},{1,3},{3,5},{5,7},{... | collective-permute-start | bytes 786440 | tf_op jit(solution)/shard_map/ppermute | solution.py:260
  5.0 11.7 %collective-permute-start.1 = (bf16[256,512]{1,0:T(8,128)(2,1)S(1)}, bf16[256,512]{1,0:T(8,128)(2,1)S(1)}, u32[]{:S(2)}, u32[]{:S(2)}) collective-permute-start(bf16[256,512]{1,0:T(8,128)(2,1)S(1)} %get-tuple-element.16), channel_id=1, source_target_pairs={{2,0},{4,2},{6,4},{8,6},{10,8},{12,10},{14,12},{3,1},{5,3},{7,5},{... | collective-permute-start | bytes 786440 | tf_op jit(solution)/shard_map/ppermute | solution.py:261
  16.7 0.7 copy-start.6
  17.4 0.7 copy-start.7
  33.7 5.9 %copy-start.1 = (bf16[19,2048]{1,0:T(8,128)(2,1)S(1)}, bf16[19,2048]{1,0:T(8,128)(2,1)}, u32[]{:S(2)}) copy-start(bf16[19,2048]{1,0:T(8,128)(2,1)} %shard_map.83) | copy-start | bytes 233476
  39.7 9.6 %collective-permute-start.2 = (bf16[19,1,8,256]{3,2,0,1:T(8,128)(2,1)S(1)}, bf16[19,1,8,256]{3,2,0,1:T(8,128)(2,1)S(1)}, u32[]{:S(2)}, u32[]{:S(2)}) collective-permute-start(bf16[19,1,8,256]{3,2,0,1:T(8,128)(2,1)S(1)} %get-tuple-element.24), channel_id=1, source_target_pairs={{2,10},{4,12},{6,14},{8,0},{3,11},{5,13},{7,15},{9,1},{18,26},{20,... | collective-permute-start | bytes 233480 | tf_op jit(solution)/shard_map/ppermute | solution.py:49
  41.9 9.6 %collective-permute-start.6 = (bf16[19,1,8,256]{3,2,0,1:T(8,128)(2,1)S(1)}, bf16[19,1,8,256]{3,2,0,1:T(8,128)(2,1)S(1)}, u32[]{:S(2)}, u32[]{:S(2)}) collective-permute-start(bf16[19,1,8,256]{3,2,0,1:T(8,128)(2,1)S(1)} %get-tuple-element.26), channel_id=1, source_target_pairs={{2,10},{4,12},{6,14},{8,0},{3,11},{5,13},{7,15},{9,1},{18,26},{20,... | collective-permute-start | bytes 233480 | tf_op jit(solution)/shard_map/ppermute | solution.py:49
  51.5 12.0 %collective-permute-start.3 = (bf16[19,1,8,256]{3,2,0,1:T(8,128)(2,1)S(1)}, bf16[19,1,8,256]{3,2,0,1:T(8,128)(2,1)S(1)}, u32[]{:S(2)}, u32[]{:S(2)}) collective-permute-start(bf16[19,1,8,256]{3,2,0,1:T(8,128)(2,1)S(1)} %get-tuple-element.20), channel_id=1, source_target_pairs={{0,4},{2,6},{4,0},{10,14},{12,8},{14,10},{1,5},{3,7},{5,1},{11,15}... | collective-permute-start | bytes 233480 | tf_op jit(solution)/shard_map/ppermute | solution.py:55
  55.5 8.1 %collective-permute-start.4 = (bf16[19,1,8,256]{3,2,0,1:T(8,128)(2,1)S(1)}, bf16[19,1,8,256]{3,2,0,1:T(8,128)(2,1)S(1)}, u32[]{:S(2)}, u32[]{:S(2)}) collective-permute-start(bf16[19,1,8,256]{3,2,0,1:T(8,128)(2,1)S(1)} %get-tuple-element.21), channel_id=1, source_target_pairs={{0,4},{8,12},{10,14},{12,8},{1,5},{9,13},{11,15},{13,9},{16,20},{2... | collective-permute-start | bytes 233480 | tf_op jit(solution)/shard_map/ppermute | solution.py:55
  57.6 6.3 %collective-permute-start.7 = (bf16[19,1,8,256]{3,2,0,1:T(8,128)(2,1)S(1)}, bf16[19,1,8,256]{3,2,0,1:T(8,128)(2,1)S(1)}, u32[]{:S(2)}, u32[]{:S(2)}) collective-permute-start(bf16[19,1,8,256]{3,2,0,1:T(8,128)(2,1)S(1)} %get-tuple-element.22), channel_id=1, source_target_pairs={{0,4},{2,6},{4,0},{10,14},{12,8},{14,10},{1,5},{3,7},{5,1},{11,15}... | collective-permute-start | bytes 233480 | tf_op jit(solution)/shard_map/ppermute | solution.py:55
  59.5 5.9 %collective-permute-start.8 = (bf16[19,1,8,256]{3,2,0,1:T(8,128)(2,1)S(1)}, bf16[19,1,8,256]{3,2,0,1:T(8,128)(2,1)S(1)}, u32[]{:S(2)}, u32[]{:S(2)}) collective-permute-start(bf16[19,1,8,256]{3,2,0,1:T(8,128)(2,1)S(1)} %get-tuple-element.23), channel_id=1, source_target_pairs={{0,4},{8,12},{10,14},{12,8},{1,5},{9,13},{11,15},{13,9},{16,20},{2... | collective-permute-start | bytes 233480 | tf_op jit(solution)/shard_map/ppermute | solution.py:55
  63.6 2.1 %collective-permute-start.5 = (bf16[19,4,8,256]{3,2,1,0:T(8,128)(2,1)S(1)}, bf16[19,4,8,256]{3,2,1,0:T(8,128)(2,1)S(1)}, u32[]{:S(2)}, u32[]{:S(2)}) collective-permute-start(bf16[19,4,8,256]{3,2,1,0:T(8,128)(2,1)S(1)} %bitcast.88), channel_id=1, source_target_pairs={{0,2},{2,0},{4,6},{6,4},{8,10},{10,8},{12,14},{14,12},{1,3},{3,1},... | collective-permute-start | bytes 933896 | tf_op jit(solution)/shard_map/ppermute | solution.py:49
  65.5 1.7 %collective-permute-start.9 = (bf16[19,4,8,256]{3,2,1,0:T(8,128)(2,1)S(1)}, bf16[19,4,8,256]{3,2,1,0:T(8,128)(2,1)S(1)}, u32[]{:S(2)}, u32[]{:S(2)}) collective-permute-start(bf16[19,4,8,256]{3,2,1,0:T(8,128)(2,1)S(1)} %bitcast.86), channel_id=1, source_target_pairs={{0,2},{2,0},{4,6},{6,4},{8,10},{10,8},{12,14},{14,12},{1,3},{3,1},... | collective-permute-start | bytes 933896 | tf_op jit(solution)/shard_map/ppermute | solution.py:49
  67.8 6.1 %collective-permute-start.10 = (bf16[19,10,256]{2,1,0:T(8,128)(2,1)S(1)}, bf16[19,10,256]{2,1,0:T(8,128)(2,1)S(1)}, u32[]{:S(2)}, u32[]{:S(2)}) collective-permute-start(bf16[19,10,256]{2,1,0:T(8,128)(2,1)S(1)} %fusion.28), channel_id=1, source_target_pairs={{0,1},{1,0},{2,3},{3,2},{4,5},{5,4},{6,7},{7,6},{8,9},{9,8},{10,11... | collective-permute-start | bytes 291848 | tf_op jit(solution)/shard_map/ppermute | solution.py:298

commit v15 on v11

--- a/solution.py
+++ b/solution.py
@@ -133,7 +133,9 @@
     lax.fori_loop(0, o_ref.shape[1] // flat, step, 0, unroll=True)
 
 
-def first_body(main_ref, top_ref, low_ref, w_ref, b_ref, s_ref, o_ref, x_ref, *, width, block, halo):
+def first_body(
+    main_ref, top_ref, low_ref, w_ref, b_ref, s_ref, o_ref, x_ref, top_buf, low_buf, sems, *, width, block, halo
+):
     lo_in, hi_in, good_cols, lo, hi = s_ref[0], s_ref[1], s_ref[2], s_ref[3], s_ref[4]
     chans = main_ref.shape[0]
     rows_main = main_ref.shape[1] // width
@@ -146,8 +148,10 @@
             keep, src, jnp.zeros_like(src)
         )
 
-    put(top_ref[...], 0, halo)
-    put(low_ref[...], halo + rows_main, halo)
+    fetch_top = pltpu.make_async_copy(top_ref, top_buf, sems.at[0])
+    fetch_low = pltpu.make_async_copy(low_ref, low_buf, sems.at[1])
+    fetch_top.start()
+    fetch_low.start()
 
     def chunk(i, carry):
         start = pl.multiple_of(i * 2 * width, width)
@@ -155,6 +159,10 @@
         return carry
 
     lax.fori_loop(0, rows_main // 2, chunk, 0)
+    fetch_top.wait()
+    fetch_low.wait()
+    put(top_buf[...], 0, halo)
+    put(low_buf[...], halo + rows_main, halo)
     run_conv(x_ref, w_ref, b_ref[pl.ds(0, chans), :], lo, hi, good_cols, o_ref, width, block)
 
 
@@ -179,6 +187,7 @@
     outs = weights.shape[2]
     block = pick_block(rows_out)
     vmem = pl.BlockSpec(memory_space=pltpu.VMEM)
+    anywhere = pl.BlockSpec(memory_space=pl.ANY)
     cost = pl.CostEstimate(
         flops=2 * 9 * rows_out * width * chans * outs,
         bytes_accessed=2 * (chans * rows_in * width + weights.size + rows_out * width * outs),
@@ -187,9 +196,14 @@
     out = pl.pallas_call(
         functools.partial(first_body, width=width, block=block, halo=halo),
         out_shape=jax.ShapeDtypeStruct((outs, rows_out * width), jnp.bfloat16),
-        in_specs=[vmem] * 5 + [pl.BlockSpec(memory_space=pltpu.SMEM)],
+        in_specs=[vmem, anywhere, anywhere, vmem, vmem, pl.BlockSpec(memory_space=pltpu.SMEM)],
         out_specs=vmem,
-        scratch_shapes=[pltpu.VMEM((chans, rows_in * width), jnp.bfloat16)],
+        scratch_shapes=[
+            pltpu.VMEM((chans, rows_in * width), jnp.bfloat16),
+            pltpu.VMEM((chans, halo * width), jnp.bfloat16),
+            pltpu.VMEM((chans, halo * width), jnp.bfloat16),
+            pltpu.SemaphoreType.DMA((2,)),
+        ],
         cost_estimate=cost,
     )(
         feat,

time: 64.3 us -> 65.1 us (1.012)
  Pallas kernels: 18.8 us -> 19.5 us
    pallas_call x1, Pallas kernels: 9.74 us -> 10.5 us  [conv_first_layer(): pl.pallas_call(functools.partial(first_body, width=width, block=block, ha...]
where the time goes in v15:
time: 65.1 us; the launch traced here: 64.7 us
  Pallas kernels  19.5 us (30%)
  starting transfers between devices  13.5 us (21%)
  waiting for transfers between devices  11.6 us (18%)
  between operations  8.14 us (13%)
  local copies, waits for them, and re-layouts  6.78 us (10%)
  matrix products  3.87 us (6%)
  other arithmetic  1.25 us (2%)
    pallas_call x1, Pallas kernels, conv_first_layer(): pl.pallas_call(functools.partial(first_body, width=width, block=block, ha...  10.5 us
    pallas_call x1, Pallas kernels, conv_second_layer(): pl.pallas_call(functools.partial(second_body, width=width, block=block),...  9.03 us
    ppermute x2, waiting for transfers between devices, gather_rows(): other = lax.ppermute(held, axis, pairs)  8.25 us
    ppermute x2, starting transfers between devices, gather_rows(): parts[p] = lax.ppermute(held[:, p:p + 1], axis, list(pairs))  6.9 us
    unnamed x16, local copies, waits for them, and re-layouts  4.97 us
    dot_general x2, matrix products, shards(): jnp.einsum('iy,cyj->icj', row_part, widened, preferred_element_type=jnp.f...  3.87 us
    ppermute x1, waiting for transfers between devices, shards(): lax.ppermute(send, 'member', [(i, (i + shift) % members) for i in range(m...  3.37 us
    ppermute x1, starting transfers between devices, shards(): lax.ppermute(flat_feat[:, (rows_dev - halo) * cols:], 'space', forward)  2.37 us
  transfers between devices with their start and end apart: 7, of which 3 were waited for; matrix products, arithmetic and copies ran while one was open for 6% of the time, Pallas kernels for 0%

profile of v15, /device:TPU:0, one launch (start us, length us, event | category | flops | bytes accessed | tf_op | source)
XLA Modules:
  0.0 64.7 jit_solution(8547463659304763366)
XLA Ops:
  0.0 2.6 %copy.13 = bf16[32,8,16,256]{3,1,2,0:T(8,128)(2,1)S(1)} copy(bf16[32,8,16,256]{3,2,1,0:T(8,128)(2,1)} %bitcast.58) | data formatting | bytes 4194304
  2.6 2.4 %collective-permute-start = (bf16[256,512]{1,0:T(8,128)(2,1)S(1)}, bf16[256,512]{1,0:T(8,128)(2,1)S(1)}, u32[]{:S(2)}, u32[]{:S(2)}) collective-permute-start(bf16[256,512]{1,0:T(8,128)(2,1)S(1)} %get-tuple-element.17), channel_id=1, source_target_pairs={{0,2},{2,4},{4,6},{6,8},{8,10},{10,12},{12,14},{1,3},{3,5},{5,7},{... | collective-permute-start | bytes 786440 | tf_op jit(solution)/shard_map/ppermute | solution.py:275
  5.0 1.3 %collective-permute-start.1 = (bf16[256,512]{1,0:T(8,128)(2,1)S(1)}, bf16[256,512]{1,0:T(8,128)(2,1)S(1)}, u32[]{:S(2)}, u32[]{:S(2)}) collective-permute-start(bf16[256,512]{1,0:T(8,128)(2,1)S(1)} %get-tuple-element.16), channel_id=1, source_target_pairs={{2,0},{4,2},{6,4},{8,6},{10,8},{12,10},{14,12},{3,1},{5,3},{7,5},{... | collective-permute-start | bytes 786440 | tf_op jit(solution)/shard_map/ppermute | solution.py:276
  6.4 0.0 copy-done.3
  6.4 0.7 %fusion.63 = (s32[]{:T(128)}, s32[]{:T(128)}, s32[]{:T(128)}) fusion(s32[2]{0:T(128)S(1)} %copy-done.3, s32[]{:T(128)S(6)} %select_n.540, s32[]{:T(128)S(6)} %select_n.493, s32[]{:T(128)S(6)} %axis_index.29), kind=kLoop, calls=%fused_computation.107 | loop fusion | flops 15 | bytes 32 | tf_op jit(solution)/shard_map/reduce_sum | solution.py:311
  9.8 0.8 %reshape.291.b_ref = f32[531,1]{1,0:T(8,128)} reshape(f32[531]{0:T(1024)S(1)} %pad_maximum_fusion) | data formatting | bytes 4248 | tf_op jit(solution)/shard_map/reshape | solution.py:281
  10.6 0.7 %stack.76.s_ref = s32[7]{0:T(128)} concatenate(s32[1]{0:T(128)} %bitcast.1, s32[1]{0:T(128)} %bitcast.2, s32[1]{0:T(128)} %bitcast.3, s32[1]{0:T(128)} %bitcast.4, s32[1]{0:T(128)} %bitcast.5, s32[1]{0:T(128)} %bitcast.6, s32[1]{0:T(128)} %bitcast.7), dimensions={0} | concatenate | bytes 56 | tf_op jit(solution)/shard_map/stack | solution.py:278
  11.3 0.0 collective-permute-done.top_ref
  11.3 0.0 collective-permute-done.1.low_ref
  11.3 0.0 copy-done
  11.3 0.7 %copy-done.5 = bf16[256,512]{1,0:T(8,128)(2,1)} copy-done((bf16[256,512]{1,0:T(8,128)(2,1)}, bf16[256,512]{1,0:T(8,128)(2,1)S(1)}, u32[]{:S(2)}) %copy-start.5) | copy-done | bytes 262168
  12.0 0.7 %copy-done.6 = bf16[256,512]{1,0:T(8,128)(2,1)} copy-done((bf16[256,512]{1,0:T(8,128)(2,1)}, bf16[256,512]{1,0:T(8,128)(2,1)S(1)}, u32[]{:S(2)}) %copy-start.6) | copy-done | bytes 262168
  12.7 10.5 %shard_map.82.x_ref = bf16[256,4608]{1,0:T(8,128)(2,1)} custom-call(bf16[256,4096]{1,0:T(8,128)(2,1)} %bitcast.55, bf16[256,512]{1,0:T(8,128)(2,1)} %copy-done.5, bf16[256,512]{1,0:T(8,128)(2,1)} %copy-done.6, bf16[3,3,256,256]{3,2,1,0:T(8,128)(2,1)} %w_ref.2, f32[531,1]{1,0:T(8,128)} %reshape.291.b_ref, s32[7]{0:T(128)} %stack.76.s_ref), custom_call_target="tpu_custom_call" | custom-call | flops 5435817984 | bytes 6160384 | tf_op jit(solution)/shard_map/pallas_call | solution.py:196
  23.2 9.0 %shard_map.83 = bf16[19,4096]{1,0:T(8,128)(2,1)} custom-call(bf16[256,4608]{1,0:T(8,128)(2,1)} %shard_map.82.x_ref, bf16[3,3,256,256]{3,2,1,0:T(8,128)(2,1)} %w_ref.3, f32[531,1]{1,0:T(8,128)} %reshape.291.b_ref, bf16[19,256]{1,0:T(8,128)(2,1)} %k_ref.1, s32[7]{0:T(128)} %stack.76.s_ref), custom_call_target="tpu_custom_call" | custom-call | flops 4871684096 | bytes 3694592 | tf_op jit(solution)/shard_map/pallas_call | solution.py:231
  32.3 1.0 %copy.14 = bf16[3,8,16,256]{3,2,1,0:T(8,128)(2,1)S(1)} copy(bf16[3,8,16,256]{3,1,2,0:T(8,128)(2,1)} %bitcast.63) | data formatting | bytes 393216
  33.3 1.3 %collective-permute-start.2 = (bf16[19,1,16,256]{3,2,0,1:T(8,128)(2,1)S(1)}, bf16[19,1,16,256]{3,2,0,1:T(8,128)(2,1)S(1)}, u32[]{:S(2)}, u32[]{:S(2)}) collective-permute-start(bf16[19,1,16,256]{3,2,0,1:T(8,128)(2,1)S(1)} %get-tuple-element.22), channel_id=1, source_target_pairs={{2,10},{4,12},{6,14},{8,0},{3,11},{5,13},{7,15},{9,1},{18,26},{20,... | collective-permute-start | bytes 466952 | tf_op jit(solution)/shard_map/ppermute | solution.py:49
  37.3 6.4 %collective-permute-done.2 = bf16[19,1,16,256]{3,2,0,1:T(8,128)(2,1)S(1)} collective-permute-done((bf16[19,1,16,256]{3,2,0,1:T(8,128)(2,1)S(1)}, bf16[19,1,16,256]{3,2,0,1:T(8,128)(2,1)S(1)}, u32[]{:S(2)}, u32[]{:S(2)}) %collective-permute-start.2) | collective-permute-done | bytes 155680 | tf_op jit(solution)/shard_map/ppermute | solution.py:49
  43.7 4.8 %collective-permute-start.3 = (bf16[19,1,16,256]{3,2,0,1:T(8,128)(2,1)S(1)}, bf16[19,1,16,256]{3,2,0,1:T(8,128)(2,1)S(1)}, u32[]{:S(2)}, u32[]{:S(2)}) collective-permute-start(bf16[19,1,16,256]{3,2,0,1:T(8,128)(2,1)S(1)} %get-tuple-element.20), channel_id=1, source_target_pairs={{0,4},{2,6},{4,0},{10,14},{12,8},{14,10},{1,5},{3,7},{5,1},{11,15}... | collective-permute-start | bytes 466952 | tf_op jit(solution)/shard_map/ppermute | solution.py:55
  48.5 2.1 %collective-permute-start.4 = (bf16[19,1,16,256]{3,2,0,1:T(8,128)(2,1)S(1)}, bf16[19,1,16,256]{3,2,0,1:T(8,128)(2,1)S(1)}, u32[]{:S(2)}, u32[]{:S(2)}) collective-permute-start(bf16[19,1,16,256]{3,2,0,1:T(8,128)(2,1)S(1)} %get-tuple-element.21), channel_id=1, source_target_pairs={{0,4},{8,12},{10,14},{12,8},{1,5},{9,13},{11,15},{13,9},{16,20},{2... | collective-permute-start | bytes 466952 | tf_op jit(solution)/shard_map/ppermute | solution.py:55
  53.2 0.0 collective-permute-done.3
  53.2 0.0 collective-permute-done.4
  53.3 0.1 maximum_select_fusion.1
  53.3 0.1 copy.11
  53.4 0.1 collective-permute-start.5
  53.7 1.9 %collective-permute-done.5 = bf16[19,4,16,256]{3,2,1,0:T(8,128)(2,1)S(1)} collective-permute-done((bf16[19,4,16,256]{3,2,1,0:T(8,128)(2,1)S(1)}, bf16[19,4,16,256]{3,2,1,0:T(8,128)(2,1)S(1)}, u32[]{:S(2)}, u32[]{:S(2)}) %collective-permute-start.5) | collective-permute-done | bytes 622624 | tf_op jit(solution)/shard_map/ppermute | solution.py:49
  55.5 0.1 maximum_select_fusion
  55.7 0.1 dynamic-slice_bitcast_fusion
  55.8 0.1 fusion.28
  55.9 1.6 %collective-permute-start.6 = (bf16[19,10,256]{2,1,0:T(8,128)(2,1)S(1)}, bf16[19,10,256]{2,1,0:T(8,128)(2,1)S(1)}, u32[]{:S(2)}, u32[]{:S(2)}) collective-permute-start(bf16[19,10,256]{2,1,0:T(8,128)(2,1)S(1)} %fusion.28), channel_id=1, source_target_pairs={{0,1},{1,0},{2,3},{3,2},{4,5},{5,4},{6,7},{7,6},{8,9},{9,8},{10,11... | collective-permute-start | bytes 291848 | tf_op jit(solution)/shard_map/ppermute | solution.py:307
  57.5 1.2 %fusion = f32[32,19,1024]{2,0,1:T(8,128)S(1)} fusion(f32[1024]{0:T(1024)S(1)} %get-tuple-element.24, s32[1024]{0:T(1024)S(1)} %get-tuple-element.27, f32[1024]{0:T(1024)S(1)} %get-tuple-element.25, s32[1024]{0:T(1024)S(1)} %get-tuple-element.26, s32[]{:T(128)S(6)} %select_n.528, bf16[1,19,10,256]{3,2,1,0:T(8,128)(2,1)S(1)} %get-tuple-element.19, ...), kind=kOutput, calls=%fused_computation.3 | convolution fusion | flops 113884864 | bytes 2701832 | tf_op jit(solution)/shard_map/iy,cyj->icj/dot_general | solution.py:322
  58.7 3.4 %collective-permute-done.6 = bf16[19,10,256]{2,1,0:T(8,128)(2,1)S(1)} collective-permute-done((bf16[19,10,256]{2,1,0:T(8,128)(2,1)S(1)}, bf16[19,10,256]{2,1,0:T(8,128)(2,1)S(1)}, u32[]{:S(2)}, u32[]{:S(2)}) %collective-permute-start.6) | collective-permute-done | bytes 97312 | tf_op jit(solution)/shard_map/ppermute | solution.py:307
  62.0 2.7 %convolution_add_fusion = f32[32,19,1024]{2,0,1:T(8,128)} fusion(f32[32,19,1024]{2,0,1:T(8,128)S(1)} %fusion, bf16[19,10,256]{2,1,0:T(8,128)(2,1)S(1)} %collective-permute-done.6, f32[1024]{0:T(1024)S(1)} %get-tuple-element.28, s32[1024]{0:T(1024)S(1)} %get-tuple-element.31, f32[1024]{0:T(1024)S(1)} %get-tuple-element.29, s32[1024]{0:T(1024)S(1)} %get-tuple-element.30, ...), kind=kOutput, calls=%fused_computation | convolution fusion | flops 114458816 | bytes 5094916 | tf_op jit(solution)/shard_map/iy,cyj->icj/dot_general | solution.py:322
  (25 shorter events, 0.4 us)
Async XLA Ops:
  0.0 6.4 %copy-start.3 = (s32[2]{0:T(128)S(1)}, s32[2]{0:T(128)}, u32[]{:S(2)}) copy-start(s32[2]{0:T(128)} %param.9) | copy-start | bytes 28
  0.0 9.7 %copy-start.1 = (f32[256]{0:T(256)S(1)}, f32[256]{0:T(256)}, u32[]{:S(2)}) copy-start(f32[256]{0:T(256)} %param.13) | copy-start | bytes 3076
  0.0 9.7 %copy-start.2 = (f32[256]{0:T(256)S(1)}, f32[256]{0:T(256)}, u32[]{:S(2)}) copy-start(f32[256]{0:T(256)} %param.11) | copy-start | bytes 3076
  0.0 9.7 %copy-start.4 = (f32[19]{0:T(128)S(1)}, f32[19]{0:T(128)}, u32[]{:S(2)}) copy-start(f32[19]{0:T(128)} %param.15) | copy-start | bytes 232
  2.6 8.7 %copy-start = (bf16[32,8,16,256]{3,1,2,0:T(8,128)(2,1)}, bf16[32,8,16,256]{3,1,2,0:T(8,128)(2,1)S(1)}, u32[]{:S(2)}) copy-start(bf16[32,8,16,256]{3,1,2,0:T(8,128)(2,1)S(1)} %copy.13) | copy-start | bytes 6291460
  2.6 8.6 %collective-permute-start = (bf16[256,512]{1,0:T(8,128)(2,1)S(1)}, bf16[256,512]{1,0:T(8,128)(2,1)S(1)}, u32[]{:S(2)}, u32[]{:S(2)}) collective-permute-start(bf16[256,512]{1,0:T(8,128)(2,1)S(1)} %get-tuple-element.17), channel_id=1, source_target_pairs={{0,2},{2,4},{4,6},{6,8},{8,10},{10,12},{12,14},{1,3},{3,5},{5,7},{... | collective-permute-start | bytes 786440 | tf_op jit(solution)/shard_map/ppermute | solution.py:275
  5.0 6.3 %collective-permute-start.1 = (bf16[256,512]{1,0:T(8,128)(2,1)S(1)}, bf16[256,512]{1,0:T(8,128)(2,1)S(1)}, u32[]{:S(2)}, u32[]{:S(2)}) collective-permute-start(bf16[256,512]{1,0:T(8,128)(2,1)S(1)} %get-tuple-element.16), channel_id=1, source_target_pairs={{2,0},{4,2},{6,4},{8,6},{10,8},{12,10},{14,12},{3,1},{5,3},{7,5},{... | collective-permute-start | bytes 786440 | tf_op jit(solution)/shard_map/ppermute | solution.py:276
  11.3 0.7 %copy-start.5 = (bf16[256,512]{1,0:T(8,128)(2,1)}, bf16[256,512]{1,0:T(8,128)(2,1)S(1)}, u32[]{:S(2)}) copy-start(bf16[256,512]{1,0:T(8,128)(2,1)S(1)} %collective-permute-done.top_ref) | copy-start | bytes 786436
  12.0 0.7 %copy-start.6 = (bf16[256,512]{1,0:T(8,128)(2,1)}, bf16[256,512]{1,0:T(8,128)(2,1)S(1)}, u32[]{:S(2)}) copy-start(bf16[256,512]{1,0:T(8,128)(2,1)S(1)} %collective-permute-done.1.low_ref) | copy-start | bytes 786436
  33.3 10.4 %collective-permute-start.2 = (bf16[19,1,16,256]{3,2,0,1:T(8,128)(2,1)S(1)}, bf16[19,1,16,256]{3,2,0,1:T(8,128)(2,1)S(1)}, u32[]{:S(2)}, u32[]{:S(2)}) collective-permute-start(bf16[19,1,16,256]{3,2,0,1:T(8,128)(2,1)S(1)} %get-tuple-element.22), channel_id=1, source_target_pairs={{2,10},{4,12},{6,14},{8,0},{3,11},{5,13},{7,15},{9,1},{18,26},{20,... | collective-permute-start | bytes 466952 | tf_op jit(solution)/shard_map/ppermute | solution.py:49
  43.7 9.5 %collective-permute-start.3 = (bf16[19,1,16,256]{3,2,0,1:T(8,128)(2,1)S(1)}, bf16[19,1,16,256]{3,2,0,1:T(8,128)(2,1)S(1)}, u32[]{:S(2)}, u32[]{:S(2)}) collective-permute-start(bf16[19,1,16,256]{3,2,0,1:T(8,128)(2,1)S(1)} %get-tuple-element.20), channel_id=1, source_target_pairs={{0,4},{2,6},{4,0},{10,14},{12,8},{14,10},{1,5},{3,7},{5,1},{11,15}... | collective-permute-start | bytes 466952 | tf_op jit(solution)/shard_map/ppermute | solution.py:55
  48.5 4.7 %collective-permute-start.4 = (bf16[19,1,16,256]{3,2,0,1:T(8,128)(2,1)S(1)}, bf16[19,1,16,256]{3,2,0,1:T(8,128)(2,1)S(1)}, u32[]{:S(2)}, u32[]{:S(2)}) collective-permute-start(bf16[19,1,16,256]{3,2,0,1:T(8,128)(2,1)S(1)} %get-tuple-element.21), channel_id=1, source_target_pairs={{0,4},{8,12},{10,14},{12,8},{1,5},{9,13},{11,15},{13,9},{16,20},{2... | collective-permute-start | bytes 466952 | tf_op jit(solution)/shard_map/ppermute | solution.py:55
  53.4 2.1 %collective-permute-start.5 = (bf16[19,4,16,256]{3,2,1,0:T(8,128)(2,1)S(1)}, bf16[19,4,16,256]{3,2,1,0:T(8,128)(2,1)S(1)}, u32[]{:S(2)}, u32[]{:S(2)}) collective-permute-start(bf16[19,4,16,256]{3,2,1,0:T(8,128)(2,1)S(1)} %bitcast.56), channel_id=1, source_target_pairs={{0,2},{2,0},{4,6},{6,4},{8,10},{10,8},{12,14},{14,12},{1,3},{3,1},... | collective-permute-start | bytes 1867784 | tf_op jit(solution)/shard_map/ppermute | solution.py:49
  55.9 6.1 %collective-permute-start.6 = (bf16[19,10,256]{2,1,0:T(8,128)(2,1)S(1)}, bf16[19,10,256]{2,1,0:T(8,128)(2,1)S(1)}, u32[]{:S(2)}, u32[]{:S(2)}) collective-permute-start(bf16[19,10,256]{2,1,0:T(8,128)(2,1)S(1)} %fusion.28), channel_id=1, source_target_pairs={{0,1},{1,0},{2,3},{3,2},{4,5},{5,4},{6,7},{7,6},{8,9},{9,8},{10,11... | collective-permute-start | bytes 291848 | tf_op jit(solution)/shard_map/ppermute | solution.py:307

commit v16 on v11

--- a/solution.py
+++ b/solution.py
@@ -155,15 +155,15 @@
         return carry
 
     lax.fori_loop(0, rows_main // 2, chunk, 0)
-    run_conv(x_ref, w_ref, b_ref[pl.ds(0, chans), :], lo, hi, good_cols, o_ref, width, block)
+    run_conv(x_ref, w_ref, b_ref[pl.ds(0, chans), 0:1], lo, hi, good_cols, o_ref, width, block)
 
 
 def second_body(x_ref, w_ref, b_ref, k_ref, s_ref, o_ref, *, width, block):
     chans = x_ref.shape[0]
     classes = k_ref.shape[0]
-    head = (k_ref[...], b_ref[pl.ds(2 * chans, classes), :])
+    head = (k_ref[...], b_ref[pl.ds(2 * chans, classes), 0:1])
     lo, hi, good_cols = s_ref[5], s_ref[6], s_ref[2]
-    run_conv(x_ref, w_ref, b_ref[pl.ds(chans, chans), :], lo, hi, good_cols, o_ref, width, block, head)
+    run_conv(x_ref, w_ref, b_ref[pl.ds(chans, chans), 0:1], lo, hi, good_cols, o_ref, width, block, head)
 
 
 def pick_block(rows):
@@ -261,10 +261,13 @@
     top_rows = lax.ppermute(flat_feat[:, (rows_dev - halo) * cols:], "space", forward)
     low_rows = lax.ppermute(flat_feat[:, : halo * cols], "space", backward)
     top = place * rows_dev
-    limits = jnp.stack(
-        [halo - top, valid_rows - top + halo, valid_cols, 1 - top, valid_rows - top + 1, -top, valid_rows - top]
-    ).astype(jnp.int32)
-    biases = jnp.concatenate([bias_first, bias_second, class_bias]).reshape(-1, 1)
+    offsets = jnp.array([halo, halo, 0, 1, 1, 0, 0], jnp.int32)
+    of_top = jnp.array([-1, -1, 0, -1, -1, -1, -1], jnp.int32)
+    of_rows = jnp.array([0, 1, 0, 0, 1, 0, 1], jnp.int32)
+    of_cols = jnp.array([0, 0, 1, 0, 0, 0, 0], jnp.int32)
+    limits = offsets + of_top * top + of_rows * valid_rows + of_cols * valid_cols
+    biases = jnp.concatenate([bias_first, bias_second, class_bias])
+    biases = jnp.broadcast_to(biases[:, None], (biases.shape[0], 128))
     hidden = conv_first_layer(flat_feat, top_rows, low_rows, cols, conv_first, biases, limits)
     logits = conv_second_layer(hidden, cols, conv_second, biases, classify, limits)
     out_rows = UP * full_rows

time: 64.3 us -> 63.4 us (0.986)
  local copies, waits for them, and re-layouts: 6.78 us -> 4.75 us
    unnamed x16 -> x24, local copies, waits for them, and re-layouts: 4.97 us -> 3.61 us
    broadcast_in_dim x0 -> x1, local copies, waits for them, and re-layouts: none -> 0.85 us  [shards(): biases = jnp.broadcast_to(biases[:, None], (biases.shape[0], 128))]
    reshape x1 -> x0, local copies, waits for them, and re-layouts: 0.85 us -> none  [shards(): jnp.concatenate([bias_first, bias_second, class_bias]).reshape(-1, 1)]
    another operation x1 -> x0, local copies, waits for them, and re-layouts: 0.67 us -> none  [shards(): jnp.stack([halo - top, valid_rows - top + halo, valid_cols, 1 - top, vali...]
  transfers between devices with their start and end apart: 7 -> 7, of which waited for: 3 -> 4; matrix products, arithmetic and copies ran while one was open for 6% -> 4% of each run, Pallas kernels for 0% -> 0%
where the time goes in v16:
time: 63.4 us; the launch traced here: 63 us
  Pallas kernels  18.7 us (29%)
  starting transfers between devices  14 us (22%)
  waiting for transfers between devices  11.8 us (19%)
  between operations  8.08 us (13%)
  local copies, waits for them, and re-layouts  4.75 us (7%)
  matrix products  3.86 us (6%)
  other arithmetic  1.79 us (3%)
    pallas_call x1, Pallas kernels, conv_first_layer(): pl.pallas_call(functools.partial(first_body, width=width, block=block, ha...  9.74 us
    pallas_call x1, Pallas kernels, conv_second_layer(): pl.pallas_call(functools.partial(second_body, width=width, block=block),...  9 us
    ppermute x2, waiting for transfers between devices, gather_rows(): other = lax.ppermute(held, axis, pairs)  8.11 us
    ppermute x2, starting transfers between devices, gather_rows(): parts[p] = lax.ppermute(held[:, p:p + 1], axis, list(pairs))  7.42 us
    dot_general x2, matrix products, shards(): jnp.einsum('iy,cyj->icj', row_part, widened, preferred_element_type=jnp.f...  3.86 us
    unnamed x24, local copies, waits for them, and re-layouts  3.61 us
    ppermute x1, waiting for transfers between devices, shards(): lax.ppermute(send, 'member', [(i, (i + shift) % members) for i in range(m...  3.38 us
    ppermute x1, starting transfers between devices, shards(): lax.ppermute(flat_feat[:, (rows_dev - halo) * cols:], 'space', forward)  2.37 us
  transfers between devices with their start and end apart: 7, of which 4 were waited for; matrix products, arithmetic and copies ran while one was open for 4% of the time, Pallas kernels for 0%

profile of v16, /device:TPU:0, one launch (start us, length us, event | category | flops | bytes accessed | tf_op | source)
XLA Modules:
  0.0 63.0 jit_solution(17749364396575210416)
XLA Ops:
  0.0 0.0 copy-start.6
  0.0 0.0 copy-start.7
  0.0 0.0 copy-start.8
  0.1 2.6 %copy.15 = bf16[32,8,16,256]{3,1,2,0:T(8,128)(2,1)S(1)} copy(bf16[32,8,16,256]{3,2,1,0:T(8,128)(2,1)} %bitcast.51) | data formatting | bytes 4194304
  2.7 2.4 %collective-permute-start = (bf16[256,512]{1,0:T(8,128)(2,1)S(1)}, bf16[256,512]{1,0:T(8,128)(2,1)S(1)}, u32[]{:S(2)}, u32[]{:S(2)}) collective-permute-start(bf16[256,512]{1,0:T(8,128)(2,1)S(1)} %get-tuple-element.17), channel_id=1, source_target_pairs={{0,2},{2,4},{4,6},{6,8},{8,10},{10,12},{12,14},{1,3},{3,5},{5,7},{... | collective-permute-start | bytes 786440 | tf_op jit(solution)/shard_map/ppermute | solution.py:261
  5.1 1.3 %collective-permute-start.1 = (bf16[256,512]{1,0:T(8,128)(2,1)S(1)}, bf16[256,512]{1,0:T(8,128)(2,1)S(1)}, u32[]{:S(2)}, u32[]{:S(2)}) collective-permute-start(bf16[256,512]{1,0:T(8,128)(2,1)S(1)} %get-tuple-element.16), channel_id=1, source_target_pairs={{2,0},{4,2},{6,4},{8,6},{10,8},{12,10},{14,12},{3,1},{5,3},{7,5},{... | collective-permute-start | bytes 786440 | tf_op jit(solution)/shard_map/ppermute | solution.py:262
  6.4 0.7 %fusion.63 = (s32[]{:T(128)}, s32[]{:T(128)}, s32[]{:T(128)}) fusion(s32[2]{0:T(128)S(1)} %copy-done.3, s32[]{:T(128)S(6)} %select_n.540, s32[]{:T(128)S(6)} %select_n.493, s32[]{:T(128)S(6)} %axis_index.29), kind=kLoop, calls=%fused_computation.107 | loop fusion | flops 15 | bytes 32 | tf_op jit(solution)/shard_map/reduce_sum | solution.py:300
  9.8 0.0 copy-done.5
  9.8 0.6 fusion.64.s_ref
  10.4 0.0 collective-permute-done.top_ref
  10.4 0.3 collective-permute-done.1.low_ref
  10.7 0.8 %broadcast_in_dim.127.b_ref = f32[531,128]{1,0:T(8,128)} broadcast(f32[531]{0:T(1024)S(1)} %pad_maximum_fusion), dimensions={0} | broadcast | bytes 273996 | tf_op jit(solution)/shard_map/broadcast_in_dim | solution.py:270
  11.6 9.7 %shard_map.118.x_ref = bf16[256,4608]{1,0:T(8,128)(2,1)} custom-call(bf16[256,4096]{1,0:T(8,128)(2,1)} %bitcast.48, bf16[256,512]{1,0:T(8,128)(2,1)} %copy-done.9, bf16[256,512]{1,0:T(8,128)(2,1)} %copy-done.10, bf16[3,3,256,256]{3,2,1,0:T(8,128)(2,1)} %w_ref.2, f32[531,128]{1,0:T(8,128)} %broadcast_in_dim.127.b_ref, s32[7]{0:T(128)} %fusion.64.s_ref), custom_call_target="tpu_custom_call" | custom-call | flops 5435817984 | bytes 6160384 | tf_op jit(solution)/shard_map/pallas_call | solution.py:187
  21.3 9.0 %shard_map.119 = bf16[19,4096]{1,0:T(8,128)(2,1)} custom-call(bf16[256,4608]{1,0:T(8,128)(2,1)} %shard_map.118.x_ref, bf16[3,3,256,256]{3,2,1,0:T(8,128)(2,1)} %w_ref.3, f32[531,128]{1,0:T(8,128)} %broadcast_in_dim.127.b_ref, bf16[19,256]{1,0:T(8,128)(2,1)} %k_ref.1, s32[7]{0:T(128)} %fusion.64.s_ref), custom_call_target="tpu_custom_call" | custom-call | flops 4871684096 | bytes 3694592 | tf_op jit(solution)/shard_map/pallas_call | solution.py:217
  30.3 1.0 %copy.16 = bf16[3,8,16,256]{3,2,1,0:T(8,128)(2,1)S(1)} copy(bf16[3,8,16,256]{3,1,2,0:T(8,128)(2,1)} %bitcast.56) | data formatting | bytes 393216
  31.3 1.3 %collective-permute-start.2 = (bf16[19,1,16,256]{3,2,0,1:T(8,128)(2,1)S(1)}, bf16[19,1,16,256]{3,2,0,1:T(8,128)(2,1)S(1)}, u32[]{:S(2)}, u32[]{:S(2)}) collective-permute-start(bf16[19,1,16,256]{3,2,0,1:T(8,128)(2,1)S(1)} %get-tuple-element.22), channel_id=1, source_target_pairs={{2,10},{4,12},{6,14},{8,0},{3,11},{5,13},{7,15},{9,1},{18,26},{20,... | collective-permute-start | bytes 466952 | tf_op jit(solution)/shard_map/ppermute | solution.py:49
  35.2 6.2 %collective-permute-done.2 = bf16[19,1,16,256]{3,2,0,1:T(8,128)(2,1)S(1)} collective-permute-done((bf16[19,1,16,256]{3,2,0,1:T(8,128)(2,1)S(1)}, bf16[19,1,16,256]{3,2,0,1:T(8,128)(2,1)S(1)}, u32[]{:S(2)}, u32[]{:S(2)}) %collective-permute-start.2) | collective-permute-done | bytes 155680 | tf_op jit(solution)/shard_map/ppermute | solution.py:49
  41.5 5.3 %collective-permute-start.3 = (bf16[19,1,16,256]{3,2,0,1:T(8,128)(2,1)S(1)}, bf16[19,1,16,256]{3,2,0,1:T(8,128)(2,1)S(1)}, u32[]{:S(2)}, u32[]{:S(2)}) collective-permute-start(bf16[19,1,16,256]{3,2,0,1:T(8,128)(2,1)S(1)} %get-tuple-element.20), channel_id=1, source_target_pairs={{0,4},{2,6},{4,0},{10,14},{12,8},{14,10},{1,5},{3,7},{5,1},{11,15}... | collective-permute-start | bytes 466952 | tf_op jit(solution)/shard_map/ppermute | solution.py:55
  46.8 2.1 %collective-permute-start.4 = (bf16[19,1,16,256]{3,2,0,1:T(8,128)(2,1)S(1)}, bf16[19,1,16,256]{3,2,0,1:T(8,128)(2,1)S(1)}, u32[]{:S(2)}, u32[]{:S(2)}) collective-permute-start(bf16[19,1,16,256]{3,2,0,1:T(8,128)(2,1)S(1)} %get-tuple-element.21), channel_id=1, source_target_pairs={{0,4},{8,12},{10,14},{12,8},{1,5},{9,13},{11,15},{13,9},{16,20},{2... | collective-permute-start | bytes 466952 | tf_op jit(solution)/shard_map/ppermute | solution.py:55
  51.6 0.0 collective-permute-done.3
  51.6 0.0 collective-permute-done.4
  51.6 0.1 maximum_select_fusion.1
  51.7 0.1 copy.13
  51.8 0.1 collective-permute-start.5
  52.0 1.9 %collective-permute-done.5 = bf16[19,4,16,256]{3,2,1,0:T(8,128)(2,1)S(1)} collective-permute-done((bf16[19,4,16,256]{3,2,1,0:T(8,128)(2,1)S(1)}, bf16[19,4,16,256]{3,2,1,0:T(8,128)(2,1)S(1)}, u32[]{:S(2)}, u32[]{:S(2)}) %collective-permute-start.5) | collective-permute-done | bytes 622624 | tf_op jit(solution)/shard_map/ppermute | solution.py:49
  53.9 0.1 maximum_select_fusion
  54.0 0.1 dynamic-slice_bitcast_fusion
  54.1 0.1 fusion.28
  54.2 1.6 %collective-permute-start.6 = (bf16[19,10,256]{2,1,0:T(8,128)(2,1)S(1)}, bf16[19,10,256]{2,1,0:T(8,128)(2,1)S(1)}, u32[]{:S(2)}, u32[]{:S(2)}) collective-permute-start(bf16[19,10,256]{2,1,0:T(8,128)(2,1)S(1)} %fusion.28), channel_id=1, source_target_pairs={{0,1},{1,0},{2,3},{3,2},{4,5},{5,4},{6,7},{7,6},{8,9},{9,8},{10,11... | collective-permute-start | bytes 291848 | tf_op jit(solution)/shard_map/ppermute | solution.py:296
  55.8 1.2 %fusion = f32[32,19,1024]{2,0,1:T(8,128)S(1)} fusion(f32[1024]{0:T(1024)S(1)} %get-tuple-element.24, s32[1024]{0:T(1024)S(1)} %get-tuple-element.27, f32[1024]{0:T(1024)S(1)} %get-tuple-element.25, s32[1024]{0:T(1024)S(1)} %get-tuple-element.26, s32[]{:T(128)S(6)} %select_n.528, bf16[1,19,10,256]{3,2,1,0:T(8,128)(2,1)S(1)} %get-tuple-element.19, ...), kind=kOutput, calls=%fused_computation.3 | convolution fusion | flops 113884864 | bytes 2701832 | tf_op jit(solution)/shard_map/iy,cyj->icj/dot_general | solution.py:311
  57.0 3.4 %collective-permute-done.6 = bf16[19,10,256]{2,1,0:T(8,128)(2,1)S(1)} collective-permute-done((bf16[19,10,256]{2,1,0:T(8,128)(2,1)S(1)}, bf16[19,10,256]{2,1,0:T(8,128)(2,1)S(1)}, u32[]{:S(2)}, u32[]{:S(2)}) %collective-permute-start.6) | collective-permute-done | bytes 97312 | tf_op jit(solution)/shard_map/ppermute | solution.py:296
  60.4 2.7 %convolution_add_fusion = f32[32,19,1024]{2,0,1:T(8,128)} fusion(f32[32,19,1024]{2,0,1:T(8,128)S(1)} %fusion, bf16[19,10,256]{2,1,0:T(8,128)(2,1)S(1)} %collective-permute-done.6, f32[1024]{0:T(1024)S(1)} %get-tuple-element.28, s32[1024]{0:T(1024)S(1)} %get-tuple-element.31, f32[1024]{0:T(1024)S(1)} %get-tuple-element.29, s32[1024]{0:T(1024)S(1)} %get-tuple-element.30, ...), kind=kOutput, calls=%fused_computation | convolution fusion | flops 114458816 | bytes 5094916 | tf_op jit(solution)/shard_map/iy,cyj->icj/dot_general | solution.py:311
  (33 shorter events, 0.4 us)
Async XLA Ops:
  0.0 6.4 %copy-start.3 = (s32[2]{0:T(128)S(1)}, s32[2]{0:T(128)}, u32[]{:S(2)}) copy-start(s32[2]{0:T(128)} %param.13) | copy-start | bytes 28
  0.0 7.1 %copy-start.1 = (f32[256]{0:T(256)S(1)}, f32[256]{0:T(256)}, u32[]{:S(2)}) copy-start(f32[256]{0:T(256)} %param.17) | copy-start | bytes 3076
  0.0 7.1 %copy-start.2 = (f32[256]{0:T(256)S(1)}, f32[256]{0:T(256)}, u32[]{:S(2)}) copy-start(f32[256]{0:T(256)} %param.15) | copy-start | bytes 3076
  0.0 7.1 %copy-start.4 = (f32[19]{0:T(128)S(1)}, f32[19]{0:T(128)}, u32[]{:S(2)}) copy-start(f32[19]{0:T(128)} %param.19) | copy-start | bytes 232
  0.0 9.8 %copy-start.5 = (s32[7]{0:T(128)S(1)}, s32[7]{0:T(128)}, u32[]{:S(2)}) copy-start(s32[7]{0:T(128)} %constant.239.clone) | copy-start | bytes 88
  0.0 9.8 %copy-start.6 = (s32[7]{0:T(128)S(1)}, s32[7]{0:T(128)}, u32[]{:S(2)}) copy-start(s32[7]{0:T(128)} %constant.240.clone) | copy-start | bytes 88
  0.0 9.8 %copy-start.7 = (s32[7]{0:T(128)S(1)}, s32[7]{0:T(128)}, u32[]{:S(2)}) copy-start(s32[7]{0:T(128)} %constant.241.clone) | copy-start | bytes 88
  0.0 9.8 %copy-start.8 = (s32[7]{0:T(128)S(1)}, s32[7]{0:T(128)}, u32[]{:S(2)}) copy-start(s32[7]{0:T(128)} %constant.242.clone) | copy-start | bytes 88
  2.7 8.9 %copy-start = (bf16[32,8,16,256]{3,1,2,0:T(8,128)(2,1)}, bf16[32,8,16,256]{3,1,2,0:T(8,128)(2,1)S(1)}, u32[]{:S(2)}) copy-start(bf16[32,8,16,256]{3,1,2,0:T(8,128)(2,1)S(1)} %copy.15) | copy-start | bytes 6291460
  2.7 7.7 %collective-permute-start = (bf16[256,512]{1,0:T(8,128)(2,1)S(1)}, bf16[256,512]{1,0:T(8,128)(2,1)S(1)}, u32[]{:S(2)}, u32[]{:S(2)}) collective-permute-start(bf16[256,512]{1,0:T(8,128)(2,1)S(1)} %get-tuple-element.17), channel_id=1, source_target_pairs={{0,2},{2,4},{4,6},{6,8},{8,10},{10,12},{12,14},{1,3},{3,5},{5,7},{... | collective-permute-start | bytes 786440 | tf_op jit(solution)/shard_map/ppermute | solution.py:261
  5.1 5.6 %collective-permute-start.1 = (bf16[256,512]{1,0:T(8,128)(2,1)S(1)}, bf16[256,512]{1,0:T(8,128)(2,1)S(1)}, u32[]{:S(2)}, u32[]{:S(2)}) collective-permute-start(bf16[256,512]{1,0:T(8,128)(2,1)S(1)} %get-tuple-element.16), channel_id=1, source_target_pairs={{2,0},{4,2},{6,4},{8,6},{10,8},{12,10},{14,12},{3,1},{5,3},{7,5},{... | collective-permute-start | bytes 786440 | tf_op jit(solution)/shard_map/ppermute | solution.py:262
  10.4 1.2 %copy-start.9 = (bf16[256,512]{1,0:T(8,128)(2,1)}, bf16[256,512]{1,0:T(8,128)(2,1)S(1)}, u32[]{:S(2)}) copy-start(bf16[256,512]{1,0:T(8,128)(2,1)S(1)} %collective-permute-done.top_ref) | copy-start | bytes 786436
  10.7 0.9 %copy-start.10 = (bf16[256,512]{1,0:T(8,128)(2,1)}, bf16[256,512]{1,0:T(8,128)(2,1)S(1)}, u32[]{:S(2)}) copy-start(bf16[256,512]{1,0:T(8,128)(2,1)S(1)} %collective-permute-done.1.low_ref) | copy-start | bytes 786436
  31.3 10.1 %collective-permute-start.2 = (bf16[19,1,16,256]{3,2,0,1:T(8,128)(2,1)S(1)}, bf16[19,1,16,256]{3,2,0,1:T(8,128)(2,1)S(1)}, u32[]{:S(2)}, u32[]{:S(2)}) collective-permute-start(bf16[19,1,16,256]{3,2,0,1:T(8,128)(2,1)S(1)} %get-tuple-element.22), channel_id=1, source_target_pairs={{2,10},{4,12},{6,14},{8,0},{3,11},{5,13},{7,15},{9,1},{18,26},{20,... | collective-permute-start | bytes 466952 | tf_op jit(solution)/shard_map/ppermute | solution.py:49
  41.5 10.1 %collective-permute-start.3 = (bf16[19,1,16,256]{3,2,0,1:T(8,128)(2,1)S(1)}, bf16[19,1,16,256]{3,2,0,1:T(8,128)(2,1)S(1)}, u32[]{:S(2)}, u32[]{:S(2)}) collective-permute-start(bf16[19,1,16,256]{3,2,0,1:T(8,128)(2,1)S(1)} %get-tuple-element.20), channel_id=1, source_target_pairs={{0,4},{2,6},{4,0},{10,14},{12,8},{14,10},{1,5},{3,7},{5,1},{11,15}... | collective-permute-start | bytes 466952 | tf_op jit(solution)/shard_map/ppermute | solution.py:55
  46.8 4.7 %collective-permute-start.4 = (bf16[19,1,16,256]{3,2,0,1:T(8,128)(2,1)S(1)}, bf16[19,1,16,256]{3,2,0,1:T(8,128)(2,1)S(1)}, u32[]{:S(2)}, u32[]{:S(2)}) collective-permute-start(bf16[19,1,16,256]{3,2,0,1:T(8,128)(2,1)S(1)} %get-tuple-element.21), channel_id=1, source_target_pairs={{0,4},{8,12},{10,14},{12,8},{1,5},{9,13},{11,15},{13,9},{16,20},{2... | collective-permute-start | bytes 466952 | tf_op jit(solution)/shard_map/ppermute | solution.py:55
  51.8 2.1 %collective-permute-start.5 = (bf16[19,4,16,256]{3,2,1,0:T(8,128)(2,1)S(1)}, bf16[19,4,16,256]{3,2,1,0:T(8,128)(2,1)S(1)}, u32[]{:S(2)}, u32[]{:S(2)}) collective-permute-start(bf16[19,4,16,256]{3,2,1,0:T(8,128)(2,1)S(1)} %bitcast.49), channel_id=1, source_target_pairs={{0,2},{2,0},{4,6},{6,4},{8,10},{10,8},{12,14},{14,12},{1,3},{3,1},... | collective-permute-start | bytes 1867784 | tf_op jit(solution)/shard_map/ppermute | solution.py:49
  54.2 6.1 %collective-permute-start.6 = (bf16[19,10,256]{2,1,0:T(8,128)(2,1)S(1)}, bf16[19,10,256]{2,1,0:T(8,128)(2,1)S(1)}, u32[]{:S(2)}, u32[]{:S(2)}) collective-permute-start(bf16[19,10,256]{2,1,0:T(8,128)(2,1)S(1)} %fusion.28), channel_id=1, source_target_pairs={{0,1},{1,0},{2,3},{3,2},{4,5},{5,4},{6,7},{7,6},{8,9},{9,8},{10,11... | collective-permute-start | bytes 291848 | tf_op jit(solution)/shard_map/ppermute | solution.py:296

commit v17 on v16

--- a/solution.py
+++ b/solution.py
@@ -261,10 +261,11 @@
     top_rows = lax.ppermute(flat_feat[:, (rows_dev - halo) * cols:], "space", forward)
     low_rows = lax.ppermute(flat_feat[:, : halo * cols], "space", backward)
     top = place * rows_dev
-    offsets = jnp.array([halo, halo, 0, 1, 1, 0, 0], jnp.int32)
-    of_top = jnp.array([-1, -1, 0, -1, -1, -1, -1], jnp.int32)
-    of_rows = jnp.array([0, 1, 0, 0, 1, 0, 1], jnp.int32)
-    of_cols = jnp.array([0, 0, 1, 0, 0, 0, 0], jnp.int32)
+    slot = lax.broadcasted_iota(jnp.int32, (7,), 0)
+    offsets = jnp.where(slot < 2, halo, jnp.where((slot == 3) | (slot == 4), 1, 0))
+    of_top = jnp.where(slot == 2, 0, -1)
+    of_rows = jnp.where((slot == 1) | (slot == 4) | (slot == 6), 1, 0)
+    of_cols = jnp.where(slot == 2, 1, 0)
     limits = offsets + of_top * top + of_rows * valid_rows + of_cols * valid_cols
     biases = jnp.concatenate([bias_first, bias_second, class_bias])
     biases = jnp.broadcast_to(biases[:, None], (biases.shape[0], 128))

time: 63.4 us -> 63.4 us (level)
    unnamed x24 -> x16, local copies, waits for them, and re-layouts: 3.61 us -> 3.57 us
where the time goes in v17:
time: 63.4 us; the launch traced here: 63 us
  Pallas kernels  18.8 us (30%)
  starting transfers between devices  14 us (22%)
  waiting for transfers between devices  11.7 us (18%)
  between operations  8.12 us (13%)
  local copies, waits for them, and re-layouts  4.71 us (7%)
  matrix products  3.87 us (6%)
  other arithmetic  1.84 us (3%)
    pallas_call x1, Pallas kernels, conv_first_layer(): pl.pallas_call(functools.partial(first_body, width=width, block=block, ha...  9.74 us
    pallas_call x1, Pallas kernels, conv_second_layer(): pl.pallas_call(functools.partial(second_body, width=width, block=block),...  9.02 us
    ppermute x2, waiting for transfers between devices, gather_rows(): other = lax.ppermute(held, axis, pairs)  8.02 us
    ppermute x2, starting transfers between devices, gather_rows(): parts[p] = lax.ppermute(held[:, p:p + 1], axis, list(pairs))  7.41 us
    dot_general x2, matrix products, shards(): jnp.einsum('iy,cyj->icj', row_part, widened, preferred_element_type=jnp.f...  3.87 us
    unnamed x16, local copies, waits for them, and re-layouts  3.57 us
    ppermute x1, waiting for transfers between devices, shards(): lax.ppermute(send, 'member', [(i, (i + shift) % members) for i in range(m...  3.36 us
    ppermute x1, starting transfers between devices, shards(): lax.ppermute(flat_feat[:, (rows_dev - halo) * cols:], 'space', forward)  2.37 us
  transfers between devices with their start and end apart: 7, of which 4 were waited for; matrix products, arithmetic and copies ran while one was open for 4% of the time, Pallas kernels for 0%

profile of v17, /device:TPU:0, one launch (start us, length us, event | category | flops | bytes accessed | tf_op | source)
XLA Modules:
  0.0 63.0 jit_solution(16998717252418561555)
XLA Ops:
  0.0 2.6 %copy.11 = bf16[32,8,16,256]{3,1,2,0:T(8,128)(2,1)S(1)} copy(bf16[32,8,16,256]{3,2,1,0:T(8,128)(2,1)} %bitcast.51) | data formatting | bytes 4194304
  2.6 0.0 copy-start
  2.6 2.4 %collective-permute-start = (bf16[256,512]{1,0:T(8,128)(2,1)S(1)}, bf16[256,512]{1,0:T(8,128)(2,1)S(1)}, u32[]{:S(2)}, u32[]{:S(2)}) collective-permute-start(bf16[256,512]{1,0:T(8,128)(2,1)S(1)} %get-tuple-element.17), channel_id=1, source_target_pairs={{0,2},{2,4},{4,6},{6,8},{8,10},{10,12},{12,14},{1,3},{3,5},{5,7},{... | collective-permute-start | bytes 786440 | tf_op jit(solution)/shard_map/ppermute | solution.py:261
  5.0 1.3 %collective-permute-start.1 = (bf16[256,512]{1,0:T(8,128)(2,1)S(1)}, bf16[256,512]{1,0:T(8,128)(2,1)S(1)}, u32[]{:S(2)}, u32[]{:S(2)}) collective-permute-start(bf16[256,512]{1,0:T(8,128)(2,1)S(1)} %get-tuple-element.16), channel_id=1, source_target_pairs={{2,0},{4,2},{6,4},{8,6},{10,8},{12,10},{14,12},{3,1},{5,3},{7,5},{... | collective-permute-start | bytes 786440 | tf_op jit(solution)/shard_map/ppermute | solution.py:262
  6.4 0.0 copy-done.3
  6.4 0.7 %fusion.69 = (s32[]{:T(128)}, s32[]{:T(128)}, s32[]{:T(128)}) fusion(s32[2]{0:T(128)S(1)} %copy-done.3, s32[]{:T(128)S(6)} %select_n.562, s32[]{:T(128)S(6)} %select_n.510, s32[]{:T(128)S(6)} %axis_index.29), kind=kLoop, calls=%fused_computation.118 | loop fusion | flops 15 | bytes 32 | tf_op jit(solution)/shard_map/reduce_sum | solution.py:301
  9.7 0.6 fusion.65.s_ref
  10.3 0.0 copy-done.1
  10.3 0.0 copy-done.2
  10.3 0.0 collective-permute-done.top_ref
  10.4 0.3 collective-permute-done.1.low_ref
  10.6 0.8 %broadcast_in_dim.145.b_ref = f32[531,128]{1,0:T(8,128)} broadcast(f32[531]{0:T(1024)S(1)} %pad_maximum_fusion), dimensions={0} | broadcast | bytes 273996 | tf_op jit(solution)/shard_map/broadcast_in_dim | solution.py:271
  11.5 9.7 %shard_map.82.x_ref = bf16[256,4608]{1,0:T(8,128)(2,1)} custom-call(bf16[256,4096]{1,0:T(8,128)(2,1)} %bitcast.48, bf16[256,512]{1,0:T(8,128)(2,1)} %copy-done.5, bf16[256,512]{1,0:T(8,128)(2,1)} %copy-done.6, bf16[3,3,256,256]{3,2,1,0:T(8,128)(2,1)} %w_ref.2, f32[531,128]{1,0:T(8,128)} %broadcast_in_dim.145.b_ref, s32[7]{0:T(128)} %fusion.65.s_ref), custom_call_target="tpu_custom_call" | custom-call | flops 5435817984 | bytes 6160384 | tf_op jit(solution)/shard_map/pallas_call | solution.py:187
  21.2 9.0 %shard_map.83 = bf16[19,4096]{1,0:T(8,128)(2,1)} custom-call(bf16[256,4608]{1,0:T(8,128)(2,1)} %shard_map.82.x_ref, bf16[3,3,256,256]{3,2,1,0:T(8,128)(2,1)} %w_ref.3, f32[531,128]{1,0:T(8,128)} %broadcast_in_dim.145.b_ref, bf16[19,256]{1,0:T(8,128)(2,1)} %k_ref.1, s32[7]{0:T(128)} %fusion.65.s_ref), custom_call_target="tpu_custom_call" | custom-call | flops 4871684096 | bytes 3694592 | tf_op jit(solution)/shard_map/pallas_call | solution.py:217
  30.3 1.0 %copy.12 = bf16[3,8,16,256]{3,2,1,0:T(8,128)(2,1)S(1)} copy(bf16[3,8,16,256]{3,1,2,0:T(8,128)(2,1)} %bitcast.56) | data formatting | bytes 393216
  31.3 1.3 %collective-permute-start.2 = (bf16[19,1,16,256]{3,2,0,1:T(8,128)(2,1)S(1)}, bf16[19,1,16,256]{3,2,0,1:T(8,128)(2,1)S(1)}, u32[]{:S(2)}, u32[]{:S(2)}) collective-permute-start(bf16[19,1,16,256]{3,2,0,1:T(8,128)(2,1)S(1)} %get-tuple-element.22), channel_id=1, source_target_pairs={{2,10},{4,12},{6,14},{8,0},{3,11},{5,13},{7,15},{9,1},{18,26},{20,... | collective-permute-start | bytes 466952 | tf_op jit(solution)/shard_map/ppermute | solution.py:49
  35.3 6.1 %collective-permute-done.2 = bf16[19,1,16,256]{3,2,0,1:T(8,128)(2,1)S(1)} collective-permute-done((bf16[19,1,16,256]{3,2,0,1:T(8,128)(2,1)S(1)}, bf16[19,1,16,256]{3,2,0,1:T(8,128)(2,1)S(1)}, u32[]{:S(2)}, u32[]{:S(2)}) %collective-permute-start.2) | collective-permute-done | bytes 155680 | tf_op jit(solution)/shard_map/ppermute | solution.py:49
  41.5 5.3 %collective-permute-start.3 = (bf16[19,1,16,256]{3,2,0,1:T(8,128)(2,1)S(1)}, bf16[19,1,16,256]{3,2,0,1:T(8,128)(2,1)S(1)}, u32[]{:S(2)}, u32[]{:S(2)}) collective-permute-start(bf16[19,1,16,256]{3,2,0,1:T(8,128)(2,1)S(1)} %get-tuple-element.20), channel_id=1, source_target_pairs={{0,4},{2,6},{4,0},{10,14},{12,8},{14,10},{1,5},{3,7},{5,1},{11,15}... | collective-permute-start | bytes 466952 | tf_op jit(solution)/shard_map/ppermute | solution.py:55
  46.8 2.1 %collective-permute-start.4 = (bf16[19,1,16,256]{3,2,0,1:T(8,128)(2,1)S(1)}, bf16[19,1,16,256]{3,2,0,1:T(8,128)(2,1)S(1)}, u32[]{:S(2)}, u32[]{:S(2)}) collective-permute-start(bf16[19,1,16,256]{3,2,0,1:T(8,128)(2,1)S(1)} %get-tuple-element.21), channel_id=1, source_target_pairs={{0,4},{8,12},{10,14},{12,8},{1,5},{9,13},{11,15},{13,9},{16,20},{2... | collective-permute-start | bytes 466952 | tf_op jit(solution)/shard_map/ppermute | solution.py:55
  51.5 0.0 collective-permute-done.3
  51.5 0.0 collective-permute-done.4
  51.6 0.1 maximum_select_fusion.1
  51.6 0.1 copy.9
  51.7 0.1 collective-permute-start.5
  51.9 1.9 %collective-permute-done.5 = bf16[19,4,16,256]{3,2,1,0:T(8,128)(2,1)S(1)} collective-permute-done((bf16[19,4,16,256]{3,2,1,0:T(8,128)(2,1)S(1)}, bf16[19,4,16,256]{3,2,1,0:T(8,128)(2,1)S(1)}, u32[]{:S(2)}, u32[]{:S(2)}) %collective-permute-start.5) | collective-permute-done | bytes 622624 | tf_op jit(solution)/shard_map/ppermute | solution.py:49
  53.8 0.1 maximum_select_fusion
  53.9 0.1 dynamic-slice_bitcast_fusion
  54.1 0.1 fusion.28
  54.2 1.6 %collective-permute-start.6 = (bf16[19,10,256]{2,1,0:T(8,128)(2,1)S(1)}, bf16[19,10,256]{2,1,0:T(8,128)(2,1)S(1)}, u32[]{:S(2)}, u32[]{:S(2)}) collective-permute-start(bf16[19,10,256]{2,1,0:T(8,128)(2,1)S(1)} %fusion.28), channel_id=1, source_target_pairs={{0,1},{1,0},{2,3},{3,2},{4,5},{5,4},{6,7},{7,6},{8,9},{9,8},{10,11... | collective-permute-start | bytes 291848 | tf_op jit(solution)/shard_map/ppermute | solution.py:297
  55.7 1.2 %fusion = f32[32,19,1024]{2,0,1:T(8,128)S(1)} fusion(f32[1024]{0:T(1024)S(1)} %get-tuple-element.24, s32[1024]{0:T(1024)S(1)} %get-tuple-element.27, f32[1024]{0:T(1024)S(1)} %get-tuple-element.25, s32[1024]{0:T(1024)S(1)} %get-tuple-element.26, s32[]{:T(128)S(6)} %select_n.550, bf16[1,19,10,256]{3,2,1,0:T(8,128)(2,1)S(1)} %get-tuple-element.19, ...), kind=kOutput, calls=%fused_computation.3 | convolution fusion | flops 113884864 | bytes 2701832 | tf_op jit(solution)/shard_map/iy,cyj->icj/dot_general | solution.py:312
  56.9 3.4 %collective-permute-done.6 = bf16[19,10,256]{2,1,0:T(8,128)(2,1)S(1)} collective-permute-done((bf16[19,10,256]{2,1,0:T(8,128)(2,1)S(1)}, bf16[19,10,256]{2,1,0:T(8,128)(2,1)S(1)}, u32[]{:S(2)}, u32[]{:S(2)}) %collective-permute-start.6) | collective-permute-done | bytes 97312 | tf_op jit(solution)/shard_map/ppermute | solution.py:297
  60.3 2.7 %convolution_add_fusion = f32[32,19,1024]{2,0,1:T(8,128)} fusion(f32[32,19,1024]{2,0,1:T(8,128)S(1)} %fusion, bf16[19,10,256]{2,1,0:T(8,128)(2,1)S(1)} %collective-permute-done.6, f32[1024]{0:T(1024)S(1)} %get-tuple-element.28, s32[1024]{0:T(1024)S(1)} %get-tuple-element.31, f32[1024]{0:T(1024)S(1)} %get-tuple-element.29, s32[1024]{0:T(1024)S(1)} %get-tuple-element.30, ...), kind=kOutput, calls=%fused_computation | convolution fusion | flops 114458816 | bytes 5094916 | tf_op jit(solution)/shard_map/iy,cyj->icj/dot_general | solution.py:312
  (25 shorter events, 0.4 us)
Async XLA Ops:
  0.0 6.4 %copy-start.3 = (s32[2]{0:T(128)S(1)}, s32[2]{0:T(128)}, u32[]{:S(2)}) copy-start(s32[2]{0:T(128)} %param.9) | copy-start | bytes 28
  0.0 10.3 %copy-start.1 = (f32[256]{0:T(256)S(1)}, f32[256]{0:T(256)}, u32[]{:S(2)}) copy-start(f32[256]{0:T(256)} %param.13) | copy-start | bytes 3076
  0.0 10.3 %copy-start.2 = (f32[256]{0:T(256)S(1)}, f32[256]{0:T(256)}, u32[]{:S(2)}) copy-start(f32[256]{0:T(256)} %param.11) | copy-start | bytes 3076
  0.0 10.3 %copy-start.4 = (f32[19]{0:T(128)S(1)}, f32[19]{0:T(128)}, u32[]{:S(2)}) copy-start(f32[19]{0:T(128)} %param.15) | copy-start | bytes 232
  2.6 8.9 %copy-start = (bf16[32,8,16,256]{3,1,2,0:T(8,128)(2,1)}, bf16[32,8,16,256]{3,1,2,0:T(8,128)(2,1)S(1)}, u32[]{:S(2)}) copy-start(bf16[32,8,16,256]{3,1,2,0:T(8,128)(2,1)S(1)} %copy.11) | copy-start | bytes 6291460
  2.6 7.7 %collective-permute-start = (bf16[256,512]{1,0:T(8,128)(2,1)S(1)}, bf16[256,512]{1,0:T(8,128)(2,1)S(1)}, u32[]{:S(2)}, u32[]{:S(2)}) collective-permute-start(bf16[256,512]{1,0:T(8,128)(2,1)S(1)} %get-tuple-element.17), channel_id=1, source_target_pairs={{0,2},{2,4},{4,6},{6,8},{8,10},{10,12},{12,14},{1,3},{3,5},{5,7},{... | collective-permute-start | bytes 786440 | tf_op jit(solution)/shard_map/ppermute | solution.py:261
  5.0 5.6 %collective-permute-start.1 = (bf16[256,512]{1,0:T(8,128)(2,1)S(1)}, bf16[256,512]{1,0:T(8,128)(2,1)S(1)}, u32[]{:S(2)}, u32[]{:S(2)}) collective-permute-start(bf16[256,512]{1,0:T(8,128)(2,1)S(1)} %get-tuple-element.16), channel_id=1, source_target_pairs={{2,0},{4,2},{6,4},{8,6},{10,8},{12,10},{14,12},{3,1},{5,3},{7,5},{... | collective-permute-start | bytes 786440 | tf_op jit(solution)/shard_map/ppermute | solution.py:262
  10.3 1.1 %copy-start.5 = (bf16[256,512]{1,0:T(8,128)(2,1)}, bf16[256,512]{1,0:T(8,128)(2,1)S(1)}, u32[]{:S(2)}) copy-start(bf16[256,512]{1,0:T(8,128)(2,1)S(1)} %collective-permute-done.top_ref) | copy-start | bytes 786436
  10.6 0.9 %copy-start.6 = (bf16[256,512]{1,0:T(8,128)(2,1)}, bf16[256,512]{1,0:T(8,128)(2,1)S(1)}, u32[]{:S(2)}) copy-start(bf16[256,512]{1,0:T(8,128)(2,1)S(1)} %collective-permute-done.1.low_ref) | copy-start | bytes 786436
  31.3 10.2 %collective-permute-start.2 = (bf16[19,1,16,256]{3,2,0,1:T(8,128)(2,1)S(1)}, bf16[19,1,16,256]{3,2,0,1:T(8,128)(2,1)S(1)}, u32[]{:S(2)}, u32[]{:S(2)}) collective-permute-start(bf16[19,1,16,256]{3,2,0,1:T(8,128)(2,1)S(1)} %get-tuple-element.22), channel_id=1, source_target_pairs={{2,10},{4,12},{6,14},{8,0},{3,11},{5,13},{7,15},{9,1},{18,26},{20,... | collective-permute-start | bytes 466952 | tf_op jit(solution)/shard_map/ppermute | solution.py:49
  41.5 10.0 %collective-permute-start.3 = (bf16[19,1,16,256]{3,2,0,1:T(8,128)(2,1)S(1)}, bf16[19,1,16,256]{3,2,0,1:T(8,128)(2,1)S(1)}, u32[]{:S(2)}, u32[]{:S(2)}) collective-permute-start(bf16[19,1,16,256]{3,2,0,1:T(8,128)(2,1)S(1)} %get-tuple-element.20), channel_id=1, source_target_pairs={{0,4},{2,6},{4,0},{10,14},{12,8},{14,10},{1,5},{3,7},{5,1},{11,15}... | collective-permute-start | bytes 466952 | tf_op jit(solution)/shard_map/ppermute | solution.py:55
  46.8 4.7 %collective-permute-start.4 = (bf16[19,1,16,256]{3,2,0,1:T(8,128)(2,1)S(1)}, bf16[19,1,16,256]{3,2,0,1:T(8,128)(2,1)S(1)}, u32[]{:S(2)}, u32[]{:S(2)}) collective-permute-start(bf16[19,1,16,256]{3,2,0,1:T(8,128)(2,1)S(1)} %get-tuple-element.21), channel_id=1, source_target_pairs={{0,4},{8,12},{10,14},{12,8},{1,5},{9,13},{11,15},{13,9},{16,20},{2... | collective-permute-start | bytes 466952 | tf_op jit(solution)/shard_map/ppermute | solution.py:55
  51.7 2.1 %collective-permute-start.5 = (bf16[19,4,16,256]{3,2,1,0:T(8,128)(2,1)S(1)}, bf16[19,4,16,256]{3,2,1,0:T(8,128)(2,1)S(1)}, u32[]{:S(2)}, u32[]{:S(2)}) collective-permute-start(bf16[19,4,16,256]{3,2,1,0:T(8,128)(2,1)S(1)} %bitcast.49), channel_id=1, source_target_pairs={{0,2},{2,0},{4,6},{6,4},{8,10},{10,8},{12,14},{14,12},{1,3},{3,1},... | collective-permute-start | bytes 1867784 | tf_op jit(solution)/shard_map/ppermute | solution.py:49
  54.2 6.1 %collective-permute-start.6 = (bf16[19,10,256]{2,1,0:T(8,128)(2,1)S(1)}, bf16[19,10,256]{2,1,0:T(8,128)(2,1)S(1)}, u32[]{:S(2)}, u32[]{:S(2)}) collective-permute-start(bf16[19,10,256]{2,1,0:T(8,128)(2,1)S(1)} %fusion.28), channel_id=1, source_target_pairs={{0,1},{1,0},{2,3},{3,2},{4,5},{5,4},{6,7},{7,6},{8,9},{9,8},{10,11... | collective-permute-start | bytes 291848 | tf_op jit(solution)/shard_map/ppermute | solution.py:297

commit v18 on v16

--- a/solution.py
+++ b/solution.py
@@ -154,7 +154,7 @@
         put(main_ref[:, pl.ds(start, 2 * width)], halo + 2 * i, 2)
         return carry
 
-    lax.fori_loop(0, rows_main // 2, chunk, 0)
+    lax.fori_loop(0, rows_main // 2, chunk, 0, unroll=True)
     run_conv(x_ref, w_ref, b_ref[pl.ds(0, chans), 0:1], lo, hi, good_cols, o_ref, width, block)
 
 

time: 63.4 us -> 63.3 us (level)
  transfers between devices with their start and end apart: 7 -> 7, of which waited for: 4 -> 5; matrix products, arithmetic and copies ran while one was open for 4% -> 4% of each run, Pallas kernels for 0% -> 0%
where the time goes in v18:
time: 63.3 us; the launch traced here: 62.8 us
  Pallas kernels  18.6 us (29%)
  starting transfers between devices  13.8 us (22%)
  waiting for transfers between devices  11.9 us (19%)
  between operations  8.07 us (13%)
  local copies, waits for them, and re-layouts  4.75 us (8%)
  matrix products  3.86 us (6%)
  other arithmetic  1.79 us (3%)
    pallas_call x1, Pallas kernels, conv_first_layer(): pl.pallas_call(functools.partial(first_body, width=width, block=block, ha...  9.61 us
    pallas_call x1, Pallas kernels, conv_second_layer(): pl.pallas_call(functools.partial(second_body, width=width, block=block),...  9 us
    ppermute x2, waiting for transfers between devices, gather_rows(): other = lax.ppermute(held, axis, pairs)  8.12 us
    ppermute x2, starting transfers between devices, gather_rows(): parts[p] = lax.ppermute(held[:, p:p + 1], axis, list(pairs))  7.24 us
    dot_general x2, matrix products, shards(): jnp.einsum('iy,cyj->icj', row_part, widened, preferred_element_type=jnp.f...  3.86 us
    unnamed x24, local copies, waits for them, and re-layouts  3.61 us
    ppermute x1, waiting for transfers between devices, shards(): lax.ppermute(send, 'member', [(i, (i + shift) % members) for i in range(m...  3.38 us
    ppermute x1, starting transfers between devices, shards(): lax.ppermute(flat_feat[:, (rows_dev - halo) * cols:], 'space', forward)  2.37 us
  transfers between devices with their start and end apart: 7, of which 5 were waited for; matrix products, arithmetic and copies ran while one was open for 4% of the time, Pallas kernels for 0%

profile of v18, /device:TPU:0, one launch (start us, length us, event | category | flops | bytes accessed | tf_op | source)
XLA Modules:
  0.0 62.8 jit_solution(17961497897176345421)
XLA Ops:
  0.0 0.0 copy-start.6
  0.0 0.0 copy-start.7
  0.0 0.0 copy-start.8
  0.1 2.6 %copy.15 = bf16[32,8,16,256]{3,1,2,0:T(8,128)(2,1)S(1)} copy(bf16[32,8,16,256]{3,2,1,0:T(8,128)(2,1)} %bitcast.51) | data formatting | bytes 4194304
  2.7 0.0 copy-start
  2.7 2.4 %collective-permute-start = (bf16[256,512]{1,0:T(8,128)(2,1)S(1)}, bf16[256,512]{1,0:T(8,128)(2,1)S(1)}, u32[]{:S(2)}, u32[]{:S(2)}) collective-permute-start(bf16[256,512]{1,0:T(8,128)(2,1)S(1)} %get-tuple-element.17), channel_id=1, source_target_pairs={{0,2},{2,4},{4,6},{6,8},{8,10},{10,12},{12,14},{1,3},{3,5},{5,7},{... | collective-permute-start | bytes 786440 | tf_op jit(solution)/shard_map/ppermute | solution.py:261
  5.1 1.3 %collective-permute-start.1 = (bf16[256,512]{1,0:T(8,128)(2,1)S(1)}, bf16[256,512]{1,0:T(8,128)(2,1)S(1)}, u32[]{:S(2)}, u32[]{:S(2)}) collective-permute-start(bf16[256,512]{1,0:T(8,128)(2,1)S(1)} %get-tuple-element.16), channel_id=1, source_target_pairs={{2,0},{4,2},{6,4},{8,6},{10,8},{12,10},{14,12},{3,1},{5,3},{7,5},{... | collective-permute-start | bytes 786440 | tf_op jit(solution)/shard_map/ppermute | solution.py:262
  6.4 0.7 %fusion.63 = (s32[]{:T(128)}, s32[]{:T(128)}, s32[]{:T(128)}) fusion(s32[2]{0:T(128)S(1)} %copy-done.3, s32[]{:T(128)S(6)} %select_n.540, s32[]{:T(128)S(6)} %select_n.493, s32[]{:T(128)S(6)} %axis_index.29), kind=kLoop, calls=%fused_computation.107 | loop fusion | flops 15 | bytes 32 | tf_op jit(solution)/shard_map/reduce_sum | solution.py:300
  9.8 0.6 fusion.64.s_ref
  10.4 0.0 collective-permute-done.top_ref
  10.4 0.3 collective-permute-done.1.low_ref
  10.7 0.8 %broadcast_in_dim.127.b_ref = f32[531,128]{1,0:T(8,128)} broadcast(f32[531]{0:T(1024)S(1)} %pad_maximum_fusion), dimensions={0} | broadcast | bytes 273996 | tf_op jit(solution)/shard_map/broadcast_in_dim | solution.py:270
  11.6 9.6 %shard_map.118.x_ref = bf16[256,4608]{1,0:T(8,128)(2,1)} custom-call(bf16[256,4096]{1,0:T(8,128)(2,1)} %bitcast.48, bf16[256,512]{1,0:T(8,128)(2,1)} %copy-done.9, bf16[256,512]{1,0:T(8,128)(2,1)} %copy-done.10, bf16[3,3,256,256]{3,2,1,0:T(8,128)(2,1)} %w_ref.2, f32[531,128]{1,0:T(8,128)} %broadcast_in_dim.127.b_ref, s32[7]{0:T(128)} %fusion.64.s_ref), custom_call_target="tpu_custom_call" | custom-call | flops 5435817984 | bytes 6160384 | tf_op jit(solution)/shard_map/pallas_call | solution.py:187
  21.2 9.0 %shard_map.119 = bf16[19,4096]{1,0:T(8,128)(2,1)} custom-call(bf16[256,4608]{1,0:T(8,128)(2,1)} %shard_map.118.x_ref, bf16[3,3,256,256]{3,2,1,0:T(8,128)(2,1)} %w_ref.3, f32[531,128]{1,0:T(8,128)} %broadcast_in_dim.127.b_ref, bf16[19,256]{1,0:T(8,128)(2,1)} %k_ref.1, s32[7]{0:T(128)} %fusion.64.s_ref), custom_call_target="tpu_custom_call" | custom-call | flops 4871684096 | bytes 3694592 | tf_op jit(solution)/shard_map/pallas_call | solution.py:217
  30.2 1.0 %copy.16 = bf16[3,8,16,256]{3,2,1,0:T(8,128)(2,1)S(1)} copy(bf16[3,8,16,256]{3,1,2,0:T(8,128)(2,1)} %bitcast.56) | data formatting | bytes 393216
  31.2 1.3 %collective-permute-start.2 = (bf16[19,1,16,256]{3,2,0,1:T(8,128)(2,1)S(1)}, bf16[19,1,16,256]{3,2,0,1:T(8,128)(2,1)S(1)}, u32[]{:S(2)}, u32[]{:S(2)}) collective-permute-start(bf16[19,1,16,256]{3,2,0,1:T(8,128)(2,1)S(1)} %get-tuple-element.22), channel_id=1, source_target_pairs={{2,10},{4,12},{6,14},{8,0},{3,11},{5,13},{7,15},{9,1},{18,26},{20,... | collective-permute-start | bytes 466952 | tf_op jit(solution)/shard_map/ppermute | solution.py:49
  35.1 6.2 %collective-permute-done.2 = bf16[19,1,16,256]{3,2,0,1:T(8,128)(2,1)S(1)} collective-permute-done((bf16[19,1,16,256]{3,2,0,1:T(8,128)(2,1)S(1)}, bf16[19,1,16,256]{3,2,0,1:T(8,128)(2,1)S(1)}, u32[]{:S(2)}, u32[]{:S(2)}) %collective-permute-start.2) | collective-permute-done | bytes 155680 | tf_op jit(solution)/shard_map/ppermute | solution.py:49
  41.4 5.3 %collective-permute-start.3 = (bf16[19,1,16,256]{3,2,0,1:T(8,128)(2,1)S(1)}, bf16[19,1,16,256]{3,2,0,1:T(8,128)(2,1)S(1)}, u32[]{:S(2)}, u32[]{:S(2)}) collective-permute-start(bf16[19,1,16,256]{3,2,0,1:T(8,128)(2,1)S(1)} %get-tuple-element.20), channel_id=1, source_target_pairs={{0,4},{2,6},{4,0},{10,14},{12,8},{14,10},{1,5},{3,7},{5,1},{11,15}... | collective-permute-start | bytes 466952 | tf_op jit(solution)/shard_map/ppermute | solution.py:55
  46.7 1.9 %collective-permute-start.4 = (bf16[19,1,16,256]{3,2,0,1:T(8,128)(2,1)S(1)}, bf16[19,1,16,256]{3,2,0,1:T(8,128)(2,1)S(1)}, u32[]{:S(2)}, u32[]{:S(2)}) collective-permute-start(bf16[19,1,16,256]{3,2,0,1:T(8,128)(2,1)S(1)} %get-tuple-element.21), channel_id=1, source_target_pairs={{0,4},{8,12},{10,14},{12,8},{1,5},{9,13},{11,15},{13,9},{16,20},{2... | collective-permute-start | bytes 466952 | tf_op jit(solution)/shard_map/ppermute | solution.py:55
  51.3 0.0 collective-permute-done.3
  51.3 0.1 collective-permute-done.4
  51.4 0.1 maximum_select_fusion.1
  51.5 0.1 copy.13
  51.6 0.1 collective-permute-start.5
  51.8 1.9 %collective-permute-done.5 = bf16[19,4,16,256]{3,2,1,0:T(8,128)(2,1)S(1)} collective-permute-done((bf16[19,4,16,256]{3,2,1,0:T(8,128)(2,1)S(1)}, bf16[19,4,16,256]{3,2,1,0:T(8,128)(2,1)S(1)}, u32[]{:S(2)}, u32[]{:S(2)}) %collective-permute-start.5) | collective-permute-done | bytes 622624 | tf_op jit(solution)/shard_map/ppermute | solution.py:49
  53.7 0.1 maximum_select_fusion
  53.8 0.1 dynamic-slice_bitcast_fusion
  53.9 0.1 fusion.28
  54.0 1.6 %collective-permute-start.6 = (bf16[19,10,256]{2,1,0:T(8,128)(2,1)S(1)}, bf16[19,10,256]{2,1,0:T(8,128)(2,1)S(1)}, u32[]{:S(2)}, u32[]{:S(2)}) collective-permute-start(bf16[19,10,256]{2,1,0:T(8,128)(2,1)S(1)} %fusion.28), channel_id=1, source_target_pairs={{0,1},{1,0},{2,3},{3,2},{4,5},{5,4},{6,7},{7,6},{8,9},{9,8},{10,11... | collective-permute-start | bytes 291848 | tf_op jit(solution)/shard_map/ppermute | solution.py:296
  55.6 1.2 %fusion = f32[32,19,1024]{2,0,1:T(8,128)S(1)} fusion(f32[1024]{0:T(1024)S(1)} %get-tuple-element.24, s32[1024]{0:T(1024)S(1)} %get-tuple-element.27, f32[1024]{0:T(1024)S(1)} %get-tuple-element.25, s32[1024]{0:T(1024)S(1)} %get-tuple-element.26, s32[]{:T(128)S(6)} %select_n.528, bf16[1,19,10,256]{3,2,1,0:T(8,128)(2,1)S(1)} %get-tuple-element.19, ...), kind=kOutput, calls=%fused_computation.3 | convolution fusion | flops 113884864 | bytes 2701832 | tf_op jit(solution)/shard_map/iy,cyj->icj/dot_general | solution.py:311
  56.8 3.4 %collective-permute-done.6 = bf16[19,10,256]{2,1,0:T(8,128)(2,1)S(1)} collective-permute-done((bf16[19,10,256]{2,1,0:T(8,128)(2,1)S(1)}, bf16[19,10,256]{2,1,0:T(8,128)(2,1)S(1)}, u32[]{:S(2)}, u32[]{:S(2)}) %collective-permute-start.6) | collective-permute-done | bytes 97312 | tf_op jit(solution)/shard_map/ppermute | solution.py:296
  60.1 2.7 %convolution_add_fusion = f32[32,19,1024]{2,0,1:T(8,128)} fusion(f32[32,19,1024]{2,0,1:T(8,128)S(1)} %fusion, bf16[19,10,256]{2,1,0:T(8,128)(2,1)S(1)} %collective-permute-done.6, f32[1024]{0:T(1024)S(1)} %get-tuple-element.28, s32[1024]{0:T(1024)S(1)} %get-tuple-element.31, f32[1024]{0:T(1024)S(1)} %get-tuple-element.29, s32[1024]{0:T(1024)S(1)} %get-tuple-element.30, ...), kind=kOutput, calls=%fused_computation | convolution fusion | flops 114458816 | bytes 5094916 | tf_op jit(solution)/shard_map/iy,cyj->icj/dot_general | solution.py:311
  (33 shorter events, 0.4 us)
Async XLA Ops:
  0.0 6.4 %copy-start.3 = (s32[2]{0:T(128)S(1)}, s32[2]{0:T(128)}, u32[]{:S(2)}) copy-start(s32[2]{0:T(128)} %param.13) | copy-start | bytes 28
  0.0 7.1 %copy-start.1 = (f32[256]{0:T(256)S(1)}, f32[256]{0:T(256)}, u32[]{:S(2)}) copy-start(f32[256]{0:T(256)} %param.17) | copy-start | bytes 3076
  0.0 7.1 %copy-start.2 = (f32[256]{0:T(256)S(1)}, f32[256]{0:T(256)}, u32[]{:S(2)}) copy-start(f32[256]{0:T(256)} %param.15) | copy-start | bytes 3076
  0.0 7.1 %copy-start.4 = (f32[19]{0:T(128)S(1)}, f32[19]{0:T(128)}, u32[]{:S(2)}) copy-start(f32[19]{0:T(128)} %param.19) | copy-start | bytes 232
  0.0 9.8 %copy-start.5 = (s32[7]{0:T(128)S(1)}, s32[7]{0:T(128)}, u32[]{:S(2)}) copy-start(s32[7]{0:T(128)} %constant.239.clone) | copy-start | bytes 88
  0.0 9.8 %copy-start.6 = (s32[7]{0:T(128)S(1)}, s32[7]{0:T(128)}, u32[]{:S(2)}) copy-start(s32[7]{0:T(128)} %constant.240.clone) | copy-start | bytes 88
  0.0 9.8 %copy-start.7 = (s32[7]{0:T(128)S(1)}, s32[7]{0:T(128)}, u32[]{:S(2)}) copy-start(s32[7]{0:T(128)} %constant.241.clone) | copy-start | bytes 88
  0.0 9.8 %copy-start.8 = (s32[7]{0:T(128)S(1)}, s32[7]{0:T(128)}, u32[]{:S(2)}) copy-start(s32[7]{0:T(128)} %constant.242.clone) | copy-start | bytes 88
  2.7 8.9 %copy-start = (bf16[32,8,16,256]{3,1,2,0:T(8,128)(2,1)}, bf16[32,8,16,256]{3,1,2,0:T(8,128)(2,1)S(1)}, u32[]{:S(2)}) copy-start(bf16[32,8,16,256]{3,1,2,0:T(8,128)(2,1)S(1)} %copy.15) | copy-start | bytes 6291460
  2.7 7.7 %collective-permute-start = (bf16[256,512]{1,0:T(8,128)(2,1)S(1)}, bf16[256,512]{1,0:T(8,128)(2,1)S(1)}, u32[]{:S(2)}, u32[]{:S(2)}) collective-permute-start(bf16[256,512]{1,0:T(8,128)(2,1)S(1)} %get-tuple-element.17), channel_id=1, source_target_pairs={{0,2},{2,4},{4,6},{6,8},{8,10},{10,12},{12,14},{1,3},{3,5},{5,7},{... | collective-permute-start | bytes 786440 | tf_op jit(solution)/shard_map/ppermute | solution.py:261
  5.1 5.6 %collective-permute-start.1 = (bf16[256,512]{1,0:T(8,128)(2,1)S(1)}, bf16[256,512]{1,0:T(8,128)(2,1)S(1)}, u32[]{:S(2)}, u32[]{:S(2)}) collective-permute-start(bf16[256,512]{1,0:T(8,128)(2,1)S(1)} %get-tuple-element.16), channel_id=1, source_target_pairs={{2,0},{4,2},{6,4},{8,6},{10,8},{12,10},{14,12},{3,1},{5,3},{7,5},{... | collective-permute-start | bytes 786440 | tf_op jit(solution)/shard_map/ppermute | solution.py:262
  10.4 1.2 %copy-start.9 = (bf16[256,512]{1,0:T(8,128)(2,1)}, bf16[256,512]{1,0:T(8,128)(2,1)S(1)}, u32[]{:S(2)}) copy-start(bf16[256,512]{1,0:T(8,128)(2,1)S(1)} %collective-permute-done.top_ref) | copy-start | bytes 786436
  10.7 0.9 %copy-start.10 = (bf16[256,512]{1,0:T(8,128)(2,1)}, bf16[256,512]{1,0:T(8,128)(2,1)S(1)}, u32[]{:S(2)}) copy-start(bf16[256,512]{1,0:T(8,128)(2,1)S(1)} %collective-permute-done.1.low_ref) | copy-start | bytes 786436
  31.2 10.1 %collective-permute-start.2 = (bf16[19,1,16,256]{3,2,0,1:T(8,128)(2,1)S(1)}, bf16[19,1,16,256]{3,2,0,1:T(8,128)(2,1)S(1)}, u32[]{:S(2)}, u32[]{:S(2)}) collective-permute-start(bf16[19,1,16,256]{3,2,0,1:T(8,128)(2,1)S(1)} %get-tuple-element.22), channel_id=1, source_target_pairs={{2,10},{4,12},{6,14},{8,0},{3,11},{5,13},{7,15},{9,1},{18,26},{20,... | collective-permute-start | bytes 466952 | tf_op jit(solution)/shard_map/ppermute | solution.py:49
  41.4 9.9 %collective-permute-start.3 = (bf16[19,1,16,256]{3,2,0,1:T(8,128)(2,1)S(1)}, bf16[19,1,16,256]{3,2,0,1:T(8,128)(2,1)S(1)}, u32[]{:S(2)}, u32[]{:S(2)}) collective-permute-start(bf16[19,1,16,256]{3,2,0,1:T(8,128)(2,1)S(1)} %get-tuple-element.20), channel_id=1, source_target_pairs={{0,4},{2,6},{4,0},{10,14},{12,8},{14,10},{1,5},{3,7},{5,1},{11,15}... | collective-permute-start | bytes 466952 | tf_op jit(solution)/shard_map/ppermute | solution.py:55
  46.7 4.7 %collective-permute-start.4 = (bf16[19,1,16,256]{3,2,0,1:T(8,128)(2,1)S(1)}, bf16[19,1,16,256]{3,2,0,1:T(8,128)(2,1)S(1)}, u32[]{:S(2)}, u32[]{:S(2)}) collective-permute-start(bf16[19,1,16,256]{3,2,0,1:T(8,128)(2,1)S(1)} %get-tuple-element.21), channel_id=1, source_target_pairs={{0,4},{8,12},{10,14},{12,8},{1,5},{9,13},{11,15},{13,9},{16,20},{2... | collective-permute-start | bytes 466952 | tf_op jit(solution)/shard_map/ppermute | solution.py:55
  51.6 2.1 %collective-permute-start.5 = (bf16[19,4,16,256]{3,2,1,0:T(8,128)(2,1)S(1)}, bf16[19,4,16,256]{3,2,1,0:T(8,128)(2,1)S(1)}, u32[]{:S(2)}, u32[]{:S(2)}) collective-permute-start(bf16[19,4,16,256]{3,2,1,0:T(8,128)(2,1)S(1)} %bitcast.49), channel_id=1, source_target_pairs={{0,2},{2,0},{4,6},{6,4},{8,10},{10,8},{12,14},{14,12},{1,3},{3,1},... | collective-permute-start | bytes 1867784 | tf_op jit(solution)/shard_map/ppermute | solution.py:49
  54.0 6.1 %collective-permute-start.6 = (bf16[19,10,256]{2,1,0:T(8,128)(2,1)S(1)}, bf16[19,10,256]{2,1,0:T(8,128)(2,1)S(1)}, u32[]{:S(2)}, u32[]{:S(2)}) collective-permute-start(bf16[19,10,256]{2,1,0:T(8,128)(2,1)S(1)} %fusion.28), channel_id=1, source_target_pairs={{0,1},{1,0},{2,3},{3,2},{4,5},{5,4},{6,7},{7,6},{8,9},{9,8},{10,11... | collective-permute-start | bytes 291848 | tf_op jit(solution)/shard_map/ppermute | solution.py:296

commit v19 on v16

--- a/solution.py
+++ b/solution.py
@@ -167,7 +167,7 @@
 
 
 def pick_block(rows):
-    return next(k for k in (4, 3, 2, 1) if rows % k == 0)
+    return next(k for k in (6, 4, 3, 2, 1) if rows % k == 0)
 
 
 def conv_first_layer(feat, top, low, width, weights, biases, limits):

time: 63.4 us -> 63.4 us (level)
  no operation moved by 1% of the time
where the time goes in v19:
time: 63.4 us; the launch traced here: 63 us
  Pallas kernels  18.7 us (29%)
  starting transfers between devices  14 us (22%)
  waiting for transfers between devices  11.8 us (19%)
  between operations  8.08 us (13%)
  local copies, waits for them, and re-layouts  4.75 us (7%)
  matrix products  3.86 us (6%)
  other arithmetic  1.79 us (3%)
    pallas_call x1, Pallas kernels, conv_first_layer(): pl.pallas_call(functools.partial(first_body, width=width, block=block, ha...  9.7 us
    pallas_call x1, Pallas kernels, conv_second_layer(): pl.pallas_call(functools.partial(second_body, width=width, block=block),...  9.01 us
    ppermute x2, waiting for transfers between devices, gather_rows(): other = lax.ppermute(held, axis, pairs)  8.12 us
    ppermute x2, starting transfers between devices, gather_rows(): parts[p] = lax.ppermute(held[:, p:p + 1], axis, list(pairs))  7.41 us
    dot_general x2, matrix products, shards(): jnp.einsum('iy,cyj->icj', row_part, widened, preferred_element_type=jnp.f...  3.86 us
    unnamed x24, local copies, waits for them, and re-layouts  3.61 us
    ppermute x1, waiting for transfers between devices, shards(): lax.ppermute(send, 'member', [(i, (i + shift) % members) for i in range(m...  3.37 us
    ppermute x1, starting transfers between devices, shards(): lax.ppermute(flat_feat[:, (rows_dev - halo) * cols:], 'space', forward)  2.37 us
  transfers between devices with their start and end apart: 7, of which 4 were waited for; matrix products, arithmetic and copies ran while one was open for 4% of the time, Pallas kernels for 0%

profile of v19, /device:TPU:0, one launch (start us, length us, event | category | flops | bytes accessed | tf_op | source)
XLA Modules:
  0.0 63.0 jit_solution(10601960668884454454)
XLA Ops:
  0.0 0.0 copy-start.6
  0.0 0.0 copy-start.7
  0.0 0.0 copy-start.8
  0.1 2.6 %copy.15 = bf16[32,8,16,256]{3,1,2,0:T(8,128)(2,1)S(1)} copy(bf16[32,8,16,256]{3,2,1,0:T(8,128)(2,1)} %bitcast.51) | data formatting | bytes 4194304
  2.7 2.4 %collective-permute-start = (bf16[256,512]{1,0:T(8,128)(2,1)S(1)}, bf16[256,512]{1,0:T(8,128)(2,1)S(1)}, u32[]{:S(2)}, u32[]{:S(2)}) collective-permute-start(bf16[256,512]{1,0:T(8,128)(2,1)S(1)} %get-tuple-element.17), channel_id=1, source_target_pairs={{0,2},{2,4},{4,6},{6,8},{8,10},{10,12},{12,14},{1,3},{3,5},{5,7},{... | collective-permute-start | bytes 786440 | tf_op jit(solution)/shard_map/ppermute | solution.py:261
  5.1 1.3 %collective-permute-start.1 = (bf16[256,512]{1,0:T(8,128)(2,1)S(1)}, bf16[256,512]{1,0:T(8,128)(2,1)S(1)}, u32[]{:S(2)}, u32[]{:S(2)}) collective-permute-start(bf16[256,512]{1,0:T(8,128)(2,1)S(1)} %get-tuple-element.16), channel_id=1, source_target_pairs={{2,0},{4,2},{6,4},{8,6},{10,8},{12,10},{14,12},{3,1},{5,3},{7,5},{... | collective-permute-start | bytes 786440 | tf_op jit(solution)/shard_map/ppermute | solution.py:262
  6.4 0.7 %fusion.63 = (s32[]{:T(128)}, s32[]{:T(128)}, s32[]{:T(128)}) fusion(s32[2]{0:T(128)S(1)} %copy-done.3, s32[]{:T(128)S(6)} %select_n.540, s32[]{:T(128)S(6)} %select_n.493, s32[]{:T(128)S(6)} %axis_index.29), kind=kLoop, calls=%fused_computation.107 | loop fusion | flops 15 | bytes 32 | tf_op jit(solution)/shard_map/reduce_sum | solution.py:300
  7.1 0.0 copy-done.2
  9.8 0.6 fusion.64.s_ref
  10.4 0.0 collective-permute-done.top_ref
  10.4 0.3 collective-permute-done.1.low_ref
  10.7 0.8 %broadcast_in_dim.127.b_ref = f32[531,128]{1,0:T(8,128)} broadcast(f32[531]{0:T(1024)S(1)} %pad_maximum_fusion), dimensions={0} | broadcast | bytes 273996 | tf_op jit(solution)/shard_map/broadcast_in_dim | solution.py:270
  11.6 9.7 %shard_map.118.x_ref = bf16[256,4608]{1,0:T(8,128)(2,1)} custom-call(bf16[256,4096]{1,0:T(8,128)(2,1)} %bitcast.48, bf16[256,512]{1,0:T(8,128)(2,1)} %copy-done.9, bf16[256,512]{1,0:T(8,128)(2,1)} %copy-done.10, bf16[3,3,256,256]{3,2,1,0:T(8,128)(2,1)} %w_ref.2, f32[531,128]{1,0:T(8,128)} %broadcast_in_dim.127.b_ref, s32[7]{0:T(128)} %fusion.64.s_ref), custom_call_target="tpu_custom_call" | custom-call | flops 5435817984 | bytes 6160384 | tf_op jit(solution)/shard_map/pallas_call | solution.py:187
  21.3 9.0 %shard_map.119 = bf16[19,4096]{1,0:T(8,128)(2,1)} custom-call(bf16[256,4608]{1,0:T(8,128)(2,1)} %shard_map.118.x_ref, bf16[3,3,256,256]{3,2,1,0:T(8,128)(2,1)} %w_ref.3, f32[531,128]{1,0:T(8,128)} %broadcast_in_dim.127.b_ref, bf16[19,256]{1,0:T(8,128)(2,1)} %k_ref.1, s32[7]{0:T(128)} %fusion.64.s_ref), custom_call_target="tpu_custom_call" | custom-call | flops 4871684096 | bytes 3694592 | tf_op jit(solution)/shard_map/pallas_call | solution.py:217
  30.3 1.0 %copy.16 = bf16[3,8,16,256]{3,2,1,0:T(8,128)(2,1)S(1)} copy(bf16[3,8,16,256]{3,1,2,0:T(8,128)(2,1)} %bitcast.56) | data formatting | bytes 393216
  31.3 1.3 %collective-permute-start.2 = (bf16[19,1,16,256]{3,2,0,1:T(8,128)(2,1)S(1)}, bf16[19,1,16,256]{3,2,0,1:T(8,128)(2,1)S(1)}, u32[]{:S(2)}, u32[]{:S(2)}) collective-permute-start(bf16[19,1,16,256]{3,2,0,1:T(8,128)(2,1)S(1)} %get-tuple-element.22), channel_id=1, source_target_pairs={{2,10},{4,12},{6,14},{8,0},{3,11},{5,13},{7,15},{9,1},{18,26},{20,... | collective-permute-start | bytes 466952 | tf_op jit(solution)/shard_map/ppermute | solution.py:49
  35.2 6.2 %collective-permute-done.2 = bf16[19,1,16,256]{3,2,0,1:T(8,128)(2,1)S(1)} collective-permute-done((bf16[19,1,16,256]{3,2,0,1:T(8,128)(2,1)S(1)}, bf16[19,1,16,256]{3,2,0,1:T(8,128)(2,1)S(1)}, u32[]{:S(2)}, u32[]{:S(2)}) %collective-permute-start.2) | collective-permute-done | bytes 155680 | tf_op jit(solution)/shard_map/ppermute | solution.py:49
  41.5 5.3 %collective-permute-start.3 = (bf16[19,1,16,256]{3,2,0,1:T(8,128)(2,1)S(1)}, bf16[19,1,16,256]{3,2,0,1:T(8,128)(2,1)S(1)}, u32[]{:S(2)}, u32[]{:S(2)}) collective-permute-start(bf16[19,1,16,256]{3,2,0,1:T(8,128)(2,1)S(1)} %get-tuple-element.20), channel_id=1, source_target_pairs={{0,4},{2,6},{4,0},{10,14},{12,8},{14,10},{1,5},{3,7},{5,1},{11,15}... | collective-permute-start | bytes 466952 | tf_op jit(solution)/shard_map/ppermute | solution.py:55
  46.8 2.1 %collective-permute-start.4 = (bf16[19,1,16,256]{3,2,0,1:T(8,128)(2,1)S(1)}, bf16[19,1,16,256]{3,2,0,1:T(8,128)(2,1)S(1)}, u32[]{:S(2)}, u32[]{:S(2)}) collective-permute-start(bf16[19,1,16,256]{3,2,0,1:T(8,128)(2,1)S(1)} %get-tuple-element.21), channel_id=1, source_target_pairs={{0,4},{8,12},{10,14},{12,8},{1,5},{9,13},{11,15},{13,9},{16,20},{2... | collective-permute-start | bytes 466952 | tf_op jit(solution)/shard_map/ppermute | solution.py:55
  51.5 0.0 collective-permute-done.3
  51.5 0.0 collective-permute-done.4
  51.6 0.1 maximum_select_fusion.1
  51.6 0.1 copy.13
  51.7 0.1 collective-permute-start.5
  52.0 1.9 %collective-permute-done.5 = bf16[19,4,16,256]{3,2,1,0:T(8,128)(2,1)S(1)} collective-permute-done((bf16[19,4,16,256]{3,2,1,0:T(8,128)(2,1)S(1)}, bf16[19,4,16,256]{3,2,1,0:T(8,128)(2,1)S(1)}, u32[]{:S(2)}, u32[]{:S(2)}) %collective-permute-start.5) | collective-permute-done | bytes 622624 | tf_op jit(solution)/shard_map/ppermute | solution.py:49
  53.8 0.1 maximum_select_fusion
  54.0 0.1 dynamic-slice_bitcast_fusion
  54.1 0.1 fusion.28
  54.2 1.6 %collective-permute-start.6 = (bf16[19,10,256]{2,1,0:T(8,128)(2,1)S(1)}, bf16[19,10,256]{2,1,0:T(8,128)(2,1)S(1)}, u32[]{:S(2)}, u32[]{:S(2)}) collective-permute-start(bf16[19,10,256]{2,1,0:T(8,128)(2,1)S(1)} %fusion.28), channel_id=1, source_target_pairs={{0,1},{1,0},{2,3},{3,2},{4,5},{5,4},{6,7},{7,6},{8,9},{9,8},{10,11... | collective-permute-start | bytes 291848 | tf_op jit(solution)/shard_map/ppermute | solution.py:296
  55.8 1.2 %fusion = f32[32,19,1024]{2,0,1:T(8,128)S(1)} fusion(f32[1024]{0:T(1024)S(1)} %get-tuple-element.24, s32[1024]{0:T(1024)S(1)} %get-tuple-element.27, f32[1024]{0:T(1024)S(1)} %get-tuple-element.25, s32[1024]{0:T(1024)S(1)} %get-tuple-element.26, s32[]{:T(128)S(6)} %select_n.528, bf16[1,19,10,256]{3,2,1,0:T(8,128)(2,1)S(1)} %get-tuple-element.19, ...), kind=kOutput, calls=%fused_computation.3 | convolution fusion | flops 113884864 | bytes 2701832 | tf_op jit(solution)/shard_map/iy,cyj->icj/dot_general | solution.py:311
  57.0 3.4 %collective-permute-done.6 = bf16[19,10,256]{2,1,0:T(8,128)(2,1)S(1)} collective-permute-done((bf16[19,10,256]{2,1,0:T(8,128)(2,1)S(1)}, bf16[19,10,256]{2,1,0:T(8,128)(2,1)S(1)}, u32[]{:S(2)}, u32[]{:S(2)}) %collective-permute-start.6) | collective-permute-done | bytes 97312 | tf_op jit(solution)/shard_map/ppermute | solution.py:296
  60.3 2.7 %convolution_add_fusion = f32[32,19,1024]{2,0,1:T(8,128)} fusion(f32[32,19,1024]{2,0,1:T(8,128)S(1)} %fusion, bf16[19,10,256]{2,1,0:T(8,128)(2,1)S(1)} %collective-permute-done.6, f32[1024]{0:T(1024)S(1)} %get-tuple-element.28, s32[1024]{0:T(1024)S(1)} %get-tuple-element.31, f32[1024]{0:T(1024)S(1)} %get-tuple-element.29, s32[1024]{0:T(1024)S(1)} %get-tuple-element.30, ...), kind=kOutput, calls=%fused_computation | convolution fusion | flops 114458816 | bytes 5094916 | tf_op jit(solution)/shard_map/iy,cyj->icj/dot_general | solution.py:311
  (33 shorter events, 0.4 us)
Async XLA Ops:
  0.0 6.4 %copy-start.3 = (s32[2]{0:T(128)S(1)}, s32[2]{0:T(128)}, u32[]{:S(2)}) copy-start(s32[2]{0:T(128)} %param.13) | copy-start | bytes 28
  0.0 7.1 %copy-start.1 = (f32[256]{0:T(256)S(1)}, f32[256]{0:T(256)}, u32[]{:S(2)}) copy-start(f32[256]{0:T(256)} %param.17) | copy-start | bytes 3076
  0.0 7.1 %copy-start.2 = (f32[256]{0:T(256)S(1)}, f32[256]{0:T(256)}, u32[]{:S(2)}) copy-start(f32[256]{0:T(256)} %param.15) | copy-start | bytes 3076
  0.0 7.1 %copy-start.4 = (f32[19]{0:T(128)S(1)}, f32[19]{0:T(128)}, u32[]{:S(2)}) copy-start(f32[19]{0:T(128)} %param.19) | copy-start | bytes 232
  0.0 9.8 %copy-start.5 = (s32[7]{0:T(128)S(1)}, s32[7]{0:T(128)}, u32[]{:S(2)}) copy-start(s32[7]{0:T(128)} %constant.239.clone) | copy-start | bytes 88
  0.0 9.8 %copy-start.6 = (s32[7]{0:T(128)S(1)}, s32[7]{0:T(128)}, u32[]{:S(2)}) copy-start(s32[7]{0:T(128)} %constant.240.clone) | copy-start | bytes 88
  0.0 9.8 %copy-start.7 = (s32[7]{0:T(128)S(1)}, s32[7]{0:T(128)}, u32[]{:S(2)}) copy-start(s32[7]{0:T(128)} %constant.241.clone) | copy-start | bytes 88
  0.0 9.8 %copy-start.8 = (s32[7]{0:T(128)S(1)}, s32[7]{0:T(128)}, u32[]{:S(2)}) copy-start(s32[7]{0:T(128)} %constant.242.clone) | copy-start | bytes 88
  2.7 8.9 %copy-start = (bf16[32,8,16,256]{3,1,2,0:T(8,128)(2,1)}, bf16[32,8,16,256]{3,1,2,0:T(8,128)(2,1)S(1)}, u32[]{:S(2)}) copy-start(bf16[32,8,16,256]{3,1,2,0:T(8,128)(2,1)S(1)} %copy.15) | copy-start | bytes 6291460
  2.7 7.7 %collective-permute-start = (bf16[256,512]{1,0:T(8,128)(2,1)S(1)}, bf16[256,512]{1,0:T(8,128)(2,1)S(1)}, u32[]{:S(2)}, u32[]{:S(2)}) collective-permute-start(bf16[256,512]{1,0:T(8,128)(2,1)S(1)} %get-tuple-element.17), channel_id=1, source_target_pairs={{0,2},{2,4},{4,6},{6,8},{8,10},{10,12},{12,14},{1,3},{3,5},{5,7},{... | collective-permute-start | bytes 786440 | tf_op jit(solution)/shard_map/ppermute | solution.py:261
  5.1 5.6 %collective-permute-start.1 = (bf16[256,512]{1,0:T(8,128)(2,1)S(1)}, bf16[256,512]{1,0:T(8,128)(2,1)S(1)}, u32[]{:S(2)}, u32[]{:S(2)}) collective-permute-start(bf16[256,512]{1,0:T(8,128)(2,1)S(1)} %get-tuple-element.16), channel_id=1, source_target_pairs={{2,0},{4,2},{6,4},{8,6},{10,8},{12,10},{14,12},{3,1},{5,3},{7,5},{... | collective-permute-start | bytes 786440 | tf_op jit(solution)/shard_map/ppermute | solution.py:262
  10.4 1.2 %copy-start.9 = (bf16[256,512]{1,0:T(8,128)(2,1)}, bf16[256,512]{1,0:T(8,128)(2,1)S(1)}, u32[]{:S(2)}) copy-start(bf16[256,512]{1,0:T(8,128)(2,1)S(1)} %collective-permute-done.top_ref) | copy-start | bytes 786436
  10.7 0.9 %copy-start.10 = (bf16[256,512]{1,0:T(8,128)(2,1)}, bf16[256,512]{1,0:T(8,128)(2,1)S(1)}, u32[]{:S(2)}) copy-start(bf16[256,512]{1,0:T(8,128)(2,1)S(1)} %collective-permute-done.1.low_ref) | copy-start | bytes 786436
  31.3 10.1 %collective-permute-start.2 = (bf16[19,1,16,256]{3,2,0,1:T(8,128)(2,1)S(1)}, bf16[19,1,16,256]{3,2,0,1:T(8,128)(2,1)S(1)}, u32[]{:S(2)}, u32[]{:S(2)}) collective-permute-start(bf16[19,1,16,256]{3,2,0,1:T(8,128)(2,1)S(1)} %get-tuple-element.22), channel_id=1, source_target_pairs={{2,10},{4,12},{6,14},{8,0},{3,11},{5,13},{7,15},{9,1},{18,26},{20,... | collective-permute-start | bytes 466952 | tf_op jit(solution)/shard_map/ppermute | solution.py:49
  41.5 10.0 %collective-permute-start.3 = (bf16[19,1,16,256]{3,2,0,1:T(8,128)(2,1)S(1)}, bf16[19,1,16,256]{3,2,0,1:T(8,128)(2,1)S(1)}, u32[]{:S(2)}, u32[]{:S(2)}) collective-permute-start(bf16[19,1,16,256]{3,2,0,1:T(8,128)(2,1)S(1)} %get-tuple-element.20), channel_id=1, source_target_pairs={{0,4},{2,6},{4,0},{10,14},{12,8},{14,10},{1,5},{3,7},{5,1},{11,15}... | collective-permute-start | bytes 466952 | tf_op jit(solution)/shard_map/ppermute | solution.py:55
  46.8 4.7 %collective-permute-start.4 = (bf16[19,1,16,256]{3,2,0,1:T(8,128)(2,1)S(1)}, bf16[19,1,16,256]{3,2,0,1:T(8,128)(2,1)S(1)}, u32[]{:S(2)}, u32[]{:S(2)}) collective-permute-start(bf16[19,1,16,256]{3,2,0,1:T(8,128)(2,1)S(1)} %get-tuple-element.21), channel_id=1, source_target_pairs={{0,4},{8,12},{10,14},{12,8},{1,5},{9,13},{11,15},{13,9},{16,20},{2... | collective-permute-start | bytes 466952 | tf_op jit(solution)/shard_map/ppermute | solution.py:55
  51.7 2.1 %collective-permute-start.5 = (bf16[19,4,16,256]{3,2,1,0:T(8,128)(2,1)S(1)}, bf16[19,4,16,256]{3,2,1,0:T(8,128)(2,1)S(1)}, u32[]{:S(2)}, u32[]{:S(2)}) collective-permute-start(bf16[19,4,16,256]{3,2,1,0:T(8,128)(2,1)S(1)} %bitcast.49), channel_id=1, source_target_pairs={{0,2},{2,0},{4,6},{6,4},{8,10},{10,8},{12,14},{14,12},{1,3},{3,1},... | collective-permute-start | bytes 1867784 | tf_op jit(solution)/shard_map/ppermute | solution.py:49
  54.2 6.1 %collective-permute-start.6 = (bf16[19,10,256]{2,1,0:T(8,128)(2,1)S(1)}, bf16[19,10,256]{2,1,0:T(8,128)(2,1)S(1)}, u32[]{:S(2)}, u32[]{:S(2)}) collective-permute-start(bf16[19,10,256]{2,1,0:T(8,128)(2,1)S(1)} %fusion.28), channel_id=1, source_target_pairs={{0,1},{1,0},{2,3},{3,2},{4,5},{5,4},{6,7},{7,6},{8,9},{9,8},{10,11... | collective-permute-start | bytes 291848 | tf_op jit(solution)/shard_map/ppermute | solution.py:296

commit v20 on v16

--- a/solution.py
+++ b/solution.py
@@ -286,16 +286,14 @@
     own_first = place * own_rows + member_index * part_rows
     positions = own_first + jnp.arange(part_rows, dtype=jnp.int32)
     result = jnp.zeros((part_rows, logits.shape[0], out_cols), jnp.float32)
-    for shift in range(members):
-        if shift == 0:
-            arrived = lax.dynamic_index_in_dim(outgoing, member_index, 0, keepdims=False)
-        else:
-            send = lax.dynamic_index_in_dim(
-                outgoing, (member_index + shift) % members, 0, keepdims=False
-            )
-            arrived = lax.ppermute(
-                send, "member", [(i, (i + shift) % members) for i in range(members)]
-            )
+    arrivals = [lax.dynamic_index_in_dim(outgoing, member_index, 0, keepdims=False)]
+    for shift in range(1, members):
+        send = lax.dynamic_index_in_dim(outgoing, (member_index + shift) % members, 0, keepdims=False)
+        arrivals.append(
+            lax.ppermute(send, "member", [(i, (i + shift) % members) for i in range(members)])
+        )
+
+    def contribution(shift, arrived):
         source = (member_index - shift) % members
         source_code = jnp.sum(jnp.where(jnp.arange(members) == source, views, 0))
         source_numer = source_code // 2
@@ -308,9 +306,13 @@
         widened = jnp.einsum(
             "cyx,jx->cyj", arrived, source_cols, preferred_element_type=jnp.float32
         ).astype(jnp.bfloat16)
-        result = result + jnp.einsum(
-            "iy,cyj->icj", row_part, widened, preferred_element_type=jnp.float32
-        )
+        return jnp.einsum("iy,cyj->icj", row_part, widened, preferred_element_type=jnp.float32)
+
+    result = result + contribution(0, arrivals[0])
+    if members > 1:
+        result, *others = lax.optimization_barrier([result] + arrivals[1:])
+        for shift in range(1, members):
+            result = result + contribution(shift, others[shift - 1])
     return result
 
 

time: 63.4 us -> 67.1 us (1.058)
  other arithmetic: 1.79 us -> 5.43 us
    add x0 -> x1, other arithmetic: none -> 3.64 us  [shards(): result = result + contribution(shift, others[shift - 1])]
where the time goes in v20:
time: 67.1 us; the launch traced here: 66.7 us
  Pallas kernels  18.7 us (28%)
  starting transfers between devices  14 us (21%)
  waiting for transfers between devices  11.8 us (18%)
  between operations  8.08 us (12%)
  other arithmetic  5.43 us (8%)
  local copies, waits for them, and re-layouts  4.75 us (7%)
  matrix products  3.86 us (6%)
    pallas_call x1, Pallas kernels, conv_first_layer(): pl.pallas_call(functools.partial(first_body, width=width, block=block, ha...  9.74 us
    pallas_call x1, Pallas kernels, conv_second_layer(): pl.pallas_call(functools.partial(second_body, width=width, block=block),...  9 us
    ppermute x2, waiting for transfers between devices, gather_rows(): other = lax.ppermute(held, axis, pairs)  8.11 us
    ppermute x2, starting transfers between devices, gather_rows(): parts[p] = lax.ppermute(held[:, p:p + 1], axis, list(pairs))  7.42 us
    dot_general x2, matrix products, contribution(): jnp.einsum('iy,cyj->icj', row_part, widened, preferred_element_type=jnp.f...  3.86 us
    add x1, other arithmetic, shards(): result = result + contribution(shift, others[shift - 1])  3.64 us
    unnamed x24, local copies, waits for them, and re-layouts  3.61 us
    ppermute x1, waiting for transfers between devices, shards(): lax.ppermute(send, 'member', [(i, (i + shift) % members) for i in range(m...  3.38 us
  transfers between devices with their start and end apart: 7, of which 4 were waited for; matrix products, arithmetic and copies ran while one was open for 4% of the time, Pallas kernels for 0%

profile of v20, /device:TPU:0, one launch (start us, length us, event | category | flops | bytes accessed | tf_op | source)
XLA Modules:
  0.0 66.7 jit_solution(11477837470264238883)
XLA Ops:
  0.0 0.0 copy-start.6
  0.0 0.0 copy-start.7
  0.0 0.0 copy-start.8
  0.1 2.6 %copy.15 = bf16[32,8,16,256]{3,1,2,0:T(8,128)(2,1)S(1)} copy(bf16[32,8,16,256]{3,2,1,0:T(8,128)(2,1)} %bitcast.51) | data formatting | bytes 4194304
  2.7 2.4 %collective-permute-start = (bf16[256,512]{1,0:T(8,128)(2,1)S(1)}, bf16[256,512]{1,0:T(8,128)(2,1)S(1)}, u32[]{:S(2)}, u32[]{:S(2)}) collective-permute-start(bf16[256,512]{1,0:T(8,128)(2,1)S(1)} %get-tuple-element.21), channel_id=1, source_target_pairs={{0,2},{2,4},{4,6},{6,8},{8,10},{10,12},{12,14},{1,3},{3,5},{5,7},{... | collective-permute-start | bytes 786440 | tf_op jit(solution)/shard_map/ppermute | solution.py:261
  5.1 1.3 %collective-permute-start.1 = (bf16[256,512]{1,0:T(8,128)(2,1)S(1)}, bf16[256,512]{1,0:T(8,128)(2,1)S(1)}, u32[]{:S(2)}, u32[]{:S(2)}) collective-permute-start(bf16[256,512]{1,0:T(8,128)(2,1)S(1)} %get-tuple-element.20), channel_id=1, source_target_pairs={{2,0},{4,2},{6,4},{8,6},{10,8},{12,10},{14,12},{3,1},{5,3},{7,5},{... | collective-permute-start | bytes 786440 | tf_op jit(solution)/shard_map/ppermute | solution.py:262
  6.4 0.7 %fusion.64 = (s32[]{:T(128)}, s32[]{:T(128)}, s32[]{:T(128)}) fusion(s32[2]{0:T(128)S(1)} %copy-done.3, s32[]{:T(128)S(6)} %select_n.542, s32[]{:T(128)S(6)} %select_n.493, s32[]{:T(128)S(6)} %axis_index.29), kind=kLoop, calls=%fused_computation.107 | loop fusion | flops 15 | bytes 32 | tf_op jit(solution)/shard_map/reduce_sum | solution.py:298
  9.8 0.6 fusion.65.s_ref
  10.4 0.0 collective-permute-done.top_ref
  10.4 0.3 collective-permute-done.1.low_ref
  10.7 0.8 %broadcast_in_dim.127.b_ref = f32[531,128]{1,0:T(8,128)} broadcast(f32[531]{0:T(1024)S(1)} %pad_maximum_fusion), dimensions={0} | broadcast | bytes 273996 | tf_op jit(solution)/shard_map/broadcast_in_dim | solution.py:270
  11.6 9.7 %shard_map.118.x_ref = bf16[256,4608]{1,0:T(8,128)(2,1)} custom-call(bf16[256,4096]{1,0:T(8,128)(2,1)} %bitcast.48, bf16[256,512]{1,0:T(8,128)(2,1)} %copy-done.9, bf16[256,512]{1,0:T(8,128)(2,1)} %copy-done.10, bf16[3,3,256,256]{3,2,1,0:T(8,128)(2,1)} %w_ref.2, f32[531,128]{1,0:T(8,128)} %broadcast_in_dim.127.b_ref, s32[7]{0:T(128)} %fusion.65.s_ref), custom_call_target="tpu_custom_call" | custom-call | flops 5435817984 | bytes 6160384 | tf_op jit(solution)/shard_map/pallas_call | solution.py:187
  21.3 9.0 %shard_map.119 = bf16[19,4096]{1,0:T(8,128)(2,1)} custom-call(bf16[256,4608]{1,0:T(8,128)(2,1)} %shard_map.118.x_ref, bf16[3,3,256,256]{3,2,1,0:T(8,128)(2,1)} %w_ref.3, f32[531,128]{1,0:T(8,128)} %broadcast_in_dim.127.b_ref, bf16[19,256]{1,0:T(8,128)(2,1)} %k_ref.1, s32[7]{0:T(128)} %fusion.65.s_ref), custom_call_target="tpu_custom_call" | custom-call | flops 4871684096 | bytes 3694592 | tf_op jit(solution)/shard_map/pallas_call | solution.py:217
  30.3 1.0 %copy.16 = bf16[3,8,16,256]{3,2,1,0:T(8,128)(2,1)S(1)} copy(bf16[3,8,16,256]{3,1,2,0:T(8,128)(2,1)} %bitcast.56) | data formatting | bytes 393216
  31.3 1.3 %collective-permute-start.2 = (bf16[19,1,16,256]{3,2,0,1:T(8,128)(2,1)S(1)}, bf16[19,1,16,256]{3,2,0,1:T(8,128)(2,1)S(1)}, u32[]{:S(2)}, u32[]{:S(2)}) collective-permute-start(bf16[19,1,16,256]{3,2,0,1:T(8,128)(2,1)S(1)} %get-tuple-element.26), channel_id=1, source_target_pairs={{2,10},{4,12},{6,14},{8,0},{3,11},{5,13},{7,15},{9,1},{18,26},{20,... | collective-permute-start | bytes 466952 | tf_op jit(solution)/shard_map/ppermute | solution.py:49
  35.2 6.2 %collective-permute-done.2 = bf16[19,1,16,256]{3,2,0,1:T(8,128)(2,1)S(1)} collective-permute-done((bf16[19,1,16,256]{3,2,0,1:T(8,128)(2,1)S(1)}, bf16[19,1,16,256]{3,2,0,1:T(8,128)(2,1)S(1)}, u32[]{:S(2)}, u32[]{:S(2)}) %collective-permute-start.2) | collective-permute-done | bytes 155680 | tf_op jit(solution)/shard_map/ppermute | solution.py:49
  41.5 5.3 %collective-permute-start.3 = (bf16[19,1,16,256]{3,2,0,1:T(8,128)(2,1)S(1)}, bf16[19,1,16,256]{3,2,0,1:T(8,128)(2,1)S(1)}, u32[]{:S(2)}, u32[]{:S(2)}) collective-permute-start(bf16[19,1,16,256]{3,2,0,1:T(8,128)(2,1)S(1)} %get-tuple-element.24), channel_id=1, source_target_pairs={{0,4},{2,6},{4,0},{10,14},{12,8},{14,10},{1,5},{3,7},{5,1},{11,15}... | collective-permute-start | bytes 466952 | tf_op jit(solution)/shard_map/ppermute | solution.py:55
  46.8 2.1 %collective-permute-start.4 = (bf16[19,1,16,256]{3,2,0,1:T(8,128)(2,1)S(1)}, bf16[19,1,16,256]{3,2,0,1:T(8,128)(2,1)S(1)}, u32[]{:S(2)}, u32[]{:S(2)}) collective-permute-start(bf16[19,1,16,256]{3,2,0,1:T(8,128)(2,1)S(1)} %get-tuple-element.25), channel_id=1, source_target_pairs={{0,4},{8,12},{10,14},{12,8},{1,5},{9,13},{11,15},{13,9},{16,20},{2... | collective-permute-start | bytes 466952 | tf_op jit(solution)/shard_map/ppermute | solution.py:55
  51.6 0.0 collective-permute-done.3
  51.6 0.0 collective-permute-done.4
  51.6 0.1 maximum_select_fusion.1
  51.7 0.1 copy.13
  51.8 0.1 collective-permute-start.5
  52.0 1.9 %collective-permute-done.5 = bf16[19,4,16,256]{3,2,1,0:T(8,128)(2,1)S(1)} collective-permute-done((bf16[19,4,16,256]{3,2,1,0:T(8,128)(2,1)S(1)}, bf16[19,4,16,256]{3,2,1,0:T(8,128)(2,1)S(1)}, u32[]{:S(2)}, u32[]{:S(2)}) %collective-permute-start.5) | collective-permute-done | bytes 622624 | tf_op jit(solution)/shard_map/ppermute | solution.py:49
  53.9 0.1 maximum_select_fusion
  54.0 0.1 dynamic-slice_bitcast_fusion
  54.1 0.1 fusion.29
  54.2 1.6 %collective-permute-start.6 = (bf16[19,10,256]{2,1,0:T(8,128)(2,1)S(1)}, bf16[19,10,256]{2,1,0:T(8,128)(2,1)S(1)}, u32[]{:S(2)}, u32[]{:S(2)}) collective-permute-start(bf16[19,10,256]{2,1,0:T(8,128)(2,1)S(1)} %fusion.29), channel_id=1, source_target_pairs={{0,1},{1,0},{2,3},{3,2},{4,5},{5,4},{6,7},{7,6},{8,9},{9,8},{10,11... | collective-permute-start | bytes 291848 | tf_op jit(solution)/shard_map/ppermute | solution.py:293
  55.8 1.2 %fusion = f32[32,19,1024]{2,0,1:T(8,128)S(1)} fusion(f32[1024]{0:T(1024)S(1)} %get-tuple-element.28, s32[1024]{0:T(1024)S(1)} %get-tuple-element.31, f32[1024]{0:T(1024)S(1)} %get-tuple-element.29, s32[1024]{0:T(1024)S(1)} %get-tuple-element.30, s32[]{:T(128)S(6)} %select_n.528, bf16[1,19,10,256]{3,2,1,0:T(8,128)(2,1)S(1)} %get-tuple-element.23, ...), kind=kOutput, calls=%fused_computation.2 | convolution fusion | flops 113884864 | bytes 2701832 | tf_op jit(solution)/shard_map/iy,cyj->icj/dot_general | solution.py:309
  57.0 3.4 %collective-permute-done.6 = bf16[19,10,256]{2,1,0:T(8,128)(2,1)S(1)} collective-permute-done((bf16[19,10,256]{2,1,0:T(8,128)(2,1)S(1)}, bf16[19,10,256]{2,1,0:T(8,128)(2,1)S(1)}, u32[]{:S(2)}, u32[]{:S(2)}) %collective-permute-start.6) | collective-permute-done | bytes 97312 | tf_op jit(solution)/shard_map/ppermute | solution.py:293
  60.4 2.7 %fusion.1 = f32[32,19,1024]{2,0,1:T(8,128)} fusion(bf16[19,10,256]{2,1,0:T(8,128)(2,1)S(1)} %collective-permute-done.6, f32[1024]{0:T(1024)S(1)} %get-tuple-element.32, s32[1024]{0:T(1024)S(1)} %get-tuple-element.35, f32[1024]{0:T(1024)S(1)} %get-tuple-element.33, s32[1024]{0:T(1024)S(1)} %get-tuple-element.34, f32[32]{0:T(128)S(1)} %get-tuple-element.15, ...), kind=kOutput, calls=%fused_computation.3 | convolution fusion | flops 113836224 | bytes 2604548 | tf_op jit(solution)/shard_map/iy,cyj->icj/dot_general | solution.py:309
  63.0 3.6 %add.358 = f32[32,19,1024]{2,0,1:T(8,128)} add(f32[32,19,1024]{2,0,1:T(8,128)S(1)} %fusion, f32[32,19,1024]{2,0,1:T(8,128)} %fusion.1) | non-fusion elementwise | flops 622592 | bytes 7471104 | tf_op jit(solution)/shard_map/add | solution.py:315
  (34 shorter events, 0.4 us)
Async XLA Ops:
  0.0 6.4 %copy-start.3 = (s32[2]{0:T(128)S(1)}, s32[2]{0:T(128)}, u32[]{:S(2)}) copy-start(s32[2]{0:T(128)} %param.13) | copy-start | bytes 28
  0.0 7.1 %copy-start.1 = (f32[256]{0:T(256)S(1)}, f32[256]{0:T(256)}, u32[]{:S(2)}) copy-start(f32[256]{0:T(256)} %param.17) | copy-start | bytes 3076
  0.0 7.1 %copy-start.2 = (f32[256]{0:T(256)S(1)}, f32[256]{0:T(256)}, u32[]{:S(2)}) copy-start(f32[256]{0:T(256)} %param.15) | copy-start | bytes 3076
  0.0 7.1 %copy-start.4 = (f32[19]{0:T(128)S(1)}, f32[19]{0:T(128)}, u32[]{:S(2)}) copy-start(f32[19]{0:T(128)} %param.19) | copy-start | bytes 232
  0.0 9.8 %copy-start.5 = (s32[7]{0:T(128)S(1)}, s32[7]{0:T(128)}, u32[]{:S(2)}) copy-start(s32[7]{0:T(128)} %constant.239.clone) | copy-start | bytes 88
  0.0 9.8 %copy-start.6 = (s32[7]{0:T(128)S(1)}, s32[7]{0:T(128)}, u32[]{:S(2)}) copy-start(s32[7]{0:T(128)} %constant.240.clone) | copy-start | bytes 88
  0.0 9.8 %copy-start.7 = (s32[7]{0:T(128)S(1)}, s32[7]{0:T(128)}, u32[]{:S(2)}) copy-start(s32[7]{0:T(128)} %constant.241.clone) | copy-start | bytes 88
  0.0 9.8 %copy-start.8 = (s32[7]{0:T(128)S(1)}, s32[7]{0:T(128)}, u32[]{:S(2)}) copy-start(s32[7]{0:T(128)} %constant.242.clone) | copy-start | bytes 88
  2.7 8.9 %copy-start = (bf16[32,8,16,256]{3,1,2,0:T(8,128)(2,1)}, bf16[32,8,16,256]{3,1,2,0:T(8,128)(2,1)S(1)}, u32[]{:S(2)}) copy-start(bf16[32,8,16,256]{3,1,2,0:T(8,128)(2,1)S(1)} %copy.15) | copy-start | bytes 6291460
  2.7 7.7 %collective-permute-start = (bf16[256,512]{1,0:T(8,128)(2,1)S(1)}, bf16[256,512]{1,0:T(8,128)(2,1)S(1)}, u32[]{:S(2)}, u32[]{:S(2)}) collective-permute-start(bf16[256,512]{1,0:T(8,128)(2,1)S(1)} %get-tuple-element.21), channel_id=1, source_target_pairs={{0,2},{2,4},{4,6},{6,8},{8,10},{10,12},{12,14},{1,3},{3,5},{5,7},{... | collective-permute-start | bytes 786440 | tf_op jit(solution)/shard_map/ppermute | solution.py:261
  5.1 5.6 %collective-permute-start.1 = (bf16[256,512]{1,0:T(8,128)(2,1)S(1)}, bf16[256,512]{1,0:T(8,128)(2,1)S(1)}, u32[]{:S(2)}, u32[]{:S(2)}) collective-permute-start(bf16[256,512]{1,0:T(8,128)(2,1)S(1)} %get-tuple-element.20), channel_id=1, source_target_pairs={{2,0},{4,2},{6,4},{8,6},{10,8},{12,10},{14,12},{3,1},{5,3},{7,5},{... | collective-permute-start | bytes 786440 | tf_op jit(solution)/shard_map/ppermute | solution.py:262
  10.4 1.2 %copy-start.9 = (bf16[256,512]{1,0:T(8,128)(2,1)}, bf16[256,512]{1,0:T(8,128)(2,1)S(1)}, u32[]{:S(2)}) copy-start(bf16[256,512]{1,0:T(8,128)(2,1)S(1)} %collective-permute-done.top_ref) | copy-start | bytes 786436
  10.7 0.9 %copy-start.10 = (bf16[256,512]{1,0:T(8,128)(2,1)}, bf16[256,512]{1,0:T(8,128)(2,1)S(1)}, u32[]{:S(2)}) copy-start(bf16[256,512]{1,0:T(8,128)(2,1)S(1)} %collective-permute-done.1.low_ref) | copy-start | bytes 786436
  31.3 10.1 %collective-permute-start.2 = (bf16[19,1,16,256]{3,2,0,1:T(8,128)(2,1)S(1)}, bf16[19,1,16,256]{3,2,0,1:T(8,128)(2,1)S(1)}, u32[]{:S(2)}, u32[]{:S(2)}) collective-permute-start(bf16[19,1,16,256]{3,2,0,1:T(8,128)(2,1)S(1)} %get-tuple-element.26), channel_id=1, source_target_pairs={{2,10},{4,12},{6,14},{8,0},{3,11},{5,13},{7,15},{9,1},{18,26},{20,... | collective-permute-start | bytes 466952 | tf_op jit(solution)/shard_map/ppermute | solution.py:49
  41.5 10.1 %collective-permute-start.3 = (bf16[19,1,16,256]{3,2,0,1:T(8,128)(2,1)S(1)}, bf16[19,1,16,256]{3,2,0,1:T(8,128)(2,1)S(1)}, u32[]{:S(2)}, u32[]{:S(2)}) collective-permute-start(bf16[19,1,16,256]{3,2,0,1:T(8,128)(2,1)S(1)} %get-tuple-element.24), channel_id=1, source_target_pairs={{0,4},{2,6},{4,0},{10,14},{12,8},{14,10},{1,5},{3,7},{5,1},{11,15}... | collective-permute-start | bytes 466952 | tf_op jit(solution)/shard_map/ppermute | solution.py:55
  46.8 4.7 %collective-permute-start.4 = (bf16[19,1,16,256]{3,2,0,1:T(8,128)(2,1)S(1)}, bf16[19,1,16,256]{3,2,0,1:T(8,128)(2,1)S(1)}, u32[]{:S(2)}, u32[]{:S(2)}) collective-permute-start(bf16[19,1,16,256]{3,2,0,1:T(8,128)(2,1)S(1)} %get-tuple-element.25), channel_id=1, source_target_pairs={{0,4},{8,12},{10,14},{12,8},{1,5},{9,13},{11,15},{13,9},{16,20},{2... | collective-permute-start | bytes 466952 | tf_op jit(solution)/shard_map/ppermute | solution.py:55
  51.8 2.1 %collective-permute-start.5 = (bf16[19,4,16,256]{3,2,1,0:T(8,128)(2,1)S(1)}, bf16[19,4,16,256]{3,2,1,0:T(8,128)(2,1)S(1)}, u32[]{:S(2)}, u32[]{:S(2)}) collective-permute-start(bf16[19,4,16,256]{3,2,1,0:T(8,128)(2,1)S(1)} %bitcast.49), channel_id=1, source_target_pairs={{0,2},{2,0},{4,6},{6,4},{8,10},{10,8},{12,14},{14,12},{1,3},{3,1},... | collective-permute-start | bytes 1867784 | tf_op jit(solution)/shard_map/ppermute | solution.py:49
  54.2 6.1 %collective-permute-start.6 = (bf16[19,10,256]{2,1,0:T(8,128)(2,1)S(1)}, bf16[19,10,256]{2,1,0:T(8,128)(2,1)S(1)}, u32[]{:S(2)}, u32[]{:S(2)}) collective-permute-start(bf16[19,10,256]{2,1,0:T(8,128)(2,1)S(1)} %fusion.29), channel_id=1, source_target_pairs={{0,1},{1,0},{2,3},{3,2},{4,5},{5,4},{6,7},{7,6},{8,9},{9,8},{10,11... | collective-permute-start | bytes 291848 | tf_op jit(solution)/shard_map/ppermute | solution.py:293

commit v21 on v19

--- a/solution.py
+++ b/solution.py
@@ -167,7 +167,7 @@
 
 
 def pick_block(rows):
-    return next(k for k in (6, 4, 3, 2, 1) if rows % k == 0)
+    return next(k for k in (8, 3, 4, 2, 1) if rows % k == 0)
 
 
 def conv_first_layer(feat, top, low, width, weights, biases, limits):

time: 63.4 us -> 62.8 us (level)
  no operation moved by 1% of the time
where the time goes in v21:
time: 62.8 us; the launch traced here: 62.4 us
  Pallas kernels  18.1 us (29%)
  starting transfers between devices  14 us (22%)
  waiting for transfers between devices  11.8 us (19%)
  between operations  8.08 us (13%)
  local copies, waits for them, and re-layouts  4.75 us (8%)
  matrix products  3.86 us (6%)
  other arithmetic  1.79 us (3%)
    pallas_call x1, Pallas kernels, conv_first_layer(): pl.pallas_call(functools.partial(first_body, width=width, block=block, ha...  9.74 us
    pallas_call x1, Pallas kernels, conv_second_layer(): pl.pallas_call(functools.partial(second_body, width=width, block=block),...  8.39 us
    ppermute x2, waiting for transfers between devices, gather_rows(): other = lax.ppermute(held, axis, pairs)  8.11 us
    ppermute x2, starting transfers between devices, gather_rows(): parts[p] = lax.ppermute(held[:, p:p + 1], axis, list(pairs))  7.42 us
    dot_general x2, matrix products, shards(): jnp.einsum('iy,cyj->icj', row_part, widened, preferred_element_type=jnp.f...  3.86 us
    unnamed x24, local copies, waits for them, and re-layouts  3.61 us
    ppermute x1, waiting for transfers between devices, shards(): lax.ppermute(send, 'member', [(i, (i + shift) % members) for i in range(m...  3.38 us
    ppermute x1, starting transfers between devices, shards(): lax.ppermute(flat_feat[:, (rows_dev - halo) * cols:], 'space', forward)  2.37 us
  transfers between devices with their start and end apart: 7, of which 4 were waited for; matrix products, arithmetic and copies ran while one was open for 4% of the time, Pallas kernels for 0%

profile of v21, /device:TPU:0, one launch (start us, length us, event | category | flops | bytes accessed | tf_op | source)
XLA Modules:
  0.0 62.4 jit_solution(13139465382757066259)
XLA Ops:
  0.0 0.0 copy-start.6
  0.0 0.0 copy-start.7
  0.0 0.0 copy-start.8
  0.1 2.6 %copy.15 = bf16[32,8,16,256]{3,1,2,0:T(8,128)(2,1)S(1)} copy(bf16[32,8,16,256]{3,2,1,0:T(8,128)(2,1)} %bitcast.51) | data formatting | bytes 4194304
  2.7 0.0 copy-start
  2.7 2.4 %collective-permute-start = (bf16[256,512]{1,0:T(8,128)(2,1)S(1)}, bf16[256,512]{1,0:T(8,128)(2,1)S(1)}, u32[]{:S(2)}, u32[]{:S(2)}) collective-permute-start(bf16[256,512]{1,0:T(8,128)(2,1)S(1)} %get-tuple-element.17), channel_id=1, source_target_pairs={{0,2},{2,4},{4,6},{6,8},{8,10},{10,12},{12,14},{1,3},{3,5},{5,7},{... | collective-permute-start | bytes 786440 | tf_op jit(solution)/shard_map/ppermute | solution.py:261
  5.1 1.3 %collective-permute-start.1 = (bf16[256,512]{1,0:T(8,128)(2,1)S(1)}, bf16[256,512]{1,0:T(8,128)(2,1)S(1)}, u32[]{:S(2)}, u32[]{:S(2)}) collective-permute-start(bf16[256,512]{1,0:T(8,128)(2,1)S(1)} %get-tuple-element.16), channel_id=1, source_target_pairs={{2,0},{4,2},{6,4},{8,6},{10,8},{12,10},{14,12},{3,1},{5,3},{7,5},{... | collective-permute-start | bytes 786440 | tf_op jit(solution)/shard_map/ppermute | solution.py:262
  6.4 0.7 %fusion.63 = (s32[]{:T(128)}, s32[]{:T(128)}, s32[]{:T(128)}) fusion(s32[2]{0:T(128)S(1)} %copy-done.3, s32[]{:T(128)S(6)} %select_n.540, s32[]{:T(128)S(6)} %select_n.493, s32[]{:T(128)S(6)} %axis_index.29), kind=kLoop, calls=%fused_computation.107 | loop fusion | flops 15 | bytes 32 | tf_op jit(solution)/shard_map/reduce_sum | solution.py:300
  9.8 0.6 fusion.64.s_ref
  10.4 0.0 collective-permute-done.top_ref
  10.4 0.3 collective-permute-done.1.low_ref
  10.7 0.8 %broadcast_in_dim.127.b_ref = f32[531,128]{1,0:T(8,128)} broadcast(f32[531]{0:T(1024)S(1)} %pad_maximum_fusion), dimensions={0} | broadcast | bytes 273996 | tf_op jit(solution)/shard_map/broadcast_in_dim | solution.py:270
  11.6 9.7 %shard_map.118.x_ref = bf16[256,4608]{1,0:T(8,128)(2,1)} custom-call(bf16[256,4096]{1,0:T(8,128)(2,1)} %bitcast.48, bf16[256,512]{1,0:T(8,128)(2,1)} %copy-done.9, bf16[256,512]{1,0:T(8,128)(2,1)} %copy-done.10, bf16[3,3,256,256]{3,2,1,0:T(8,128)(2,1)} %w_ref.2, f32[531,128]{1,0:T(8,128)} %broadcast_in_dim.127.b_ref, s32[7]{0:T(128)} %fusion.64.s_ref), custom_call_target="tpu_custom_call" | custom-call | flops 5435817984 | bytes 6160384 | tf_op jit(solution)/shard_map/pallas_call | solution.py:187
  21.3 8.4 %shard_map.119 = bf16[19,4096]{1,0:T(8,128)(2,1)} custom-call(bf16[256,4608]{1,0:T(8,128)(2,1)} %shard_map.118.x_ref, bf16[3,3,256,256]{3,2,1,0:T(8,128)(2,1)} %w_ref.3, f32[531,128]{1,0:T(8,128)} %broadcast_in_dim.127.b_ref, bf16[19,256]{1,0:T(8,128)(2,1)} %k_ref.1, s32[7]{0:T(128)} %fusion.64.s_ref), custom_call_target="tpu_custom_call" | custom-call | flops 4871684096 | bytes 3694592 | tf_op jit(solution)/shard_map/pallas_call | solution.py:217
  29.7 1.0 %copy.16 = bf16[3,8,16,256]{3,2,1,0:T(8,128)(2,1)S(1)} copy(bf16[3,8,16,256]{3,1,2,0:T(8,128)(2,1)} %bitcast.56) | data formatting | bytes 393216
  30.7 1.3 %collective-permute-start.2 = (bf16[19,1,16,256]{3,2,0,1:T(8,128)(2,1)S(1)}, bf16[19,1,16,256]{3,2,0,1:T(8,128)(2,1)S(1)}, u32[]{:S(2)}, u32[]{:S(2)}) collective-permute-start(bf16[19,1,16,256]{3,2,0,1:T(8,128)(2,1)S(1)} %get-tuple-element.22), channel_id=1, source_target_pairs={{2,10},{4,12},{6,14},{8,0},{3,11},{5,13},{7,15},{9,1},{18,26},{20,... | collective-permute-start | bytes 466952 | tf_op jit(solution)/shard_map/ppermute | solution.py:49
  34.6 6.2 %collective-permute-done.2 = bf16[19,1,16,256]{3,2,0,1:T(8,128)(2,1)S(1)} collective-permute-done((bf16[19,1,16,256]{3,2,0,1:T(8,128)(2,1)S(1)}, bf16[19,1,16,256]{3,2,0,1:T(8,128)(2,1)S(1)}, u32[]{:S(2)}, u32[]{:S(2)}) %collective-permute-start.2) | collective-permute-done | bytes 155680 | tf_op jit(solution)/shard_map/ppermute | solution.py:49
  40.9 5.3 %collective-permute-start.3 = (bf16[19,1,16,256]{3,2,0,1:T(8,128)(2,1)S(1)}, bf16[19,1,16,256]{3,2,0,1:T(8,128)(2,1)S(1)}, u32[]{:S(2)}, u32[]{:S(2)}) collective-permute-start(bf16[19,1,16,256]{3,2,0,1:T(8,128)(2,1)S(1)} %get-tuple-element.20), channel_id=1, source_target_pairs={{0,4},{2,6},{4,0},{10,14},{12,8},{14,10},{1,5},{3,7},{5,1},{11,15}... | collective-permute-start | bytes 466952 | tf_op jit(solution)/shard_map/ppermute | solution.py:55
  46.2 2.1 %collective-permute-start.4 = (bf16[19,1,16,256]{3,2,0,1:T(8,128)(2,1)S(1)}, bf16[19,1,16,256]{3,2,0,1:T(8,128)(2,1)S(1)}, u32[]{:S(2)}, u32[]{:S(2)}) collective-permute-start(bf16[19,1,16,256]{3,2,0,1:T(8,128)(2,1)S(1)} %get-tuple-element.21), channel_id=1, source_target_pairs={{0,4},{8,12},{10,14},{12,8},{1,5},{9,13},{11,15},{13,9},{16,20},{2... | collective-permute-start | bytes 466952 | tf_op jit(solution)/shard_map/ppermute | solution.py:55
  50.9 0.0 collective-permute-done.3
  50.9 0.0 collective-permute-done.4
  51.0 0.1 maximum_select_fusion.1
  51.1 0.1 copy.13
  51.2 0.1 collective-permute-start.5
  51.4 1.9 %collective-permute-done.5 = bf16[19,4,16,256]{3,2,1,0:T(8,128)(2,1)S(1)} collective-permute-done((bf16[19,4,16,256]{3,2,1,0:T(8,128)(2,1)S(1)}, bf16[19,4,16,256]{3,2,1,0:T(8,128)(2,1)S(1)}, u32[]{:S(2)}, u32[]{:S(2)}) %collective-permute-start.5) | collective-permute-done | bytes 622624 | tf_op jit(solution)/shard_map/ppermute | solution.py:49
  53.3 0.1 maximum_select_fusion
  53.4 0.1 dynamic-slice_bitcast_fusion
  53.5 0.1 fusion.28
  53.6 1.6 %collective-permute-start.6 = (bf16[19,10,256]{2,1,0:T(8,128)(2,1)S(1)}, bf16[19,10,256]{2,1,0:T(8,128)(2,1)S(1)}, u32[]{:S(2)}, u32[]{:S(2)}) collective-permute-start(bf16[19,10,256]{2,1,0:T(8,128)(2,1)S(1)} %fusion.28), channel_id=1, source_target_pairs={{0,1},{1,0},{2,3},{3,2},{4,5},{5,4},{6,7},{7,6},{8,9},{9,8},{10,11... | collective-permute-start | bytes 291848 | tf_op jit(solution)/shard_map/ppermute | solution.py:296
  55.2 1.2 %fusion = f32[32,19,1024]{2,0,1:T(8,128)S(1)} fusion(f32[1024]{0:T(1024)S(1)} %get-tuple-element.24, s32[1024]{0:T(1024)S(1)} %get-tuple-element.27, f32[1024]{0:T(1024)S(1)} %get-tuple-element.25, s32[1024]{0:T(1024)S(1)} %get-tuple-element.26, s32[]{:T(128)S(6)} %select_n.528, bf16[1,19,10,256]{3,2,1,0:T(8,128)(2,1)S(1)} %get-tuple-element.19, ...), kind=kOutput, calls=%fused_computation.3 | convolution fusion | flops 113884864 | bytes 2701832 | tf_op jit(solution)/shard_map/iy,cyj->icj/dot_general | solution.py:311
  56.4 3.4 %collective-permute-done.6 = bf16[19,10,256]{2,1,0:T(8,128)(2,1)S(1)} collective-permute-done((bf16[19,10,256]{2,1,0:T(8,128)(2,1)S(1)}, bf16[19,10,256]{2,1,0:T(8,128)(2,1)S(1)}, u32[]{:S(2)}, u32[]{:S(2)}) %collective-permute-start.6) | collective-permute-done | bytes 97312 | tf_op jit(solution)/shard_map/ppermute | solution.py:296
  59.7 2.7 %convolution_add_fusion = f32[32,19,1024]{2,0,1:T(8,128)} fusion(f32[32,19,1024]{2,0,1:T(8,128)S(1)} %fusion, bf16[19,10,256]{2,1,0:T(8,128)(2,1)S(1)} %collective-permute-done.6, f32[1024]{0:T(1024)S(1)} %get-tuple-element.28, s32[1024]{0:T(1024)S(1)} %get-tuple-element.31, f32[1024]{0:T(1024)S(1)} %get-tuple-element.29, s32[1024]{0:T(1024)S(1)} %get-tuple-element.30, ...), kind=kOutput, calls=%fused_computation | convolution fusion | flops 114458816 | bytes 5094916 | tf_op jit(solution)/shard_map/iy,cyj->icj/dot_general | solution.py:311
  (33 shorter events, 0.4 us)
Async XLA Ops:
  0.0 6.4 %copy-start.3 = (s32[2]{0:T(128)S(1)}, s32[2]{0:T(128)}, u32[]{:S(2)}) copy-start(s32[2]{0:T(128)} %param.13) | copy-start | bytes 28
  0.0 7.1 %copy-start.1 = (f32[256]{0:T(256)S(1)}, f32[256]{0:T(256)}, u32[]{:S(2)}) copy-start(f32[256]{0:T(256)} %param.17) | copy-start | bytes 3076
  0.0 7.1 %copy-start.2 = (f32[256]{0:T(256)S(1)}, f32[256]{0:T(256)}, u32[]{:S(2)}) copy-start(f32[256]{0:T(256)} %param.15) | copy-start | bytes 3076
  0.0 7.1 %copy-start.4 = (f32[19]{0:T(128)S(1)}, f32[19]{0:T(128)}, u32[]{:S(2)}) copy-start(f32[19]{0:T(128)} %param.19) | copy-start | bytes 232
  0.0 9.8 %copy-start.5 = (s32[7]{0:T(128)S(1)}, s32[7]{0:T(128)}, u32[]{:S(2)}) copy-start(s32[7]{0:T(128)} %constant.239.clone) | copy-start | bytes 88
  0.0 9.8 %copy-start.6 = (s32[7]{0:T(128)S(1)}, s32[7]{0:T(128)}, u32[]{:S(2)}) copy-start(s32[7]{0:T(128)} %constant.240.clone) | copy-start | bytes 88
  0.0 9.8 %copy-start.7 = (s32[7]{0:T(128)S(1)}, s32[7]{0:T(128)}, u32[]{:S(2)}) copy-start(s32[7]{0:T(128)} %constant.241.clone) | copy-start | bytes 88
  0.0 9.8 %copy-start.8 = (s32[7]{0:T(128)S(1)}, s32[7]{0:T(128)}, u32[]{:S(2)}) copy-start(s32[7]{0:T(128)} %constant.242.clone) | copy-start | bytes 88
  2.7 8.9 %copy-start = (bf16[32,8,16,256]{3,1,2,0:T(8,128)(2,1)}, bf16[32,8,16,256]{3,1,2,0:T(8,128)(2,1)S(1)}, u32[]{:S(2)}) copy-start(bf16[32,8,16,256]{3,1,2,0:T(8,128)(2,1)S(1)} %copy.15) | copy-start | bytes 6291460
  2.7 7.7 %collective-permute-start = (bf16[256,512]{1,0:T(8,128)(2,1)S(1)}, bf16[256,512]{1,0:T(8,128)(2,1)S(1)}, u32[]{:S(2)}, u32[]{:S(2)}) collective-permute-start(bf16[256,512]{1,0:T(8,128)(2,1)S(1)} %get-tuple-element.17), channel_id=1, source_target_pairs={{0,2},{2,4},{4,6},{6,8},{8,10},{10,12},{12,14},{1,3},{3,5},{5,7},{... | collective-permute-start | bytes 786440 | tf_op jit(solution)/shard_map/ppermute | solution.py:261
  5.1 5.6 %collective-permute-start.1 = (bf16[256,512]{1,0:T(8,128)(2,1)S(1)}, bf16[256,512]{1,0:T(8,128)(2,1)S(1)}, u32[]{:S(2)}, u32[]{:S(2)}) collective-permute-start(bf16[256,512]{1,0:T(8,128)(2,1)S(1)} %get-tuple-element.16), channel_id=1, source_target_pairs={{2,0},{4,2},{6,4},{8,6},{10,8},{12,10},{14,12},{3,1},{5,3},{7,5},{... | collective-permute-start | bytes 786440 | tf_op jit(solution)/shard_map/ppermute | solution.py:262
  10.4 1.2 %copy-start.9 = (bf16[256,512]{1,0:T(8,128)(2,1)}, bf16[256,512]{1,0:T(8,128)(2,1)S(1)}, u32[]{:S(2)}) copy-start(bf16[256,512]{1,0:T(8,128)(2,1)S(1)} %collective-permute-done.top_ref) | copy-start | bytes 786436
  10.7 0.9 %copy-start.10 = (bf16[256,512]{1,0:T(8,128)(2,1)}, bf16[256,512]{1,0:T(8,128)(2,1)S(1)}, u32[]{:S(2)}) copy-start(bf16[256,512]{1,0:T(8,128)(2,1)S(1)} %collective-permute-done.1.low_ref) | copy-start | bytes 786436
  30.7 10.1 %collective-permute-start.2 = (bf16[19,1,16,256]{3,2,0,1:T(8,128)(2,1)S(1)}, bf16[19,1,16,256]{3,2,0,1:T(8,128)(2,1)S(1)}, u32[]{:S(2)}, u32[]{:S(2)}) collective-permute-start(bf16[19,1,16,256]{3,2,0,1:T(8,128)(2,1)S(1)} %get-tuple-element.22), channel_id=1, source_target_pairs={{2,10},{4,12},{6,14},{8,0},{3,11},{5,13},{7,15},{9,1},{18,26},{20,... | collective-permute-start | bytes 466952 | tf_op jit(solution)/shard_map/ppermute | solution.py:49
  40.9 10.0 %collective-permute-start.3 = (bf16[19,1,16,256]{3,2,0,1:T(8,128)(2,1)S(1)}, bf16[19,1,16,256]{3,2,0,1:T(8,128)(2,1)S(1)}, u32[]{:S(2)}, u32[]{:S(2)}) collective-permute-start(bf16[19,1,16,256]{3,2,0,1:T(8,128)(2,1)S(1)} %get-tuple-element.20), channel_id=1, source_target_pairs={{0,4},{2,6},{4,0},{10,14},{12,8},{14,10},{1,5},{3,7},{5,1},{11,15}... | collective-permute-start | bytes 466952 | tf_op jit(solution)/shard_map/ppermute | solution.py:55
  46.2 4.7 %collective-permute-start.4 = (bf16[19,1,16,256]{3,2,0,1:T(8,128)(2,1)S(1)}, bf16[19,1,16,256]{3,2,0,1:T(8,128)(2,1)S(1)}, u32[]{:S(2)}, u32[]{:S(2)}) collective-permute-start(bf16[19,1,16,256]{3,2,0,1:T(8,128)(2,1)S(1)} %get-tuple-element.21), channel_id=1, source_target_pairs={{0,4},{8,12},{10,14},{12,8},{1,5},{9,13},{11,15},{13,9},{16,20},{2... | collective-permute-start | bytes 466952 | tf_op jit(solution)/shard_map/ppermute | solution.py:55
  51.2 2.1 %collective-permute-start.5 = (bf16[19,4,16,256]{3,2,1,0:T(8,128)(2,1)S(1)}, bf16[19,4,16,256]{3,2,1,0:T(8,128)(2,1)S(1)}, u32[]{:S(2)}, u32[]{:S(2)}) collective-permute-start(bf16[19,4,16,256]{3,2,1,0:T(8,128)(2,1)S(1)} %bitcast.49), channel_id=1, source_target_pairs={{0,2},{2,0},{4,6},{6,4},{8,10},{10,8},{12,14},{14,12},{1,3},{3,1},... | collective-permute-start | bytes 1867784 | tf_op jit(solution)/shard_map/ppermute | solution.py:49
  53.6 6.1 %collective-permute-start.6 = (bf16[19,10,256]{2,1,0:T(8,128)(2,1)S(1)}, bf16[19,10,256]{2,1,0:T(8,128)(2,1)S(1)}, u32[]{:S(2)}, u32[]{:S(2)}) collective-permute-start(bf16[19,10,256]{2,1,0:T(8,128)(2,1)S(1)} %fusion.28), channel_id=1, source_target_pairs={{0,1},{1,0},{2,3},{3,2},{4,5},{5,4},{6,7},{7,6},{8,9},{9,8},{10,11... | collective-permute-start | bytes 291848 | tf_op jit(solution)/shard_map/ppermute | solution.py:296

commit v22 on v21

--- a/solution.py
+++ b/solution.py
@@ -167,7 +167,7 @@
 
 
 def pick_block(rows):
-    return next(k for k in (8, 3, 4, 2, 1) if rows % k == 0)
+    return next(k for k in (16, 3, 4, 2, 1) if rows % k == 0)
 
 
 def conv_first_layer(feat, top, low, width, weights, biases, limits):

time: 62.8 us -> 62.6 us (level)
  no operation moved by 1% of the time
where the time goes in v22:
time: 62.6 us; the launch traced here: 62.2 us
  Pallas kernels  17.9 us (29%)
  starting transfers between devices  14 us (22%)
  waiting for transfers between devices  11.8 us (19%)
  between operations  8.08 us (13%)
  local copies, waits for them, and re-layouts  4.75 us (8%)
  matrix products  3.86 us (6%)
  other arithmetic  1.79 us (3%)
    pallas_call x1, Pallas kernels, conv_first_layer(): pl.pallas_call(functools.partial(first_body, width=width, block=block, ha...  9.74 us
    pallas_call x1, Pallas kernels, conv_second_layer(): pl.pallas_call(functools.partial(second_body, width=width, block=block),...  8.19 us
    ppermute x2, waiting for transfers between devices, gather_rows(): other = lax.ppermute(held, axis, pairs)  8.11 us
    ppermute x2, starting transfers between devices, gather_rows(): parts[p] = lax.ppermute(held[:, p:p + 1], axis, list(pairs))  7.42 us
    dot_general x2, matrix products, shards(): jnp.einsum('iy,cyj->icj', row_part, widened, preferred_element_type=jnp.f...  3.86 us
    unnamed x24, local copies, waits for them, and re-layouts  3.61 us
    ppermute x1, waiting for transfers between devices, shards(): lax.ppermute(send, 'member', [(i, (i + shift) % members) for i in range(m...  3.38 us
    ppermute x1, starting transfers between devices, shards(): lax.ppermute(flat_feat[:, (rows_dev - halo) * cols:], 'space', forward)  2.37 us
  transfers between devices with their start and end apart: 7, of which 4 were waited for; matrix products, arithmetic and copies ran while one was open for 4% of the time, Pallas kernels for 0%

profile of v22, /device:TPU:0, one launch (start us, length us, event | category | flops | bytes accessed | tf_op | source)
XLA Modules:
  0.0 62.2 jit_solution(1978208503377504597)
XLA Ops:
  0.0 0.0 copy-start.6
  0.0 0.0 copy-start.7
  0.0 0.0 copy-start.8
  0.1 2.6 %copy.15 = bf16[32,8,16,256]{3,1,2,0:T(8,128)(2,1)S(1)} copy(bf16[32,8,16,256]{3,2,1,0:T(8,128)(2,1)} %bitcast.51) | data formatting | bytes 4194304
  2.7 0.0 copy-start
  2.7 2.4 %collective-permute-start = (bf16[256,512]{1,0:T(8,128)(2,1)S(1)}, bf16[256,512]{1,0:T(8,128)(2,1)S(1)}, u32[]{:S(2)}, u32[]{:S(2)}) collective-permute-start(bf16[256,512]{1,0:T(8,128)(2,1)S(1)} %get-tuple-element.17), channel_id=1, source_target_pairs={{0,2},{2,4},{4,6},{6,8},{8,10},{10,12},{12,14},{1,3},{3,5},{5,7},{... | collective-permute-start | bytes 786440 | tf_op jit(solution)/shard_map/ppermute | solution.py:261
  5.1 1.3 %collective-permute-start.1 = (bf16[256,512]{1,0:T(8,128)(2,1)S(1)}, bf16[256,512]{1,0:T(8,128)(2,1)S(1)}, u32[]{:S(2)}, u32[]{:S(2)}) collective-permute-start(bf16[256,512]{1,0:T(8,128)(2,1)S(1)} %get-tuple-element.16), channel_id=1, source_target_pairs={{2,0},{4,2},{6,4},{8,6},{10,8},{12,10},{14,12},{3,1},{5,3},{7,5},{... | collective-permute-start | bytes 786440 | tf_op jit(solution)/shard_map/ppermute | solution.py:262
  6.4 0.7 %fusion.63 = (s32[]{:T(128)}, s32[]{:T(128)}, s32[]{:T(128)}) fusion(s32[2]{0:T(128)S(1)} %copy-done.3, s32[]{:T(128)S(6)} %select_n.540, s32[]{:T(128)S(6)} %select_n.493, s32[]{:T(128)S(6)} %axis_index.29), kind=kLoop, calls=%fused_computation.107 | loop fusion | flops 15 | bytes 32 | tf_op jit(solution)/shard_map/reduce_sum | solution.py:300
  9.8 0.6 fusion.64.s_ref
  10.4 0.0 collective-permute-done.top_ref
  10.4 0.3 collective-permute-done.1.low_ref
  10.7 0.8 %broadcast_in_dim.127.b_ref = f32[531,128]{1,0:T(8,128)} broadcast(f32[531]{0:T(1024)S(1)} %pad_maximum_fusion), dimensions={0} | broadcast | bytes 273996 | tf_op jit(solution)/shard_map/broadcast_in_dim | solution.py:270
  11.6 9.7 %shard_map.118.x_ref = bf16[256,4608]{1,0:T(8,128)(2,1)} custom-call(bf16[256,4096]{1,0:T(8,128)(2,1)} %bitcast.48, bf16[256,512]{1,0:T(8,128)(2,1)} %copy-done.9, bf16[256,512]{1,0:T(8,128)(2,1)} %copy-done.10, bf16[3,3,256,256]{3,2,1,0:T(8,128)(2,1)} %w_ref.2, f32[531,128]{1,0:T(8,128)} %broadcast_in_dim.127.b_ref, s32[7]{0:T(128)} %fusion.64.s_ref), custom_call_target="tpu_custom_call" | custom-call | flops 5435817984 | bytes 6160384 | tf_op jit(solution)/shard_map/pallas_call | solution.py:187
  21.3 8.2 %shard_map.119 = bf16[19,4096]{1,0:T(8,128)(2,1)} custom-call(bf16[256,4608]{1,0:T(8,128)(2,1)} %shard_map.118.x_ref, bf16[3,3,256,256]{3,2,1,0:T(8,128)(2,1)} %w_ref.3, f32[531,128]{1,0:T(8,128)} %broadcast_in_dim.127.b_ref, bf16[19,256]{1,0:T(8,128)(2,1)} %k_ref.1, s32[7]{0:T(128)} %fusion.64.s_ref), custom_call_target="tpu_custom_call" | custom-call | flops 4871684096 | bytes 3694592 | tf_op jit(solution)/shard_map/pallas_call | solution.py:217
  29.5 1.0 %copy.16 = bf16[3,8,16,256]{3,2,1,0:T(8,128)(2,1)S(1)} copy(bf16[3,8,16,256]{3,1,2,0:T(8,128)(2,1)} %bitcast.56) | data formatting | bytes 393216
  30.5 1.3 %collective-permute-start.2 = (bf16[19,1,16,256]{3,2,0,1:T(8,128)(2,1)S(1)}, bf16[19,1,16,256]{3,2,0,1:T(8,128)(2,1)S(1)}, u32[]{:S(2)}, u32[]{:S(2)}) collective-permute-start(bf16[19,1,16,256]{3,2,0,1:T(8,128)(2,1)S(1)} %get-tuple-element.22), channel_id=1, source_target_pairs={{2,10},{4,12},{6,14},{8,0},{3,11},{5,13},{7,15},{9,1},{18,26},{20,... | collective-permute-start | bytes 466952 | tf_op jit(solution)/shard_map/ppermute | solution.py:49
  34.4 6.2 %collective-permute-done.2 = bf16[19,1,16,256]{3,2,0,1:T(8,128)(2,1)S(1)} collective-permute-done((bf16[19,1,16,256]{3,2,0,1:T(8,128)(2,1)S(1)}, bf16[19,1,16,256]{3,2,0,1:T(8,128)(2,1)S(1)}, u32[]{:S(2)}, u32[]{:S(2)}) %collective-permute-start.2) | collective-permute-done | bytes 155680 | tf_op jit(solution)/shard_map/ppermute | solution.py:49
  40.7 5.3 %collective-permute-start.3 = (bf16[19,1,16,256]{3,2,0,1:T(8,128)(2,1)S(1)}, bf16[19,1,16,256]{3,2,0,1:T(8,128)(2,1)S(1)}, u32[]{:S(2)}, u32[]{:S(2)}) collective-permute-start(bf16[19,1,16,256]{3,2,0,1:T(8,128)(2,1)S(1)} %get-tuple-element.20), channel_id=1, source_target_pairs={{0,4},{2,6},{4,0},{10,14},{12,8},{14,10},{1,5},{3,7},{5,1},{11,15}... | collective-permute-start | bytes 466952 | tf_op jit(solution)/shard_map/ppermute | solution.py:55
  46.0 2.1 %collective-permute-start.4 = (bf16[19,1,16,256]{3,2,0,1:T(8,128)(2,1)S(1)}, bf16[19,1,16,256]{3,2,0,1:T(8,128)(2,1)S(1)}, u32[]{:S(2)}, u32[]{:S(2)}) collective-permute-start(bf16[19,1,16,256]{3,2,0,1:T(8,128)(2,1)S(1)} %get-tuple-element.21), channel_id=1, source_target_pairs={{0,4},{8,12},{10,14},{12,8},{1,5},{9,13},{11,15},{13,9},{16,20},{2... | collective-permute-start | bytes 466952 | tf_op jit(solution)/shard_map/ppermute | solution.py:55
  50.7 0.0 collective-permute-done.3
  50.8 0.0 collective-permute-done.4
  50.8 0.1 maximum_select_fusion.1
  50.9 0.1 copy.13
  51.0 0.1 collective-permute-start.5
  51.2 1.9 %collective-permute-done.5 = bf16[19,4,16,256]{3,2,1,0:T(8,128)(2,1)S(1)} collective-permute-done((bf16[19,4,16,256]{3,2,1,0:T(8,128)(2,1)S(1)}, bf16[19,4,16,256]{3,2,1,0:T(8,128)(2,1)S(1)}, u32[]{:S(2)}, u32[]{:S(2)}) %collective-permute-start.5) | collective-permute-done | bytes 622624 | tf_op jit(solution)/shard_map/ppermute | solution.py:49
  53.1 0.1 maximum_select_fusion
  53.2 0.1 dynamic-slice_bitcast_fusion
  53.3 0.1 fusion.28
  53.4 1.6 %collective-permute-start.6 = (bf16[19,10,256]{2,1,0:T(8,128)(2,1)S(1)}, bf16[19,10,256]{2,1,0:T(8,128)(2,1)S(1)}, u32[]{:S(2)}, u32[]{:S(2)}) collective-permute-start(bf16[19,10,256]{2,1,0:T(8,128)(2,1)S(1)} %fusion.28), channel_id=1, source_target_pairs={{0,1},{1,0},{2,3},{3,2},{4,5},{5,4},{6,7},{7,6},{8,9},{9,8},{10,11... | collective-permute-start | bytes 291848 | tf_op jit(solution)/shard_map/ppermute | solution.py:296
  55.0 1.2 %fusion = f32[32,19,1024]{2,0,1:T(8,128)S(1)} fusion(f32[1024]{0:T(1024)S(1)} %get-tuple-element.24, s32[1024]{0:T(1024)S(1)} %get-tuple-element.27, f32[1024]{0:T(1024)S(1)} %get-tuple-element.25, s32[1024]{0:T(1024)S(1)} %get-tuple-element.26, s32[]{:T(128)S(6)} %select_n.528, bf16[1,19,10,256]{3,2,1,0:T(8,128)(2,1)S(1)} %get-tuple-element.19, ...), kind=kOutput, calls=%fused_computation.3 | convolution fusion | flops 113884864 | bytes 2701832 | tf_op jit(solution)/shard_map/iy,cyj->icj/dot_general | solution.py:311
  56.2 3.4 %collective-permute-done.6 = bf16[19,10,256]{2,1,0:T(8,128)(2,1)S(1)} collective-permute-done((bf16[19,10,256]{2,1,0:T(8,128)(2,1)S(1)}, bf16[19,10,256]{2,1,0:T(8,128)(2,1)S(1)}, u32[]{:S(2)}, u32[]{:S(2)}) %collective-permute-start.6) | collective-permute-done | bytes 97312 | tf_op jit(solution)/shard_map/ppermute | solution.py:296
  59.6 2.7 %convolution_add_fusion = f32[32,19,1024]{2,0,1:T(8,128)} fusion(f32[32,19,1024]{2,0,1:T(8,128)S(1)} %fusion, bf16[19,10,256]{2,1,0:T(8,128)(2,1)S(1)} %collective-permute-done.6, f32[1024]{0:T(1024)S(1)} %get-tuple-element.28, s32[1024]{0:T(1024)S(1)} %get-tuple-element.31, f32[1024]{0:T(1024)S(1)} %get-tuple-element.29, s32[1024]{0:T(1024)S(1)} %get-tuple-element.30, ...), kind=kOutput, calls=%fused_computation | convolution fusion | flops 114458816 | bytes 5094916 | tf_op jit(solution)/shard_map/iy,cyj->icj/dot_general | solution.py:311
  (33 shorter events, 0.4 us)
Async XLA Ops:
  0.0 6.4 %copy-start.3 = (s32[2]{0:T(128)S(1)}, s32[2]{0:T(128)}, u32[]{:S(2)}) copy-start(s32[2]{0:T(128)} %param.13) | copy-start | bytes 28
  0.0 7.1 %copy-start.1 = (f32[256]{0:T(256)S(1)}, f32[256]{0:T(256)}, u32[]{:S(2)}) copy-start(f32[256]{0:T(256)} %param.17) | copy-start | bytes 3076
  0.0 7.1 %copy-start.2 = (f32[256]{0:T(256)S(1)}, f32[256]{0:T(256)}, u32[]{:S(2)}) copy-start(f32[256]{0:T(256)} %param.15) | copy-start | bytes 3076
  0.0 7.1 %copy-start.4 = (f32[19]{0:T(128)S(1)}, f32[19]{0:T(128)}, u32[]{:S(2)}) copy-start(f32[19]{0:T(128)} %param.19) | copy-start | bytes 232
  0.0 9.8 %copy-start.5 = (s32[7]{0:T(128)S(1)}, s32[7]{0:T(128)}, u32[]{:S(2)}) copy-start(s32[7]{0:T(128)} %constant.239.clone) | copy-start | bytes 88
  0.0 9.8 %copy-start.6 = (s32[7]{0:T(128)S(1)}, s32[7]{0:T(128)}, u32[]{:S(2)}) copy-start(s32[7]{0:T(128)} %constant.240.clone) | copy-start | bytes 88
  0.0 9.8 %copy-start.7 = (s32[7]{0:T(128)S(1)}, s32[7]{0:T(128)}, u32[]{:S(2)}) copy-start(s32[7]{0:T(128)} %constant.241.clone) | copy-start | bytes 88
  0.0 9.8 %copy-start.8 = (s32[7]{0:T(128)S(1)}, s32[7]{0:T(128)}, u32[]{:S(2)}) copy-start(s32[7]{0:T(128)} %constant.242.clone) | copy-start | bytes 88
  2.7 8.9 %copy-start = (bf16[32,8,16,256]{3,1,2,0:T(8,128)(2,1)}, bf16[32,8,16,256]{3,1,2,0:T(8,128)(2,1)S(1)}, u32[]{:S(2)}) copy-start(bf16[32,8,16,256]{3,1,2,0:T(8,128)(2,1)S(1)} %copy.15) | copy-start | bytes 6291460
  2.7 7.7 %collective-permute-start = (bf16[256,512]{1,0:T(8,128)(2,1)S(1)}, bf16[256,512]{1,0:T(8,128)(2,1)S(1)}, u32[]{:S(2)}, u32[]{:S(2)}) collective-permute-start(bf16[256,512]{1,0:T(8,128)(2,1)S(1)} %get-tuple-element.17), channel_id=1, source_target_pairs={{0,2},{2,4},{4,6},{6,8},{8,10},{10,12},{12,14},{1,3},{3,5},{5,7},{... | collective-permute-start | bytes 786440 | tf_op jit(solution)/shard_map/ppermute | solution.py:261
  5.1 5.6 %collective-permute-start.1 = (bf16[256,512]{1,0:T(8,128)(2,1)S(1)}, bf16[256,512]{1,0:T(8,128)(2,1)S(1)}, u32[]{:S(2)}, u32[]{:S(2)}) collective-permute-start(bf16[256,512]{1,0:T(8,128)(2,1)S(1)} %get-tuple-element.16), channel_id=1, source_target_pairs={{2,0},{4,2},{6,4},{8,6},{10,8},{12,10},{14,12},{3,1},{5,3},{7,5},{... | collective-permute-start | bytes 786440 | tf_op jit(solution)/shard_map/ppermute | solution.py:262
  10.4 1.2 %copy-start.9 = (bf16[256,512]{1,0:T(8,128)(2,1)}, bf16[256,512]{1,0:T(8,128)(2,1)S(1)}, u32[]{:S(2)}) copy-start(bf16[256,512]{1,0:T(8,128)(2,1)S(1)} %collective-permute-done.top_ref) | copy-start | bytes 786436
  10.7 0.9 %copy-start.10 = (bf16[256,512]{1,0:T(8,128)(2,1)}, bf16[256,512]{1,0:T(8,128)(2,1)S(1)}, u32[]{:S(2)}) copy-start(bf16[256,512]{1,0:T(8,128)(2,1)S(1)} %collective-permute-done.1.low_ref) | copy-start | bytes 786436
  30.5 10.1 %collective-permute-start.2 = (bf16[19,1,16,256]{3,2,0,1:T(8,128)(2,1)S(1)}, bf16[19,1,16,256]{3,2,0,1:T(8,128)(2,1)S(1)}, u32[]{:S(2)}, u32[]{:S(2)}) collective-permute-start(bf16[19,1,16,256]{3,2,0,1:T(8,128)(2,1)S(1)} %get-tuple-element.22), channel_id=1, source_target_pairs={{2,10},{4,12},{6,14},{8,0},{3,11},{5,13},{7,15},{9,1},{18,26},{20,... | collective-permute-start | bytes 466952 | tf_op jit(solution)/shard_map/ppermute | solution.py:49
  40.7 10.0 %collective-permute-start.3 = (bf16[19,1,16,256]{3,2,0,1:T(8,128)(2,1)S(1)}, bf16[19,1,16,256]{3,2,0,1:T(8,128)(2,1)S(1)}, u32[]{:S(2)}, u32[]{:S(2)}) collective-permute-start(bf16[19,1,16,256]{3,2,0,1:T(8,128)(2,1)S(1)} %get-tuple-element.20), channel_id=1, source_target_pairs={{0,4},{2,6},{4,0},{10,14},{12,8},{14,10},{1,5},{3,7},{5,1},{11,15}... | collective-permute-start | bytes 466952 | tf_op jit(solution)/shard_map/ppermute | solution.py:55
  46.0 4.7 %collective-permute-start.4 = (bf16[19,1,16,256]{3,2,0,1:T(8,128)(2,1)S(1)}, bf16[19,1,16,256]{3,2,0,1:T(8,128)(2,1)S(1)}, u32[]{:S(2)}, u32[]{:S(2)}) collective-permute-start(bf16[19,1,16,256]{3,2,0,1:T(8,128)(2,1)S(1)} %get-tuple-element.21), channel_id=1, source_target_pairs={{0,4},{8,12},{10,14},{12,8},{1,5},{9,13},{11,15},{13,9},{16,20},{2... | collective-permute-start | bytes 466952 | tf_op jit(solution)/shard_map/ppermute | solution.py:55
  51.0 2.1 %collective-permute-start.5 = (bf16[19,4,16,256]{3,2,1,0:T(8,128)(2,1)S(1)}, bf16[19,4,16,256]{3,2,1,0:T(8,128)(2,1)S(1)}, u32[]{:S(2)}, u32[]{:S(2)}) collective-permute-start(bf16[19,4,16,256]{3,2,1,0:T(8,128)(2,1)S(1)} %bitcast.49), channel_id=1, source_target_pairs={{0,2},{2,0},{4,6},{6,4},{8,10},{10,8},{12,14},{14,12},{1,3},{3,1},... | collective-permute-start | bytes 1867784 | tf_op jit(solution)/shard_map/ppermute | solution.py:49
  53.4 6.1 %collective-permute-start.6 = (bf16[19,10,256]{2,1,0:T(8,128)(2,1)S(1)}, bf16[19,10,256]{2,1,0:T(8,128)(2,1)S(1)}, u32[]{:S(2)}, u32[]{:S(2)}) collective-permute-start(bf16[19,10,256]{2,1,0:T(8,128)(2,1)S(1)} %fusion.28), channel_id=1, source_target_pairs={{0,1},{1,0},{2,3},{3,2},{4,5},{5,4},{6,7},{7,6},{8,9},{9,8},{10,11... | collective-permute-start | bytes 291848 | tf_op jit(solution)/shard_map/ppermute | solution.py:296

commit v23 on v22

--- a/solution.py
+++ b/solution.py
@@ -167,7 +167,7 @@
 
 
 def pick_block(rows):
-    return next(k for k in (16, 3, 4, 2, 1) if rows % k == 0)
+    return next(k for k in (18, 16, 3, 4, 2, 1) if rows % k == 0)
 
 
 def conv_first_layer(feat, top, low, width, weights, biases, limits):

time: 62.6 us -> 62.5 us (level)
  no operation moved by 1% of the time
where the time goes in v23:
time: 62.5 us; the launch traced here: 62.1 us
  Pallas kernels  17.8 us (28%)
  starting transfers between devices  14 us (22%)
  waiting for transfers between devices  11.8 us (19%)
  between operations  8.08 us (13%)
  local copies, waits for them, and re-layouts  4.75 us (8%)
  matrix products  3.85 us (6%)
  other arithmetic  1.79 us (3%)
    pallas_call x1, Pallas kernels, conv_first_layer(): pl.pallas_call(functools.partial(first_body, width=width, block=block, ha...  9.65 us
    pallas_call x1, Pallas kernels, conv_second_layer(): pl.pallas_call(functools.partial(second_body, width=width, block=block),...  8.19 us
    ppermute x2, waiting for transfers between devices, gather_rows(): other = lax.ppermute(held, axis, pairs)  8.11 us
    ppermute x2, starting transfers between devices, gather_rows(): parts[p] = lax.ppermute(held[:, p:p + 1], axis, list(pairs))  7.42 us
    dot_general x2, matrix products, shards(): jnp.einsum('iy,cyj->icj', row_part, widened, preferred_element_type=jnp.f...  3.85 us
    unnamed x24, local copies, waits for them, and re-layouts  3.61 us
    ppermute x1, waiting for transfers between devices, shards(): lax.ppermute(send, 'member', [(i, (i + shift) % members) for i in range(m...  3.38 us
    ppermute x1, starting transfers between devices, shards(): lax.ppermute(flat_feat[:, (rows_dev - halo) * cols:], 'space', forward)  2.37 us
  transfers between devices with their start and end apart: 7, of which 4 were waited for; matrix products, arithmetic and copies ran while one was open for 4% of the time, Pallas kernels for 0%

profile of v23, /device:TPU:0, one launch (start us, length us, event | category | flops | bytes accessed | tf_op | source)
XLA Modules:
  0.0 62.1 jit_solution(9820428869256949057)
XLA Ops:
  0.0 0.0 copy-start.6
  0.0 0.0 copy-start.7
  0.0 0.0 copy-start.8
  0.1 2.6 %copy.15 = bf16[32,8,16,256]{3,1,2,0:T(8,128)(2,1)S(1)} copy(bf16[32,8,16,256]{3,2,1,0:T(8,128)(2,1)} %bitcast.51) | data formatting | bytes 4194304
  2.7 2.4 %collective-permute-start = (bf16[256,512]{1,0:T(8,128)(2,1)S(1)}, bf16[256,512]{1,0:T(8,128)(2,1)S(1)}, u32[]{:S(2)}, u32[]{:S(2)}) collective-permute-start(bf16[256,512]{1,0:T(8,128)(2,1)S(1)} %get-tuple-element.17), channel_id=1, source_target_pairs={{0,2},{2,4},{4,6},{6,8},{8,10},{10,12},{12,14},{1,3},{3,5},{5,7},{... | collective-permute-start | bytes 786440 | tf_op jit(solution)/shard_map/ppermute | solution.py:261
  5.1 1.3 %collective-permute-start.1 = (bf16[256,512]{1,0:T(8,128)(2,1)S(1)}, bf16[256,512]{1,0:T(8,128)(2,1)S(1)}, u32[]{:S(2)}, u32[]{:S(2)}) collective-permute-start(bf16[256,512]{1,0:T(8,128)(2,1)S(1)} %get-tuple-element.16), channel_id=1, source_target_pairs={{2,0},{4,2},{6,4},{8,6},{10,8},{12,10},{14,12},{3,1},{5,3},{7,5},{... | collective-permute-start | bytes 786440 | tf_op jit(solution)/shard_map/ppermute | solution.py:262
  6.4 0.7 %fusion.63 = (s32[]{:T(128)}, s32[]{:T(128)}, s32[]{:T(128)}) fusion(s32[2]{0:T(128)S(1)} %copy-done.3, s32[]{:T(128)S(6)} %select_n.540, s32[]{:T(128)S(6)} %select_n.493, s32[]{:T(128)S(6)} %axis_index.29), kind=kLoop, calls=%fused_computation.107 | loop fusion | flops 15 | bytes 32 | tf_op jit(solution)/shard_map/reduce_sum | solution.py:300
  7.1 0.0 copy-done.1
  9.8 0.6 fusion.64.s_ref
  10.4 0.0 collective-permute-done.top_ref
  10.4 0.3 collective-permute-done.1.low_ref
  10.7 0.8 %broadcast_in_dim.127.b_ref = f32[531,128]{1,0:T(8,128)} broadcast(f32[531]{0:T(1024)S(1)} %pad_maximum_fusion), dimensions={0} | broadcast | bytes 273996 | tf_op jit(solution)/shard_map/broadcast_in_dim | solution.py:270
  11.6 9.6 %shard_map.118.x_ref = bf16[256,4608]{1,0:T(8,128)(2,1)} custom-call(bf16[256,4096]{1,0:T(8,128)(2,1)} %bitcast.48, bf16[256,512]{1,0:T(8,128)(2,1)} %copy-done.9, bf16[256,512]{1,0:T(8,128)(2,1)} %copy-done.10, bf16[3,3,256,256]{3,2,1,0:T(8,128)(2,1)} %w_ref.2, f32[531,128]{1,0:T(8,128)} %broadcast_in_dim.127.b_ref, s32[7]{0:T(128)} %fusion.64.s_ref), custom_call_target="tpu_custom_call" | custom-call | flops 5435817984 | bytes 6160384 | tf_op jit(solution)/shard_map/pallas_call | solution.py:187
  21.2 8.2 %shard_map.119 = bf16[19,4096]{1,0:T(8,128)(2,1)} custom-call(bf16[256,4608]{1,0:T(8,128)(2,1)} %shard_map.118.x_ref, bf16[3,3,256,256]{3,2,1,0:T(8,128)(2,1)} %w_ref.3, f32[531,128]{1,0:T(8,128)} %broadcast_in_dim.127.b_ref, bf16[19,256]{1,0:T(8,128)(2,1)} %k_ref.1, s32[7]{0:T(128)} %fusion.64.s_ref), custom_call_target="tpu_custom_call" | custom-call | flops 4871684096 | bytes 3694592 | tf_op jit(solution)/shard_map/pallas_call | solution.py:217
  29.4 1.0 %copy.16 = bf16[3,8,16,256]{3,2,1,0:T(8,128)(2,1)S(1)} copy(bf16[3,8,16,256]{3,1,2,0:T(8,128)(2,1)} %bitcast.56) | data formatting | bytes 393216
  30.4 1.3 %collective-permute-start.2 = (bf16[19,1,16,256]{3,2,0,1:T(8,128)(2,1)S(1)}, bf16[19,1,16,256]{3,2,0,1:T(8,128)(2,1)S(1)}, u32[]{:S(2)}, u32[]{:S(2)}) collective-permute-start(bf16[19,1,16,256]{3,2,0,1:T(8,128)(2,1)S(1)} %get-tuple-element.22), channel_id=1, source_target_pairs={{2,10},{4,12},{6,14},{8,0},{3,11},{5,13},{7,15},{9,1},{18,26},{20,... | collective-permute-start | bytes 466952 | tf_op jit(solution)/shard_map/ppermute | solution.py:49
  34.3 6.2 %collective-permute-done.2 = bf16[19,1,16,256]{3,2,0,1:T(8,128)(2,1)S(1)} collective-permute-done((bf16[19,1,16,256]{3,2,0,1:T(8,128)(2,1)S(1)}, bf16[19,1,16,256]{3,2,0,1:T(8,128)(2,1)S(1)}, u32[]{:S(2)}, u32[]{:S(2)}) %collective-permute-start.2) | collective-permute-done | bytes 155680 | tf_op jit(solution)/shard_map/ppermute | solution.py:49
  40.6 5.3 %collective-permute-start.3 = (bf16[19,1,16,256]{3,2,0,1:T(8,128)(2,1)S(1)}, bf16[19,1,16,256]{3,2,0,1:T(8,128)(2,1)S(1)}, u32[]{:S(2)}, u32[]{:S(2)}) collective-permute-start(bf16[19,1,16,256]{3,2,0,1:T(8,128)(2,1)S(1)} %get-tuple-element.20), channel_id=1, source_target_pairs={{0,4},{2,6},{4,0},{10,14},{12,8},{14,10},{1,5},{3,7},{5,1},{11,15}... | collective-permute-start | bytes 466952 | tf_op jit(solution)/shard_map/ppermute | solution.py:55
  45.9 2.1 %collective-permute-start.4 = (bf16[19,1,16,256]{3,2,0,1:T(8,128)(2,1)S(1)}, bf16[19,1,16,256]{3,2,0,1:T(8,128)(2,1)S(1)}, u32[]{:S(2)}, u32[]{:S(2)}) collective-permute-start(bf16[19,1,16,256]{3,2,0,1:T(8,128)(2,1)S(1)} %get-tuple-element.21), channel_id=1, source_target_pairs={{0,4},{8,12},{10,14},{12,8},{1,5},{9,13},{11,15},{13,9},{16,20},{2... | collective-permute-start | bytes 466952 | tf_op jit(solution)/shard_map/ppermute | solution.py:55
  50.7 0.0 collective-permute-done.3
  50.7 0.0 collective-permute-done.4
  50.7 0.1 maximum_select_fusion.1
  50.8 0.1 copy.13
  50.9 0.1 collective-permute-start.5
  51.1 1.9 %collective-permute-done.5 = bf16[19,4,16,256]{3,2,1,0:T(8,128)(2,1)S(1)} collective-permute-done((bf16[19,4,16,256]{3,2,1,0:T(8,128)(2,1)S(1)}, bf16[19,4,16,256]{3,2,1,0:T(8,128)(2,1)S(1)}, u32[]{:S(2)}, u32[]{:S(2)}) %collective-permute-start.5) | collective-permute-done | bytes 622624 | tf_op jit(solution)/shard_map/ppermute | solution.py:49
  53.0 0.1 maximum_select_fusion
  53.1 0.1 dynamic-slice_bitcast_fusion
  53.2 0.1 fusion.28
  53.3 1.6 %collective-permute-start.6 = (bf16[19,10,256]{2,1,0:T(8,128)(2,1)S(1)}, bf16[19,10,256]{2,1,0:T(8,128)(2,1)S(1)}, u32[]{:S(2)}, u32[]{:S(2)}) collective-permute-start(bf16[19,10,256]{2,1,0:T(8,128)(2,1)S(1)} %fusion.28), channel_id=1, source_target_pairs={{0,1},{1,0},{2,3},{3,2},{4,5},{5,4},{6,7},{7,6},{8,9},{9,8},{10,11... | collective-permute-start | bytes 291848 | tf_op jit(solution)/shard_map/ppermute | solution.py:296
  54.9 1.2 %fusion = f32[32,19,1024]{2,0,1:T(8,128)S(1)} fusion(f32[1024]{0:T(1024)S(1)} %get-tuple-element.24, s32[1024]{0:T(1024)S(1)} %get-tuple-element.27, f32[1024]{0:T(1024)S(1)} %get-tuple-element.25, s32[1024]{0:T(1024)S(1)} %get-tuple-element.26, s32[]{:T(128)S(6)} %select_n.528, bf16[1,19,10,256]{3,2,1,0:T(8,128)(2,1)S(1)} %get-tuple-element.19, ...), kind=kOutput, calls=%fused_computation.3 | convolution fusion | flops 113884864 | bytes 2701832 | tf_op jit(solution)/shard_map/iy,cyj->icj/dot_general | solution.py:311
  56.1 3.4 %collective-permute-done.6 = bf16[19,10,256]{2,1,0:T(8,128)(2,1)S(1)} collective-permute-done((bf16[19,10,256]{2,1,0:T(8,128)(2,1)S(1)}, bf16[19,10,256]{2,1,0:T(8,128)(2,1)S(1)}, u32[]{:S(2)}, u32[]{:S(2)}) %collective-permute-start.6) | collective-permute-done | bytes 97312 | tf_op jit(solution)/shard_map/ppermute | solution.py:296
  59.5 2.7 %convolution_add_fusion = f32[32,19,1024]{2,0,1:T(8,128)} fusion(f32[32,19,1024]{2,0,1:T(8,128)S(1)} %fusion, bf16[19,10,256]{2,1,0:T(8,128)(2,1)S(1)} %collective-permute-done.6, f32[1024]{0:T(1024)S(1)} %get-tuple-element.28, s32[1024]{0:T(1024)S(1)} %get-tuple-element.31, f32[1024]{0:T(1024)S(1)} %get-tuple-element.29, s32[1024]{0:T(1024)S(1)} %get-tuple-element.30, ...), kind=kOutput, calls=%fused_computation | convolution fusion | flops 114458816 | bytes 5094916 | tf_op jit(solution)/shard_map/iy,cyj->icj/dot_general | solution.py:311
  (33 shorter events, 0.4 us)
Async XLA Ops:
  0.0 6.4 %copy-start.3 = (s32[2]{0:T(128)S(1)}, s32[2]{0:T(128)}, u32[]{:S(2)}) copy-start(s32[2]{0:T(128)} %param.13) | copy-start | bytes 28
  0.0 7.1 %copy-start.1 = (f32[256]{0:T(256)S(1)}, f32[256]{0:T(256)}, u32[]{:S(2)}) copy-start(f32[256]{0:T(256)} %param.17) | copy-start | bytes 3076
  0.0 7.1 %copy-start.2 = (f32[256]{0:T(256)S(1)}, f32[256]{0:T(256)}, u32[]{:S(2)}) copy-start(f32[256]{0:T(256)} %param.15) | copy-start | bytes 3076
  0.0 7.1 %copy-start.4 = (f32[19]{0:T(128)S(1)}, f32[19]{0:T(128)}, u32[]{:S(2)}) copy-start(f32[19]{0:T(128)} %param.19) | copy-start | bytes 232
  0.0 9.8 %copy-start.5 = (s32[7]{0:T(128)S(1)}, s32[7]{0:T(128)}, u32[]{:S(2)}) copy-start(s32[7]{0:T(128)} %constant.239.clone) | copy-start | bytes 88
  0.0 9.8 %copy-start.6 = (s32[7]{0:T(128)S(1)}, s32[7]{0:T(128)}, u32[]{:S(2)}) copy-start(s32[7]{0:T(128)} %constant.240.clone) | copy-start | bytes 88
  0.0 9.8 %copy-start.7 = (s32[7]{0:T(128)S(1)}, s32[7]{0:T(128)}, u32[]{:S(2)}) copy-start(s32[7]{0:T(128)} %constant.241.clone) | copy-start | bytes 88
  0.0 9.8 %copy-start.8 = (s32[7]{0:T(128)S(1)}, s32[7]{0:T(128)}, u32[]{:S(2)}) copy-start(s32[7]{0:T(128)} %constant.242.clone) | copy-start | bytes 88
  2.7 8.9 %copy-start = (bf16[32,8,16,256]{3,1,2,0:T(8,128)(2,1)}, bf16[32,8,16,256]{3,1,2,0:T(8,128)(2,1)S(1)}, u32[]{:S(2)}) copy-start(bf16[32,8,16,256]{3,1,2,0:T(8,128)(2,1)S(1)} %copy.15) | copy-start | bytes 6291460
  2.7 7.7 %collective-permute-start = (bf16[256,512]{1,0:T(8,128)(2,1)S(1)}, bf16[256,512]{1,0:T(8,128)(2,1)S(1)}, u32[]{:S(2)}, u32[]{:S(2)}) collective-permute-start(bf16[256,512]{1,0:T(8,128)(2,1)S(1)} %get-tuple-element.17), channel_id=1, source_target_pairs={{0,2},{2,4},{4,6},{6,8},{8,10},{10,12},{12,14},{1,3},{3,5},{5,7},{... | collective-permute-start | bytes 786440 | tf_op jit(solution)/shard_map/ppermute | solution.py:261
  5.1 5.6 %collective-permute-start.1 = (bf16[256,512]{1,0:T(8,128)(2,1)S(1)}, bf16[256,512]{1,0:T(8,128)(2,1)S(1)}, u32[]{:S(2)}, u32[]{:S(2)}) collective-permute-start(bf16[256,512]{1,0:T(8,128)(2,1)S(1)} %get-tuple-element.16), channel_id=1, source_target_pairs={{2,0},{4,2},{6,4},{8,6},{10,8},{12,10},{14,12},{3,1},{5,3},{7,5},{... | collective-permute-start | bytes 786440 | tf_op jit(solution)/shard_map/ppermute | solution.py:262
  10.4 1.2 %copy-start.9 = (bf16[256,512]{1,0:T(8,128)(2,1)}, bf16[256,512]{1,0:T(8,128)(2,1)S(1)}, u32[]{:S(2)}) copy-start(bf16[256,512]{1,0:T(8,128)(2,1)S(1)} %collective-permute-done.top_ref) | copy-start | bytes 786436
  10.7 0.9 %copy-start.10 = (bf16[256,512]{1,0:T(8,128)(2,1)}, bf16[256,512]{1,0:T(8,128)(2,1)S(1)}, u32[]{:S(2)}) copy-start(bf16[256,512]{1,0:T(8,128)(2,1)S(1)} %collective-permute-done.1.low_ref) | copy-start | bytes 786436
  30.4 10.1 %collective-permute-start.2 = (bf16[19,1,16,256]{3,2,0,1:T(8,128)(2,1)S(1)}, bf16[19,1,16,256]{3,2,0,1:T(8,128)(2,1)S(1)}, u32[]{:S(2)}, u32[]{:S(2)}) collective-permute-start(bf16[19,1,16,256]{3,2,0,1:T(8,128)(2,1)S(1)} %get-tuple-element.22), channel_id=1, source_target_pairs={{2,10},{4,12},{6,14},{8,0},{3,11},{5,13},{7,15},{9,1},{18,26},{20,... | collective-permute-start | bytes 466952 | tf_op jit(solution)/shard_map/ppermute | solution.py:49
  40.6 10.0 %collective-permute-start.3 = (bf16[19,1,16,256]{3,2,0,1:T(8,128)(2,1)S(1)}, bf16[19,1,16,256]{3,2,0,1:T(8,128)(2,1)S(1)}, u32[]{:S(2)}, u32[]{:S(2)}) collective-permute-start(bf16[19,1,16,256]{3,2,0,1:T(8,128)(2,1)S(1)} %get-tuple-element.20), channel_id=1, source_target_pairs={{0,4},{2,6},{4,0},{10,14},{12,8},{14,10},{1,5},{3,7},{5,1},{11,15}... | collective-permute-start | bytes 466952 | tf_op jit(solution)/shard_map/ppermute | solution.py:55
  45.9 4.7 %collective-permute-start.4 = (bf16[19,1,16,256]{3,2,0,1:T(8,128)(2,1)S(1)}, bf16[19,1,16,256]{3,2,0,1:T(8,128)(2,1)S(1)}, u32[]{:S(2)}, u32[]{:S(2)}) collective-permute-start(bf16[19,1,16,256]{3,2,0,1:T(8,128)(2,1)S(1)} %get-tuple-element.21), channel_id=1, source_target_pairs={{0,4},{8,12},{10,14},{12,8},{1,5},{9,13},{11,15},{13,9},{16,20},{2... | collective-permute-start | bytes 466952 | tf_op jit(solution)/shard_map/ppermute | solution.py:55
  50.9 2.1 %collective-permute-start.5 = (bf16[19,4,16,256]{3,2,1,0:T(8,128)(2,1)S(1)}, bf16[19,4,16,256]{3,2,1,0:T(8,128)(2,1)S(1)}, u32[]{:S(2)}, u32[]{:S(2)}) collective-permute-start(bf16[19,4,16,256]{3,2,1,0:T(8,128)(2,1)S(1)} %bitcast.49), channel_id=1, source_target_pairs={{0,2},{2,0},{4,6},{6,4},{8,10},{10,8},{12,14},{14,12},{1,3},{3,1},... | collective-permute-start | bytes 1867784 | tf_op jit(solution)/shard_map/ppermute | solution.py:49
  53.3 6.1 %collective-permute-start.6 = (bf16[19,10,256]{2,1,0:T(8,128)(2,1)S(1)}, bf16[19,10,256]{2,1,0:T(8,128)(2,1)S(1)}, u32[]{:S(2)}, u32[]{:S(2)}) collective-permute-start(bf16[19,10,256]{2,1,0:T(8,128)(2,1)S(1)} %fusion.28), channel_id=1, source_target_pairs={{0,1},{1,0},{2,3},{3,2},{4,5},{5,4},{6,7},{7,6},{8,9},{9,8},{10,11... | collective-permute-start | bytes 291848 | tf_op jit(solution)/shard_map/ppermute | solution.py:296
